TPU v7x, 32 devices: a whole 2x2x4 slice. The times are simulated.
32 devices in a mesh: grp: 2 (over y), seq: 4 (over z), head: 2 (over x), rep: 2 (over core).
Axes of the slice: x: 2, y: 2, z: 4, core: 2. Of those that a mesh axis runs over, the one named last changes fastest.
Arguments:
- query: bfloat16 [8192, 1280], P(('grp', 'seq', 'rep'), 'head'), parts along dimension 0, may hold values from -22 to 22
- key_value: bfloat16 [2, 8192, 1280], P(None, ('grp', 'seq'), 'head'), parts along dimension 1, may hold values from -6 to 6
- key_blocks: int32 [64, 8], P(('grp', 'seq', 'rep')), parts along dimension 0, may hold values from -1 to 31, as said below
Outputs:
- attended: bfloat16 [8192, 1280], P(('grp', 'seq', 'rep'), 'head'), parts along dimension 0
There are 2 independent parts, one for each index of `grp`. A program takes and returns all parts, laid end to end along the dimension named above; each array names one. Nothing has to cross between parts.
Inputs may be any that keep to these rules, and one draw needn't show every extreme that they name: `key_blocks`: slab q holds blocks q * 8 to (q + 1) * 8 - 1. Entry j = 2 * k + s (k < 4, s in 0, 1) of the row of a query block of slab q names one block of slab p = q + (1 - 2 * s) * 2^(k + 1) if 0 <= p < 4, and is -1 otherwise. The blocks named in column j by all rows of slab q are p * 8 + phase + 4 * c with c in 0 to 1 and one phase in 0 to 3 common to all rows of slab q in that column.
All inputs are finite; a program needn't handle non-finite values.
Results may differ from a plain program's by a relative error of at most 0.0049.
Values may be sent and summed in bfloat16 or wider, within the bound.
No kernel may reach another device: no remote copies, remote signals or barrier semaphores. Data moves between devices by JAX's collectives and lax.ppermute only.
A program may use at most 64 MiB of HBM per device.

v0:
```python
import math

import jax
import jax.numpy as jnp
from jax import lax
from jax.sharding import PartitionSpec as P

HEAD_WIDTH = 128
MASK_BLOCK_SIZE = 128
BLOCKS_PER_FRAME = 4
FAR_STRIDE = 4
LEVELS = 4


def padded(block, sides, width):
    for axis, dim in sides:
        count = lax.axis_size(axis)
        forward = [(i, i + 1) for i in range(count - 1)]
        backward = [(target, source) for source, target in forward]
        low = lax.ppermute(
            lax.slice_in_dim(block, block.shape[dim] - width, None, axis=dim), axis, forward
        )
        high = lax.ppermute(lax.slice_in_dim(block, 0, width, axis=dim), axis, backward)
        block = jnp.concatenate([low, block, high], axis=dim)
    return block


def from_behind(shard, axis, by):
    count = lax.axis_size(axis)
    pairs = [(i, i + by) for i in range(count) if 0 <= i + by < count]
    return lax.ppermute(shard, axis, pairs)


def head_attention(
    query_rows,
    near_pair,
    far_key_pairing,
    near_valid,
    frame_pick,
    frame_valid,
    head_index,
    score_scale,
):
    frame_rows = query_rows.shape[0]
    block_count = frame_pick.shape[0]
    slot_count = frame_pick.shape[1]
    query_head = lax.dynamic_slice_in_dim(query_rows, head_index * HEAD_WIDTH, HEAD_WIDTH, 1)
    near_part = lax.dynamic_slice_in_dim(near_pair, head_index * HEAD_WIDTH, HEAD_WIDTH, 2)
    far_part = lax.dynamic_slice_in_dim(far_key_pairing, head_index * HEAD_WIDTH, HEAD_WIDTH, 4)
    slot_ids = jnp.arange(slot_count, dtype=jnp.int32)
    selected_blocks = far_part[:, slot_ids[None, :], frame_pick]
    selected_blocks = selected_blocks.reshape(
        2, block_count, slot_count * MASK_BLOCK_SIZE, HEAD_WIDTH
    )
    near_scores = (
        jnp.einsum("qd,kd->qk", query_head, near_part[0], preferred_element_type=jnp.float32)
        * score_scale
    )
    near_scores = jnp.where(near_valid[None, :], near_scores, -jnp.inf)
    query_block_list = query_head.reshape(block_count, MASK_BLOCK_SIZE, HEAD_WIDTH)
    far_scores = (
        jnp.einsum(
            "oxg,oug->oxu", query_block_list, selected_blocks[0], preferred_element_type=jnp.float32
        )
        * score_scale
    )
    key_valid = jnp.repeat(frame_valid, MASK_BLOCK_SIZE, axis=1)
    far_scores = jnp.where(key_valid[:, None, :], far_scores, -jnp.inf).reshape(
        frame_rows, slot_count * MASK_BLOCK_SIZE
    )
    row_top = jnp.maximum(jnp.max(near_scores, axis=1), jnp.max(far_scores, axis=1))[:, None]
    near_exp = jnp.exp(near_scores - row_top)
    far_exp = jnp.exp(far_scores - row_top)
    row_total = jnp.sum(near_exp, axis=1, keepdims=True) + jnp.sum(far_exp, axis=1, keepdims=True)
    near_prob = (near_exp / row_total).astype(jnp.bfloat16)
    far_probability = (far_exp / row_total).astype(jnp.bfloat16)
    mixed = jnp.dot(near_prob, near_part[1], preferred_element_type=jnp.float32)
    far_probability = far_probability.reshape(
        block_count, MASK_BLOCK_SIZE, slot_count * MASK_BLOCK_SIZE
    )
    far_blend_output = jnp.einsum(
        "xzf,xfn->xzn", far_probability, selected_blocks[1], preferred_element_type=jnp.float32
    )
    return mixed + far_blend_output.reshape(frame_rows, HEAD_WIDTH)


def per_device(query, key_value, key_blocks):
    frame_rows = BLOCKS_PER_FRAME * MASK_BLOCK_SIZE
    query_count = query.shape[0]
    slab_rows = key_value.shape[1]
    columns = key_value.shape[2]
    head_count = columns // HEAD_WIDTH
    slab_blocks = slab_rows // MASK_BLOCK_SIZE
    slab_frames = slab_rows // frame_rows
    far_count = slab_blocks // FAR_STRIDE
    seq_count = lax.axis_size("seq")
    slab_index = lax.axis_index("seq")
    rep_index = lax.axis_index("rep")
    query_frames = query_count // frame_rows
    all_frames = seq_count * slab_frames
    score_scale = 1.0 / math.sqrt(HEAD_WIDTH)
    extended = padded(key_value, (("seq", 1),), frame_rows)
    phases = jnp.maximum(key_blocks[0], 0) % FAR_STRIDE
    stride_grid = key_value.reshape(2, far_count, FAR_STRIDE, MASK_BLOCK_SIZE, columns)
    received = []
    pick_list = []
    valid_list = []
    for tier_index in range(LEVELS):
        distance = 2 ** (tier_index + 1)
        if distance < seq_count:
            for direction in range(2):
                slot_index = 2 * tier_index + direction
                offset = (1 - 2 * direction) * distance
                wanted = from_behind(phases[slot_index : slot_index + 1], "seq", offset)[0]
                chosen = lax.dynamic_index_in_dim(stride_grid, wanted, 2, keepdims=False)
                received.append(from_behind(chosen, "seq", -offset))
                partner = slab_index + offset
                inside = (partner >= 0) & (partner < seq_count)
                named = key_blocks[:, slot_index]
                pick = (named - partner * slab_blocks - phases[slot_index]) // FAR_STRIDE
                pick_list.append(jnp.clip(pick, 0, far_count - 1))
                valid_list.append((named >= 0) & inside)
    far_stack = jnp.stack(received, 1)
    far_pick = jnp.stack(pick_list, 1)
    far_valid = jnp.stack(valid_list, 1)

    def one_frame(frame_local):
        slab_frame = rep_index * query_frames + frame_local
        near_pair = lax.dynamic_slice_in_dim(extended, slab_frame * frame_rows, 3 * frame_rows, 1)
        near_frame = (
            slab_index * slab_frames
            + slab_frame
            - 1
            + jnp.arange(3 * frame_rows, dtype=jnp.int32) // frame_rows
        )
        near_valid = (near_frame >= 0) & (near_frame < all_frames)

        def one_head(head_index):
            return head_attention(
                query,
                near_pair,
                far_stack,
                near_valid,
                far_pick,
                far_valid,
                head_index,
                score_scale,
            )

        per_head = lax.map(one_head, jnp.arange(head_count, dtype=jnp.int32))
        return jnp.transpose(per_head, (1, 0, 2)).reshape(frame_rows, columns).astype(jnp.bfloat16)

    attended = lax.map(one_frame, jnp.arange(query_frames, dtype=jnp.int32))
    return attended.reshape(query_count, columns)


def solution(mesh):
    in_specs = (
        P(("grp", "seq", "rep"), "head"),
        P(None, ("grp", "seq"), "head"),
        P(("grp", "seq", "rep"), None),
    )
    out_specs = P(("grp", "seq", "rep"), "head")
    return jax.shard_map(
        per_device, mesh=mesh, in_specs=in_specs, out_specs=out_specs, check_vma=False
    )
```

profile of v0, /device:TPU:0, one launch (start us, length us, event | category | flops | bytes accessed | tf_op | source)
XLA Modules:
  0.0 142.5 jit_solution(8483250019488040782)
XLA Ops:
  0.0 0.8 and_select_fusion.2
  0.8 0.7 fusion.31
  1.5 6.5 %collective-permute-start.2 = (s32[1]{0:T(128)}, s32[1]{0:T(128)}, u32[]{:S(2)}, u32[]{:S(2)}) collective-permute-start(s32[1]{0:T(128)} %get-tuple-element.140), channel_id=1, source_target_pairs={{0,8},{4,12},{1,9},{5,13},{2,10},{6,14},{3,11},{7,15},{16,24},{20,... | collective-permute-start | bytes 20 | tf_op jit(solution)/shard_map/ppermute | solution.py:31
  8.0 1.3 collective-permute-start.4
  9.3 3.5 %fusion.29 = (bf16[2,512,640]{2,1,0:T(8,128)(2,1)}, bf16[2,512,640]{2,1,0:T(8,128)(2,1)}) fusion(bf16[2,1024,640]{2,1,0:T(8,128)(2,1)} %param.6), kind=kLoop, calls=%fused_computation.70 | loop fusion | bytes 5242880 | tf_op jit(solution)/shard_map/slice | solution.py:23
  12.8 4.6 %collective-permute-start = (bf16[2,512,640]{2,1,0:T(8,128)(2,1)}, bf16[2,512,640]{2,1,0:T(8,128)(2,1)}, u32[]{:S(2)}, u32[]{:S(2)}) collective-permute-start(bf16[2,512,640]{2,1,0:T(8,128)(2,1)} %get-tuple-element.137), channel_id=1, source_target_pairs={{0,4},{4,8},{8,12},{1,5},{5,9},{9,13},{2,6},{6,10},{10,14},{3,7},{... | collective-permute-start | bytes 3932168 | tf_op jit(solution)/shard_map/ppermute | solution.py:20
  17.3 1.3 collective-permute-start.1
  22.8 1.3 collective-permute-start.3
  24.1 6.0 %collective-permute-start.5 = (bf16[2,2,128,640]{3,2,1,0:T(8,128)(2,1)S(1)}, bf16[2,2,128,640]{3,2,1,0:T(8,128)(2,1)S(1)}, u32[]{:S(2)}, u32[]{:S(2)}) collective-permute-start(bf16[2,2,128,640]{3,2,1,0:T(8,128)(2,1)S(1)} %get-tuple-element.135), channel_id=1, source_target_pairs={{0,8},{4,12},{1,9},{5,13},{2,10},{6,14},{3,11},{7,15},{16,24},{20,... | collective-permute-start | bytes 1966088 | tf_op jit(solution)/shard_map/ppermute | solution.py:31
  30.2 0.7 fusion.24
  30.9 0.6 fusion.25
  31.5 47.0 %collective-permute-done.3 = bf16[2,2,128,640]{3,2,1,0:T(8,128)(2,1)S(1)} collective-permute-done((bf16[2,2,128,640]{3,2,1,0:T(8,128)(2,1)S(1)}, bf16[2,2,128,640]{3,2,1,0:T(8,128)(2,1)S(1)}, u32[]{:S(2)}, u32[]{:S(2)}) %collective-permute-start.3) | collective-permute-done | bytes 655392 | tf_op jit(solution)/shard_map/ppermute | solution.py:31
  78.6 1.2 pad_maximum_fusion
  79.8 6.6 %fusion.23 = bf16[2,1536,640]{2,1,0:T(8,128)(2,1)} fusion(s32[]{:T(128)S(6)} %select_n.59, bf16[2,512,640]{2,1,0:T(8,128)(2,1)} %collective-permute-done, bf16[2,1024,640]{2,1,0:T(8,128)(2,1)S(1)} %copy-done, bf16[2,512,640]{2,1,0:T(8,128)(2,1)} %collective-permute-done.1), kind=kLoop, calls=%fused_computation.48 | loop fusion | flops 11796480 | bytes 9175044 | tf_op jit(solution)/shard_map/concatenate | solution.py:24
  86.4 0.5 iota.14
  86.9 53.5 %while.18 = (s32[]{:T(128)}, bf16[5,512,128]{1,2,0:T(8,128)(2,1)}, s32[5]{0:T(128)}, bf16[512,640]{1,0:T(8,128)(2,1)}, bf16[2,1536,640]{2,1,0:T(8,128)(2,1)}, /*...) while((s32[]{:T(128)}, bf16[5,512,128]{1,2,0:T(8,128)(2,1)}, ...), condition=%wide.region_5.6_spmd.clone, body=%wide.region_0.5_spmd.clone.sunk | while | flops 477251648 | bytes 17746920 | solution.py:150
  86.9 1.3 dynamic_slice.62
  88.9 1.0 constant_dynamic-slice_fusion.5
  90.0 0.7 gather_fusion
  90.8 0.9 constant_dynamic-slice_fusion.6
  91.8 0.3 fusion.52
  92.1 1.7 %fusion.54 = (f32[512]{0:T(512)S(1)}, f32[512,1536]{1,0:T(8,128)S(1)}) fusion(bf16[2,1536,640]{2,1,0:T(8,128)(2,1)} %get-tuple-element.243, s32[]{:T(128)S(6)} %select_n.109, bf16[512,640]{1,0:T(8,128)(2,1)} %get-tuple-element.242, pred[1536]{0:T(1024)(128)(4,1)S(1)} %fusion.53), kind=kOutput, calls=%fused_computation.69.clone.1 | convolution fusion | flops 203685376 | bytes 3674624 | tf_op jit(solution)/shard_map/while/body/eval_jaxpr/while/body/eval_jaxpr/qd,kd->qk/dot_general | solution.py:56
  93.9 0.6 fusion.56
  94.7 0.3 fusion.57
  95.1 1.7 %fusion.58 = bf16[1,512,128]{2,1,0:T(8,128)(2,1)S(1)} fusion(f32[512,128]{1,0:T(8,128)S(1)} %bitcast.103, f32[512,1536]{1,0:T(8,128)S(1)} %get-tuple-element.210, f32[512]{0:T(512)S(1)} %bitcast_add_fusion.5, f32[512]{0:T(512)S(1)} %bitcast_maximum_fusion.5, bf16[2,1536,640]{2,1,0:T(8,128)(2,1)} %get-tuple-element.243, s32[]{:T(128)S(6)} %add.150, ...), kind=kOutput, calls=%fused_computation.11.clone.1 | convolution fusion | flops 203816960 | bytes 3936264 | tf_op jit(solution)/shard_map/while/body/eval_jaxpr/while/body/eval_jaxpr/dot_general | solution.py:77
  96.9 0.7 constant_dynamic-update-slice_fusion.2
  97.6 1.3 dynamic_slice.62
  99.5 1.0 constant_dynamic-slice_fusion.5
  100.7 0.7 gather_fusion
  101.5 0.9 constant_dynamic-slice_fusion.6
  102.8 1.7 %fusion.54 = (f32[512]{0:T(512)S(1)}, f32[512,1536]{1,0:T(8,128)S(1)}) fusion(bf16[2,1536,640]{2,1,0:T(8,128)(2,1)} %get-tuple-element.243, s32[]{:T(128)S(6)} %select_n.109, bf16[512,640]{1,0:T(8,128)(2,1)} %get-tuple-element.242, pred[1536]{0:T(1024)(128)(4,1)S(1)} %fusion.53), kind=kOutput, calls=%fused_computation.69.clone.1 | convolution fusion | flops 203685376 | bytes 3674624 | tf_op jit(solution)/shard_map/while/body/eval_jaxpr/while/body/eval_jaxpr/qd,kd->qk/dot_general | solution.py:56
  104.6 0.6 fusion.56
  105.4 0.3 fusion.57
  105.7 1.7 %fusion.58 = bf16[1,512,128]{2,1,0:T(8,128)(2,1)S(1)} fusion(f32[512,128]{1,0:T(8,128)S(1)} %bitcast.103, f32[512,1536]{1,0:T(8,128)S(1)} %get-tuple-element.210, f32[512]{0:T(512)S(1)} %bitcast_add_fusion.5, f32[512]{0:T(512)S(1)} %bitcast_maximum_fusion.5, bf16[2,1536,640]{2,1,0:T(8,128)(2,1)} %get-tuple-element.243, s32[]{:T(128)S(6)} %add.150, ...), kind=kOutput, calls=%fused_computation.11.clone.1 | convolution fusion | flops 203816960 | bytes 3936264 | tf_op jit(solution)/shard_map/while/body/eval_jaxpr/while/body/eval_jaxpr/dot_general | solution.py:77
  107.6 0.7 constant_dynamic-update-slice_fusion.2
  108.3 1.3 dynamic_slice.62
  110.2 1.0 constant_dynamic-slice_fusion.5
  111.4 0.7 gather_fusion
  112.2 0.9 constant_dynamic-slice_fusion.6
  113.2 0.3 fusion.52
  113.5 1.7 %fusion.54 = (f32[512]{0:T(512)S(1)}, f32[512,1536]{1,0:T(8,128)S(1)}) fusion(bf16[2,1536,640]{2,1,0:T(8,128)(2,1)} %get-tuple-element.243, s32[]{:T(128)S(6)} %select_n.109, bf16[512,640]{1,0:T(8,128)(2,1)} %get-tuple-element.242, pred[1536]{0:T(1024)(128)(4,1)S(1)} %fusion.53), kind=kOutput, calls=%fused_computation.69.clone.1 | convolution fusion | flops 203685376 | bytes 3674624 | tf_op jit(solution)/shard_map/while/body/eval_jaxpr/while/body/eval_jaxpr/qd,kd->qk/dot_general | solution.py:56
  115.2 0.6 fusion.56
  116.1 0.3 fusion.57
  116.4 1.7 %fusion.58 = bf16[1,512,128]{2,1,0:T(8,128)(2,1)S(1)} fusion(f32[512,128]{1,0:T(8,128)S(1)} %bitcast.103, f32[512,1536]{1,0:T(8,128)S(1)} %get-tuple-element.210, f32[512]{0:T(512)S(1)} %bitcast_add_fusion.5, f32[512]{0:T(512)S(1)} %bitcast_maximum_fusion.5, bf16[2,1536,640]{2,1,0:T(8,128)(2,1)} %get-tuple-element.243, s32[]{:T(128)S(6)} %add.150, ...), kind=kOutput, calls=%fused_computation.11.clone.1 | convolution fusion | flops 203816960 | bytes 3936264 | tf_op jit(solution)/shard_map/while/body/eval_jaxpr/while/body/eval_jaxpr/dot_general | solution.py:77
  118.3 0.7 constant_dynamic-update-slice_fusion.2
  119.0 1.3 dynamic_slice.62
  120.9 1.0 constant_dynamic-slice_fusion.5
  122.1 0.7 gather_fusion
  122.9 0.9 constant_dynamic-slice_fusion.6
  124.2 1.7 %fusion.54 = (f32[512]{0:T(512)S(1)}, f32[512,1536]{1,0:T(8,128)S(1)}) fusion(bf16[2,1536,640]{2,1,0:T(8,128)(2,1)} %get-tuple-element.243, s32[]{:T(128)S(6)} %select_n.109, bf16[512,640]{1,0:T(8,128)(2,1)} %get-tuple-element.242, pred[1536]{0:T(1024)(128)(4,1)S(1)} %fusion.53), kind=kOutput, calls=%fused_computation.69.clone.1 | convolution fusion | flops 203685376 | bytes 3674624 | tf_op jit(solution)/shard_map/while/body/eval_jaxpr/while/body/eval_jaxpr/qd,kd->qk/dot_general | solution.py:56
  125.9 0.6 fusion.56
  126.8 0.3 fusion.57
  127.1 1.7 %fusion.58 = bf16[1,512,128]{2,1,0:T(8,128)(2,1)S(1)} fusion(f32[512,128]{1,0:T(8,128)S(1)} %bitcast.103, f32[512,1536]{1,0:T(8,128)S(1)} %get-tuple-element.210, f32[512]{0:T(512)S(1)} %bitcast_add_fusion.5, f32[512]{0:T(512)S(1)} %bitcast_maximum_fusion.5, bf16[2,1536,640]{2,1,0:T(8,128)(2,1)} %get-tuple-element.243, s32[]{:T(128)S(6)} %add.150, ...), kind=kOutput, calls=%fused_computation.11.clone.1 | convolution fusion | flops 203816960 | bytes 3936264 | tf_op jit(solution)/shard_map/while/body/eval_jaxpr/while/body/eval_jaxpr/dot_general | solution.py:77
  129.0 0.7 constant_dynamic-update-slice_fusion.2
  129.7 1.3 dynamic_slice.62
  131.6 1.0 constant_dynamic-slice_fusion.5
  132.8 0.7 gather_fusion
  133.6 0.9 constant_dynamic-slice_fusion.6
  134.9 1.7 %fusion.54 = (f32[512]{0:T(512)S(1)}, f32[512,1536]{1,0:T(8,128)S(1)}) fusion(bf16[2,1536,640]{2,1,0:T(8,128)(2,1)} %get-tuple-element.243, s32[]{:T(128)S(6)} %select_n.109, bf16[512,640]{1,0:T(8,128)(2,1)} %get-tuple-element.242, pred[1536]{0:T(1024)(128)(4,1)S(1)} %fusion.53), kind=kOutput, calls=%fused_computation.69.clone.1 | convolution fusion | flops 203685376 | bytes 3674624 | tf_op jit(solution)/shard_map/while/body/eval_jaxpr/while/body/eval_jaxpr/qd,kd->qk/dot_general | solution.py:56
  136.7 0.6 fusion.56
  137.5 0.3 fusion.57
  137.8 1.7 %fusion.58 = bf16[1,512,128]{2,1,0:T(8,128)(2,1)S(1)} fusion(f32[512,128]{1,0:T(8,128)S(1)} %bitcast.103, f32[512,1536]{1,0:T(8,128)S(1)} %get-tuple-element.210, f32[512]{0:T(512)S(1)} %bitcast_add_fusion.5, f32[512]{0:T(512)S(1)} %bitcast_maximum_fusion.5, bf16[2,1536,640]{2,1,0:T(8,128)(2,1)} %get-tuple-element.243, s32[]{:T(128)S(6)} %add.150, ...), kind=kOutput, calls=%fused_computation.11.clone.1 | convolution fusion | flops 203816960 | bytes 3936264 | tf_op jit(solution)/shard_map/while/body/eval_jaxpr/while/body/eval_jaxpr/dot_general | solution.py:77
  139.7 0.7 constant_dynamic-update-slice_fusion.2
  140.3 2.2 %copy.19 = bf16[512,640]{1,0:T(8,128)(2,1)} copy(bf16[512,640]{0,1:T(8,128)(2,1)} %bitcast.102) | data formatting | bytes 1310720 | tf_op jit(solution)/shard_map/while/body/eval_jaxpr/convert_element_type | solution.py:151
  (85 shorter events, 5.1 us)
Async XLA Ops:
  0.0 18.6 %copy-start.1 = (s32[4,8]{1,0:T(4,128)S(1)}, s32[4,8]{1,0:T(4,128)}, u32[]{:S(2)}) copy-start(s32[4,8]{1,0:T(4,128)} %param.7) | copy-start | bytes 388
  0.0 22.7 %copy-start = (bf16[2,1024,640]{2,1,0:T(8,128)(2,1)S(1)}, bf16[2,1024,640]{2,1,0:T(8,128)(2,1)}, u32[]{:S(2)}) copy-start(bf16[2,1024,640]{2,1,0:T(8,128)(2,1)} %param.6) | copy-start | bytes 7864324
  1.5 17.4 %collective-permute-start.2 = (s32[1]{0:T(128)}, s32[1]{0:T(128)}, u32[]{:S(2)}, u32[]{:S(2)}) collective-permute-start(s32[1]{0:T(128)} %get-tuple-element.140), channel_id=1, source_target_pairs={{0,8},{4,12},{1,9},{5,13},{2,10},{6,14},{3,11},{7,15},{16,24},{20,... | collective-permute-start | bytes 20 | tf_op jit(solution)/shard_map/ppermute | solution.py:31
  8.0 12.3 %collective-permute-start.4 = (s32[1]{0:T(128)}, s32[1]{0:T(128)}, u32[]{:S(2)}, u32[]{:S(2)}) collective-permute-start(s32[1]{0:T(128)} %get-tuple-element.141), channel_id=1, source_target_pairs={{8,0},{12,4},{9,1},{13,5},{10,2},{14,6},{11,3},{15,7},{24,16},{28,... | collective-permute-start | bytes 20 | tf_op jit(solution)/shard_map/ppermute | solution.py:31
  12.8 67.0 %collective-permute-start = (bf16[2,512,640]{2,1,0:T(8,128)(2,1)}, bf16[2,512,640]{2,1,0:T(8,128)(2,1)}, u32[]{:S(2)}, u32[]{:S(2)}) collective-permute-start(bf16[2,512,640]{2,1,0:T(8,128)(2,1)} %get-tuple-element.137), channel_id=1, source_target_pairs={{0,4},{4,8},{8,12},{1,5},{5,9},{9,13},{2,6},{6,10},{10,14},{3,7},{... | collective-permute-start | bytes 3932168 | tf_op jit(solution)/shard_map/ppermute | solution.py:20
  17.3 62.4 %collective-permute-start.1 = (bf16[2,512,640]{2,1,0:T(8,128)(2,1)}, bf16[2,512,640]{2,1,0:T(8,128)(2,1)}, u32[]{:S(2)}, u32[]{:S(2)}) collective-permute-start(bf16[2,512,640]{2,1,0:T(8,128)(2,1)} %get-tuple-element.136), channel_id=1, source_target_pairs={{4,0},{8,4},{12,8},{5,1},{9,5},{13,9},{6,2},{10,6},{14,10},{7,3},{... | collective-permute-start | bytes 3932168 | tf_op jit(solution)/shard_map/ppermute | solution.py:23
  22.8 55.7 %collective-permute-start.3 = (bf16[2,2,128,640]{3,2,1,0:T(8,128)(2,1)S(1)}, bf16[2,2,128,640]{3,2,1,0:T(8,128)(2,1)S(1)}, u32[]{:S(2)}, u32[]{:S(2)}) collective-permute-start(bf16[2,2,128,640]{3,2,1,0:T(8,128)(2,1)S(1)} %get-tuple-element.134), channel_id=1, source_target_pairs={{8,0},{12,4},{9,1},{13,5},{10,2},{14,6},{11,3},{15,7},{24,16},{28,... | collective-permute-start | bytes 1966088 | tf_op jit(solution)/shard_map/ppermute | solution.py:31
  24.1 54.4 %collective-permute-start.5 = (bf16[2,2,128,640]{3,2,1,0:T(8,128)(2,1)S(1)}, bf16[2,2,128,640]{3,2,1,0:T(8,128)(2,1)S(1)}, u32[]{:S(2)}, u32[]{:S(2)}) collective-permute-start(bf16[2,2,128,640]{3,2,1,0:T(8,128)(2,1)S(1)} %get-tuple-element.135), channel_id=1, source_target_pairs={{0,8},{4,12},{1,9},{5,13},{2,10},{6,14},{3,11},{7,15},{16,24},{20,... | collective-permute-start | bytes 1966088 | tf_op jit(solution)/shard_map/ppermute | solution.py:31
where the time goes:
time: 144 us; the launch traced here: 143 us
  waiting for transfers between devices  47 us (33%)
  local copies, waits for them, and re-layouts  31.8 us (22%)
  starting transfers between devices  20.9 us (15%)
  matrix products  20.5 us (14%)
  other arithmetic  14.3 us (10%)
  loops' own time  3.93 us (3%)
  between operations  3.87 us (3%)
    ppermute x4, waiting for transfers between devices, from_behind(): return lax.ppermute(shard, axis, pairs)  47 us
    ppermute x4, starting transfers between devices, from_behind(): return lax.ppermute(shard, axis, pairs)  15.1 us
    dot_general x5, matrix products, head_attention(): jnp.einsum('qd,kd->qk', query_head, near_part[0], preferred_element_type=...  8.74 us
    dot_general x5, matrix products, head_attention(): mixed = jnp.dot(near_prob, near_part[1], preferred_element_type=jnp.float32)  8.61 us
    concatenate x1, other arithmetic, padded(): block = jnp.concatenate([low, block, high], axis=dim)  6.59 us
    dynamic_slice x5, local copies, waits for them, and re-layouts, one_frame(): per_head = lax.map(one_head, jnp.arange(head_count, dtype=jnp.int32))  6.34 us
    dynamic_slice x5, local copies, waits for them, and re-layouts, head_attention(): lax.dynamic_slice_in_dim(far_key_pairing, head_index * HEAD_WIDTH, HEAD_W...  4.87 us
    dynamic_slice x5, local copies, waits for them, and re-layouts, head_attention(): lax.dynamic_slice_in_dim(query_rows, head_index * HEAD_WIDTH, HEAD_WIDTH, 1)  4.6 us
  transfers between devices with their start and end apart: 6, of which 1 were waited for; matrix products, arithmetic and copies ran while one was open for 5% of the time, Pallas kernels for 0%

commit v1 on v0

v1 whole, which is shorter than its diff:
```python
import math

import jax
import jax.numpy as jnp
from jax import lax
from jax.sharding import PartitionSpec as P

HEAD_WIDTH = 128
MASK_BLOCK_SIZE = 128
BLOCKS_PER_FRAME = 4
FAR_STRIDE = 4
LEVELS = 4


def from_behind(shard, axis, by):
    count = lax.axis_size(axis)
    pairs = [(i, i + by) for i in range(count) if 0 <= i + by < count]
    return lax.ppermute(shard, axis, pairs)


def halo_frame(key_value, frame_rows, seq_count, rep_count, rep_index):
    slab_rows = key_value.shape[1]
    start = jnp.where(rep_index == rep_count - 1, slab_rows - frame_rows, 0)
    payload = lax.dynamic_slice_in_dim(key_value, start, frame_rows, 1)
    pairs = []
    for s in range(seq_count - 1):
        pairs.append((s * rep_count + rep_count - 1, (s + 1) * rep_count))
    for s in range(1, seq_count):
        pairs.append((s * rep_count, (s - 1) * rep_count + rep_count - 1))
    return lax.ppermute(payload, ("seq", "rep"), pairs)


def per_device(query, key_value, key_blocks):
    frame_rows = BLOCKS_PER_FRAME * MASK_BLOCK_SIZE
    query_count = query.shape[0]
    slab_rows = key_value.shape[1]
    columns = key_value.shape[2]
    head_count = columns // HEAD_WIDTH
    slab_blocks = slab_rows // MASK_BLOCK_SIZE
    slab_frames = slab_rows // frame_rows
    far_count = slab_blocks // FAR_STRIDE
    seq_count = lax.axis_size("seq")
    rep_count = lax.axis_size("rep")
    slab_index = lax.axis_index("seq")
    rep_index = lax.axis_index("rep")
    query_frames = query_count // frame_rows
    query_blocks = query_count // MASK_BLOCK_SIZE
    score_scale = 1.0 / math.sqrt(HEAD_WIDTH)
    assert rep_count >= 2 and query_frames * rep_count == slab_frames
    assert far_count % rep_count == 0
    far_share = far_count // rep_count

    halo = halo_frame(key_value, frame_rows, seq_count, rep_count, rep_index)

    phases = jnp.maximum(key_blocks[0], 0) % FAR_STRIDE
    stride_grid = key_value.reshape(2, far_count, FAR_STRIDE, MASK_BLOCK_SIZE, columns)
    share_grid = lax.dynamic_slice_in_dim(stride_grid, rep_index * far_share, far_share, 1)
    received = []
    pick_list = []
    valid_list = []
    for tier_index in range(LEVELS):
        distance = 2 ** (tier_index + 1)
        if distance < seq_count:
            for direction in range(2):
                slot_index = 2 * tier_index + direction
                offset = (1 - 2 * direction) * distance
                wanted = from_behind(phases[slot_index : slot_index + 1], "seq", offset)[0]
                chosen = lax.dynamic_index_in_dim(share_grid, wanted, 2, keepdims=False)
                received.append(from_behind(chosen, "seq", -offset))
                partner = slab_index + offset
                inside = (partner >= 0) & (partner < seq_count)
                named = key_blocks[:, slot_index]
                pick = (named - partner * slab_blocks - phases[slot_index]) // FAR_STRIDE
                pick_list.append(pick)
                valid_list.append((named >= 0) & inside)
    slot_count = len(received)
    mine = jnp.stack(received, 1)
    parts = [mine]
    sources = [rep_index]
    for k in range(1, rep_count):
        shift = [(r, (r + k) % rep_count) for r in range(rep_count)]
        parts.append(lax.ppermute(mine, "rep", shift))
        sources.append((rep_index - k) % rep_count)
    far_pair = jnp.stack(parts, 2).reshape(2, slot_count * far_count * MASK_BLOCK_SIZE, columns)
    far_pick = jnp.stack(pick_list, 1)
    far_valid = jnp.stack(valid_list, 1)
    share_ids = jnp.arange(far_share, dtype=jnp.int32)
    candidates = (jnp.stack(sources)[:, None] * far_share + share_ids[None, :]).reshape(far_count)
    far_mask = far_valid[:, :, None] & (far_pick[:, :, None] == candidates[None, None, :])
    far_mask = jnp.repeat(far_mask.reshape(query_blocks, slot_count * far_count), MASK_BLOCK_SIZE, axis=1)
    far_mask = jnp.repeat(far_mask, MASK_BLOCK_SIZE, axis=0)

    query_heads = query.reshape(query_count, head_count, HEAD_WIDTH)
    own_pair = key_value.reshape(2, slab_rows, head_count, HEAD_WIDTH)

    own_scores = (
        jnp.einsum("qhd,khd->hqk", query_heads, own_pair[0], preferred_element_type=jnp.float32)
        * score_scale
    )
    own_top = jnp.max(own_scores, axis=2, keepdims=True)
    own_exp = jnp.exp(own_scores - own_top)
    own_total = jnp.sum(own_exp, axis=2, keepdims=True)

    halo_pair = halo.reshape(2, frame_rows, head_count, HEAD_WIDTH)
    far_heads = far_pair.reshape(2, far_pair.shape[1], head_count, HEAD_WIDTH)
    halo_valid = ((rep_index == 0) & (slab_index > 0)) | (
        (rep_index == rep_count - 1) & (slab_index < seq_count - 1)
    )
    halo_scores = (
        jnp.einsum("qhd,khd->hqk", query_heads, halo_pair[0], preferred_element_type=jnp.float32)
        * score_scale
    )
    halo_scores = jnp.where(halo_valid, halo_scores, -jnp.inf)
    far_scores = (
        jnp.einsum("qhd,khd->hqk", query_heads, far_heads[0], preferred_element_type=jnp.float32)
        * score_scale
    )
    far_scores = jnp.where(far_mask[None], far_scores, -jnp.inf)
    row_top = jnp.maximum(
        own_top,
        jnp.maximum(
            jnp.max(halo_scores, axis=2, keepdims=True), jnp.max(far_scores, axis=2, keepdims=True)
        ),
    )
    own_factor = jnp.exp(own_top - row_top)
    halo_exp = jnp.exp(halo_scores - row_top)
    far_exp = jnp.exp(far_scores - row_top)
    row_total = (
        own_total * own_factor
        + jnp.sum(halo_exp, axis=2, keepdims=True)
        + jnp.sum(far_exp, axis=2, keepdims=True)
    )
    own_prob = (own_exp * (own_factor / row_total)).astype(jnp.bfloat16)
    halo_prob = (halo_exp / row_total).astype(jnp.bfloat16)
    far_prob = (far_exp / row_total).astype(jnp.bfloat16)
    mixed = jnp.einsum("hqk,khd->qhd", own_prob, own_pair[1], preferred_element_type=jnp.float32)
    mixed = mixed + jnp.einsum(
        "hqk,khd->qhd", halo_prob, halo_pair[1], preferred_element_type=jnp.float32
    )
    mixed = mixed + jnp.einsum(
        "hqk,khd->qhd", far_prob, far_heads[1], preferred_element_type=jnp.float32
    )
    return mixed.reshape(query_count, columns).astype(jnp.bfloat16)


def solution(mesh):
    in_specs = (
        P(("grp", "seq", "rep"), "head"),
        P(None, ("grp", "seq"), "head"),
        P(("grp", "seq", "rep"), None),
    )
    out_specs = P(("grp", "seq", "rep"), "head")
    return jax.shard_map(
        per_device, mesh=mesh, in_specs=in_specs, out_specs=out_specs, check_vma=False
    )
```

time: 144 us -> 82.8 us (0.57)
  waiting for transfers between devices: 47 us -> 10.9 us
  local copies, waits for them, and re-layouts: 31.8 us -> 21.8 us
  matrix products: 20.5 us -> 16 us
  loops' own time: 3.93 us -> 0 us
  starting transfers between devices: 20.9 us -> 17 us
    ppermute x4, waiting for transfers between devices: 47 us -> 10.9 us  [from_behind(): return lax.ppermute(shard, axis, pairs)]
    dynamic_slice x15 -> x1, local copies, waits for them, and re-layouts: 15.8 us -> 2.52 us  [halo_frame(): payload = lax.dynamic_slice_in_dim(key_value, start, frame_rows, 1)]
    unnamed x6 -> x20, local copies, waits for them, and re-layouts: 0.19 us -> 7.67 us
    concatenate x6 -> x0, other arithmetic: 6.63 us -> none  [the longest x1 6.59 us: padded(): block = jnp.concatenate([low, block, high], axis=dim)]
    dot_general x20 -> x6, matrix products: 20.5 us -> 16 us  [the longest x1 6.98 us: per_device(): jnp.einsum('qhd,khd->hqk', query_heads, own_pair[0], preferred_element_ty...]
    reduce_sum x10 -> x2, other arithmetic: 4.13 us -> 8.11 us  [the longest x1 5.94 us: per_device(): own_total = jnp.sum(own_exp, axis=2, keepdims=True)]
    ppermute x2, starting transfers between devices: 5.86 us -> 1.89 us  [the longest x1 1.77 us: halo_frame(): return lax.ppermute(payload, ('seq', 'rep'), pairs)]
    another operation x1 -> x0, loops' own time: 3.93 us -> none  [one_frame(): per_head = lax.map(one_head, jnp.arange(head_count, dtype=jnp.int32))]
  transfers between devices with their start and end apart: 6 -> 6, of which waited for: 1 -> 1; matrix products, arithmetic and copies ran while one was open for 5% -> 43% of each run, Pallas kernels for 0% -> 0%
where the time goes in v1:
time: 82.8 us; the launch traced here: 82.3 us
  local copies, waits for them, and re-layouts  21.8 us (26%)
  starting transfers between devices  17 us (21%)
  matrix products  16 us (19%)
  other arithmetic  12.9 us (16%)
  waiting for transfers between devices  10.9 us (13%)
  between operations  3.65 us (4%)
    ppermute x4, starting transfers between devices, from_behind(): return lax.ppermute(shard, axis, pairs)  15.1 us
    ppermute x4, waiting for transfers between devices, from_behind(): return lax.ppermute(shard, axis, pairs)  10.9 us
    unnamed x20, local copies, waits for them, and re-layouts  7.67 us
    dot_general x1, matrix products, per_device(): jnp.einsum('qhd,khd->hqk', query_heads, own_pair[0], preferred_element_ty...  6.98 us
    reduce_sum x1, other arithmetic, per_device(): own_total = jnp.sum(own_exp, axis=2, keepdims=True)  5.94 us
    dot_general x1, matrix products, per_device(): jnp.einsum('hqk,khd->qhd', own_prob, own_pair[1], preferred_element_type=...  3.69 us
    slice x2, local copies, waits for them, and re-layouts, per_device(): own_pair[1]  3.22 us
    dynamic_slice x1, local copies, waits for them, and re-layouts, halo_frame(): payload = lax.dynamic_slice_in_dim(key_value, start, frame_rows, 1)  2.52 us
  transfers between devices with their start and end apart: 6, of which 1 were waited for; matrix products, arithmetic and copies ran while one was open for 43% of the time, Pallas kernels for 0%

profile of v1, /device:TPU:0, one launch (start us, length us, event | category | flops | bytes accessed | tf_op | source)
XLA Modules:
  0.0 82.3 jit_solution(690039797342457625)
XLA Ops:
  0.0 0.0 copy-start
  0.0 0.8 %and_select_fusion = s32[8]{0:T(128)S(1)} fusion(s32[4,8]{1,0:T(4,128)} %param.5), kind=kLoop, calls=%fused_computation.55 | loop fusion | flops 56 | bytes 64 | tf_op jit(solution)/shard_map/jit(remainder)/select_n | solution.py:55
  0.8 0.6 fusion.28
  1.5 6.4 %collective-permute-start.1 = (s32[1]{0:T(128)}, s32[1]{0:T(128)}, u32[]{:S(2)}, u32[]{:S(2)}) collective-permute-start(s32[1]{0:T(128)} %get-tuple-element.23), channel_id=1, source_target_pairs={{0,8},{4,12},{1,9},{5,13},{2,10},{6,14},{3,11},{7,15},{16,24},{20,... | collective-permute-start | bytes 20 | tf_op jit(solution)/shard_map/ppermute | solution.py:18
  7.9 1.3 %collective-permute-start.3 = (s32[1]{0:T(128)}, s32[1]{0:T(128)}, u32[]{:S(2)}, u32[]{:S(2)}) collective-permute-start(s32[1]{0:T(128)} %get-tuple-element.24), channel_id=1, source_target_pairs={{8,0},{12,4},{9,1},{13,5},{10,2},{14,6},{11,3},{15,7},{24,16},{28,... | collective-permute-start | bytes 20 | tf_op jit(solution)/shard_map/ppermute | solution.py:18
  9.2 0.0 copy-start.4
  9.2 2.5 %constant_dynamic-slice_fusion = bf16[2,512,640]{2,1,0:T(8,128)(2,1)} fusion(bf16[2,1024,640]{2,1,0:T(8,128)(2,1)} %param.4, s32[]{:T(128)S(6)} %select_n.60), kind=kLoop, calls=%fused_computation.58 | loop fusion | bytes 2621444 | tf_op jit(solution)/shard_map/dynamic_slice | solution.py:24
  11.7 2.4 %copy.50 = bf16[2,512,640]{1,2,0:T(8,128)(2,1)} copy(bf16[2,512,640]{2,1,0:T(8,128)(2,1)} %constant_dynamic-slice_fusion) | data formatting | bytes 2621440
  14.1 1.8 %collective-permute-start = (bf16[2,512,640]{1,2,0:T(8,128)(2,1)}, bf16[2,512,640]{1,2,0:T(8,128)(2,1)}, u32[]{:S(2)}, u32[]{:S(2)}) collective-permute-start(bf16[2,512,640]{1,2,0:T(8,128)(2,1)} %copy.50), channel_id=1, source_target_pairs={{1,4},{5,8},{9,12},{4,1},{8,5},{12,9},{3,6},{7,10},{11,14},{6,3},{... | collective-permute-start | bytes 3932168 | tf_op jit(solution)/shard_map/ppermute | solution.py:30
  15.9 0.0 copy-done
  15.9 1.7 %fusion.26 = (bf16[1,1024,640]{2,1,0:T(8,128)(2,1)}, bf16[1,1024,640]{2,1,0:T(8,128)(2,1)}) fusion(bf16[2,1024,640]{2,1,0:T(8,128)(2,1)S(1)} %copy-done), kind=kLoop, calls=%fused_computation.66 | loop fusion | bytes 5242880 | tf_op jit(solution)/shard_map/slice | solution.py:136
  17.6 0.0 copy-done.4
  17.6 0.1 compare_and_fusion.2
  17.7 0.1 pad_add_fusion.1
  17.8 0.1 copy.26
  17.9 1.4 %add_select_fusion.1 = (s32[4,1]{1,0:T(4,128)S(1)}, s32[4,1]{1,0:T(4,128)S(1)}) fusion(s32[4,8]{1,0:T(4,128)S(1)} %copy-done.4, s32[]{:T(128)} %bitcast.5, s32[]{:T(128)S(6)} %mul.44, s32[]{:T(128)} %bitcast.6, s32[]{:T(128)S(6)} %mul.45), kind=kLoop, calls=%fused_computation.40 | loop fusion | flops 136 | bytes 80 | tf_op jit(solution)/shard_map/jit(floor_divide)/jit(_where)/select_n | solution.py:73
  19.3 0.1 pad_add_fusion
  19.4 0.1 copy.27
  19.5 0.1 pad_add_fusion.2
  19.6 0.1 eq.36
  19.6 1.3 %copy.18 = bf16[512,640]{0,1:T(8,128)(2,1)S(1)} copy(bf16[512,640]{1,0:T(8,128)(2,1)} %param.3) | data formatting | bytes 1310720 | tf_op args[0]
  21.0 2.5 %copy.49 = bf16[1,1024,640]{1,2,0:T(8,128)(2,1)} copy(bf16[1,1024,640]{2,1,0:T(8,128)(2,1)} %get-tuple-element.10) | data formatting | bytes 2621440
  23.5 0.0 collective-permute-done.1
  24.6 0.0 collective-permute-done.3
  26.8 0.1 dynamic-slice_bitcast_fusion.1
  26.9 6.1 %collective-permute-start.4 = (bf16[2,1,128,640]{3,2,0,1:T(8,128)(2,1)S(1)}, bf16[2,1,128,640]{3,2,0,1:T(8,128)(2,1)S(1)}, u32[]{:S(2)}, u32[]{:S(2)}) collective-permute-start(bf16[2,1,128,640]{3,2,0,1:T(8,128)(2,1)S(1)} %get-tuple-element.12), channel_id=1, source_target_pairs={{0,8},{4,12},{1,9},{5,13},{2,10},{6,14},{3,11},{7,15},{16,24},{20,... | collective-permute-start | bytes 983048 | tf_op jit(solution)/shard_map/ppermute | solution.py:18
  33.0 1.3 %collective-permute-start.2 = (bf16[2,1,128,640]{3,2,0,1:T(8,128)(2,1)S(1)}, bf16[2,1,128,640]{3,2,0,1:T(8,128)(2,1)S(1)}, u32[]{:S(2)}, u32[]{:S(2)}) collective-permute-start(bf16[2,1,128,640]{3,2,0,1:T(8,128)(2,1)S(1)} %get-tuple-element.11), channel_id=1, source_target_pairs={{8,0},{12,4},{9,1},{13,5},{10,2},{14,6},{11,3},{15,7},{24,16},{28,... | collective-permute-start | bytes 983048 | tf_op jit(solution)/shard_map/ppermute | solution.py:18
  34.3 0.0 copy-start.1
  34.4 7.0 %multiply_reduce_fusion = (f32[5,512]{1,0:T(8,128)S(1)}, f32[5,512,1024]{2,1,0:T(8,128)}) fusion(bf16[512,5,128]{0,2,1:T(8,128)(2,1)S(1)} %bitcast.94, bf16[1024,5,128]{0,2,1:T(8,128)(2,1)} %bitcast.98), kind=kOutput, calls=%fused_computation.2 | convolution fusion | flops 676328960 | bytes 12462080 | tf_op jit(solution)/shard_map/qhd,khd->hqk/dot_general | solution.py:97
  41.3 0.0 collective-permute-done.4
  41.3 10.9 %collective-permute-done.2 = bf16[2,1,128,640]{3,2,0,1:T(8,128)(2,1)S(1)} collective-permute-done((bf16[2,1,128,640]{3,2,0,1:T(8,128)(2,1)S(1)}, bf16[2,1,128,640]{3,2,0,1:T(8,128)(2,1)S(1)}, u32[]{:S(2)}, u32[]{:S(2)}) %collective-permute-start.2) | collective-permute-done | bytes 327712 | tf_op jit(solution)/shard_map/ppermute | solution.py:18
  52.3 0.9 %fusion.25 = (bf16[2,2,1,1,128,640]{5,4,0,1,3,2:T(8,128)(2,1)S(1)}, bf16[2,2,1,128,640]{4,3,0,2,1:T(8,128)(2,1)}) fusion(bf16[2,1,1,128,640]{4,3,0,2,1:T(8,128)(2,1)S(1)} %bitcast.107, bf16[2,1,1,128,640]{4,3,0,2,1:T(8,128)(2,1)S(1)} %bitcast.108), kind=kLoop, calls=%fused_computation.65 | loop fusion | flops 327680 | bytes 1966080 | tf_op jit(solution)/shard_map/stack | solution.py:84
  53.2 0.1 collective-permute-start.5
  53.3 0.1 compare_and_fusion
  53.4 1.8 %broadcast_in_dim.32 = pred[4,128,512]{1,0,2:T(4,128)(4,1)S(1)} broadcast(pred[4,512]{0,1:T(8,128)(4,1)S(1)} %bitcast.109), dimensions={0,2} | broadcast | bytes 264192 | tf_op jit(solution)/shard_map/broadcast_in_dim | solution.py:91
  55.2 0.1 copy.58
  55.4 0.0 copy-done.1
  55.4 1.5 %copy.35 = bf16[1,1024,640]{1,2,0:T(8,128)(2,1)} copy(bf16[1,1024,640]{2,1,0:T(8,128)(2,1)S(1)} %copy-done.1) | data formatting | bytes 2621440 | tf_op jit(solution)/shard_map/slice | solution.py:136
  56.9 5.9 %fusion = f32[5,512]{1,0:T(8,128)S(1)} fusion(f32[5,512,1024]{2,1,0:T(8,128)} %get-tuple-element.26, f32[5,512]{1,0:T(8,128)S(1)} %get-tuple-element.25), kind=kLoop, calls=%fused_computation.3 | loop fusion | flops 7861760 | bytes 10506240 | tf_op jit(solution)/shard_map/reduce_sum | solution.py:102
  62.8 0.0 collective-permute-done.5
  62.8 1.2 %fusion.14 = (bf16[1,2,2,1,128,640]{5,4,0,1,3,2:T(8,128)(2,1)S(1)}, bf16[1,2,2,1,128,640]{5,4,0,1,3,2:T(8,128)(2,1)S(1)}) fusion(bf16[2,2,1,1,128,640]{5,4,0,1,3,2:T(8,128)(2,1)S(1)} %get-tuple-element.17, bf16[2,2,1,1,128,640]{5,4,0,1,3,2:T(8,128)(2,1)} %bitcast.19), kind=kLoop, calls=%fused_computation.27 | loop fusion | flops 655360 | bytes 2621440 | tf_op jit(solution)/shard_map/stack | solution.py:84
  64.0 0.9 %copy.37 = bf16[1,2,2,1,128,640]{4,2,1,5,3,0:T(2,128)(2,1)S(1)} copy(bf16[1,2,2,1,128,640]{5,4,0,1,3,2:T(8,128)(2,1)S(1)} %get-tuple-element.16) | data formatting | bytes 1310720 | tf_op jit(solution)/shard_map/slice | solution.py:141
  65.0 1.1 %squeeze.51 = bf16[512,5,128]{0,2,1:T(8,128)(2,1)} reshape(bf16[1,2,2,1,128,640]{4,2,1,5,3,0:T(2,128)(2,1)S(1)} %copy.37) | data formatting | bytes 1310720 | tf_op jit(solution)/shard_map/squeeze | solution.py:141
  66.1 0.9 %copy.32 = bf16[1,2,2,1,128,640]{4,2,1,5,3,0:T(2,128)(2,1)S(1)} copy(bf16[1,2,2,1,128,640]{5,4,0,1,3,2:T(8,128)(2,1)S(1)} %get-tuple-element.15) | data formatting | bytes 1310720 | tf_op jit(solution)/shard_map/slice | solution.py:115
  67.0 0.2 squeeze.48
  67.2 1.1 %fusion.5 = (f32[5,512]{1,0:T(8,128)S(1)}, f32[5,512,512]{2,1,0:T(8,128)S(1)}) fusion(pred[512,512]{0,1:T(8,128)(4,1)S(1)} %bitcast.100, bf16[512,5,128]{0,2,1:T(8,128)(2,1)S(1)} %squeeze.48, bf16[512,5,128]{0,2,1:T(8,128)(2,1)S(1)} %bitcast.95), kind=kOutput, calls=%fused_computation.15 | convolution fusion | flops 339473920 | bytes 6825984 | tf_op jit(solution)/shard_map/qhd,khd->hqk/dot_general | solution.py:115
  68.3 0.0 collective-permute-done
  68.3 1.4 %fusion.27 = (bf16[1,512,640]{1,2,0:T(8,128)(2,1)S(1)}, bf16[1,512,640]{1,2,0:T(8,128)(2,1)S(1)}) fusion(bf16[2,512,640]{1,2,0:T(8,128)(2,1)} %collective-permute-done), kind=kLoop, calls=%fused_computation.67 | loop fusion | bytes 2621440 | tf_op jit(solution)/shard_map/slice | solution.py:138
  69.7 0.9 %bitcast_reduce_fusion = (f32[5,512]{1,0:T(8,128)S(1)}, f32[5,512,512]{2,1,0:T(8,128)S(1)}) fusion(pred[]{:T(512)S(6)} %or.3, bf16[512,5,128]{0,2,1:T(8,128)(2,1)S(1)} %bitcast.99, bf16[512,5,128]{0,2,1:T(8,128)(2,1)S(1)} %bitcast.96), kind=kOutput, calls=%fused_computation.6 | convolution fusion | flops 339473920 | bytes 6563841 | tf_op jit(solution)/shard_map/qhd,khd->hqk/dot_general | solution.py:110
  70.6 0.0 copy-start.3
  70.6 0.0 slice-start
  70.6 2.2 %fusion.4 = (f32[5,512]{1,0:T(8,128)S(1)}, f32[5,512]{1,0:T(8,128)S(1)}) fusion(f32[5,512,512]{2,1,0:T(8,128)S(1)} %get-tuple-element.28, f32[5,512]{1,0:T(8,128)S(1)} %maximum_maximum_fusion, pred[]{:T(512)S(6)} %or.3, f32[5,512,512]{2,1,0:T(8,128)S(1)} %get-tuple-element.30, pred[512,512]{0,1:T(8,128)(4,1)S(1)} %bitcast.101), kind=kLoop, calls=%fused_computation.14 | loop fusion | flops 10480640 | bytes 10778625 | tf_op jit(solution)/shard_map/reduce_sum | solution.py:130
  72.8 0.0 copy-done.3
  72.9 0.0 slice-start.1
  72.9 0.0 slice-start.2
  72.9 0.0 copy-start.2
  72.9 1.8 %fusion.8 = f32[512,5,128]{0,2,1:T(8,128)S(1)} fusion(bf16[512,5,128]{0,2,1:T(8,128)(2,1)S(1)} %copy-done.3, f32[5,512,512]{2,1,0:T(8,128)S(1)} %get-tuple-element.30, f32[5,512]{1,0:T(8,128)S(1)} %get-tuple-element.8, f32[5,512]{1,0:T(8,128)S(1)} %maximum_maximum_fusion, pred[512,512]{0,1:T(8,128)(4,1)S(1)} %bitcast.102), kind=kOutput, calls=%fused_computation.18 | convolution fusion | flops 342097920 | bytes 7491584 | tf_op jit(solution)/shard_map/hqk,khd->qhd/dot_general | solution.py:140
  74.7 0.0 slice-done
  74.7 0.4 slice-done.1
  75.1 0.6 slice-done.2
  75.7 0.3 copy-done.2
  76.0 3.7 %fusion.10 = f32[512,5,128]{0,2,1:T(8,128)S(1)} fusion(bf16[1024,5,128]{0,2,1:T(8,128)(2,1)S(1)} %bitcast.103, f32[5,512,1024]{2,1,0:T(8,128)S(1)} %bitcast.93, f32[5,512]{1,0:T(8,128)S(1)} %get-tuple-element.7, f32[5,512]{1,0:T(8,128)S(1)} %get-tuple-element.25), kind=kOutput, calls=%fused_computation.20 | convolution fusion | flops 681574400 | bytes 13127680 | tf_op jit(solution)/shard_map/hqk,khd->qhd/dot_general | solution.py:136
  79.7 1.5 %fusion.13 = bf16[512,5,128]{0,2,1:T(8,128)(2,1)S(1)} fusion(f32[512,5,128]{0,2,1:T(8,128)S(1)} %fusion.8, f32[512,5,128]{0,2,1:T(8,128)S(1)} %fusion.10, bf16[512,5,128]{0,2,1:T(8,128)(2,1)S(1)} %bitcast.105, f32[5,512,512]{2,1,0:T(8,128)S(1)} %get-tuple-element.28, f32[5,512]{1,0:T(8,128)S(1)} %get-tuple-element.8, f32[5,512]{1,0:T(8,128)S(1)} %maximum_maximum_fusion, ...), kind=kOutput, calls=%fused_computation.23 | convolution fusion | flops 343080960 | bytes 9195521 | tf_op jit(solution)/shard_map/hqk,khd->qhd/dot_general | solution.py:137
  81.2 1.1 %copy.39 = bf16[512,640]{1,0:T(8,128)(2,1)} copy(bf16[512,640]{0,1:T(8,128)(2,1)S(1)} %bitcast.106) | data formatting | bytes 1310720 | tf_op jit(solution)/shard_map/convert_element_type | solution.py:143
  (8 shorter events, 0.1 us)
Async XLA Ops:
  0.0 15.9 %copy-start = (bf16[2,1024,640]{2,1,0:T(8,128)(2,1)S(1)}, bf16[2,1024,640]{2,1,0:T(8,128)(2,1)}, u32[]{:S(2)}) copy-start(bf16[2,1024,640]{2,1,0:T(8,128)(2,1)} %param.4) | copy-start | bytes 7864324
  1.5 22.0 %collective-permute-start.1 = (s32[1]{0:T(128)}, s32[1]{0:T(128)}, u32[]{:S(2)}, u32[]{:S(2)}) collective-permute-start(s32[1]{0:T(128)} %get-tuple-element.23), channel_id=1, source_target_pairs={{0,8},{4,12},{1,9},{5,13},{2,10},{6,14},{3,11},{7,15},{16,24},{20,... | collective-permute-start | bytes 20 | tf_op jit(solution)/shard_map/ppermute | solution.py:18
  7.9 16.7 %collective-permute-start.3 = (s32[1]{0:T(128)}, s32[1]{0:T(128)}, u32[]{:S(2)}, u32[]{:S(2)}) collective-permute-start(s32[1]{0:T(128)} %get-tuple-element.24), channel_id=1, source_target_pairs={{8,0},{12,4},{9,1},{13,5},{10,2},{14,6},{11,3},{15,7},{24,16},{28,... | collective-permute-start | bytes 20 | tf_op jit(solution)/shard_map/ppermute | solution.py:18
  9.2 8.5 %copy-start.4 = (s32[4,8]{1,0:T(4,128)S(1)}, s32[4,8]{1,0:T(4,128)}, u32[]{:S(2)}) copy-start(s32[4,8]{1,0:T(4,128)} %param.5) | copy-start | bytes 388
  14.1 54.2 %collective-permute-start = (bf16[2,512,640]{1,2,0:T(8,128)(2,1)}, bf16[2,512,640]{1,2,0:T(8,128)(2,1)}, u32[]{:S(2)}, u32[]{:S(2)}) collective-permute-start(bf16[2,512,640]{1,2,0:T(8,128)(2,1)} %copy.50), channel_id=1, source_target_pairs={{1,4},{5,8},{9,12},{4,1},{8,5},{12,9},{3,6},{7,10},{11,14},{6,3},{... | collective-permute-start | bytes 3932168 | tf_op jit(solution)/shard_map/ppermute | solution.py:30
  26.9 14.4 %collective-permute-start.4 = (bf16[2,1,128,640]{3,2,0,1:T(8,128)(2,1)S(1)}, bf16[2,1,128,640]{3,2,0,1:T(8,128)(2,1)S(1)}, u32[]{:S(2)}, u32[]{:S(2)}) collective-permute-start(bf16[2,1,128,640]{3,2,0,1:T(8,128)(2,1)S(1)} %get-tuple-element.12), channel_id=1, source_target_pairs={{0,8},{4,12},{1,9},{5,13},{2,10},{6,14},{3,11},{7,15},{16,24},{20,... | collective-permute-start | bytes 983048 | tf_op jit(solution)/shard_map/ppermute | solution.py:18
  33.0 19.2 %collective-permute-start.2 = (bf16[2,1,128,640]{3,2,0,1:T(8,128)(2,1)S(1)}, bf16[2,1,128,640]{3,2,0,1:T(8,128)(2,1)S(1)}, u32[]{:S(2)}, u32[]{:S(2)}) collective-permute-start(bf16[2,1,128,640]{3,2,0,1:T(8,128)(2,1)S(1)} %get-tuple-element.11), channel_id=1, source_target_pairs={{8,0},{12,4},{9,1},{13,5},{10,2},{14,6},{11,3},{15,7},{24,16},{28,... | collective-permute-start | bytes 983048 | tf_op jit(solution)/shard_map/ppermute | solution.py:18
  34.3 21.0 %copy-start.1 = (bf16[1,1024,640]{2,1,0:T(8,128)(2,1)S(1)}, bf16[1,1024,640]{2,1,0:T(8,128)(2,1)}, u32[]{:S(2)}) copy-start(bf16[1,1024,640]{2,1,0:T(8,128)(2,1)} %get-tuple-element.9) | copy-start | bytes 3932164
  53.2 9.6 %collective-permute-start.5 = (bf16[2,2,1,128,640]{4,3,0,2,1:T(8,128)(2,1)}, bf16[2,2,1,128,640]{4,3,0,2,1:T(8,128)(2,1)}, u32[]{:S(2)}, u32[]{:S(2)}) collective-permute-start(bf16[2,2,1,128,640]{4,3,0,2,1:T(8,128)(2,1)} %get-tuple-element.18), channel_id=1, source_target_pairs={{0,1},{1,0},{2,3},{3,2},{4,5},{5,4},{6,7},{7,6},{8,9},{9,8},{10,11... | collective-permute-start | bytes 1966088 | tf_op jit(solution)/shard_map/ppermute | solution.py:82
  70.6 2.2 %copy-start.3 = (bf16[512,5,128]{0,2,1:T(8,128)(2,1)S(1)}, bf16[512,5,128]{0,2,1:T(8,128)(2,1)}, u32[]{:S(2)}) copy-start(bf16[512,5,128]{0,2,1:T(8,128)(2,1)} %squeeze.51) | copy-start | bytes 1966084
  70.6 4.1 %slice-start = ((s8[10485760]{0:T(1024)(128)(4,1)}), s8[4194304]{0:T(1024)(128)(4,1)S(1)}, s32[]{:S(2)}) async-start(s8[10485760]{0:T(1024)(128)(4,1)} %bitcast.92), calls=%async_computation | async-start | bytes 8388608
  72.9 2.2 %slice-start.1 = ((s8[10485760]{0:T(1024)(128)(4,1)}), s8[4194304]{0:T(1024)(128)(4,1)S(1)}, s32[]{:S(2)}) async-start(s8[10485760]{0:T(1024)(128)(4,1)} %bitcast.92), calls=%async_computation.1 | async-start | bytes 8388608
  72.9 2.8 %slice-start.2 = ((s8[10485760]{0:T(1024)(128)(4,1)}), s8[2097152]{0:T(1024)(128)(4,1)S(1)}, s32[]{:S(2)}) async-start(s8[10485760]{0:T(1024)(128)(4,1)} %bitcast.92), calls=%async_computation.2 | async-start | bytes 4194304
  72.9 3.1 %copy-start.2 = (bf16[1,1024,640]{1,2,0:T(8,128)(2,1)S(1)}, bf16[1,1024,640]{1,2,0:T(8,128)(2,1)}, u32[]{:S(2)}) copy-start(bf16[1,1024,640]{1,2,0:T(8,128)(2,1)} %copy.35) | copy-start | bytes 3932164

commit v2 on v1

v2 whole, which is shorter than its diff:
```python
import math

import jax
import jax.numpy as jnp
from jax import lax
from jax.sharding import PartitionSpec as P

HEAD_WIDTH = 128
MASK_BLOCK_SIZE = 128
BLOCKS_PER_FRAME = 4
FAR_STRIDE = 4
LEVELS = 4


def from_behind(shard, axis, by):
    count = lax.axis_size(axis)
    pairs = [(i, i + by) for i in range(count) if 0 <= i + by < count]
    return lax.ppermute(shard, axis, pairs)


def halo_frame(key_value, frame_rows, seq_count, rep_count, rep_index):
    slab_rows = key_value.shape[1]
    last = lax.slice_in_dim(key_value, slab_rows - frame_rows, slab_rows, axis=1)
    first = lax.slice_in_dim(key_value, 0, frame_rows, axis=1)
    forward = [(s * rep_count + rep_count - 1, (s + 1) * rep_count) for s in range(seq_count - 1)]
    backward = [(s * rep_count, (s - 1) * rep_count + rep_count - 1) for s in range(1, seq_count)]
    low = lax.ppermute(last, ("seq", "rep"), forward)
    high = lax.ppermute(first, ("seq", "rep"), backward)
    return jnp.where(rep_index == 0, low, high)


def per_device(query, key_value, key_blocks):
    frame_rows = BLOCKS_PER_FRAME * MASK_BLOCK_SIZE
    query_count = query.shape[0]
    slab_rows = key_value.shape[1]
    columns = key_value.shape[2]
    head_count = columns // HEAD_WIDTH
    slab_blocks = slab_rows // MASK_BLOCK_SIZE
    slab_frames = slab_rows // frame_rows
    far_count = slab_blocks // FAR_STRIDE
    seq_count = lax.axis_size("seq")
    rep_count = lax.axis_size("rep")
    slab_index = lax.axis_index("seq")
    rep_index = lax.axis_index("rep")
    query_frames = query_count // frame_rows
    query_blocks = query_count // MASK_BLOCK_SIZE
    score_scale = 1.0 / math.sqrt(HEAD_WIDTH)
    assert rep_count >= 2 and query_frames * rep_count == slab_frames
    assert far_count % rep_count == 0
    far_share = far_count // rep_count

    halo = halo_frame(key_value, frame_rows, seq_count, rep_count, rep_index)

    phases = jnp.maximum(key_blocks[0], 0) % FAR_STRIDE
    stride_grid = key_value.reshape(2, far_count, FAR_STRIDE, MASK_BLOCK_SIZE, columns)
    share_grid = lax.dynamic_slice_in_dim(stride_grid, rep_index * far_share, far_share, 1)
    received = []
    pick_list = []
    valid_list = []
    for tier_index in range(LEVELS):
        distance = 2 ** (tier_index + 1)
        if distance < seq_count:
            for direction in range(2):
                slot_index = 2 * tier_index + direction
                offset = (1 - 2 * direction) * distance
                wanted = from_behind(phases[slot_index : slot_index + 1], "seq", offset)[0]
                chosen = lax.dynamic_index_in_dim(share_grid, wanted, 2, keepdims=False)
                received.append((chosen, -offset))
                partner = slab_index + offset
                inside = (partner >= 0) & (partner < seq_count)
                named = key_blocks[:, slot_index]
                pick = (named - partner * slab_blocks - phases[slot_index]) // FAR_STRIDE
                pick_list.append(pick)
                valid_list.append((named >= 0) & inside)
    query, payloads = lax.optimization_barrier((query, [chosen for chosen, _ in received]))
    received = [from_behind(chosen, "seq", by) for chosen, (_, by) in zip(payloads, received)]
    slot_count = len(received)
    mine = jnp.stack(received, 1)
    parts = [mine]
    sources = [rep_index]
    for k in range(1, rep_count):
        shift = [(r, (r + k) % rep_count) for r in range(rep_count)]
        parts.append(lax.ppermute(mine, "rep", shift))
        sources.append((rep_index - k) % rep_count)
    far_pair = jnp.stack(parts, 2).reshape(2, slot_count * far_count * MASK_BLOCK_SIZE, columns)
    far_pick = jnp.stack(pick_list, 1)
    far_valid = jnp.stack(valid_list, 1)
    share_ids = jnp.arange(far_share, dtype=jnp.int32)
    candidates = (jnp.stack(sources)[:, None] * far_share + share_ids[None, :]).reshape(far_count)
    far_mask = far_valid[:, :, None] & (far_pick[:, :, None] == candidates[None, None, :])
    far_mask = jnp.repeat(far_mask.reshape(query_blocks, slot_count * far_count), MASK_BLOCK_SIZE, axis=1)
    far_mask = jnp.repeat(far_mask, MASK_BLOCK_SIZE, axis=0)

    halo_valid = ((rep_index == 0) & (slab_index > 0)) | (
        (rep_index == rep_count - 1) & (slab_index < seq_count - 1)
    )
    outputs = []
    for head in range(head_count):
        cols = slice(head * HEAD_WIDTH, (head + 1) * HEAD_WIDTH)
        query_head = query[:, cols]
        own_scores = (
            jnp.dot(query_head, key_value[0, :, cols].T, preferred_element_type=jnp.float32)
            * score_scale
        )
        own_top = jnp.max(own_scores, axis=1, keepdims=True)
        own_exp = jnp.exp(own_scores - own_top)
        own_total = jnp.sum(own_exp, axis=1, keepdims=True)
        halo_scores = (
            jnp.dot(query_head, halo[0, :, cols].T, preferred_element_type=jnp.float32)
            * score_scale
        )
        halo_scores = jnp.where(halo_valid, halo_scores, -jnp.inf)
        far_scores = (
            jnp.dot(query_head, far_pair[0, :, cols].T, preferred_element_type=jnp.float32)
            * score_scale
        )
        far_scores = jnp.where(far_mask, far_scores, -jnp.inf)
        row_top = jnp.maximum(
            own_top,
            jnp.maximum(
                jnp.max(halo_scores, axis=1, keepdims=True),
                jnp.max(far_scores, axis=1, keepdims=True),
            ),
        )
        own_factor = jnp.exp(own_top - row_top)
        halo_exp = jnp.exp(halo_scores - row_top)
        far_exp = jnp.exp(far_scores - row_top)
        row_total = (
            own_total * own_factor
            + jnp.sum(halo_exp, axis=1, keepdims=True)
            + jnp.sum(far_exp, axis=1, keepdims=True)
        )
        own_prob = (own_exp * (own_factor / row_total)).astype(jnp.bfloat16)
        halo_prob = (halo_exp / row_total).astype(jnp.bfloat16)
        far_prob = (far_exp / row_total).astype(jnp.bfloat16)
        mixed = jnp.dot(own_prob, key_value[1, :, cols], preferred_element_type=jnp.float32)
        mixed = mixed + jnp.dot(halo_prob, halo[1, :, cols], preferred_element_type=jnp.float32)
        mixed = mixed + jnp.dot(far_prob, far_pair[1, :, cols], preferred_element_type=jnp.float32)
        outputs.append(mixed.astype(jnp.bfloat16))
    return jnp.concatenate(outputs, axis=1)


def solution(mesh):
    in_specs = (
        P(("grp", "seq", "rep"), "head"),
        P(None, ("grp", "seq"), "head"),
        P(("grp", "seq", "rep"), None),
    )
    out_specs = P(("grp", "seq", "rep"), "head")
    return jax.shard_map(
        per_device, mesh=mesh, in_specs=in_specs, out_specs=out_specs, check_vma=False
    )
```

time: 82.8 us -> 69.7 us (0.84)
  local copies, waits for them, and re-layouts: 21.8 us -> 7.35 us
  waiting for transfers between devices: 10.9 us -> 16.4 us
  other arithmetic: 12.9 us -> 8.36 us
  matrix products: 16 us -> 13 us
  starting transfers between devices: 17 us -> 20 us
    unnamed x20 -> x6, local copies, waits for them, and re-layouts: 7.67 us -> 0.02 us
    ppermute x4, waiting for transfers between devices: 10.9 us -> 15.9 us  [from_behind(): return lax.ppermute(shard, axis, pairs)]
    reduce_sum x2 -> x10, other arithmetic: 8.11 us -> 4.14 us  [the longest x5 2.64 us: per_device(): own_total = jnp.sum(own_exp, axis=1, keepdims=True)]
    slice x6 -> x2, local copies, waits for them, and re-layouts: 7.05 us -> 4.05 us  [the longest x1 3.44 us: halo_frame(): first = lax.slice_in_dim(key_value, 0, frame_rows, axis=1)]
    dot_general x6 -> x30, matrix products: 16 us -> 13 us  [the longest x5 3.65 us: per_device(): jnp.dot(own_prob, key_value[1, :, cols], preferred_element_type=jnp.float32)]
    dynamic_slice x1 -> x0, local copies, waits for them, and re-layouts: 2.52 us -> none  [halo_frame(): payload = lax.dynamic_slice_in_dim(key_value, start, frame_rows, 1)]
    another operation x2, other arithmetic: 2.16 us -> 0.24 us  [per_device(): jnp.stack(parts, 2)]
    ppermute x1 -> x2, starting transfers between devices: 1.77 us -> 3.49 us  [the longest x1 1.74 us: halo_frame(): high = lax.ppermute(first, ('seq', 'rep'), backward)]
  transfers between devices with their start and end apart: 6 -> 7, of which waited for: 1 -> 3; matrix products, arithmetic and copies ran while one was open for 43% -> 21% of each run, Pallas kernels for 0% -> 0%
where the time goes in v2:
time: 69.7 us; the launch traced here: 69.3 us
  starting transfers between devices  20 us (29%)
  waiting for transfers between devices  16.4 us (24%)
  matrix products  13 us (19%)
  other arithmetic  8.36 us (12%)
  local copies, waits for them, and re-layouts  7.35 us (11%)
  between operations  4.15 us (6%)
    ppermute x4, starting transfers between devices, from_behind(): return lax.ppermute(shard, axis, pairs)  16.5 us
    ppermute x4, waiting for transfers between devices, from_behind(): return lax.ppermute(shard, axis, pairs)  15.9 us
    dot_general x5, matrix products, per_device(): jnp.dot(own_prob, key_value[1, :, cols], preferred_element_type=jnp.float32)  3.65 us
    slice x1, local copies, waits for them, and re-layouts, halo_frame(): first = lax.slice_in_dim(key_value, 0, frame_rows, axis=1)  3.44 us
    reduce_sum x5, other arithmetic, per_device(): own_total = jnp.sum(own_exp, axis=1, keepdims=True)  2.64 us
    dot_general x5, matrix products, per_device(): jnp.dot(query_head, key_value[0, :, cols].T, preferred_element_type=jnp.f...  2.6 us
    broadcast_in_dim x1, local copies, waits for them, and re-layouts, per_device(): far_mask = jnp.repeat(far_mask, MASK_BLOCK_SIZE, axis=0)  1.78 us
    dot_general x5, matrix products, per_device(): jnp.dot(query_head, far_pair[0, :, cols].T, preferred_element_type=jnp.fl...  1.76 us
  transfers between devices with their start and end apart: 7, of which 3 were waited for; matrix products, arithmetic and copies ran while one was open for 21% of the time, Pallas kernels for 0%

profile of v2, /device:TPU:0, one launch (start us, length us, event | category | flops | bytes accessed | tf_op | source)
XLA Modules:
  0.0 69.3 jit_solution(11374995196929898930)
XLA Ops:
  0.0 0.7 and_select_fusion
  0.7 0.6 fusion.106
  1.3 1.3 %collective-permute-start.1 = (s32[1]{0:T(128)}, s32[1]{0:T(128)}, u32[]{:S(2)}, u32[]{:S(2)}) collective-permute-start(s32[1]{0:T(128)} %get-tuple-element.41), channel_id=1, source_target_pairs={{8,0},{12,4},{9,1},{13,5},{10,2},{14,6},{11,3},{15,7},{24,16},{28,... | collective-permute-start | bytes 20 | tf_op jit(solution)/shard_map/ppermute | solution.py:18
  2.6 7.2 %collective-permute-start = (s32[1]{0:T(128)}, s32[1]{0:T(128)}, u32[]{:S(2)}, u32[]{:S(2)}) collective-permute-start(s32[1]{0:T(128)} %get-tuple-element.42), channel_id=1, source_target_pairs={{0,8},{4,12},{1,9},{5,13},{2,10},{6,14},{3,11},{7,15},{16,24},{20,... | collective-permute-start | bytes 20 | tf_op jit(solution)/shard_map/ppermute | solution.py:18
  9.9 3.4 %fusion.105 = (bf16[2,512,640]{2,1,0:T(8,128)(2,1)}, bf16[2,512,640]{2,1,0:T(8,128)(2,1)}) fusion(bf16[2,1024,640]{2,1,0:T(8,128)(2,1)} %param.4), kind=kLoop, calls=%fused_computation.219 | loop fusion | bytes 5242880 | tf_op jit(solution)/shard_map/slice | solution.py:24
  13.3 1.7 %collective-permute-start.2 = (bf16[2,512,640]{2,1,0:T(8,128)(2,1)}, bf16[2,512,640]{2,1,0:T(8,128)(2,1)}, u32[]{:S(2)}, u32[]{:S(2)}) collective-permute-start(bf16[2,512,640]{2,1,0:T(8,128)(2,1)} %get-tuple-element.32), channel_id=1, source_target_pairs={{1,4},{5,8},{9,12},{3,6},{7,10},{11,14},{17,20},{21,24},{25,28},{1... | collective-permute-start | bytes 3932168 | tf_op jit(solution)/shard_map/ppermute | solution.py:27
  15.1 1.7 %collective-permute-start.3 = (bf16[2,512,640]{2,1,0:T(8,128)(2,1)}, bf16[2,512,640]{2,1,0:T(8,128)(2,1)}, u32[]{:S(2)}, u32[]{:S(2)}) collective-permute-start(bf16[2,512,640]{2,1,0:T(8,128)(2,1)} %get-tuple-element.31), channel_id=1, source_target_pairs={{4,1},{8,5},{12,9},{6,3},{10,7},{14,11},{20,17},{24,21},{28,25},{2... | collective-permute-start | bytes 3932168 | tf_op jit(solution)/shard_map/ppermute | solution.py:28
  16.8 0.1 compare_and_fusion.2
  16.9 0.1 pad_add_fusion.1
  17.0 0.1 copy.9
  17.1 1.3 %add_select_fusion.1 = (s32[4,1]{1,0:T(4,128)S(1)}, s32[4,1]{1,0:T(4,128)S(1)}) fusion(s32[4,8]{1,0:T(4,128)S(1)} %copy-done.2, s32[]{:T(128)} %bitcast.8, s32[]{:T(128)S(6)} %mul.148, s32[]{:T(128)} %bitcast.9, s32[]{:T(128)S(6)} %mul.149), kind=kLoop, calls=%fused_computation.174 | loop fusion | flops 136 | bytes 80 | tf_op jit(solution)/shard_map/jit(floor_divide)/jit(_where)/select_n | solution.py:72
  18.4 0.1 pad_add_fusion
  18.5 0.1 copy.10
  18.7 0.1 eq.36
  22.8 0.5 multiply_reduce_fusion.4
  23.3 0.5 multiply_reduce_fusion.3
  23.8 0.5 multiply_reduce_fusion.2
  24.3 6.7 %collective-permute-start.5 = (bf16[2,1,128,640]{3,2,0,1:T(8,128)(2,1)S(1)}, bf16[2,1,128,640]{3,2,0,1:T(8,128)(2,1)S(1)}, u32[]{:S(2)}, u32[]{:S(2)}) collective-permute-start(bf16[2,1,128,640]{3,2,0,1:T(8,128)(2,1)S(1)} %get-tuple-element.10), channel_id=1, source_target_pairs={{0,8},{4,12},{1,9},{5,13},{2,10},{6,14},{3,11},{7,15},{16,24},{20,... | collective-permute-start | bytes 983048 | tf_op jit(solution)/shard_map/ppermute | solution.py:18
  31.0 1.3 %collective-permute-start.4 = (bf16[2,1,128,640]{3,2,0,1:T(8,128)(2,1)S(1)}, bf16[2,1,128,640]{3,2,0,1:T(8,128)(2,1)S(1)}, u32[]{:S(2)}, u32[]{:S(2)}) collective-permute-start(bf16[2,1,128,640]{3,2,0,1:T(8,128)(2,1)S(1)} %get-tuple-element.9), channel_id=1, source_target_pairs={{8,0},{12,4},{9,1},{13,5},{10,2},{14,6},{11,3},{15,7},{24,16},{28,... | collective-permute-start | bytes 983048 | tf_op jit(solution)/shard_map/ppermute | solution.py:18
  32.3 0.5 fusion
  32.8 0.5 fusion.1
  33.3 0.5 fusion.2
  33.9 0.5 multiply_reduce_fusion.1
  34.4 4.8 %collective-permute-done.5 = bf16[2,1,128,640]{3,2,0,1:T(8,128)(2,1)S(1)} collective-permute-done((bf16[2,1,128,640]{3,2,0,1:T(8,128)(2,1)S(1)}, bf16[2,1,128,640]{3,2,0,1:T(8,128)(2,1)S(1)}, u32[]{:S(2)}, u32[]{:S(2)}) %collective-permute-start.5) | collective-permute-done | bytes 327712 | tf_op jit(solution)/shard_map/ppermute | solution.py:18
  39.2 11.1 %collective-permute-done.4 = bf16[2,1,128,640]{3,2,0,1:T(8,128)(2,1)S(1)} collective-permute-done((bf16[2,1,128,640]{3,2,0,1:T(8,128)(2,1)S(1)}, bf16[2,1,128,640]{3,2,0,1:T(8,128)(2,1)S(1)}, u32[]{:S(2)}, u32[]{:S(2)}) %collective-permute-start.4) | collective-permute-done | bytes 327712 | tf_op jit(solution)/shard_map/ppermute | solution.py:18
  50.3 0.1 fusion.104
  50.5 0.5 fusion.3
  51.0 0.5 multiply_reduce_fusion
  51.5 0.5 fusion.4
  52.0 0.5 collective-permute-done.6
  52.5 0.1 pad_maximum_fusion
  52.7 1.8 %broadcast_in_dim.20 = pred[4,128,512]{1,0,2:T(4,128)(4,1)S(1)} broadcast(pred[4,512]{0,1:T(8,128)(4,1)S(1)} %bitcast.177), dimensions={0,2} | broadcast | bytes 264192 | tf_op jit(solution)/shard_map/broadcast_in_dim | solution.py:92
  54.5 0.4 fusion.108
  54.9 0.4 fusion.110
  55.2 0.4 fusion.112
  55.6 0.4 fusion.114
  55.9 0.4 fusion.116
  56.3 1.5 %broadcast_select_fusion = bf16[2,512,640]{2,1,0:T(8,128)(2,1)S(1)} fusion(bf16[2,512,640]{2,1,0:T(8,128)(2,1)} %collective-permute-done.2, bf16[2,512,640]{2,1,0:T(8,128)(2,1)} %collective-permute-done.3, pred[]{:T(512)S(6)} %eq.31), kind=kLoop, calls=%fused_computation.41 | loop fusion | flops 655360 | bytes 3932161 | tf_op jit(solution)/shard_map/jit(_where)/select_n | solution.py:29
  57.8 0.3 fusion.107
  58.1 0.3 fusion.109
  58.4 0.3 fusion.111
  58.7 0.3 fusion.113
  59.0 0.3 fusion.115
  59.4 0.3 fusion.30
  59.7 0.7 %fusion.25 = f32[512,128]{0,1:T(8,128)S(1)} fusion(f32[512,1024]{1,0:T(8,128)S(1)} %get-tuple-element.44, f32[512]{0:T(512)S(1)} %get-tuple-element.29, f32[512]{0:T(512)S(1)} %get-tuple-element.43, bf16[2,1024,640]{2,1,0:T(8,128)(2,1)S(1)} %copy-done), kind=kOutput, calls=%fused_computation.82 | convolution fusion | flops 136314880 | bytes 2625536 | tf_op jit(solution)/shard_map/dot_general | solution.py:136
  60.4 0.3 convolution_add_fusion.9
  60.8 0.3 fusion.16
  61.1 0.3 fusion.32
  61.5 0.7 %fusion.26 = f32[512,128]{0,1:T(8,128)S(1)} fusion(f32[512,1024]{1,0:T(8,128)S(1)} %get-tuple-element.50, f32[512]{0:T(512)S(1)} %get-tuple-element.27, f32[512]{0:T(512)S(1)} %get-tuple-element.49, bf16[2,1024,640]{2,1,0:T(8,128)(2,1)S(1)} %copy-done), kind=kOutput, calls=%fused_computation.83 | convolution fusion | flops 136314880 | bytes 2625536 | tf_op jit(solution)/shard_map/dot_general | solution.py:136
  62.2 0.3 fusion.34
  62.5 0.7 %fusion.27 = f32[512,128]{0,1:T(8,128)S(1)} fusion(f32[512,1024]{1,0:T(8,128)S(1)} %get-tuple-element.56, f32[512]{0:T(512)S(1)} %get-tuple-element.25, f32[512]{0:T(512)S(1)} %get-tuple-element.55, bf16[2,1024,640]{2,1,0:T(8,128)(2,1)S(1)} %copy-done), kind=kOutput, calls=%fused_computation.84 | convolution fusion | flops 136314880 | bytes 2625536 | tf_op jit(solution)/shard_map/dot_general | solution.py:136
  63.3 0.3 fusion.36
  63.6 0.7 %fusion.28 = f32[512,128]{0,1:T(8,128)S(1)} fusion(f32[512,1024]{1,0:T(8,128)S(1)} %get-tuple-element.62, f32[512]{0:T(512)S(1)} %get-tuple-element.23, f32[512]{0:T(512)S(1)} %get-tuple-element.61, bf16[2,1024,640]{2,1,0:T(8,128)(2,1)S(1)} %copy-done), kind=kOutput, calls=%fused_computation.85 | convolution fusion | flops 136314880 | bytes 2625536 | tf_op jit(solution)/shard_map/dot_general | solution.py:136
  64.4 0.3 fusion.38
  64.7 0.7 %fusion.29 = f32[512,128]{0,1:T(8,128)S(1)} fusion(f32[512,1024]{1,0:T(8,128)S(1)} %get-tuple-element.68, f32[512]{0:T(512)S(1)} %get-tuple-element.21, f32[512]{0:T(512)S(1)} %get-tuple-element.67, bf16[2,1024,640]{2,1,0:T(8,128)(2,1)S(1)} %copy-done), kind=kOutput, calls=%fused_computation.86 | convolution fusion | flops 136314880 | bytes 2625536 | tf_op jit(solution)/shard_map/dot_general | solution.py:136
  65.4 0.3 convolution_add_fusion.7
  65.8 0.3 fusion.18
  66.1 0.3 convolution_add_fusion.5
  66.5 0.3 fusion.20
  66.8 0.3 convolution_add_fusion.3
  67.2 0.3 fusion.22
  67.5 0.3 convolution_add_fusion.1
  67.9 0.3 fusion.24
  68.2 1.1 %copy.12 = bf16[512,640]{1,0:T(8,128)(2,1)} copy(bf16[512,640]{0,1:T(8,128)(2,1)S(1)} %fusion.24) | data formatting | bytes 1310720 | tf_op jit(solution)/shard_map/concatenate | solution.py:140
  (29 shorter events, 0.5 us)
Async XLA Ops:
  1.3 17.6 %collective-permute-start.1 = (s32[1]{0:T(128)}, s32[1]{0:T(128)}, u32[]{:S(2)}, u32[]{:S(2)}) collective-permute-start(s32[1]{0:T(128)} %get-tuple-element.41), channel_id=1, source_target_pairs={{8,0},{12,4},{9,1},{13,5},{10,2},{14,6},{11,3},{15,7},{24,16},{28,... | collective-permute-start | bytes 20 | tf_op jit(solution)/shard_map/ppermute | solution.py:18
  2.6 14.2 %copy-start.2 = (s32[4,8]{1,0:T(4,128)S(1)}, s32[4,8]{1,0:T(4,128)}, u32[]{:S(2)}) copy-start(s32[4,8]{1,0:T(4,128)} %param.5) | copy-start | bytes 388
  2.6 20.1 %copy-start = (bf16[2,1024,640]{2,1,0:T(8,128)(2,1)S(1)}, bf16[2,1024,640]{2,1,0:T(8,128)(2,1)}, u32[]{:S(2)}) copy-start(bf16[2,1024,640]{2,1,0:T(8,128)(2,1)} %param.4) | copy-start | bytes 7864324
  2.6 20.1 %copy-start.1 = (bf16[512,640]{1,0:T(8,128)(2,1)S(1)}, bf16[512,640]{1,0:T(8,128)(2,1)}, u32[]{:S(2)}) copy-start(bf16[512,640]{1,0:T(8,128)(2,1)} %param.3) | copy-start | bytes 1966084
  2.6 17.6 %collective-permute-start = (s32[1]{0:T(128)}, s32[1]{0:T(128)}, u32[]{:S(2)}, u32[]{:S(2)}) collective-permute-start(s32[1]{0:T(128)} %get-tuple-element.42), channel_id=1, source_target_pairs={{0,8},{4,12},{1,9},{5,13},{2,10},{6,14},{3,11},{7,15},{16,24},{20,... | collective-permute-start | bytes 20 | tf_op jit(solution)/shard_map/ppermute | solution.py:18
  13.3 43.0 %collective-permute-start.2 = (bf16[2,512,640]{2,1,0:T(8,128)(2,1)}, bf16[2,512,640]{2,1,0:T(8,128)(2,1)}, u32[]{:S(2)}, u32[]{:S(2)}) collective-permute-start(bf16[2,512,640]{2,1,0:T(8,128)(2,1)} %get-tuple-element.32), channel_id=1, source_target_pairs={{1,4},{5,8},{9,12},{3,6},{7,10},{11,14},{17,20},{21,24},{25,28},{1... | collective-permute-start | bytes 3932168 | tf_op jit(solution)/shard_map/ppermute | solution.py:27
  15.1 41.2 %collective-permute-start.3 = (bf16[2,512,640]{2,1,0:T(8,128)(2,1)}, bf16[2,512,640]{2,1,0:T(8,128)(2,1)}, u32[]{:S(2)}, u32[]{:S(2)}) collective-permute-start(bf16[2,512,640]{2,1,0:T(8,128)(2,1)} %get-tuple-element.31), channel_id=1, source_target_pairs={{4,1},{8,5},{12,9},{6,3},{10,7},{14,11},{20,17},{24,21},{28,25},{2... | collective-permute-start | bytes 3932168 | tf_op jit(solution)/shard_map/ppermute | solution.py:28
  24.3 14.8 %collective-permute-start.5 = (bf16[2,1,128,640]{3,2,0,1:T(8,128)(2,1)S(1)}, bf16[2,1,128,640]{3,2,0,1:T(8,128)(2,1)S(1)}, u32[]{:S(2)}, u32[]{:S(2)}) collective-permute-start(bf16[2,1,128,640]{3,2,0,1:T(8,128)(2,1)S(1)} %get-tuple-element.10), channel_id=1, source_target_pairs={{0,8},{4,12},{1,9},{5,13},{2,10},{6,14},{3,11},{7,15},{16,24},{20,... | collective-permute-start | bytes 983048 | tf_op jit(solution)/shard_map/ppermute | solution.py:18
  31.0 19.3 %collective-permute-start.4 = (bf16[2,1,128,640]{3,2,0,1:T(8,128)(2,1)S(1)}, bf16[2,1,128,640]{3,2,0,1:T(8,128)(2,1)S(1)}, u32[]{:S(2)}, u32[]{:S(2)}) collective-permute-start(bf16[2,1,128,640]{3,2,0,1:T(8,128)(2,1)S(1)} %get-tuple-element.9), channel_id=1, source_target_pairs={{8,0},{12,4},{9,1},{13,5},{10,2},{14,6},{11,3},{15,7},{24,16},{28,... | collective-permute-start | bytes 983048 | tf_op jit(solution)/shard_map/ppermute | solution.py:18
  50.4 2.2 %collective-permute-start.6 = (bf16[2,2,1,128,640]{4,3,1,0,2:T(8,128)(2,1)S(1)}, bf16[2,2,1,128,640]{4,3,1,0,2:T(8,128)(2,1)S(1)}, u32[]{:S(2)}, u32[]{:S(2)}) collective-permute-start(bf16[2,2,1,128,640]{4,3,1,0,2:T(8,128)(2,1)S(1)} %get-tuple-element.36), channel_id=1, source_target_pairs={{0,1},{1,0},{2,3},{3,2},{4,5},{5,4},{6,7},{7,6},{8,9},{9,8},{10,11... | collective-permute-start | bytes 1966088 | tf_op jit(solution)/shard_map/ppermute | solution.py:83

commit v3 on v2

--- a/solution.py
+++ b/solution.py
@@ -59,21 +59,31 @@
     valid_list = []
     for tier_index in range(LEVELS):
         distance = 2 ** (tier_index + 1)
-        if distance < seq_count:
-            for direction in range(2):
-                slot_index = 2 * tier_index + direction
-                offset = (1 - 2 * direction) * distance
-                wanted = from_behind(phases[slot_index : slot_index + 1], "seq", offset)[0]
-                chosen = lax.dynamic_index_in_dim(share_grid, wanted, 2, keepdims=False)
-                received.append((chosen, -offset))
-                partner = slab_index + offset
-                inside = (partner >= 0) & (partner < seq_count)
-                named = key_blocks[:, slot_index]
-                pick = (named - partner * slab_blocks - phases[slot_index]) // FAR_STRIDE
-                pick_list.append(pick)
-                valid_list.append((named >= 0) & inside)
+        if distance >= seq_count:
+            continue
+        if seq_count <= 2 * distance:
+            ahead = [(q, q + distance) for q in range(seq_count - distance)]
+            behind = [(q, q - distance) for q in range(distance, seq_count) if q + distance >= seq_count]
+            side = (slab_index + distance >= seq_count).astype(jnp.int32)
+            slots = [(ahead + behind, side)]
+        else:
+            ahead = [(q, q + distance) for q in range(seq_count - distance)]
+            behind = [(q, q - distance) for q in range(distance, seq_count)]
+            slots = [(ahead, jnp.int32(0)), (behind, jnp.int32(1))]
+        for pairs, side in slots:
+            slot_index = 2 * tier_index + side
+            phase = lax.dynamic_index_in_dim(phases, slot_index, 0, keepdims=False)
+            wanted = lax.ppermute(phase[None], "seq", pairs)[0]
+            chosen = lax.dynamic_index_in_dim(share_grid, wanted, 2, keepdims=False)
+            received.append((chosen, [(b, a) for a, b in pairs]))
+            partner = slab_index + (1 - 2 * side) * distance
+            inside = (partner >= 0) & (partner < seq_count)
+            named = lax.dynamic_index_in_dim(key_blocks, slot_index, 1, keepdims=False)
+            pick = (named - partner * slab_blocks - phase) // FAR_STRIDE
+            pick_list.append(pick)
+            valid_list.append((named >= 0) & inside)
     query, payloads = lax.optimization_barrier((query, [chosen for chosen, _ in received]))
-    received = [from_behind(chosen, "seq", by) for chosen, (_, by) in zip(payloads, received)]
+    received = [lax.ppermute(chosen, "seq", back) for chosen, (_, back) in zip(payloads, received)]
     slot_count = len(received)
     mine = jnp.stack(received, 1)
     parts = [mine]
@@ -88,8 +98,7 @@
     share_ids = jnp.arange(far_share, dtype=jnp.int32)
     candidates = (jnp.stack(sources)[:, None] * far_share + share_ids[None, :]).reshape(far_count)
     far_mask = far_valid[:, :, None] & (far_pick[:, :, None] == candidates[None, None, :])
-    far_mask = jnp.repeat(far_mask.reshape(query_blocks, slot_count * far_count), MASK_BLOCK_SIZE, axis=1)
-    far_mask = jnp.repeat(far_mask, MASK_BLOCK_SIZE, axis=0)
+    far_mask = jnp.repeat(far_mask.reshape(query_blocks, 1, slot_count * far_count), MASK_BLOCK_SIZE, axis=2)
 
     halo_valid = ((rep_index == 0) & (slab_index > 0)) | (
         (rep_index == rep_count - 1) & (slab_index < seq_count - 1)
@@ -114,7 +123,9 @@
             jnp.dot(query_head, far_pair[0, :, cols].T, preferred_element_type=jnp.float32)
             * score_scale
         )
-        far_scores = jnp.where(far_mask, far_scores, -jnp.inf)
+        far_scores = jnp.where(
+            far_mask, far_scores.reshape(query_blocks, MASK_BLOCK_SIZE, -1), -jnp.inf
+        ).reshape(query_count, -1)
         row_top = jnp.maximum(
             own_top,
             jnp.maximum(

time: 69.7 us -> 61.6 us (0.88)
  starting transfers between devices: 20 us -> 12 us
  waiting for transfers between devices: 16.4 us -> 21.9 us
  between operations: 4.15 us -> 2.19 us
  local copies, waits for them, and re-layouts: 7.35 us -> 5.53 us
  matrix products: 13 us -> 12.1 us
  other arithmetic: 8.36 us -> 7.66 us
    ppermute x4 -> x2, starting transfers between devices: 16.5 us -> 8.5 us  [the longest x1 4.46 us: per_device(): lax.ppermute(chosen, 'seq', back)]
    ppermute x4 -> x2, waiting for transfers between devices: 15.9 us -> 21.3 us  [the longest x1 21.3 us: per_device(): lax.ppermute(chosen, 'seq', back)]
    broadcast_in_dim x2, local copies, waits for them, and re-layouts: 1.8 us -> 0.35 us  [the longest x1 0.34 us: per_device(): jnp.where(far_mask, far_scores.reshape(query_blocks, MASK_BLOCK_SIZE, -1)...]
    select_n x1, other arithmetic: 1.34 us -> 0.01 us  [per_device(): pick = (named - partner * slab_blocks - phase) // FAR_STRIDE]
    sub x0 -> x1, other arithmetic: none -> 0.82 us  [per_device(): pick = (named - partner * slab_blocks - phase) // FAR_STRIDE]
  transfers between devices with their start and end apart: 7 -> 5, of which waited for: 3 -> 2; matrix products, arithmetic and copies ran while one was open for 21% -> 19% of each run, Pallas kernels for 0% -> 0%
where the time goes in v3:
time: 61.6 us; the launch traced here: 61.4 us
  waiting for transfers between devices  21.9 us (36%)
  matrix products  12.1 us (20%)
  starting transfers between devices  12 us (19%)
  other arithmetic  7.66 us (12%)
  local copies, waits for them, and re-layouts  5.53 us (9%)
  between operations  2.19 us (4%)
    ppermute x1, waiting for transfers between devices, per_device(): lax.ppermute(chosen, 'seq', back)  21.3 us
    ppermute x1, starting transfers between devices, per_device(): lax.ppermute(chosen, 'seq', back)  4.46 us
    ppermute x1, starting transfers between devices, per_device(): wanted = lax.ppermute(phase[None], 'seq', pairs)[0]  4.04 us
    dot_general x5, matrix products, per_device(): jnp.dot(own_prob, key_value[1, :, cols], preferred_element_type=jnp.float32)  3.67 us
    slice x1, local copies, waits for them, and re-layouts, halo_frame(): first = lax.slice_in_dim(key_value, 0, frame_rows, axis=1)  3.44 us
    reduce_sum x5, other arithmetic, per_device(): own_total = jnp.sum(own_exp, axis=1, keepdims=True)  2.63 us
    dot_general x5, matrix products, per_device(): jnp.dot(query_head, key_value[0, :, cols].T, preferred_element_type=jnp.f...  2.59 us
    ppermute x1, starting transfers between devices, halo_frame(): high = lax.ppermute(first, ('seq', 'rep'), backward)  1.74 us
  transfers between devices with their start and end apart: 5, of which 2 were waited for; matrix products, arithmetic and copies ran while one was open for 19% of the time, Pallas kernels for 0%

profile of v3, /device:TPU:0, one launch (start us, length us, event | category | flops | bytes accessed | tf_op | source)
XLA Modules:
  0.0 61.4 jit_solution(12548630840837811616)
XLA Ops:
  0.0 0.7 %and_select_fusion.1 = s32[8]{0:T(128)S(1)} fusion(s32[4,8]{1,0:T(4,128)} %param.5), kind=kLoop, calls=%fused_computation.187 | loop fusion | flops 56 | bytes 64 | tf_op jit(solution)/shard_map/jit(remainder)/select_n | solution.py:54
  0.7 0.6 dynamic_slice.14
  1.3 4.0 %collective-permute-start = (s32[1]{0:T(128)}, s32[1]{0:T(128)}, u32[]{:S(2)}, u32[]{:S(2)}) collective-permute-start(s32[1]{0:T(128)} %dynamic_slice.14), channel_id=1, source_target_pairs={{0,8},{4,12},{8,0},{12,4},{1,9},{5,13},{9,1},{13,5},{2,10},{6,14},... | collective-permute-start | bytes 20 | tf_op jit(solution)/shard_map/ppermute | solution.py:76
  5.3 3.4 %fusion.100 = (bf16[2,512,640]{2,1,0:T(8,128)(2,1)}, bf16[2,512,640]{2,1,0:T(8,128)(2,1)}) fusion(bf16[2,1024,640]{2,1,0:T(8,128)(2,1)} %param.4), kind=kLoop, calls=%fused_computation.202 | loop fusion | bytes 5242880 | tf_op jit(solution)/shard_map/slice | solution.py:24
  8.8 1.7 %collective-permute-start.1 = (bf16[2,512,640]{2,1,0:T(8,128)(2,1)}, bf16[2,512,640]{2,1,0:T(8,128)(2,1)}, u32[]{:S(2)}, u32[]{:S(2)}) collective-permute-start(bf16[2,512,640]{2,1,0:T(8,128)(2,1)} %get-tuple-element.20), channel_id=1, source_target_pairs={{1,4},{5,8},{9,12},{3,6},{7,10},{11,14},{17,20},{21,24},{25,28},{1... | collective-permute-start | bytes 3932168 | tf_op jit(solution)/shard_map/ppermute | solution.py:27
  10.5 1.7 %collective-permute-start.2 = (bf16[2,512,640]{2,1,0:T(8,128)(2,1)}, bf16[2,512,640]{2,1,0:T(8,128)(2,1)}, u32[]{:S(2)}, u32[]{:S(2)}) collective-permute-start(bf16[2,512,640]{2,1,0:T(8,128)(2,1)} %get-tuple-element.19), channel_id=1, source_target_pairs={{4,1},{8,5},{12,9},{6,3},{10,7},{14,11},{20,17},{24,21},{28,25},{2... | collective-permute-start | bytes 3932168 | tf_op jit(solution)/shard_map/ppermute | solution.py:28
  12.3 0.2 and_reduce_fusion
  12.5 0.8 %subtract_reduce_fusion = s32[4]{0:T(128)S(1)} fusion(s32[4,8]{1,0:T(4,128)S(1)} %copy-done.2, s32[]{:T(128)S(6)} %select_n.95, s32[]{:T(128)} %bitcast.6, s32[]{:T(128)S(6)} %mul.153), kind=kLoop, calls=%fused_computation.183 | loop fusion | flops 8 | bytes 44 | tf_op jit(solution)/shard_map/sub | solution.py:82
  13.3 0.1 pad_add_fusion
  13.4 0.1 compare_and_fusion
  15.4 0.5 multiply_reduce_fusion.4
  16.0 0.5 multiply_reduce_fusion.3
  16.5 0.5 multiply_reduce_fusion.2
  17.0 0.5 multiply_reduce_fusion.1
  17.5 4.5 %collective-permute-start.3 = (bf16[2,1,128,640]{3,2,0,1:T(8,128)(2,1)S(1)}, bf16[2,1,128,640]{3,2,0,1:T(8,128)(2,1)S(1)}, u32[]{:S(2)}, u32[]{:S(2)}) collective-permute-start(bf16[2,1,128,640]{3,2,0,1:T(8,128)(2,1)S(1)} %dynamic-slice_bitcast_fusion), channel_id=1, source_target_pairs={{8,0},{12,4},{0,8},{4,12},{9,1},{13,5},{1,9},{5,13},{10,2},{14,6},... | collective-permute-start | bytes 983048 | tf_op jit(solution)/shard_map/ppermute | solution.py:86
  22.0 0.5 fusion
  22.5 0.5 fusion.1
  23.0 0.5 fusion.2
  23.6 0.5 multiply_reduce_fusion
  24.1 21.3 %collective-permute-done.3 = bf16[2,1,128,640]{3,2,0,1:T(8,128)(2,1)S(1)} collective-permute-done((bf16[2,1,128,640]{3,2,0,1:T(8,128)(2,1)S(1)}, bf16[2,1,128,640]{3,2,0,1:T(8,128)(2,1)S(1)}, u32[]{:S(2)}, u32[]{:S(2)}) %collective-permute-start.3) | collective-permute-done | bytes 327712 | tf_op jit(solution)/shard_map/ppermute | solution.py:86
  45.4 0.0 collective-permute-start.4
  45.4 0.5 fusion.3
  45.9 0.5 fusion.4
  46.5 0.6 collective-permute-done.4
  47.0 0.1 pad_maximum_fusion
  47.1 0.3 broadcast_in_dim.77
  47.5 0.3 fusion.102
  47.7 0.3 fusion.104
  48.0 0.3 fusion.106
  48.2 0.3 fusion.108
  48.5 0.3 fusion.110
  48.8 0.0 collective-permute-done.1
  48.8 1.5 %broadcast_select_fusion = bf16[2,512,640]{2,1,0:T(8,128)(2,1)S(1)} fusion(bf16[2,512,640]{2,1,0:T(8,128)(2,1)} %collective-permute-done.1, bf16[2,512,640]{2,1,0:T(8,128)(2,1)} %collective-permute-done.2, pred[]{:T(512)S(6)} %eq.27), kind=kLoop, calls=%fused_computation.30 | loop fusion | flops 655360 | bytes 3932161 | tf_op jit(solution)/shard_map/jit(_where)/select_n | solution.py:29
  50.3 0.3 fusion.101
  50.6 0.3 fusion.103
  50.9 0.3 fusion.105
  51.2 0.3 fusion.107
  51.5 0.3 fusion.109
  51.9 0.1 fusion.35
  52.0 0.2 fusion.30
  52.2 0.7 %fusion.25 = f32[512,128]{0,1:T(8,128)S(1)} fusion(f32[512,1024]{1,0:T(8,128)S(1)} %get-tuple-element.22, f32[512]{0:T(512)S(1)} %get-tuple-element.17, f32[512]{0:T(512)S(1)} %get-tuple-element.21, bf16[2,1024,640]{2,1,0:T(8,128)(2,1)S(1)} %copy-done), kind=kOutput, calls=%fused_computation.71 | convolution fusion | flops 136314880 | bytes 2625536 | tf_op jit(solution)/shard_map/dot_general | solution.py:147
  52.9 0.3 convolution_add_fusion.9
  53.3 0.3 fusion.16
  53.6 0.1 fusion.36
  53.7 0.2 fusion.31
  53.9 0.7 %fusion.26 = f32[512,128]{0,1:T(8,128)S(1)} fusion(f32[512,1024]{1,0:T(8,128)S(1)} %get-tuple-element.28, f32[512]{0:T(512)S(1)} %get-tuple-element.15, f32[512]{0:T(512)S(1)} %get-tuple-element.27, bf16[2,1024,640]{2,1,0:T(8,128)(2,1)S(1)} %copy-done), kind=kOutput, calls=%fused_computation.72 | convolution fusion | flops 136314880 | bytes 2625536 | tf_op jit(solution)/shard_map/dot_general | solution.py:147
  54.6 0.1 fusion.37
  54.7 0.2 fusion.32
  54.9 0.7 %fusion.27 = f32[512,128]{0,1:T(8,128)S(1)} fusion(f32[512,1024]{1,0:T(8,128)S(1)} %get-tuple-element.34, f32[512]{0:T(512)S(1)} %get-tuple-element.13, f32[512]{0:T(512)S(1)} %get-tuple-element.33, bf16[2,1024,640]{2,1,0:T(8,128)(2,1)S(1)} %copy-done), kind=kOutput, calls=%fused_computation.73 | convolution fusion | flops 136314880 | bytes 2625536 | tf_op jit(solution)/shard_map/dot_general | solution.py:147
  55.7 0.1 fusion.38
  55.8 0.2 fusion.33
  56.0 0.7 %fusion.28 = f32[512,128]{0,1:T(8,128)S(1)} fusion(f32[512,1024]{1,0:T(8,128)S(1)} %get-tuple-element.40, f32[512]{0:T(512)S(1)} %get-tuple-element.11, f32[512]{0:T(512)S(1)} %get-tuple-element.39, bf16[2,1024,640]{2,1,0:T(8,128)(2,1)S(1)} %copy-done), kind=kOutput, calls=%fused_computation.74 | convolution fusion | flops 136314880 | bytes 2625536 | tf_op jit(solution)/shard_map/dot_general | solution.py:147
  56.8 0.1 fusion.39
  56.9 0.2 fusion.34
  57.1 0.7 %fusion.29 = f32[512,128]{0,1:T(8,128)S(1)} fusion(f32[512,1024]{1,0:T(8,128)S(1)} %get-tuple-element.46, f32[512]{0:T(512)S(1)} %get-tuple-element.9, f32[512]{0:T(512)S(1)} %get-tuple-element.45, bf16[2,1024,640]{2,1,0:T(8,128)(2,1)S(1)} %copy-done), kind=kOutput, calls=%fused_computation.75 | convolution fusion | flops 136314880 | bytes 2625536 | tf_op jit(solution)/shard_map/dot_general | solution.py:147
  57.8 0.3 convolution_add_fusion.7
  58.2 0.2 fusion.18
  58.4 0.3 convolution_add_fusion.5
  58.8 0.2 fusion.20
  59.1 0.3 convolution_add_fusion.3
  59.4 0.2 fusion.22
  59.7 0.3 convolution_add_fusion.1
  60.0 0.3 fusion.24
  60.3 1.1 %copy.7 = bf16[512,640]{1,0:T(8,128)(2,1)} copy(bf16[512,640]{0,1:T(8,128)(2,1)S(1)} %fusion.24) | data formatting | bytes 1310720 | tf_op jit(solution)/shard_map/concatenate | solution.py:151
  (21 shorter events, 0.2 us)
Async XLA Ops:
  1.3 11.0 %copy-start.2 = (s32[4,8]{1,0:T(4,128)S(1)}, s32[4,8]{1,0:T(4,128)}, u32[]{:S(2)}) copy-start(s32[4,8]{1,0:T(4,128)} %param.5) | copy-start | bytes 388
  1.3 14.1 %copy-start = (bf16[2,1024,640]{2,1,0:T(8,128)(2,1)S(1)}, bf16[2,1024,640]{2,1,0:T(8,128)(2,1)}, u32[]{:S(2)}) copy-start(bf16[2,1024,640]{2,1,0:T(8,128)(2,1)} %param.4) | copy-start | bytes 7864324
  1.3 14.1 %copy-start.1 = (bf16[512,640]{1,0:T(8,128)(2,1)S(1)}, bf16[512,640]{1,0:T(8,128)(2,1)}, u32[]{:S(2)}) copy-start(bf16[512,640]{1,0:T(8,128)(2,1)} %param.3) | copy-start | bytes 1966084
  1.3 12.2 %collective-permute-start = (s32[1]{0:T(128)}, s32[1]{0:T(128)}, u32[]{:S(2)}, u32[]{:S(2)}) collective-permute-start(s32[1]{0:T(128)} %dynamic_slice.14), channel_id=1, source_target_pairs={{0,8},{4,12},{8,0},{12,4},{1,9},{5,13},{9,1},{13,5},{2,10},{6,14},... | collective-permute-start | bytes 20 | tf_op jit(solution)/shard_map/ppermute | solution.py:76
  8.8 40.0 %collective-permute-start.1 = (bf16[2,512,640]{2,1,0:T(8,128)(2,1)}, bf16[2,512,640]{2,1,0:T(8,128)(2,1)}, u32[]{:S(2)}, u32[]{:S(2)}) collective-permute-start(bf16[2,512,640]{2,1,0:T(8,128)(2,1)} %get-tuple-element.20), channel_id=1, source_target_pairs={{1,4},{5,8},{9,12},{3,6},{7,10},{11,14},{17,20},{21,24},{25,28},{1... | collective-permute-start | bytes 3932168 | tf_op jit(solution)/shard_map/ppermute | solution.py:27
  10.5 38.2 %collective-permute-start.2 = (bf16[2,512,640]{2,1,0:T(8,128)(2,1)}, bf16[2,512,640]{2,1,0:T(8,128)(2,1)}, u32[]{:S(2)}, u32[]{:S(2)}) collective-permute-start(bf16[2,512,640]{2,1,0:T(8,128)(2,1)} %get-tuple-element.19), channel_id=1, source_target_pairs={{4,1},{8,5},{12,9},{6,3},{10,7},{14,11},{20,17},{24,21},{28,25},{2... | collective-permute-start | bytes 3932168 | tf_op jit(solution)/shard_map/ppermute | solution.py:28
  17.5 27.9 %collective-permute-start.3 = (bf16[2,1,128,640]{3,2,0,1:T(8,128)(2,1)S(1)}, bf16[2,1,128,640]{3,2,0,1:T(8,128)(2,1)S(1)}, u32[]{:S(2)}, u32[]{:S(2)}) collective-permute-start(bf16[2,1,128,640]{3,2,0,1:T(8,128)(2,1)S(1)} %dynamic-slice_bitcast_fusion), channel_id=1, source_target_pairs={{8,0},{12,4},{0,8},{4,12},{9,1},{13,5},{1,9},{5,13},{10,2},{14,6},... | collective-permute-start | bytes 983048 | tf_op jit(solution)/shard_map/ppermute | solution.py:86
  45.4 1.6 %collective-permute-start.4 = (bf16[2,1,1,128,640]{4,3,0,2,1:T(8,128)(2,1)S(1)}, bf16[2,1,1,128,640]{4,3,0,2,1:T(8,128)(2,1)S(1)}, u32[]{:S(2)}, u32[]{:S(2)}) collective-permute-start(bf16[2,1,1,128,640]{4,3,0,2,1:T(8,128)(2,1)S(1)} %bitcast.158), channel_id=1, source_target_pairs={{0,1},{1,0},{2,3},{3,2},{4,5},{5,4},{6,7},{7,6},{8,9},{9,8},{10,11... | collective-permute-start | bytes 983048 | tf_op jit(solution)/shard_map/ppermute | solution.py:93

commit v4 on v3

--- a/solution.py
+++ b/solution.py
@@ -85,6 +85,34 @@
     query, payloads = lax.optimization_barrier((query, [chosen for chosen, _ in received]))
     received = [lax.ppermute(chosen, "seq", back) for chosen, (_, back) in zip(payloads, received)]
     slot_count = len(received)
+    halo_valid = ((rep_index == 0) & (slab_index > 0)) | (
+        (rep_index == rep_count - 1) & (slab_index < seq_count - 1)
+    )
+
+    near = []
+    for head in range(head_count):
+        cols = slice(head * HEAD_WIDTH, (head + 1) * HEAD_WIDTH)
+        query_head = query[:, cols]
+        own_scores = (
+            jnp.dot(query_head, key_value[0, :, cols].T, preferred_element_type=jnp.float32)
+            * score_scale
+        )
+        halo_scores = (
+            jnp.dot(query_head, halo[0, :, cols].T, preferred_element_type=jnp.float32)
+            * score_scale
+        )
+        halo_scores = jnp.where(halo_valid, halo_scores, -jnp.inf)
+        near_top = jnp.maximum(
+            jnp.max(own_scores, axis=1, keepdims=True), jnp.max(halo_scores, axis=1, keepdims=True)
+        )
+        own_exp = jnp.exp(own_scores - near_top)
+        halo_exp = jnp.exp(halo_scores - near_top)
+        near_total = jnp.sum(own_exp, axis=1, keepdims=True) + jnp.sum(
+            halo_exp, axis=1, keepdims=True
+        )
+        near.append((near_top, own_exp, halo_exp, near_total))
+    received, near = lax.optimization_barrier((received, near))
+
     mine = jnp.stack(received, 1)
     parts = [mine]
     sources = [rep_index]
@@ -100,49 +128,24 @@
     far_mask = far_valid[:, :, None] & (far_pick[:, :, None] == candidates[None, None, :])
     far_mask = jnp.repeat(far_mask.reshape(query_blocks, 1, slot_count * far_count), MASK_BLOCK_SIZE, axis=2)
 
-    halo_valid = ((rep_index == 0) & (slab_index > 0)) | (
-        (rep_index == rep_count - 1) & (slab_index < seq_count - 1)
-    )
     outputs = []
     for head in range(head_count):
         cols = slice(head * HEAD_WIDTH, (head + 1) * HEAD_WIDTH)
-        query_head = query[:, cols]
-        own_scores = (
-            jnp.dot(query_head, key_value[0, :, cols].T, preferred_element_type=jnp.float32)
-            * score_scale
-        )
-        own_top = jnp.max(own_scores, axis=1, keepdims=True)
-        own_exp = jnp.exp(own_scores - own_top)
-        own_total = jnp.sum(own_exp, axis=1, keepdims=True)
-        halo_scores = (
-            jnp.dot(query_head, halo[0, :, cols].T, preferred_element_type=jnp.float32)
-            * score_scale
-        )
-        halo_scores = jnp.where(halo_valid, halo_scores, -jnp.inf)
+        near_top, own_exp, halo_exp, near_total = near[head]
         far_scores = (
-            jnp.dot(query_head, far_pair[0, :, cols].T, preferred_element_type=jnp.float32)
+            jnp.dot(query[:, cols], far_pair[0, :, cols].T, preferred_element_type=jnp.float32)
             * score_scale
         )
         far_scores = jnp.where(
             far_mask, far_scores.reshape(query_blocks, MASK_BLOCK_SIZE, -1), -jnp.inf
         ).reshape(query_count, -1)
-        row_top = jnp.maximum(
-            own_top,
-            jnp.maximum(
-                jnp.max(halo_scores, axis=1, keepdims=True),
-                jnp.max(far_scores, axis=1, keepdims=True),
-            ),
-        )
-        own_factor = jnp.exp(own_top - row_top)
-        halo_exp = jnp.exp(halo_scores - row_top)
+        row_top = jnp.maximum(near_top, jnp.max(far_scores, axis=1, keepdims=True))
+        near_factor = jnp.exp(near_top - row_top)
         far_exp = jnp.exp(far_scores - row_top)
-        row_total = (
-            own_total * own_factor
-            + jnp.sum(halo_exp, axis=1, keepdims=True)
-            + jnp.sum(far_exp, axis=1, keepdims=True)
-        )
-        own_prob = (own_exp * (own_factor / row_total)).astype(jnp.bfloat16)
-        halo_prob = (halo_exp / row_total).astype(jnp.bfloat16)
+        row_total = near_total * near_factor + jnp.sum(far_exp, axis=1, keepdims=True)
+        near_scale = near_factor / row_total
+        own_prob = (own_exp * near_scale).astype(jnp.bfloat16)
+        halo_prob = (halo_exp * near_scale).astype(jnp.bfloat16)
         far_prob = (far_exp / row_total).astype(jnp.bfloat16)
         mixed = jnp.dot(own_prob, key_value[1, :, cols], preferred_element_type=jnp.float32)
         mixed = mixed + jnp.dot(halo_prob, halo[1, :, cols], preferred_element_type=jnp.float32)

time: 61.6 us -> 57.2 us (0.929); the launches traced: 61.4 us -> 56.1 us
  waiting for transfers between devices: 21.9 us -> 18.2 us
  matrix products: 12.1 us -> 10.9 us
    ppermute x1, waiting for transfers between devices: 21.3 us -> 16.7 us  [per_device(): lax.ppermute(chosen, 'seq', back)]
    ppermute x1, waiting for transfers between devices: 0.57 us -> 1.47 us  [per_device(): parts.append(lax.ppermute(mine, 'rep', shift))]
    dot_general x5, matrix products: 3.67 us -> 2.87 us  [per_device(): jnp.dot(own_prob, key_value[1, :, cols], preferred_element_type=jnp.float32)]
    reduce_sum x5 -> x3, other arithmetic: 2.63 us -> 2.32 us  [per_device(): jnp.sum(own_exp, axis=1, keepdims=True)]
  transfers between devices with their start and end apart: 5 -> 5, of which waited for: 2 -> 2; matrix products, arithmetic and copies ran while one was open for 19% -> 24% of each run, Pallas kernels for 0% -> 0%
where the time goes in v4:
time: 57.2 us; the launch traced here: 56.1 us
  waiting for transfers between devices  18.2 us (32%)
  starting transfers between devices  12 us (21%)
  matrix products  10.9 us (19%)
  other arithmetic  7.23 us (13%)
  local copies, waits for them, and re-layouts  5.53 us (10%)
  between operations  2.23 us (4%)
    ppermute x1, waiting for transfers between devices, per_device(): lax.ppermute(chosen, 'seq', back)  16.7 us
    ppermute x1, starting transfers between devices, per_device(): lax.ppermute(chosen, 'seq', back)  4.46 us
    ppermute x1, starting transfers between devices, per_device(): wanted = lax.ppermute(phase[None], 'seq', pairs)[0]  4.04 us
    slice x1, local copies, waits for them, and re-layouts, halo_frame(): first = lax.slice_in_dim(key_value, 0, frame_rows, axis=1)  3.44 us
    dot_general x5, matrix products, per_device(): jnp.dot(own_prob, key_value[1, :, cols], preferred_element_type=jnp.float32)  2.87 us
    dot_general x5, matrix products, per_device(): jnp.dot(query_head, key_value[0, :, cols].T, preferred_element_type=jnp.f...  2.6 us
    reduce_sum x3, other arithmetic, per_device(): jnp.sum(own_exp, axis=1, keepdims=True)  2.32 us
    ppermute x1, starting transfers between devices, halo_frame(): high = lax.ppermute(first, ('seq', 'rep'), backward)  1.74 us
  transfers between devices with their start and end apart: 5, of which 2 were waited for; matrix products, arithmetic and copies ran while one was open for 24% of the time, Pallas kernels for 0%

profile of v4, /device:TPU:0, one launch (start us, length us, event | category | flops | bytes accessed | tf_op | source)
XLA Modules:
  0.0 56.1 jit_solution(1584045199273578915)
XLA Ops:
  0.0 0.7 %and_select_fusion.1 = s32[8]{0:T(128)S(1)} fusion(s32[4,8]{1,0:T(4,128)} %param.5), kind=kLoop, calls=%fused_computation.187 | loop fusion | flops 56 | bytes 64 | tf_op jit(solution)/shard_map/jit(remainder)/select_n | solution.py:54
  0.7 0.6 %dynamic_slice.14 = s32[1]{0:T(128)} dynamic-slice(s32[8]{0:T(128)S(1)} %and_select_fusion.1, s32[]{:T(128)S(6)} %select_n.95), dynamic_slice_sizes={1} | dynamic-slice | bytes 12 | tf_op jit(solution)/shard_map/jit(dynamic_index_in_dim)/dynamic_slice | solution.py:75
  1.3 4.0 %collective-permute-start = (s32[1]{0:T(128)}, s32[1]{0:T(128)}, u32[]{:S(2)}, u32[]{:S(2)}) collective-permute-start(s32[1]{0:T(128)} %dynamic_slice.14), channel_id=1, source_target_pairs={{0,8},{4,12},{8,0},{12,4},{1,9},{5,13},{9,1},{13,5},{2,10},{6,14},... | collective-permute-start | bytes 20 | tf_op jit(solution)/shard_map/ppermute | solution.py:76
  5.3 3.4 %fusion.115 = (bf16[2,512,640]{2,1,0:T(8,128)(2,1)}, bf16[2,512,640]{2,1,0:T(8,128)(2,1)}) fusion(bf16[2,1024,640]{2,1,0:T(8,128)(2,1)} %param.4), kind=kLoop, calls=%fused_computation.207 | loop fusion | bytes 5242880 | tf_op jit(solution)/shard_map/slice | solution.py:24
  8.8 1.7 %collective-permute-start.2 = (bf16[2,512,640]{2,1,0:T(8,128)(2,1)}, bf16[2,512,640]{2,1,0:T(8,128)(2,1)}, u32[]{:S(2)}, u32[]{:S(2)}) collective-permute-start(bf16[2,512,640]{2,1,0:T(8,128)(2,1)} %get-tuple-element.82), channel_id=1, source_target_pairs={{1,4},{5,8},{9,12},{3,6},{7,10},{11,14},{17,20},{21,24},{25,28},{1... | collective-permute-start | bytes 3932168 | tf_op jit(solution)/shard_map/ppermute | solution.py:27
  10.5 1.7 %collective-permute-start.3 = (bf16[2,512,640]{2,1,0:T(8,128)(2,1)}, bf16[2,512,640]{2,1,0:T(8,128)(2,1)}, u32[]{:S(2)}, u32[]{:S(2)}) collective-permute-start(bf16[2,512,640]{2,1,0:T(8,128)(2,1)} %get-tuple-element.81), channel_id=1, source_target_pairs={{4,1},{8,5},{12,9},{6,3},{10,7},{14,11},{20,17},{24,21},{28,25},{2... | collective-permute-start | bytes 3932168 | tf_op jit(solution)/shard_map/ppermute | solution.py:28
  12.3 0.0 copy-done.2
  12.3 0.8 %subtract_reduce_fusion = s32[4]{0:T(128)S(1)} fusion(s32[4,8]{1,0:T(4,128)S(1)} %copy-done.2, s32[]{:T(128)S(6)} %select_n.95, s32[]{:T(128)} %bitcast.24, s32[]{:T(128)S(6)} %mul.171), kind=kLoop, calls=%fused_computation.183 | loop fusion | flops 8 | bytes 44 | tf_op jit(solution)/shard_map/sub | solution.py:82
  13.1 0.2 and_reduce_fusion
  13.3 0.0 collective-permute-done
  15.2 0.0 copy-done
  15.3 4.5 %collective-permute-start.1 = (bf16[2,1,128,640]{3,2,0,1:T(8,128)(2,1)S(1)}, bf16[2,1,128,640]{3,2,0,1:T(8,128)(2,1)S(1)}, u32[]{:S(2)}, u32[]{:S(2)}) collective-permute-start(bf16[2,1,128,640]{3,2,0,1:T(8,128)(2,1)S(1)} %dynamic-slice_bitcast_fusion), channel_id=1, source_target_pairs={{8,0},{12,4},{0,8},{4,12},{9,1},{13,5},{1,9},{5,13},{10,2},{14,6},... | collective-permute-start | bytes 983048 | tf_op jit(solution)/shard_map/ppermute | solution.py:86
  19.8 0.5 multiply_reduce_fusion.1
  20.3 0.5 multiply_reduce_fusion
  20.8 0.5 multiply_reduce_fusion.3
  21.3 0.5 multiply_reduce_fusion.2
  21.8 0.5 multiply_reduce_fusion.4
  22.4 0.0 collective-permute-done.2
  22.4 0.0 collective-permute-done.3
  22.4 1.5 %broadcast_select_fusion = bf16[2,512,640]{2,1,0:T(8,128)(2,1)S(1)} fusion(bf16[2,512,640]{2,1,0:T(8,128)(2,1)} %collective-permute-done.2, bf16[2,512,640]{2,1,0:T(8,128)(2,1)} %collective-permute-done.3, pred[]{:T(512)S(6)} %eq.27), kind=kLoop, calls=%fused_computation.25 | loop fusion | flops 655360 | bytes 3932161 | tf_op jit(solution)/shard_map/jit(_where)/select_n | solution.py:29
  23.8 0.3 fusion.119
  24.2 0.3 fusion.120
  24.5 0.3 fusion.117
  24.8 0.3 fusion.118
  25.1 0.3 fusion.116
  25.5 0.3 fusion.105
  25.8 0.9 %fusion.106 = (f32[512]{0:T(512)S(1)}, f32[512,1024]{1,0:T(8,128)S(1)}, f32[512]{0:T(512)S(1)}, f32[512,1024]{1,0:T(8,128)S(1)}) fusion(f32[512]{0:T(512)S(1)} %max.103, f32[512,1024]{1,0:T(8,128)S(1)} %get-tuple-element.100, f32[512]{0:T(512)S(1)} %max.101, f32[512,1024]{1,0:T(8,128)S(1)} %get-tuple-element.96), kind=kLoop, calls=%fused_computation.198 | loop fusion | flops 3144704 | bytes 8396800 | tf_op jit(solution)/shard_map/reduce_sum | solution.py:110
  26.7 0.3 fusion.109
  27.0 0.9 %fusion.110 = (f32[512]{0:T(512)S(1)}, f32[512,1024]{1,0:T(8,128)S(1)}, f32[512]{0:T(512)S(1)}, f32[512,1024]{1,0:T(8,128)S(1)}) fusion(f32[512]{0:T(512)S(1)} %max.99, f32[512,1024]{1,0:T(8,128)S(1)} %get-tuple-element.92, f32[512]{0:T(512)S(1)} %max.97, f32[512,1024]{1,0:T(8,128)S(1)} %get-tuple-element.88), kind=kLoop, calls=%fused_computation.202 | loop fusion | flops 3144704 | bytes 8396800 | tf_op jit(solution)/shard_map/reduce_sum | solution.py:110
  27.9 0.2 fusion.113
  28.1 0.5 fusion.114
  28.7 16.7 %collective-permute-done.1 = bf16[2,1,128,640]{3,2,0,1:T(8,128)(2,1)S(1)} collective-permute-done((bf16[2,1,128,640]{3,2,0,1:T(8,128)(2,1)S(1)}, bf16[2,1,128,640]{3,2,0,1:T(8,128)(2,1)S(1)}, u32[]{:S(2)}, u32[]{:S(2)}) %collective-permute-start.1) | collective-permute-done | bytes 327712 | tf_op jit(solution)/shard_map/ppermute | solution.py:86
  45.4 0.0 collective-permute-start.4
  45.4 0.1 pad_add_fusion
  45.5 0.1 compare_and_fusion
  45.6 1.5 %collective-permute-done.4 = bf16[2,1,1,128,640]{4,3,0,2,1:T(8,128)(2,1)S(1)} collective-permute-done((bf16[2,1,1,128,640]{4,3,0,2,1:T(8,128)(2,1)S(1)}, bf16[2,1,1,128,640]{4,3,0,2,1:T(8,128)(2,1)S(1)}, u32[]{:S(2)}, u32[]{:S(2)}) %collective-permute-start.4) | collective-permute-done | bytes 327712 | tf_op jit(solution)/shard_map/ppermute | solution.py:121
  47.0 0.1 pad_maximum_fusion
  47.1 0.3 broadcast_in_dim.97
  47.5 0.3 fusion.125
  47.7 0.3 fusion.124
  48.0 0.3 fusion.123
  48.2 0.3 fusion.122
  48.5 0.3 fusion.121
  48.8 0.1 fusion.49
  48.9 0.3 fusion.39
  49.2 0.6 %fusion.29 = f32[512,128]{0,1:T(8,128)S(1)} fusion(f32[512,128]{0,1:T(8,128)S(1)} %fusion.39, f32[512,1024]{1,0:T(8,128)S(1)} %get-tuple-element.47, f32[512]{0:T(512)S(1)} %bitcast.215, bf16[2,1024,640]{2,1,0:T(8,128)(2,1)S(1)} %copy-done), kind=kOutput, calls=%fused_computation.60 | convolution fusion | flops 135331840 | bytes 2885632 | tf_op jit(solution)/shard_map/dot_general | solution.py:150
  49.8 0.1 fusion.48
  49.9 0.3 fusion.38
  50.2 0.6 %fusion.27 = f32[512,128]{0,1:T(8,128)S(1)} fusion(f32[512,128]{0,1:T(8,128)S(1)} %fusion.38, f32[512,1024]{1,0:T(8,128)S(1)} %get-tuple-element.43, f32[512]{0:T(512)S(1)} %bitcast.217, bf16[2,1024,640]{2,1,0:T(8,128)(2,1)S(1)} %copy-done), kind=kOutput, calls=%fused_computation.58 | convolution fusion | flops 135331840 | bytes 2885632 | tf_op jit(solution)/shard_map/dot_general | solution.py:150
  50.8 0.1 fusion.47
  50.9 0.3 fusion.37
  51.2 0.6 %fusion.25 = f32[512,128]{0,1:T(8,128)S(1)} fusion(f32[512,128]{0,1:T(8,128)S(1)} %fusion.37, f32[512,1024]{1,0:T(8,128)S(1)} %get-tuple-element.39, f32[512]{0:T(512)S(1)} %bitcast.219, bf16[2,1024,640]{2,1,0:T(8,128)(2,1)S(1)} %copy-done), kind=kOutput, calls=%fused_computation.56 | convolution fusion | flops 135331840 | bytes 2885632 | tf_op jit(solution)/shard_map/dot_general | solution.py:150
  51.8 0.1 fusion.46
  51.9 0.3 fusion.36
  52.2 0.6 %fusion.23 = f32[512,128]{0,1:T(8,128)S(1)} fusion(f32[512,128]{0,1:T(8,128)S(1)} %fusion.36, f32[512,1024]{1,0:T(8,128)S(1)} %get-tuple-element.35, f32[512]{0:T(512)S(1)} %bitcast.221, bf16[2,1024,640]{2,1,0:T(8,128)(2,1)S(1)} %copy-done), kind=kOutput, calls=%fused_computation.54 | convolution fusion | flops 135331840 | bytes 2885632 | tf_op jit(solution)/shard_map/dot_general | solution.py:150
  52.8 0.1 fusion.45
  52.9 0.3 fusion.35
  53.2 0.6 %fusion.21 = f32[512,128]{0,1:T(8,128)S(1)} fusion(f32[512,128]{0,1:T(8,128)S(1)} %fusion.35, f32[512,1024]{1,0:T(8,128)S(1)} %get-tuple-element.30, f32[512]{0:T(512)S(1)} %bitcast.213, bf16[2,1024,640]{2,1,0:T(8,128)(2,1)S(1)} %copy-done), kind=kOutput, calls=%fused_computation.52 | convolution fusion | flops 135331840 | bytes 2885632 | tf_op jit(solution)/shard_map/dot_general | solution.py:150
  53.8 0.2 fusion.11
  54.0 0.3 fusion.13
  54.3 0.2 fusion.15
  54.5 0.3 fusion.17
  54.8 0.2 fusion.19
  55.1 1.1 %copy.7 = bf16[512,640]{1,0:T(8,128)(2,1)} copy(bf16[512,640]{0,1:T(8,128)(2,1)S(1)} %fusion.19) | data formatting | bytes 1310720 | tf_op jit(solution)/shard_map/concatenate | solution.py:154
  (27 shorter events, 0.2 us)
Async XLA Ops:
  1.3 11.0 %copy-start.2 = (s32[4,8]{1,0:T(4,128)S(1)}, s32[4,8]{1,0:T(4,128)}, u32[]{:S(2)}) copy-start(s32[4,8]{1,0:T(4,128)} %param.5) | copy-start | bytes 388
  1.3 13.9 %copy-start = (bf16[2,1024,640]{2,1,0:T(8,128)(2,1)S(1)}, bf16[2,1024,640]{2,1,0:T(8,128)(2,1)}, u32[]{:S(2)}) copy-start(bf16[2,1024,640]{2,1,0:T(8,128)(2,1)} %param.4) | copy-start | bytes 7864324
  1.3 18.4 %copy-start.1 = (bf16[512,640]{1,0:T(8,128)(2,1)S(1)}, bf16[512,640]{1,0:T(8,128)(2,1)}, u32[]{:S(2)}) copy-start(bf16[512,640]{1,0:T(8,128)(2,1)} %param.3) | copy-start | bytes 1966084
  1.3 12.0 %collective-permute-start = (s32[1]{0:T(128)}, s32[1]{0:T(128)}, u32[]{:S(2)}, u32[]{:S(2)}) collective-permute-start(s32[1]{0:T(128)} %dynamic_slice.14), channel_id=1, source_target_pairs={{0,8},{4,12},{8,0},{12,4},{1,9},{5,13},{9,1},{13,5},{2,10},{6,14},... | collective-permute-start | bytes 20 | tf_op jit(solution)/shard_map/ppermute | solution.py:76
  8.8 13.6 %collective-permute-start.2 = (bf16[2,512,640]{2,1,0:T(8,128)(2,1)}, bf16[2,512,640]{2,1,0:T(8,128)(2,1)}, u32[]{:S(2)}, u32[]{:S(2)}) collective-permute-start(bf16[2,512,640]{2,1,0:T(8,128)(2,1)} %get-tuple-element.82), channel_id=1, source_target_pairs={{1,4},{5,8},{9,12},{3,6},{7,10},{11,14},{17,20},{21,24},{25,28},{1... | collective-permute-start | bytes 3932168 | tf_op jit(solution)/shard_map/ppermute | solution.py:27
  10.5 11.8 %collective-permute-start.3 = (bf16[2,512,640]{2,1,0:T(8,128)(2,1)}, bf16[2,512,640]{2,1,0:T(8,128)(2,1)}, u32[]{:S(2)}, u32[]{:S(2)}) collective-permute-start(bf16[2,512,640]{2,1,0:T(8,128)(2,1)} %get-tuple-element.81), channel_id=1, source_target_pairs={{4,1},{8,5},{12,9},{6,3},{10,7},{14,11},{20,17},{24,21},{28,25},{2... | collective-permute-start | bytes 3932168 | tf_op jit(solution)/shard_map/ppermute | solution.py:28
  15.3 30.1 %collective-permute-start.1 = (bf16[2,1,128,640]{3,2,0,1:T(8,128)(2,1)S(1)}, bf16[2,1,128,640]{3,2,0,1:T(8,128)(2,1)S(1)}, u32[]{:S(2)}, u32[]{:S(2)}) collective-permute-start(bf16[2,1,128,640]{3,2,0,1:T(8,128)(2,1)S(1)} %dynamic-slice_bitcast_fusion), channel_id=1, source_target_pairs={{8,0},{12,4},{0,8},{4,12},{9,1},{13,5},{1,9},{5,13},{10,2},{14,6},... | collective-permute-start | bytes 983048 | tf_op jit(solution)/shard_map/ppermute | solution.py:86
  45.4 1.6 %collective-permute-start.4 = (bf16[2,1,1,128,640]{4,3,0,2,1:T(8,128)(2,1)S(1)}, bf16[2,1,1,128,640]{4,3,0,2,1:T(8,128)(2,1)S(1)}, u32[]{:S(2)}, u32[]{:S(2)}) collective-permute-start(bf16[2,1,1,128,640]{4,3,0,2,1:T(8,128)(2,1)S(1)} %bitcast.193), channel_id=1, source_target_pairs={{0,1},{1,0},{2,3},{3,2},{4,5},{5,4},{6,7},{7,6},{8,9},{9,8},{10,11... | collective-permute-start | bytes 983048 | tf_op jit(solution)/shard_map/ppermute | solution.py:121

commit v5 on v4

--- a/solution.py
+++ b/solution.py
@@ -27,6 +27,20 @@
     low = lax.ppermute(last, ("seq", "rep"), forward)
     high = lax.ppermute(first, ("seq", "rep"), backward)
     return jnp.where(rep_index == 0, low, high)
+
+
+def send_far(chosen, pairs):
+    if any(abs(b - a) != 2 for a, b in pairs):
+        return lax.ppermute(chosen, "seq", pairs)
+    total = None
+    for sign in (1, -1):
+        moving = [(a, b) for a, b in pairs if (b - a) * sign > 0]
+        if not moving:
+            continue
+        hop = lax.ppermute(chosen, "seq", [(a, a + sign) for a, _ in moving])
+        hop = lax.ppermute(hop, "seq", [(a + sign, b) for a, b in moving])
+        total = hop if total is None else total + hop
+    return total
 
 
 def per_device(query, key_value, key_blocks):
@@ -83,7 +97,7 @@
             pick_list.append(pick)
             valid_list.append((named >= 0) & inside)
     query, payloads = lax.optimization_barrier((query, [chosen for chosen, _ in received]))
-    received = [lax.ppermute(chosen, "seq", back) for chosen, (_, back) in zip(payloads, received)]
+    received = [send_far(chosen, back) for chosen, (_, back) in zip(payloads, received)]
     slot_count = len(received)
     halo_valid = ((rep_index == 0) & (slab_index > 0)) | (
         (rep_index == rep_count - 1) & (slab_index < seq_count - 1)

time: 57.2 us -> 65.1 us (1.14); the launches traced: 56.1 us -> 64.8 us
  starting transfers between devices: 12 us -> 18.2 us
  waiting for transfers between devices: 18.2 us -> 20.7 us
    ppermute x1 -> x4, starting transfers between devices: 4.46 us -> 10.6 us  [the longest x2 8.42 us: send_far(): hop = lax.ppermute(chosen, 'seq', [(a, a + sign) for a, _ in moving])]
    ppermute x1 -> x4, waiting for transfers between devices: 16.7 us -> 19.2 us  [the longest x2 13.4 us: send_far(): hop = lax.ppermute(hop, 'seq', [(a + sign, b) for a, b in moving])]
  transfers between devices with their start and end apart: 5 -> 8, of which waited for: 2 -> 3; matrix products, arithmetic and copies ran while one was open for 24% -> 11% of each run, Pallas kernels for 0% -> 0%
where the time goes in v5:
time: 65.1 us; the launch traced here: 64.8 us
  waiting for transfers between devices  20.7 us (32%)
  starting transfers between devices  18.2 us (28%)
  matrix products  10.8 us (17%)
  other arithmetic  7.29 us (11%)
  local copies, waits for them, and re-layouts  5.53 us (8%)
  between operations  2.32 us (4%)
    ppermute x2, waiting for transfers between devices, send_far(): hop = lax.ppermute(hop, 'seq', [(a + sign, b) for a, b in moving])  13.4 us
    ppermute x2, starting transfers between devices, send_far(): hop = lax.ppermute(chosen, 'seq', [(a, a + sign) for a, _ in moving])  8.42 us
    ppermute x2, waiting for transfers between devices, send_far(): hop = lax.ppermute(chosen, 'seq', [(a, a + sign) for a, _ in moving])  5.87 us
    ppermute x1, starting transfers between devices, per_device(): wanted = lax.ppermute(phase[None], 'seq', pairs)[0]  4.04 us
    slice x1, local copies, waits for them, and re-layouts, halo_frame(): first = lax.slice_in_dim(key_value, 0, frame_rows, axis=1)  3.44 us
    dot_general x5, matrix products, per_device(): jnp.dot(own_prob, key_value[1, :, cols], preferred_element_type=jnp.float32)  2.82 us
    dot_general x5, matrix products, per_device(): jnp.dot(query_head, key_value[0, :, cols].T, preferred_element_type=jnp.f...  2.6 us
    reduce_sum x3, other arithmetic, per_device(): jnp.sum(own_exp, axis=1, keepdims=True)  2.3 us
  transfers between devices with their start and end apart: 8, of which 3 were waited for; matrix products, arithmetic and copies ran while one was open for 11% of the time, Pallas kernels for 0%

profile of v5, /device:TPU:0, one launch (start us, length us, event | category | flops | bytes accessed | tf_op | source)
XLA Modules:
  0.0 64.8 jit_solution(6091607715665685955)
XLA Ops:
  0.0 0.7 %and_select_fusion.1 = s32[8]{0:T(128)S(1)} fusion(s32[4,8]{1,0:T(4,128)} %param.5), kind=kLoop, calls=%fused_computation.182 | loop fusion | flops 56 | bytes 64 | tf_op jit(solution)/shard_map/jit(remainder)/select_n | solution.py:68
  0.7 0.6 dynamic_slice.14
  1.3 4.0 %collective-permute-start = (s32[1]{0:T(128)}, s32[1]{0:T(128)}, u32[]{:S(2)}, u32[]{:S(2)}) collective-permute-start(s32[1]{0:T(128)} %dynamic_slice.14), channel_id=1, source_target_pairs={{0,8},{4,12},{8,0},{12,4},{1,9},{5,13},{9,1},{13,5},{2,10},{6,14},... | collective-permute-start | bytes 20 | tf_op jit(solution)/shard_map/ppermute | solution.py:90
  5.3 3.4 %fusion.105 = (bf16[2,512,640]{2,1,0:T(8,128)(2,1)}, bf16[2,512,640]{2,1,0:T(8,128)(2,1)}) fusion(bf16[2,1024,640]{2,1,0:T(8,128)(2,1)} %param.4), kind=kLoop, calls=%fused_computation.202 | loop fusion | bytes 5242880 | tf_op jit(solution)/shard_map/slice | solution.py:24
  8.8 1.7 %collective-permute-start.5 = (bf16[2,512,640]{2,1,0:T(8,128)(2,1)}, bf16[2,512,640]{2,1,0:T(8,128)(2,1)}, u32[]{:S(2)}, u32[]{:S(2)}) collective-permute-start(bf16[2,512,640]{2,1,0:T(8,128)(2,1)} %get-tuple-element.82), channel_id=1, source_target_pairs={{1,4},{5,8},{9,12},{3,6},{7,10},{11,14},{17,20},{21,24},{25,28},{1... | collective-permute-start | bytes 3932168 | tf_op jit(solution)/shard_map/ppermute | solution.py:27
  10.5 1.7 %collective-permute-start.6 = (bf16[2,512,640]{2,1,0:T(8,128)(2,1)}, bf16[2,512,640]{2,1,0:T(8,128)(2,1)}, u32[]{:S(2)}, u32[]{:S(2)}) collective-permute-start(bf16[2,512,640]{2,1,0:T(8,128)(2,1)} %get-tuple-element.81), channel_id=1, source_target_pairs={{4,1},{8,5},{12,9},{6,3},{10,7},{14,11},{20,17},{24,21},{28,25},{2... | collective-permute-start | bytes 3932168 | tf_op jit(solution)/shard_map/ppermute | solution.py:28
  12.3 0.8 %subtract_reduce_fusion = s32[4]{0:T(128)S(1)} fusion(s32[4,8]{1,0:T(4,128)S(1)} %copy-done.2, s32[]{:T(128)S(6)} %select_n.95, s32[]{:T(128)} %bitcast.24, s32[]{:T(128)S(6)} %mul.171), kind=kLoop, calls=%fused_computation.178 | loop fusion | flops 8 | bytes 44 | tf_op jit(solution)/shard_map/sub | solution.py:96
  13.1 0.2 and_reduce_fusion
  15.3 7.7 %collective-permute-start.1 = (bf16[2,1,128,640]{3,2,0,1:T(8,128)(2,1)S(1)}, bf16[2,1,128,640]{3,2,0,1:T(8,128)(2,1)S(1)}, u32[]{:S(2)}, u32[]{:S(2)}) collective-permute-start(bf16[2,1,128,640]{3,2,0,1:T(8,128)(2,1)S(1)} %dynamic-slice_bitcast_fusion), channel_id=1, source_target_pairs={{0,4},{4,8},{1,5},{5,9},{2,6},{6,10},{3,7},{7,11},{16,20},{20,24},... | collective-permute-start | bytes 983048 | tf_op jit(solution)/shard_map/ppermute | solution.py:40
  23.0 0.7 %collective-permute-start.3 = (bf16[2,1,128,640]{3,2,0,1:T(8,128)(2,1)S(1)}, bf16[2,1,128,640]{3,2,0,1:T(8,128)(2,1)S(1)}, u32[]{:S(2)}, u32[]{:S(2)}) collective-permute-start(bf16[2,1,128,640]{3,2,0,1:T(8,128)(2,1)S(1)} %dynamic-slice_bitcast_fusion), channel_id=1, source_target_pairs={{8,4},{12,8},{9,5},{13,9},{10,6},{14,10},{11,7},{15,11},{24,20},{2... | collective-permute-start | bytes 983048 | tf_op jit(solution)/shard_map/ppermute | solution.py:40
  23.7 0.5 multiply_reduce_fusion.1
  24.2 0.5 multiply_reduce_fusion
  24.8 0.5 multiply_reduce_fusion.3
  25.3 5.9 %collective-permute-done.1 = bf16[2,1,128,640]{3,2,0,1:T(8,128)(2,1)S(1)} collective-permute-done((bf16[2,1,128,640]{3,2,0,1:T(8,128)(2,1)S(1)}, bf16[2,1,128,640]{3,2,0,1:T(8,128)(2,1)S(1)}, u32[]{:S(2)}, u32[]{:S(2)}) %collective-permute-start.1) | collective-permute-done | bytes 327712 | tf_op jit(solution)/shard_map/ppermute | solution.py:40
  31.2 0.7 %collective-permute-start.2 = (bf16[2,1,128,640]{3,2,0,1:T(8,128)(2,1)S(1)}, bf16[2,1,128,640]{3,2,0,1:T(8,128)(2,1)S(1)}, u32[]{:S(2)}, u32[]{:S(2)}) collective-permute-start(bf16[2,1,128,640]{3,2,0,1:T(8,128)(2,1)S(1)} %collective-permute-done.1), channel_id=1, source_target_pairs={{4,8},{8,12},{5,9},{9,13},{6,10},{10,14},{7,11},{11,15},{20,24},{2... | collective-permute-start | bytes 983048 | tf_op jit(solution)/shard_map/ppermute | solution.py:41
  31.8 1.5 %collective-permute-start.4 = (bf16[2,1,128,640]{3,2,0,1:T(8,128)(2,1)S(1)}, bf16[2,1,128,640]{3,2,0,1:T(8,128)(2,1)S(1)}, u32[]{:S(2)}, u32[]{:S(2)}) collective-permute-start(bf16[2,1,128,640]{3,2,0,1:T(8,128)(2,1)S(1)} %collective-permute-done.3), channel_id=1, source_target_pairs={{4,0},{8,4},{5,1},{9,5},{6,2},{10,6},{7,3},{11,7},{20,16},{24,20},... | collective-permute-start | bytes 983048 | tf_op jit(solution)/shard_map/ppermute | solution.py:41
  33.3 0.5 multiply_reduce_fusion.2
  33.8 0.5 multiply_reduce_fusion.4
  34.4 13.4 %collective-permute-done.4 = bf16[2,1,128,640]{3,2,0,1:T(8,128)(2,1)S(1)} collective-permute-done((bf16[2,1,128,640]{3,2,0,1:T(8,128)(2,1)S(1)}, bf16[2,1,128,640]{3,2,0,1:T(8,128)(2,1)S(1)}, u32[]{:S(2)}, u32[]{:S(2)}) %collective-permute-start.4) | collective-permute-done | bytes 327712 | tf_op jit(solution)/shard_map/ppermute | solution.py:41
  47.7 0.1 add.163
  47.8 1.5 %broadcast_select_fusion = bf16[2,512,640]{2,1,0:T(8,128)(2,1)S(1)} fusion(bf16[2,512,640]{2,1,0:T(8,128)(2,1)} %collective-permute-done.5, bf16[2,512,640]{2,1,0:T(8,128)(2,1)} %collective-permute-done.6, pred[]{:T(512)S(6)} %eq.27), kind=kLoop, calls=%fused_computation.25 | loop fusion | flops 655360 | bytes 3932161 | tf_op jit(solution)/shard_map/jit(_where)/select_n | solution.py:29
  49.3 0.3 fusion.109
  49.6 0.3 fusion.110
  49.9 0.3 fusion.107
  50.2 0.3 fusion.108
  50.5 0.3 fusion.106
  50.9 0.2 fusion.103
  51.1 0.5 fusion.104
  51.6 0.3 fusion.95
  51.9 0.9 %fusion.96 = (f32[512]{0:T(512)S(1)}, f32[512,1024]{1,0:T(8,128)S(1)}, f32[512]{0:T(512)S(1)}, f32[512,1024]{1,0:T(8,128)S(1)}) fusion(f32[512]{0:T(512)S(1)} %max.103, f32[512,1024]{1,0:T(8,128)S(1)} %get-tuple-element.100, f32[512]{0:T(512)S(1)} %max.101, f32[512,1024]{1,0:T(8,128)S(1)} %get-tuple-element.96), kind=kLoop, calls=%fused_computation.193 | loop fusion | flops 3144704 | bytes 8396800 | tf_op jit(solution)/shard_map/reduce_sum | solution.py:124
  52.8 0.3 fusion.99
  53.1 0.9 %fusion.100 = (f32[512]{0:T(512)S(1)}, f32[512,1024]{1,0:T(8,128)S(1)}, f32[512]{0:T(512)S(1)}, f32[512,1024]{1,0:T(8,128)S(1)}) fusion(f32[512]{0:T(512)S(1)} %max.99, f32[512,1024]{1,0:T(8,128)S(1)} %get-tuple-element.92, f32[512]{0:T(512)S(1)} %max.97, f32[512,1024]{1,0:T(8,128)S(1)} %get-tuple-element.88), kind=kLoop, calls=%fused_computation.197 | loop fusion | flops 3144704 | bytes 8396800 | tf_op jit(solution)/shard_map/reduce_sum | solution.py:124
  54.1 0.1 collective-permute-start.7
  54.2 0.1 pad_add_fusion
  54.2 0.1 compare_and_fusion
  54.3 1.5 %collective-permute-done.7 = bf16[2,1,1,128,640]{4,3,0,2,1:T(8,128)(2,1)S(1)} collective-permute-done((bf16[2,1,1,128,640]{4,3,0,2,1:T(8,128)(2,1)S(1)}, bf16[2,1,1,128,640]{4,3,0,2,1:T(8,128)(2,1)S(1)}, u32[]{:S(2)}, u32[]{:S(2)}) %collective-permute-start.7) | collective-permute-done | bytes 327712 | tf_op jit(solution)/shard_map/ppermute | solution.py:135
  55.8 0.1 pad_maximum_fusion
  55.9 0.3 broadcast_in_dim.97
  56.2 0.3 fusion.115
  56.5 0.3 fusion.114
  56.7 0.3 fusion.113
  57.0 0.3 fusion.112
  57.2 0.3 fusion.111
  57.5 0.1 fusion.39
  57.6 0.6 fusion.24
  58.2 0.3 convolution_add_fusion.1
  58.5 0.1 fusion.38
  58.6 0.6 fusion.23
  59.2 0.3 convolution_add_fusion.3
  59.5 0.1 fusion.37
  59.6 0.6 fusion.22
  60.2 0.3 convolution_add_fusion.5
  60.5 0.1 fusion.36
  60.6 0.6 fusion.21
  61.2 0.3 convolution_add_fusion.7
  61.5 0.1 fusion.35
  61.6 0.6 fusion.20
  62.2 0.3 convolution_add_fusion.9
  62.5 0.3 fusion.11
  62.7 0.3 fusion.13
  63.0 0.2 fusion.15
  63.2 0.2 fusion.17
  63.5 0.2 fusion.19
  63.7 1.1 %copy.7 = bf16[512,640]{1,0:T(8,128)(2,1)} copy(bf16[512,640]{0,1:T(8,128)(2,1)S(1)} %fusion.19) | data formatting | bytes 1310720 | tf_op jit(solution)/shard_map/concatenate | solution.py:168
  (34 shorter events, 0.2 us)
Async XLA Ops:
  1.3 11.0 %copy-start.2 = (s32[4,8]{1,0:T(4,128)S(1)}, s32[4,8]{1,0:T(4,128)}, u32[]{:S(2)}) copy-start(s32[4,8]{1,0:T(4,128)} %param.5) | copy-start | bytes 388
  1.3 13.9 %copy-start = (bf16[2,1024,640]{2,1,0:T(8,128)(2,1)S(1)}, bf16[2,1024,640]{2,1,0:T(8,128)(2,1)}, u32[]{:S(2)}) copy-start(bf16[2,1024,640]{2,1,0:T(8,128)(2,1)} %param.4) | copy-start | bytes 7864324
  1.3 22.4 %copy-start.1 = (bf16[512,640]{1,0:T(8,128)(2,1)S(1)}, bf16[512,640]{1,0:T(8,128)(2,1)}, u32[]{:S(2)}) copy-start(bf16[512,640]{1,0:T(8,128)(2,1)} %param.3) | copy-start | bytes 1966084
  1.3 12.0 %collective-permute-start = (s32[1]{0:T(128)}, s32[1]{0:T(128)}, u32[]{:S(2)}, u32[]{:S(2)}) collective-permute-start(s32[1]{0:T(128)} %dynamic_slice.14), channel_id=1, source_target_pairs={{0,8},{4,12},{8,0},{12,4},{1,9},{5,13},{9,1},{13,5},{2,10},{6,14},... | collective-permute-start | bytes 20 | tf_op jit(solution)/shard_map/ppermute | solution.py:90
  8.8 39.0 %collective-permute-start.5 = (bf16[2,512,640]{2,1,0:T(8,128)(2,1)}, bf16[2,512,640]{2,1,0:T(8,128)(2,1)}, u32[]{:S(2)}, u32[]{:S(2)}) collective-permute-start(bf16[2,512,640]{2,1,0:T(8,128)(2,1)} %get-tuple-element.82), channel_id=1, source_target_pairs={{1,4},{5,8},{9,12},{3,6},{7,10},{11,14},{17,20},{21,24},{25,28},{1... | collective-permute-start | bytes 3932168 | tf_op jit(solution)/shard_map/ppermute | solution.py:27
  10.5 37.3 %collective-permute-start.6 = (bf16[2,512,640]{2,1,0:T(8,128)(2,1)}, bf16[2,512,640]{2,1,0:T(8,128)(2,1)}, u32[]{:S(2)}, u32[]{:S(2)}) collective-permute-start(bf16[2,512,640]{2,1,0:T(8,128)(2,1)} %get-tuple-element.81), channel_id=1, source_target_pairs={{4,1},{8,5},{12,9},{6,3},{10,7},{14,11},{20,17},{24,21},{28,25},{2... | collective-permute-start | bytes 3932168 | tf_op jit(solution)/shard_map/ppermute | solution.py:28
  15.3 15.9 %collective-permute-start.1 = (bf16[2,1,128,640]{3,2,0,1:T(8,128)(2,1)S(1)}, bf16[2,1,128,640]{3,2,0,1:T(8,128)(2,1)S(1)}, u32[]{:S(2)}, u32[]{:S(2)}) collective-permute-start(bf16[2,1,128,640]{3,2,0,1:T(8,128)(2,1)S(1)} %dynamic-slice_bitcast_fusion), channel_id=1, source_target_pairs={{0,4},{4,8},{1,5},{5,9},{2,6},{6,10},{3,7},{7,11},{16,20},{20,24},... | collective-permute-start | bytes 983048 | tf_op jit(solution)/shard_map/ppermute | solution.py:40
  23.0 8.8 %collective-permute-start.3 = (bf16[2,1,128,640]{3,2,0,1:T(8,128)(2,1)S(1)}, bf16[2,1,128,640]{3,2,0,1:T(8,128)(2,1)S(1)}, u32[]{:S(2)}, u32[]{:S(2)}) collective-permute-start(bf16[2,1,128,640]{3,2,0,1:T(8,128)(2,1)S(1)} %dynamic-slice_bitcast_fusion), channel_id=1, source_target_pairs={{8,4},{12,8},{9,5},{13,9},{10,6},{14,10},{11,7},{15,11},{24,20},{2... | collective-permute-start | bytes 983048 | tf_op jit(solution)/shard_map/ppermute | solution.py:40
  31.2 3.2 %collective-permute-start.2 = (bf16[2,1,128,640]{3,2,0,1:T(8,128)(2,1)S(1)}, bf16[2,1,128,640]{3,2,0,1:T(8,128)(2,1)S(1)}, u32[]{:S(2)}, u32[]{:S(2)}) collective-permute-start(bf16[2,1,128,640]{3,2,0,1:T(8,128)(2,1)S(1)} %collective-permute-done.1), channel_id=1, source_target_pairs={{4,8},{8,12},{5,9},{9,13},{6,10},{10,14},{7,11},{11,15},{20,24},{2... | collective-permute-start | bytes 983048 | tf_op jit(solution)/shard_map/ppermute | solution.py:41
  31.8 15.9 %collective-permute-start.4 = (bf16[2,1,128,640]{3,2,0,1:T(8,128)(2,1)S(1)}, bf16[2,1,128,640]{3,2,0,1:T(8,128)(2,1)S(1)}, u32[]{:S(2)}, u32[]{:S(2)}) collective-permute-start(bf16[2,1,128,640]{3,2,0,1:T(8,128)(2,1)S(1)} %collective-permute-done.3), channel_id=1, source_target_pairs={{4,0},{8,4},{5,1},{9,5},{6,2},{10,6},{7,3},{11,7},{20,16},{24,20},... | collective-permute-start | bytes 983048 | tf_op jit(solution)/shard_map/ppermute | solution.py:41
  54.1 1.7 %collective-permute-start.7 = (bf16[2,1,1,128,640]{4,3,0,2,1:T(8,128)(2,1)S(1)}, bf16[2,1,1,128,640]{4,3,0,2,1:T(8,128)(2,1)S(1)}, u32[]{:S(2)}, u32[]{:S(2)}) collective-permute-start(bf16[2,1,1,128,640]{4,3,0,2,1:T(8,128)(2,1)S(1)} %bitcast.183), channel_id=1, source_target_pairs={{0,1},{1,0},{2,3},{3,2},{4,5},{5,4},{6,7},{7,6},{8,9},{9,8},{10,11... | collective-permute-start | bytes 983048 | tf_op jit(solution)/shard_map/ppermute | solution.py:135

commit v6 on v4

--- a/solution.py
+++ b/solution.py
@@ -18,15 +18,16 @@
     return lax.ppermute(shard, axis, pairs)
 
 
-def halo_frame(key_value, frame_rows, seq_count, rep_count, rep_index):
+def halo_frame(key_value, key_blocks, frame_rows, seq_count, rep_count, rep_index):
     slab_rows = key_value.shape[1]
     last = lax.slice_in_dim(key_value, slab_rows - frame_rows, slab_rows, axis=1)
     first = lax.slice_in_dim(key_value, 0, frame_rows, axis=1)
+    key_blocks, last, first = lax.optimization_barrier((key_blocks, last, first))
     forward = [(s * rep_count + rep_count - 1, (s + 1) * rep_count) for s in range(seq_count - 1)]
     backward = [(s * rep_count, (s - 1) * rep_count + rep_count - 1) for s in range(1, seq_count)]
     low = lax.ppermute(last, ("seq", "rep"), forward)
     high = lax.ppermute(first, ("seq", "rep"), backward)
-    return jnp.where(rep_index == 0, low, high)
+    return jnp.where(rep_index == 0, low, high), key_blocks
 
 
 def per_device(query, key_value, key_blocks):
@@ -49,7 +50,7 @@
     assert far_count % rep_count == 0
     far_share = far_count // rep_count
 
-    halo = halo_frame(key_value, frame_rows, seq_count, rep_count, rep_index)
+    halo, key_blocks = halo_frame(key_value, key_blocks, frame_rows, seq_count, rep_count, rep_index)
 
     phases = jnp.maximum(key_blocks[0], 0) % FAR_STRIDE
     stride_grid = key_value.reshape(2, far_count, FAR_STRIDE, MASK_BLOCK_SIZE, columns)

time: 57.2 us -> 56.5 us (0.988)
  other arithmetic: 7.23 us -> 6.55 us
    select_n x1, other arithmetic: 0.69 us -> 0.01 us  [per_device(): phases = jnp.maximum(key_blocks[0], 0) % FAR_STRIDE]
  transfers between devices with their start and end apart: 5 -> 5, of which waited for: 2 -> 2; matrix products, arithmetic and copies ran while one was open for 24% -> 18% of each run, Pallas kernels for 0% -> 0%
where the time goes in v6:
time: 56.5 us; the launch traced here: 55.5 us
  waiting for transfers between devices  18 us (32%)
  starting transfers between devices  11.8 us (21%)
  matrix products  10.9 us (19%)
  other arithmetic  6.55 us (12%)
  local copies, waits for them, and re-layouts  5.73 us (10%)
  between operations  2.41 us (4%)
    ppermute x1, waiting for transfers between devices, per_device(): lax.ppermute(chosen, 'seq', back)  16.6 us
    ppermute x1, starting transfers between devices, per_device(): lax.ppermute(chosen, 'seq', back)  4.3 us
    ppermute x1, starting transfers between devices, per_device(): wanted = lax.ppermute(phase[None], 'seq', pairs)[0]  4.04 us
    slice x1, local copies, waits for them, and re-layouts, halo_frame(): first = lax.slice_in_dim(key_value, 0, frame_rows, axis=1)  3.59 us
    dot_general x5, matrix products, per_device(): jnp.dot(own_prob, key_value[1, :, cols], preferred_element_type=jnp.float32)  2.86 us
    dot_general x5, matrix products, per_device(): jnp.dot(query_head, key_value[0, :, cols].T, preferred_element_type=jnp.f...  2.6 us
    reduce_sum x3, other arithmetic, per_device(): jnp.sum(own_exp, axis=1, keepdims=True)  2.32 us
    ppermute x1, starting transfers between devices, halo_frame(): high = lax.ppermute(first, ('seq', 'rep'), backward)  1.74 us
  transfers between devices with their start and end apart: 5, of which 2 were waited for; matrix products, arithmetic and copies ran while one was open for 18% of the time, Pallas kernels for 0%

profile of v6, /device:TPU:0, one launch (start us, length us, event | category | flops | bytes accessed | tf_op | source)
XLA Modules:
  0.0 55.5 jit_solution(14572086009194180484)
XLA Ops:
  0.0 3.6 %fusion.115 = (bf16[2,512,640]{2,1,0:T(8,128)(2,1)}, bf16[2,512,640]{2,1,0:T(8,128)(2,1)}) fusion(bf16[2,1024,640]{2,1,0:T(8,128)(2,1)} %param.4), kind=kLoop, calls=%fused_computation.207 | loop fusion | bytes 5242880 | tf_op jit(solution)/shard_map/slice | solution.py:24
  3.6 0.0 copy-done.2
  3.6 0.7 %dynamic_slice.14 = s32[1]{0:T(128)} dynamic-slice(s32[8]{0:T(128)S(1)} %and_select_fusion.1, s32[]{:T(128)S(6)} %select_n.95), dynamic_slice_sizes={1} | dynamic-slice | bytes 12 | tf_op jit(solution)/shard_map/jit(dynamic_index_in_dim)/dynamic_slice | solution.py:76
  4.3 4.0 %collective-permute-start = (s32[1]{0:T(128)}, s32[1]{0:T(128)}, u32[]{:S(2)}, u32[]{:S(2)}) collective-permute-start(s32[1]{0:T(128)} %dynamic_slice.14), channel_id=1, source_target_pairs={{0,8},{4,12},{8,0},{12,4},{1,9},{5,13},{9,1},{13,5},{2,10},{6,14},... | collective-permute-start | bytes 20 | tf_op jit(solution)/shard_map/ppermute | solution.py:77
  8.3 1.7 %collective-permute-start.2 = (bf16[2,512,640]{2,1,0:T(8,128)(2,1)}, bf16[2,512,640]{2,1,0:T(8,128)(2,1)}, u32[]{:S(2)}, u32[]{:S(2)}) collective-permute-start(bf16[2,512,640]{2,1,0:T(8,128)(2,1)} %get-tuple-element.34), channel_id=1, source_target_pairs={{1,4},{5,8},{9,12},{3,6},{7,10},{11,14},{17,20},{21,24},{25,28},{1... | collective-permute-start | bytes 3932168 | tf_op jit(solution)/shard_map/ppermute | solution.py:28
  10.1 1.7 %collective-permute-start.3 = (bf16[2,512,640]{2,1,0:T(8,128)(2,1)}, bf16[2,512,640]{2,1,0:T(8,128)(2,1)}, u32[]{:S(2)}, u32[]{:S(2)}) collective-permute-start(bf16[2,512,640]{2,1,0:T(8,128)(2,1)} %get-tuple-element.35), channel_id=1, source_target_pairs={{4,1},{8,5},{12,9},{6,3},{10,7},{14,11},{20,17},{24,21},{28,25},{2... | collective-permute-start | bytes 3932168 | tf_op jit(solution)/shard_map/ppermute | solution.py:29
  11.8 0.8 %subtract_reduce_fusion = s32[4]{0:T(128)S(1)} fusion(s32[4,8]{1,0:T(4,128)S(1)} %copy-done.2, s32[]{:T(128)S(6)} %select_n.95, s32[]{:T(128)} %bitcast.24, s32[]{:T(128)S(6)} %mul.171), kind=kLoop, calls=%fused_computation.183 | loop fusion | flops 8 | bytes 44 | tf_op jit(solution)/shard_map/sub | solution.py:83
  12.6 0.2 and_reduce_fusion
  12.8 0.0 collective-permute-done
  14.9 0.0 copy-done
  15.0 4.3 %collective-permute-start.1 = (bf16[2,1,128,640]{3,2,0,1:T(8,128)(2,1)S(1)}, bf16[2,1,128,640]{3,2,0,1:T(8,128)(2,1)S(1)}, u32[]{:S(2)}, u32[]{:S(2)}) collective-permute-start(bf16[2,1,128,640]{3,2,0,1:T(8,128)(2,1)S(1)} %dynamic-slice_bitcast_fusion), channel_id=1, source_target_pairs={{8,0},{12,4},{0,8},{4,12},{9,1},{13,5},{1,9},{5,13},{10,2},{14,6},... | collective-permute-start | bytes 983048 | tf_op jit(solution)/shard_map/ppermute | solution.py:87
  19.3 0.0 copy-done.1
  19.3 0.5 multiply_reduce_fusion.1
  19.8 0.5 multiply_reduce_fusion
  20.3 0.5 multiply_reduce_fusion.2
  20.8 0.5 multiply_reduce_fusion.3
  21.4 0.5 multiply_reduce_fusion.4
  21.9 0.0 collective-permute-done.2
  21.9 0.0 collective-permute-done.3
  21.9 1.5 %broadcast_select_fusion = bf16[2,512,640]{2,1,0:T(8,128)(2,1)S(1)} fusion(bf16[2,512,640]{2,1,0:T(8,128)(2,1)} %collective-permute-done.2, bf16[2,512,640]{2,1,0:T(8,128)(2,1)} %collective-permute-done.3, pred[]{:T(512)S(6)} %eq.27), kind=kLoop, calls=%fused_computation.25 | loop fusion | flops 655360 | bytes 3932161 | tf_op jit(solution)/shard_map/jit(_where)/select_n | solution.py:30
  23.4 0.3 fusion.119
  23.7 0.3 fusion.120
  24.0 0.3 fusion.118
  24.3 0.3 fusion.117
  24.6 0.3 fusion.116
  25.0 0.3 fusion.105
  25.3 0.9 %fusion.106 = (f32[512]{0:T(512)S(1)}, f32[512,1024]{1,0:T(8,128)S(1)}, f32[512]{0:T(512)S(1)}, f32[512,1024]{1,0:T(8,128)S(1)}) fusion(f32[512]{0:T(512)S(1)} %max.103, f32[512,1024]{1,0:T(8,128)S(1)} %get-tuple-element.106, f32[512]{0:T(512)S(1)} %max.101, f32[512,1024]{1,0:T(8,128)S(1)} %get-tuple-element.102), kind=kLoop, calls=%fused_computation.198 | loop fusion | flops 3144704 | bytes 8396800 | tf_op jit(solution)/shard_map/reduce_sum | solution.py:111
  26.2 0.3 fusion.109
  26.5 0.9 %fusion.110 = (f32[512]{0:T(512)S(1)}, f32[512,1024]{1,0:T(8,128)S(1)}, f32[512]{0:T(512)S(1)}, f32[512,1024]{1,0:T(8,128)S(1)}) fusion(f32[512]{0:T(512)S(1)} %max.99, f32[512,1024]{1,0:T(8,128)S(1)} %get-tuple-element.98, f32[512]{0:T(512)S(1)} %max.97, f32[512,1024]{1,0:T(8,128)S(1)} %get-tuple-element.94), kind=kLoop, calls=%fused_computation.202 | loop fusion | flops 3144704 | bytes 8396800 | tf_op jit(solution)/shard_map/reduce_sum | solution.py:111
  27.5 0.2 fusion.113
  27.7 0.5 fusion.114
  28.2 16.6 %collective-permute-done.1 = bf16[2,1,128,640]{3,2,0,1:T(8,128)(2,1)S(1)} collective-permute-done((bf16[2,1,128,640]{3,2,0,1:T(8,128)(2,1)S(1)}, bf16[2,1,128,640]{3,2,0,1:T(8,128)(2,1)S(1)}, u32[]{:S(2)}, u32[]{:S(2)}) %collective-permute-start.1) | collective-permute-done | bytes 327712 | tf_op jit(solution)/shard_map/ppermute | solution.py:87
  44.8 0.0 collective-permute-start.4
  44.8 0.1 pad_add_fusion
  44.8 0.1 compare_and_fusion
  44.9 1.5 %collective-permute-done.4 = bf16[2,1,1,128,640]{4,3,0,2,1:T(8,128)(2,1)S(1)} collective-permute-done((bf16[2,1,1,128,640]{4,3,0,2,1:T(8,128)(2,1)S(1)}, bf16[2,1,1,128,640]{4,3,0,2,1:T(8,128)(2,1)S(1)}, u32[]{:S(2)}, u32[]{:S(2)}) %collective-permute-start.4) | collective-permute-done | bytes 327712 | tf_op jit(solution)/shard_map/ppermute | solution.py:122
  46.4 0.1 pad_maximum_fusion
  46.5 0.3 broadcast_in_dim.97
  46.8 0.3 fusion.125
  47.1 0.3 fusion.124
  47.3 0.3 fusion.123
  47.6 0.3 fusion.122
  47.9 0.3 fusion.121
  48.1 0.1 fusion.49
  48.3 0.3 fusion.39
  48.5 0.6 %fusion.29 = f32[512,128]{0,1:T(8,128)S(1)} fusion(f32[512,128]{0,1:T(8,128)S(1)} %fusion.39, f32[512,1024]{1,0:T(8,128)S(1)} %get-tuple-element.53, f32[512]{0:T(512)S(1)} %bitcast.215, bf16[2,1024,640]{2,1,0:T(8,128)(2,1)S(1)} %copy-done), kind=kOutput, calls=%fused_computation.60 | convolution fusion | flops 135331840 | bytes 2885632 | tf_op jit(solution)/shard_map/dot_general | solution.py:151
  49.1 0.1 fusion.48
  49.3 0.3 fusion.38
  49.5 0.6 %fusion.27 = f32[512,128]{0,1:T(8,128)S(1)} fusion(f32[512,128]{0,1:T(8,128)S(1)} %fusion.38, f32[512,1024]{1,0:T(8,128)S(1)} %get-tuple-element.49, f32[512]{0:T(512)S(1)} %bitcast.217, bf16[2,1024,640]{2,1,0:T(8,128)(2,1)S(1)} %copy-done), kind=kOutput, calls=%fused_computation.58 | convolution fusion | flops 135331840 | bytes 2885632 | tf_op jit(solution)/shard_map/dot_general | solution.py:151
  50.1 0.1 fusion.47
  50.3 0.3 fusion.37
  50.5 0.6 %fusion.25 = f32[512,128]{0,1:T(8,128)S(1)} fusion(f32[512,128]{0,1:T(8,128)S(1)} %fusion.37, f32[512,1024]{1,0:T(8,128)S(1)} %get-tuple-element.45, f32[512]{0:T(512)S(1)} %bitcast.219, bf16[2,1024,640]{2,1,0:T(8,128)(2,1)S(1)} %copy-done), kind=kOutput, calls=%fused_computation.56 | convolution fusion | flops 135331840 | bytes 2885632 | tf_op jit(solution)/shard_map/dot_general | solution.py:151
  51.1 0.1 fusion.46
  51.3 0.3 fusion.36
  51.5 0.6 %fusion.23 = f32[512,128]{0,1:T(8,128)S(1)} fusion(f32[512,128]{0,1:T(8,128)S(1)} %fusion.36, f32[512,1024]{1,0:T(8,128)S(1)} %get-tuple-element.41, f32[512]{0:T(512)S(1)} %bitcast.221, bf16[2,1024,640]{2,1,0:T(8,128)(2,1)S(1)} %copy-done), kind=kOutput, calls=%fused_computation.54 | convolution fusion | flops 135331840 | bytes 2885632 | tf_op jit(solution)/shard_map/dot_general | solution.py:151
  52.1 0.1 fusion.45
  52.3 0.3 fusion.35
  52.5 0.6 %fusion.21 = f32[512,128]{0,1:T(8,128)S(1)} fusion(f32[512,128]{0,1:T(8,128)S(1)} %fusion.35, f32[512,1024]{1,0:T(8,128)S(1)} %get-tuple-element.36, f32[512]{0:T(512)S(1)} %bitcast.213, bf16[2,1024,640]{2,1,0:T(8,128)(2,1)S(1)} %copy-done), kind=kOutput, calls=%fused_computation.52 | convolution fusion | flops 135331840 | bytes 2885632 | tf_op jit(solution)/shard_map/dot_general | solution.py:151
  53.1 0.2 fusion.11
  53.4 0.3 fusion.13
  53.7 0.2 fusion.15
  53.9 0.2 fusion.17
  54.2 0.2 fusion.19
  54.4 1.1 %copy.7 = bf16[512,640]{1,0:T(8,128)(2,1)} copy(bf16[512,640]{0,1:T(8,128)(2,1)S(1)} %fusion.19) | data formatting | bytes 1310720 | tf_op jit(solution)/shard_map/concatenate | solution.py:155
  (27 shorter events, 0.2 us)
Async XLA Ops:
  0.0 3.6 %copy-start.2 = (s32[4,8]{1,0:T(4,128)S(1)}, s32[4,8]{1,0:T(4,128)}, u32[]{:S(2)}) copy-start(s32[4,8]{1,0:T(4,128)} %param.5) | copy-start | bytes 388
  0.0 14.9 %copy-start = (bf16[2,1024,640]{2,1,0:T(8,128)(2,1)S(1)}, bf16[2,1024,640]{2,1,0:T(8,128)(2,1)}, u32[]{:S(2)}) copy-start(bf16[2,1024,640]{2,1,0:T(8,128)(2,1)} %param.4) | copy-start | bytes 7864324
  0.0 19.3 %copy-start.1 = (bf16[512,640]{1,0:T(8,128)(2,1)S(1)}, bf16[512,640]{1,0:T(8,128)(2,1)}, u32[]{:S(2)}) copy-start(bf16[512,640]{1,0:T(8,128)(2,1)} %param.3) | copy-start | bytes 1966084
  4.3 8.6 %collective-permute-start = (s32[1]{0:T(128)}, s32[1]{0:T(128)}, u32[]{:S(2)}, u32[]{:S(2)}) collective-permute-start(s32[1]{0:T(128)} %dynamic_slice.14), channel_id=1, source_target_pairs={{0,8},{4,12},{8,0},{12,4},{1,9},{5,13},{9,1},{13,5},{2,10},{6,14},... | collective-permute-start | bytes 20 | tf_op jit(solution)/shard_map/ppermute | solution.py:77
  8.3 13.6 %collective-permute-start.2 = (bf16[2,512,640]{2,1,0:T(8,128)(2,1)}, bf16[2,512,640]{2,1,0:T(8,128)(2,1)}, u32[]{:S(2)}, u32[]{:S(2)}) collective-permute-start(bf16[2,512,640]{2,1,0:T(8,128)(2,1)} %get-tuple-element.34), channel_id=1, source_target_pairs={{1,4},{5,8},{9,12},{3,6},{7,10},{11,14},{17,20},{21,24},{25,28},{1... | collective-permute-start | bytes 3932168 | tf_op jit(solution)/shard_map/ppermute | solution.py:28
  10.1 11.8 %collective-permute-start.3 = (bf16[2,512,640]{2,1,0:T(8,128)(2,1)}, bf16[2,512,640]{2,1,0:T(8,128)(2,1)}, u32[]{:S(2)}, u32[]{:S(2)}) collective-permute-start(bf16[2,512,640]{2,1,0:T(8,128)(2,1)} %get-tuple-element.35), channel_id=1, source_target_pairs={{4,1},{8,5},{12,9},{6,3},{10,7},{14,11},{20,17},{24,21},{28,25},{2... | collective-permute-start | bytes 3932168 | tf_op jit(solution)/shard_map/ppermute | solution.py:29
  15.0 29.8 %collective-permute-start.1 = (bf16[2,1,128,640]{3,2,0,1:T(8,128)(2,1)S(1)}, bf16[2,1,128,640]{3,2,0,1:T(8,128)(2,1)S(1)}, u32[]{:S(2)}, u32[]{:S(2)}) collective-permute-start(bf16[2,1,128,640]{3,2,0,1:T(8,128)(2,1)S(1)} %dynamic-slice_bitcast_fusion), channel_id=1, source_target_pairs={{8,0},{12,4},{0,8},{4,12},{9,1},{13,5},{1,9},{5,13},{10,2},{14,6},... | collective-permute-start | bytes 983048 | tf_op jit(solution)/shard_map/ppermute | solution.py:87
  44.8 1.6 %collective-permute-start.4 = (bf16[2,1,1,128,640]{4,3,0,2,1:T(8,128)(2,1)S(1)}, bf16[2,1,1,128,640]{4,3,0,2,1:T(8,128)(2,1)S(1)}, u32[]{:S(2)}, u32[]{:S(2)}) collective-permute-start(bf16[2,1,1,128,640]{4,3,0,2,1:T(8,128)(2,1)S(1)} %bitcast.193), channel_id=1, source_target_pairs={{0,1},{1,0},{2,3},{3,2},{4,5},{5,4},{6,7},{7,6},{8,9},{9,8},{10,11... | collective-permute-start | bytes 983048 | tf_op jit(solution)/shard_map/ppermute | solution.py:122

commit v7 on v6

--- a/solution.py
+++ b/solution.py
@@ -20,14 +20,12 @@
 
 def halo_frame(key_value, key_blocks, frame_rows, seq_count, rep_count, rep_index):
     slab_rows = key_value.shape[1]
-    last = lax.slice_in_dim(key_value, slab_rows - frame_rows, slab_rows, axis=1)
-    first = lax.slice_in_dim(key_value, 0, frame_rows, axis=1)
-    key_blocks, last, first = lax.optimization_barrier((key_blocks, last, first))
-    forward = [(s * rep_count + rep_count - 1, (s + 1) * rep_count) for s in range(seq_count - 1)]
-    backward = [(s * rep_count, (s - 1) * rep_count + rep_count - 1) for s in range(1, seq_count)]
-    low = lax.ppermute(last, ("seq", "rep"), forward)
-    high = lax.ppermute(first, ("seq", "rep"), backward)
-    return jnp.where(rep_index == 0, low, high), key_blocks
+    start = jnp.where(rep_index == rep_count - 1, slab_rows - frame_rows, 0)
+    payload = lax.dynamic_slice_in_dim(key_value, start, frame_rows, 1)
+    key_blocks, payload = lax.optimization_barrier((key_blocks, payload))
+    pairs = [(s * rep_count + rep_count - 1, (s + 1) * rep_count) for s in range(seq_count - 1)]
+    pairs += [(s * rep_count, (s - 1) * rep_count + rep_count - 1) for s in range(1, seq_count)]
+    return lax.ppermute(payload, ("seq", "rep"), pairs), key_blocks
 
 
 def per_device(query, key_value, key_blocks):

time: 56.5 us -> 60.3 us (1.067)
  the two profiles are of different devices: /device:TPU:0 before, /device:TPU:11 now
where the time goes in v7:
time: 60.3 us; the launch traced here: 60 us
  waiting for transfers between devices  23.1 us (38%)
  matrix products  19.9 us (33%)
  other arithmetic  5.07 us (8%)
  starting transfers between devices  4.82 us (8%)
  local copies, waits for them, and re-layouts  4.73 us (8%)
  between operations  2.31 us (4%)
    ppermute x1, waiting for transfers between devices, halo_frame(): return (lax.ppermute(payload, ('seq', 'rep'), pairs), key_blocks)  21.7 us
    dot_general x5, matrix products, per_device(): jnp.dot(query_head, halo[0, :, cols].T, preferred_element_type=jnp.float32)  6.08 us
    dot_general x5, matrix products, per_device(): jnp.dot(halo_prob, halo[1, :, cols], preferred_element_type=jnp.float32)  5.89 us
    dot_general x5, matrix products, per_device(): jnp.dot(own_prob, key_value[1, :, cols], preferred_element_type=jnp.float32)  2.86 us
    dynamic_slice x1, local copies, waits for them, and re-layouts, halo_frame(): payload = lax.dynamic_slice_in_dim(key_value, start, frame_rows, 1)  2.65 us
    dot_general x5, matrix products, per_device(): jnp.dot(query_head, key_value[0, :, cols].T, preferred_element_type=jnp.f...  2.6 us
    reduce_sum x3, other arithmetic, per_device(): jnp.sum(own_exp, axis=1, keepdims=True)  2.32 us
    ppermute x1, starting transfers between devices, per_device(): wanted = lax.ppermute(phase[None], 'seq', pairs)[0]  2.31 us
  transfers between devices with their start and end apart: 4, of which 2 were waited for; matrix products, arithmetic and copies ran while one was open for 22% of the time, Pallas kernels for 0%

profile of v7, /device:TPU:11, one launch (start us, length us, event | category | flops | bytes accessed | tf_op | source)
XLA Modules:
  0.0 60.0 jit_solution(12078056774419577446)
XLA Ops:
  0.0 0.0 copy-start
  0.0 0.0 copy-start.2
  0.0 0.0 copy-start.1
  0.0 2.6 %constant_dynamic-slice_fusion = bf16[2,512,640]{2,1,0:T(8,128)(2,1)} fusion(bf16[2,1024,640]{2,1,0:T(8,128)(2,1)} %param.4, s32[]{:T(128)S(6)} %select_n.91), kind=kLoop, calls=%fused_computation.190 | loop fusion | bytes 2621444 | tf_op jit(solution)/shard_map/dynamic_slice | solution.py:24
  2.7 0.0 copy-done.2
  2.7 0.6 dynamic_slice.18
  3.3 2.3 %collective-permute-start = (s32[1]{0:T(128)}, s32[1]{0:T(128)}, u32[]{:S(2)}, u32[]{:S(2)}) collective-permute-start(s32[1]{0:T(128)} %dynamic_slice.18), channel_id=1, source_target_pairs={{0,8},{4,12},{8,0},{12,4},{1,9},{5,13},{9,1},{13,5},{2,10},{6,14},... | collective-permute-start | bytes 20 | tf_op jit(solution)/shard_map/ppermute | solution.py:75
  5.6 1.9 %collective-permute-start.2 = (bf16[2,512,640]{2,1,0:T(8,128)(2,1)}, bf16[2,512,640]{2,1,0:T(8,128)(2,1)}, u32[]{:S(2)}, u32[]{:S(2)}) collective-permute-start(bf16[2,512,640]{2,1,0:T(8,128)(2,1)} %constant_dynamic-slice_fusion), channel_id=1, source_target_pairs={{1,4},{5,8},{9,12},{4,1},{8,5},{12,9},{3,6},{7,10},{11,14},{6,3},{... | collective-permute-start | bytes 3932168 | tf_op jit(solution)/shard_map/ppermute | solution.py:28
  7.6 0.8 %subtract_reduce_fusion = s32[4]{0:T(128)S(1)} fusion(s32[4,8]{1,0:T(4,128)S(1)} %copy-done.2, s32[]{:T(128)S(6)} %select_n.93, s32[]{:T(128)} %bitcast.24, s32[]{:T(128)S(6)} %mul.171), kind=kLoop, calls=%fused_computation.182 | loop fusion | flops 8 | bytes 44 | tf_op jit(solution)/shard_map/sub | solution.py:81
  8.4 0.2 and_reduce_fusion
  8.6 0.0 collective-permute-done
  10.5 0.0 copy-done
  10.5 0.5 collective-permute-start.1
  11.1 0.0 copy-done.1
  11.1 0.5 multiply_reduce_fusion.1
  11.6 0.5 multiply_reduce_fusion
  12.1 0.5 multiply_reduce_fusion.3
  12.6 0.5 multiply_reduce_fusion.2
  13.2 0.5 multiply_reduce_fusion.4
  13.7 21.7 %collective-permute-done.2 = bf16[2,512,640]{2,1,0:T(8,128)(2,1)} collective-permute-done((bf16[2,512,640]{2,1,0:T(8,128)(2,1)}, bf16[2,512,640]{2,1,0:T(8,128)(2,1)}, u32[]{:S(2)}, u32[]{:S(2)}) %collective-permute-start.2) | collective-permute-done | bytes 1310752 | tf_op jit(solution)/shard_map/ppermute | solution.py:28
  35.4 1.2 %fusion.118 = (f32[512]{0:T(512)S(1)}, f32[512,512]{0,1:T(8,128)S(1)}) fusion(bf16[2,512,640]{2,1,0:T(8,128)(2,1)} %collective-permute-done.2, bf16[512,640]{1,0:T(8,128)(2,1)S(1)} %copy-done.1, pred[]{:T(512)S(6)} %or.3), kind=kOutput, calls=%fused_computation.210 | convolution fusion | flops 67894784 | bytes 1312769 | tf_op jit(solution)/shard_map/dot_general | solution.py:100
  36.6 1.2 %fusion.119 = (f32[512]{0:T(512)S(1)}, f32[512,512]{0,1:T(8,128)S(1)}) fusion(bf16[2,512,640]{2,1,0:T(8,128)(2,1)} %collective-permute-done.2, bf16[512,640]{1,0:T(8,128)(2,1)S(1)} %copy-done.1, pred[]{:T(512)S(6)} %or.3), kind=kOutput, calls=%fused_computation.211 | convolution fusion | flops 67894784 | bytes 1312769 | tf_op jit(solution)/shard_map/dot_general | solution.py:100
  37.8 0.3 fusion.105
  38.1 0.9 %fusion.106 = (f32[512]{0:T(512)S(1)}, f32[512,1024]{1,0:T(8,128)S(1)}, f32[512]{0:T(512)S(1)}, f32[512,1024]{1,0:T(8,128)S(1)}) fusion(f32[512]{0:T(512)S(1)} %max.103, f32[512,1024]{1,0:T(8,128)S(1)} %get-tuple-element.102, f32[512]{0:T(512)S(1)} %max.101, f32[512,1024]{1,0:T(8,128)S(1)} %get-tuple-element.98), kind=kLoop, calls=%fused_computation.198 | loop fusion | flops 3144704 | bytes 8396800 | tf_op jit(solution)/shard_map/reduce_sum | solution.py:109
  39.0 1.2 %fusion.116 = (f32[512]{0:T(512)S(1)}, f32[512,512]{0,1:T(8,128)S(1)}) fusion(bf16[2,512,640]{2,1,0:T(8,128)(2,1)} %collective-permute-done.2, bf16[512,640]{1,0:T(8,128)(2,1)S(1)} %copy-done.1, pred[]{:T(512)S(6)} %or.3), kind=kOutput, calls=%fused_computation.208 | convolution fusion | flops 67894784 | bytes 1312769 | tf_op jit(solution)/shard_map/dot_general | solution.py:100
  40.3 1.2 %fusion.117 = (f32[512]{0:T(512)S(1)}, f32[512,512]{0,1:T(8,128)S(1)}) fusion(bf16[2,512,640]{2,1,0:T(8,128)(2,1)} %collective-permute-done.2, bf16[512,640]{1,0:T(8,128)(2,1)S(1)} %copy-done.1, pred[]{:T(512)S(6)} %or.3), kind=kOutput, calls=%fused_computation.209 | convolution fusion | flops 67894784 | bytes 1312769 | tf_op jit(solution)/shard_map/dot_general | solution.py:100
  41.5 0.3 fusion.109
  41.8 0.9 %fusion.110 = (f32[512]{0:T(512)S(1)}, f32[512,1024]{1,0:T(8,128)S(1)}, f32[512]{0:T(512)S(1)}, f32[512,1024]{1,0:T(8,128)S(1)}) fusion(f32[512]{0:T(512)S(1)} %max.99, f32[512,1024]{1,0:T(8,128)S(1)} %get-tuple-element.94, f32[512]{0:T(512)S(1)} %max.97, f32[512,1024]{1,0:T(8,128)S(1)} %get-tuple-element.90), kind=kLoop, calls=%fused_computation.202 | loop fusion | flops 3144704 | bytes 8396800 | tf_op jit(solution)/shard_map/reduce_sum | solution.py:109
  42.7 1.2 %fusion.115 = (f32[512]{0:T(512)S(1)}, f32[512,512]{0,1:T(8,128)S(1)}) fusion(bf16[2,512,640]{2,1,0:T(8,128)(2,1)} %collective-permute-done.2, bf16[512,640]{1,0:T(8,128)(2,1)S(1)} %copy-done.1, pred[]{:T(512)S(6)} %or.3), kind=kOutput, calls=%fused_computation.207 | convolution fusion | flops 67894784 | bytes 1312769 | tf_op jit(solution)/shard_map/dot_general | solution.py:100
  44.0 0.2 fusion.113
  44.2 0.5 fusion.114
  44.7 0.0 collective-permute-done.1
  44.7 0.1 collective-permute-start.3
  44.8 0.1 pad_add_fusion
  44.9 0.1 compare_and_fusion
  44.9 1.5 %collective-permute-done.3 = bf16[2,1,1,128,640]{4,3,0,2,1:T(8,128)(2,1)S(1)} collective-permute-done((bf16[2,1,1,128,640]{4,3,0,2,1:T(8,128)(2,1)S(1)}, bf16[2,1,1,128,640]{4,3,0,2,1:T(8,128)(2,1)S(1)}, u32[]{:S(2)}, u32[]{:S(2)}) %collective-permute-start.3) | collective-permute-done | bytes 327712 | tf_op jit(solution)/shard_map/ppermute | solution.py:120
  46.4 0.1 pad_maximum_fusion
  46.5 0.3 broadcast_in_dim.97
  46.8 0.3 fusion.124
  47.1 0.3 fusion.123
  47.3 0.3 fusion.122
  47.6 0.3 fusion.121
  47.9 0.3 fusion.120
  48.1 0.1 fusion.49
  48.3 1.2 %fusion.39 = f32[512,128]{0,1:T(8,128)S(1)} fusion(f32[512,512]{0,1:T(8,128)S(1)} %get-tuple-element.54, f32[512]{0:T(512)S(1)} %bitcast.214, bf16[2,512,640]{2,1,0:T(8,128)(2,1)} %collective-permute-done.2), kind=kOutput, calls=%fused_computation.80 | convolution fusion | flops 67633152 | bytes 1443840 | tf_op jit(solution)/shard_map/dot_general | solution.py:150
  49.4 0.6 fusion.29
  50.0 0.1 fusion.48
  50.2 1.2 %fusion.38 = f32[512,128]{0,1:T(8,128)S(1)} fusion(f32[512,512]{0,1:T(8,128)S(1)} %get-tuple-element.50, f32[512]{0:T(512)S(1)} %bitcast.216, bf16[2,512,640]{2,1,0:T(8,128)(2,1)} %collective-permute-done.2), kind=kOutput, calls=%fused_computation.79 | convolution fusion | flops 67633152 | bytes 1443840 | tf_op jit(solution)/shard_map/dot_general | solution.py:150
  51.3 0.6 fusion.27
  51.9 0.1 fusion.47
  52.1 1.2 %fusion.37 = f32[512,128]{0,1:T(8,128)S(1)} fusion(f32[512,512]{0,1:T(8,128)S(1)} %get-tuple-element.46, f32[512]{0:T(512)S(1)} %bitcast.218, bf16[2,512,640]{2,1,0:T(8,128)(2,1)} %collective-permute-done.2), kind=kOutput, calls=%fused_computation.78 | convolution fusion | flops 67633152 | bytes 1443840 | tf_op jit(solution)/shard_map/dot_general | solution.py:150
  53.2 0.6 fusion.25
  53.8 0.1 fusion.46
  54.0 1.2 %fusion.36 = f32[512,128]{0,1:T(8,128)S(1)} fusion(f32[512,512]{0,1:T(8,128)S(1)} %get-tuple-element.42, f32[512]{0:T(512)S(1)} %bitcast.220, bf16[2,512,640]{2,1,0:T(8,128)(2,1)} %collective-permute-done.2), kind=kOutput, calls=%fused_computation.77 | convolution fusion | flops 67633152 | bytes 1443840 | tf_op jit(solution)/shard_map/dot_general | solution.py:150
  55.1 0.6 fusion.23
  55.7 0.1 fusion.45
  55.9 1.2 %fusion.35 = f32[512,128]{0,1:T(8,128)S(1)} fusion(f32[512,512]{0,1:T(8,128)S(1)} %get-tuple-element.38, f32[512]{0:T(512)S(1)} %bitcast.212, bf16[2,512,640]{2,1,0:T(8,128)(2,1)} %collective-permute-done.2), kind=kOutput, calls=%fused_computation.76 | convolution fusion | flops 67633152 | bytes 1443840 | tf_op jit(solution)/shard_map/dot_general | solution.py:150
  57.0 0.6 fusion.21
  57.6 0.2 fusion.11
  57.9 0.2 fusion.13
  58.2 0.3 fusion.15
  58.4 0.2 fusion.17
  58.7 0.3 fusion.19
  58.9 1.1 %copy.7 = bf16[512,640]{1,0:T(8,128)(2,1)} copy(bf16[512,640]{0,1:T(8,128)(2,1)S(1)} %fusion.19) | data formatting | bytes 1310720 | tf_op jit(solution)/shard_map/concatenate | solution.py:153
  (24 shorter events, 0.2 us)
Async XLA Ops:
  0.0 10.5 %copy-start = (bf16[2,1024,640]{2,1,0:T(8,128)(2,1)S(1)}, bf16[2,1024,640]{2,1,0:T(8,128)(2,1)}, u32[]{:S(2)}) copy-start(bf16[2,1024,640]{2,1,0:T(8,128)(2,1)} %param.4) | copy-start | bytes 7864324
  0.0 2.7 %copy-start.2 = (s32[4,8]{1,0:T(4,128)S(1)}, s32[4,8]{1,0:T(4,128)}, u32[]{:S(2)}) copy-start(s32[4,8]{1,0:T(4,128)} %param.5) | copy-start | bytes 388
  0.0 11.1 %copy-start.1 = (bf16[512,640]{1,0:T(8,128)(2,1)S(1)}, bf16[512,640]{1,0:T(8,128)(2,1)}, u32[]{:S(2)}) copy-start(bf16[512,640]{1,0:T(8,128)(2,1)} %param.3) | copy-start | bytes 1966084
  3.3 5.3 %collective-permute-start = (s32[1]{0:T(128)}, s32[1]{0:T(128)}, u32[]{:S(2)}, u32[]{:S(2)}) collective-permute-start(s32[1]{0:T(128)} %dynamic_slice.18), channel_id=1, source_target_pairs={{0,8},{4,12},{8,0},{12,4},{1,9},{5,13},{9,1},{13,5},{2,10},{6,14},... | collective-permute-start | bytes 20 | tf_op jit(solution)/shard_map/ppermute | solution.py:75
  5.6 29.8 %collective-permute-start.2 = (bf16[2,512,640]{2,1,0:T(8,128)(2,1)}, bf16[2,512,640]{2,1,0:T(8,128)(2,1)}, u32[]{:S(2)}, u32[]{:S(2)}) collective-permute-start(bf16[2,512,640]{2,1,0:T(8,128)(2,1)} %constant_dynamic-slice_fusion), channel_id=1, source_target_pairs={{1,4},{5,8},{9,12},{4,1},{8,5},{12,9},{3,6},{7,10},{11,14},{6,3},{... | collective-permute-start | bytes 3932168 | tf_op jit(solution)/shard_map/ppermute | solution.py:28
  10.5 34.2 %collective-permute-start.1 = (bf16[2,1,128,640]{3,2,0,1:T(8,128)(2,1)S(1)}, bf16[2,1,128,640]{3,2,0,1:T(8,128)(2,1)S(1)}, u32[]{:S(2)}, u32[]{:S(2)}) collective-permute-start(bf16[2,1,128,640]{3,2,0,1:T(8,128)(2,1)S(1)} %dynamic-slice_bitcast_fusion), channel_id=1, source_target_pairs={{8,0},{12,4},{0,8},{4,12},{9,1},{13,5},{1,9},{5,13},{10,2},{14,6},... | collective-permute-start | bytes 983048 | tf_op jit(solution)/shard_map/ppermute | solution.py:85
  44.7 1.7 %collective-permute-start.3 = (bf16[2,1,1,128,640]{4,3,0,2,1:T(8,128)(2,1)S(1)}, bf16[2,1,1,128,640]{4,3,0,2,1:T(8,128)(2,1)S(1)}, u32[]{:S(2)}, u32[]{:S(2)}) collective-permute-start(bf16[2,1,1,128,640]{4,3,0,2,1:T(8,128)(2,1)S(1)} %bitcast.193), channel_id=1, source_target_pairs={{0,1},{1,0},{2,3},{3,2},{4,5},{5,4},{6,7},{7,6},{8,9},{9,8},{10,11... | collective-permute-start | bytes 983048 | tf_op jit(solution)/shard_map/ppermute | solution.py:120

commit v8 on v7

--- a/solution.py
+++ b/solution.py
@@ -49,6 +49,10 @@
     far_share = far_count // rep_count
 
     halo, key_blocks = halo_frame(key_value, key_blocks, frame_rows, seq_count, rep_count, rep_index)
+    halo_valid = ((rep_index == 0) & (slab_index > 0)) | (
+        (rep_index == rep_count - 1) & (slab_index < seq_count - 1)
+    )
+    halo = jnp.where(halo_valid, halo, jnp.zeros_like(halo))
 
     phases = jnp.maximum(key_blocks[0], 0) % FAR_STRIDE
     stride_grid = key_value.reshape(2, far_count, FAR_STRIDE, MASK_BLOCK_SIZE, columns)
@@ -84,9 +88,6 @@
     query, payloads = lax.optimization_barrier((query, [chosen for chosen, _ in received]))
     received = [lax.ppermute(chosen, "seq", back) for chosen, (_, back) in zip(payloads, received)]
     slot_count = len(received)
-    halo_valid = ((rep_index == 0) & (slab_index > 0)) | (
-        (rep_index == rep_count - 1) & (slab_index < seq_count - 1)
-    )
 
     near = []
     for head in range(head_count):

time: 60.3 us -> 52.7 us (0.87)
  the two profiles are of different devices: /device:TPU:11 before, /device:TPU:0 now
where the time goes in v8:
time: 52.7 us; the launch traced here: 52 us
  waiting for transfers between devices  20.8 us (39%)
  matrix products  10.9 us (21%)
  starting transfers between devices  8.27 us (16%)
  other arithmetic  5.21 us (10%)
  local copies, waits for them, and re-layouts  4.79 us (9%)
  between operations  2.01 us (4%)
    ppermute x1, waiting for transfers between devices, per_device(): lax.ppermute(chosen, 'seq', back)  19.3 us
    ppermute x1, starting transfers between devices, per_device(): wanted = lax.ppermute(phase[None], 'seq', pairs)[0]  4.05 us
    dot_general x5, matrix products, per_device(): jnp.dot(own_prob, key_value[1, :, cols], preferred_element_type=jnp.float32)  2.86 us
    dynamic_slice x1, local copies, waits for them, and re-layouts, halo_frame(): payload = lax.dynamic_slice_in_dim(key_value, start, frame_rows, 1)  2.65 us
    dot_general x5, matrix products, per_device(): jnp.dot(query_head, key_value[0, :, cols].T, preferred_element_type=jnp.f...  2.6 us
    ppermute x1, starting transfers between devices, per_device(): lax.ppermute(chosen, 'seq', back)  2.48 us
    reduce_sum x3, other arithmetic, per_device(): jnp.sum(own_exp, axis=1, keepdims=True)  2.32 us
    ppermute x1, starting transfers between devices, halo_frame(): return (lax.ppermute(payload, ('seq', 'rep'), pairs), key_blocks)  1.74 us
  transfers between devices with their start and end apart: 4, of which 2 were waited for; matrix products, arithmetic and copies ran while one was open for 17% of the time, Pallas kernels for 0%

profile of v8, /device:TPU:0, one launch (start us, length us, event | category | flops | bytes accessed | tf_op | source)
XLA Modules:
  0.0 52.0 jit_solution(12913960715105219926)
XLA Ops:
  0.0 0.0 copy-start
  0.0 0.0 copy-start.2
  0.0 2.7 %constant_dynamic-slice_fusion = bf16[2,512,640]{2,1,0:T(8,128)(2,1)} fusion(bf16[2,1024,640]{2,1,0:T(8,128)(2,1)} %param.4, s32[]{:T(128)S(6)} %select_n.99), kind=kLoop, calls=%fused_computation.191 | loop fusion | bytes 2621444 | tf_op jit(solution)/shard_map/dynamic_slice | solution.py:24
  2.7 0.0 copy-done.2
  2.7 0.7 %dynamic_slice.18 = s32[1]{0:T(128)} dynamic-slice(s32[8]{0:T(128)S(1)} %and_select_fusion.1, s32[]{:T(128)S(6)} %select_n.101), dynamic_slice_sizes={1} | dynamic-slice | bytes 12 | tf_op jit(solution)/shard_map/jit(dynamic_index_in_dim)/dynamic_slice | solution.py:78
  3.3 4.0 %collective-permute-start = (s32[1]{0:T(128)}, s32[1]{0:T(128)}, u32[]{:S(2)}, u32[]{:S(2)}) collective-permute-start(s32[1]{0:T(128)} %dynamic_slice.18), channel_id=1, source_target_pairs={{0,8},{4,12},{8,0},{12,4},{1,9},{5,13},{9,1},{13,5},{2,10},{6,14},... | collective-permute-start | bytes 20 | tf_op jit(solution)/shard_map/ppermute | solution.py:79
  7.4 1.7 %collective-permute-start.2 = (bf16[2,512,640]{2,1,0:T(8,128)(2,1)}, bf16[2,512,640]{2,1,0:T(8,128)(2,1)}, u32[]{:S(2)}, u32[]{:S(2)}) collective-permute-start(bf16[2,512,640]{2,1,0:T(8,128)(2,1)} %constant_dynamic-slice_fusion), channel_id=1, source_target_pairs={{1,4},{5,8},{9,12},{4,1},{8,5},{12,9},{3,6},{7,10},{11,14},{6,3},{... | collective-permute-start | bytes 3932168 | tf_op jit(solution)/shard_map/ppermute | solution.py:28
  9.1 0.8 %subtract_reduce_fusion = s32[4]{0:T(128)S(1)} fusion(s32[4,8]{1,0:T(4,128)S(1)} %copy-done.2, s32[]{:T(128)S(6)} %select_n.101, s32[]{:T(128)} %bitcast.24, s32[]{:T(128)S(6)} %mul.171), kind=kLoop, calls=%fused_computation.183 | loop fusion | flops 8 | bytes 44 | tf_op jit(solution)/shard_map/sub | solution.py:85
  9.9 0.2 and_reduce_fusion
  10.2 0.0 collective-permute-done
  11.8 0.0 copy-done
  11.9 2.5 %collective-permute-start.1 = (bf16[2,1,128,640]{3,2,0,1:T(8,128)(2,1)S(1)}, bf16[2,1,128,640]{3,2,0,1:T(8,128)(2,1)S(1)}, u32[]{:S(2)}, u32[]{:S(2)}) collective-permute-start(bf16[2,1,128,640]{3,2,0,1:T(8,128)(2,1)S(1)} %dynamic-slice_bitcast_fusion), channel_id=1, source_target_pairs={{8,0},{12,4},{0,8},{4,12},{9,1},{13,5},{1,9},{5,13},{10,2},{14,6},... | collective-permute-start | bytes 983048 | tf_op jit(solution)/shard_map/ppermute | solution.py:89
  14.4 0.0 copy-done.1
  14.4 0.5 multiply_reduce_fusion.1
  14.9 0.5 %multiply_reduce_fusion = (f32[512]{0:T(512)S(1)}, f32[512,1024]{1,0:T(8,128)S(1)}) fusion(bf16[2,1024,640]{2,1,0:T(8,128)(2,1)S(1)} %copy-done, bf16[512,640]{1,0:T(8,128)(2,1)S(1)} %copy-done.1), kind=kOutput, calls=%fused_computation.10 | convolution fusion | flops 135265792 | bytes 2492416 | tf_op jit(solution)/shard_map/dot_general | solution.py:97
  15.4 0.5 %multiply_reduce_fusion.3 = (f32[512]{0:T(512)S(1)}, f32[512,1024]{1,0:T(8,128)S(1)}) fusion(bf16[2,1024,640]{2,1,0:T(8,128)(2,1)S(1)} %copy-done, bf16[512,640]{1,0:T(8,128)(2,1)S(1)} %copy-done.1), kind=kOutput, calls=%fused_computation.13 | convolution fusion | flops 135265792 | bytes 2492416 | tf_op jit(solution)/shard_map/dot_general | solution.py:97
  15.9 0.5 %multiply_reduce_fusion.2 = (f32[512]{0:T(512)S(1)}, f32[512,1024]{1,0:T(8,128)S(1)}) fusion(bf16[2,1024,640]{2,1,0:T(8,128)(2,1)S(1)} %copy-done, bf16[512,640]{1,0:T(8,128)(2,1)S(1)} %copy-done.1), kind=kOutput, calls=%fused_computation.12 | convolution fusion | flops 135265792 | bytes 2492416 | tf_op jit(solution)/shard_map/dot_general | solution.py:97
  16.5 0.5 %multiply_reduce_fusion.4 = (f32[512]{0:T(512)S(1)}, f32[512,1024]{1,0:T(8,128)S(1)}) fusion(bf16[2,1024,640]{2,1,0:T(8,128)(2,1)S(1)} %copy-done, bf16[512,640]{1,0:T(8,128)(2,1)S(1)} %copy-done.1), kind=kOutput, calls=%fused_computation.14 | convolution fusion | flops 135265792 | bytes 2492416 | tf_op jit(solution)/shard_map/dot_general | solution.py:97
  17.0 0.0 collective-permute-done.2
  17.0 0.1 broadcast_select_fusion
  17.1 0.3 fusion.118
  17.4 0.3 fusion.119
  17.8 0.3 fusion.116
  18.1 0.3 fusion.117
  18.4 0.3 fusion.115
  18.7 0.3 fusion.105
  19.0 0.9 %fusion.106 = (f32[512]{0:T(512)S(1)}, f32[512,1024]{1,0:T(8,128)S(1)}, f32[512]{0:T(512)S(1)}, f32[512,1024]{1,0:T(8,128)S(1)}) fusion(f32[512]{0:T(512)S(1)} %max.103, f32[512,1024]{1,0:T(8,128)S(1)} %get-tuple-element.102, f32[512]{0:T(512)S(1)} %max.101, f32[512,1024]{1,0:T(8,128)S(1)} %get-tuple-element.98), kind=kLoop, calls=%fused_computation.199 | loop fusion | flops 3144704 | bytes 8396800 | tf_op jit(solution)/shard_map/reduce_sum | solution.py:110
  20.0 0.3 fusion.109
  20.3 0.9 %fusion.110 = (f32[512]{0:T(512)S(1)}, f32[512,1024]{1,0:T(8,128)S(1)}, f32[512]{0:T(512)S(1)}, f32[512,1024]{1,0:T(8,128)S(1)}) fusion(f32[512]{0:T(512)S(1)} %max.99, f32[512,1024]{1,0:T(8,128)S(1)} %get-tuple-element.94, f32[512]{0:T(512)S(1)} %max.97, f32[512,1024]{1,0:T(8,128)S(1)} %get-tuple-element.90), kind=kLoop, calls=%fused_computation.203 | loop fusion | flops 3144704 | bytes 8396800 | tf_op jit(solution)/shard_map/reduce_sum | solution.py:110
  21.2 0.2 fusion.113
  21.4 0.5 %fusion.114 = (f32[512]{0:T(512)S(1)}, f32[512,1024]{1,0:T(8,128)S(1)}) fusion(f32[512]{0:T(512)S(1)} %max.95, f32[512,1024]{1,0:T(8,128)S(1)} %get-tuple-element.86), kind=kLoop, calls=%fused_computation.207 | loop fusion | flops 1572352 | bytes 4198400 | tf_op jit(solution)/shard_map/reduce_sum | solution.py:110
  21.9 19.3 %collective-permute-done.1 = bf16[2,1,128,640]{3,2,0,1:T(8,128)(2,1)S(1)} collective-permute-done((bf16[2,1,128,640]{3,2,0,1:T(8,128)(2,1)S(1)}, bf16[2,1,128,640]{3,2,0,1:T(8,128)(2,1)S(1)}, u32[]{:S(2)}, u32[]{:S(2)}) %collective-permute-start.1) | collective-permute-done | bytes 327712 | tf_op jit(solution)/shard_map/ppermute | solution.py:89
  41.3 0.0 collective-permute-start.3
  41.3 0.1 pad_add_fusion
  41.4 0.1 compare_and_fusion
  41.5 1.5 %collective-permute-done.3 = bf16[2,1,1,128,640]{4,3,0,2,1:T(8,128)(2,1)S(1)} collective-permute-done((bf16[2,1,1,128,640]{4,3,0,2,1:T(8,128)(2,1)S(1)}, bf16[2,1,1,128,640]{4,3,0,2,1:T(8,128)(2,1)S(1)}, u32[]{:S(2)}, u32[]{:S(2)}) %collective-permute-start.3) | collective-permute-done | bytes 327712 | tf_op jit(solution)/shard_map/ppermute | solution.py:121
  42.9 0.1 pad_maximum_fusion
  43.0 0.3 broadcast_in_dim.101
  43.4 0.3 fusion.124
  43.6 0.3 fusion.123
  43.9 0.3 fusion.122
  44.1 0.3 fusion.121
  44.4 0.3 fusion.120
  44.7 0.1 fusion.49
  44.8 0.3 fusion.39
  45.1 0.6 %fusion.29 = f32[512,128]{0,1:T(8,128)S(1)} fusion(f32[512,128]{0,1:T(8,128)S(1)} %fusion.39, f32[512,1024]{1,0:T(8,128)S(1)} %get-tuple-element.51, f32[512]{0:T(512)S(1)} %bitcast.215, bf16[2,1024,640]{2,1,0:T(8,128)(2,1)S(1)} %copy-done), kind=kOutput, calls=%fused_computation.60 | convolution fusion | flops 135331840 | bytes 2885632 | tf_op jit(solution)/shard_map/dot_general | solution.py:150
  45.7 0.1 fusion.48
  45.8 0.3 fusion.38
  46.1 0.6 %fusion.27 = f32[512,128]{0,1:T(8,128)S(1)} fusion(f32[512,128]{0,1:T(8,128)S(1)} %fusion.38, f32[512,1024]{1,0:T(8,128)S(1)} %get-tuple-element.47, f32[512]{0:T(512)S(1)} %bitcast.217, bf16[2,1024,640]{2,1,0:T(8,128)(2,1)S(1)} %copy-done), kind=kOutput, calls=%fused_computation.58 | convolution fusion | flops 135331840 | bytes 2885632 | tf_op jit(solution)/shard_map/dot_general | solution.py:150
  46.7 0.1 fusion.47
  46.8 0.3 fusion.37
  47.1 0.6 %fusion.25 = f32[512,128]{0,1:T(8,128)S(1)} fusion(f32[512,128]{0,1:T(8,128)S(1)} %fusion.37, f32[512,1024]{1,0:T(8,128)S(1)} %get-tuple-element.43, f32[512]{0:T(512)S(1)} %bitcast.219, bf16[2,1024,640]{2,1,0:T(8,128)(2,1)S(1)} %copy-done), kind=kOutput, calls=%fused_computation.56 | convolution fusion | flops 135331840 | bytes 2885632 | tf_op jit(solution)/shard_map/dot_general | solution.py:150
  47.7 0.1 fusion.46
  47.8 0.3 fusion.36
  48.1 0.6 %fusion.23 = f32[512,128]{0,1:T(8,128)S(1)} fusion(f32[512,128]{0,1:T(8,128)S(1)} %fusion.36, f32[512,1024]{1,0:T(8,128)S(1)} %get-tuple-element.39, f32[512]{0:T(512)S(1)} %bitcast.221, bf16[2,1024,640]{2,1,0:T(8,128)(2,1)S(1)} %copy-done), kind=kOutput, calls=%fused_computation.54 | convolution fusion | flops 135331840 | bytes 2885632 | tf_op jit(solution)/shard_map/dot_general | solution.py:150
  48.6 0.1 fusion.45
  48.8 0.3 fusion.35
  49.1 0.6 %fusion.21 = f32[512,128]{0,1:T(8,128)S(1)} fusion(f32[512,128]{0,1:T(8,128)S(1)} %fusion.35, f32[512,1024]{1,0:T(8,128)S(1)} %get-tuple-element.34, f32[512]{0:T(512)S(1)} %bitcast.213, bf16[2,1024,640]{2,1,0:T(8,128)(2,1)S(1)} %copy-done), kind=kOutput, calls=%fused_computation.52 | convolution fusion | flops 135331840 | bytes 2885632 | tf_op jit(solution)/shard_map/dot_general | solution.py:150
  49.7 0.2 fusion.11
  49.9 0.3 fusion.13
  50.2 0.2 fusion.15
  50.4 0.2 fusion.17
  50.7 0.2 fusion.19
  50.9 1.1 %copy.7 = bf16[512,640]{1,0:T(8,128)(2,1)} copy(bf16[512,640]{0,1:T(8,128)(2,1)S(1)} %fusion.19) | data formatting | bytes 1310720 | tf_op jit(solution)/shard_map/concatenate | solution.py:154
  (25 shorter events, 0.2 us)
Async XLA Ops:
  0.0 11.8 %copy-start = (bf16[2,1024,640]{2,1,0:T(8,128)(2,1)S(1)}, bf16[2,1024,640]{2,1,0:T(8,128)(2,1)}, u32[]{:S(2)}) copy-start(bf16[2,1024,640]{2,1,0:T(8,128)(2,1)} %param.4) | copy-start | bytes 7864324
  0.0 2.7 %copy-start.2 = (s32[4,8]{1,0:T(4,128)S(1)}, s32[4,8]{1,0:T(4,128)}, u32[]{:S(2)}) copy-start(s32[4,8]{1,0:T(4,128)} %param.5) | copy-start | bytes 388
  0.0 14.4 %copy-start.1 = (bf16[512,640]{1,0:T(8,128)(2,1)S(1)}, bf16[512,640]{1,0:T(8,128)(2,1)}, u32[]{:S(2)}) copy-start(bf16[512,640]{1,0:T(8,128)(2,1)} %param.3) | copy-start | bytes 1966084
  3.3 6.8 %collective-permute-start = (s32[1]{0:T(128)}, s32[1]{0:T(128)}, u32[]{:S(2)}, u32[]{:S(2)}) collective-permute-start(s32[1]{0:T(128)} %dynamic_slice.18), channel_id=1, source_target_pairs={{0,8},{4,12},{8,0},{12,4},{1,9},{5,13},{9,1},{13,5},{2,10},{6,14},... | collective-permute-start | bytes 20 | tf_op jit(solution)/shard_map/ppermute | solution.py:79
  7.4 9.6 %collective-permute-start.2 = (bf16[2,512,640]{2,1,0:T(8,128)(2,1)}, bf16[2,512,640]{2,1,0:T(8,128)(2,1)}, u32[]{:S(2)}, u32[]{:S(2)}) collective-permute-start(bf16[2,512,640]{2,1,0:T(8,128)(2,1)} %constant_dynamic-slice_fusion), channel_id=1, source_target_pairs={{1,4},{5,8},{9,12},{4,1},{8,5},{12,9},{3,6},{7,10},{11,14},{6,3},{... | collective-permute-start | bytes 3932168 | tf_op jit(solution)/shard_map/ppermute | solution.py:28
  11.9 29.4 %collective-permute-start.1 = (bf16[2,1,128,640]{3,2,0,1:T(8,128)(2,1)S(1)}, bf16[2,1,128,640]{3,2,0,1:T(8,128)(2,1)S(1)}, u32[]{:S(2)}, u32[]{:S(2)}) collective-permute-start(bf16[2,1,128,640]{3,2,0,1:T(8,128)(2,1)S(1)} %dynamic-slice_bitcast_fusion), channel_id=1, source_target_pairs={{8,0},{12,4},{0,8},{4,12},{9,1},{13,5},{1,9},{5,13},{10,2},{14,6},... | collective-permute-start | bytes 983048 | tf_op jit(solution)/shard_map/ppermute | solution.py:89
  41.3 1.6 %collective-permute-start.3 = (bf16[2,1,1,128,640]{4,3,0,2,1:T(8,128)(2,1)S(1)}, bf16[2,1,1,128,640]{4,3,0,2,1:T(8,128)(2,1)S(1)}, u32[]{:S(2)}, u32[]{:S(2)}) collective-permute-start(bf16[2,1,1,128,640]{4,3,0,2,1:T(8,128)(2,1)S(1)} %bitcast.193), channel_id=1, source_target_pairs={{0,1},{1,0},{2,3},{3,2},{4,5},{5,4},{6,7},{7,6},{8,9},{9,8},{10,11... | collective-permute-start | bytes 983048 | tf_op jit(solution)/shard_map/ppermute | solution.py:121

commit v9 on v8

--- a/solution.py
+++ b/solution.py
@@ -120,38 +120,49 @@
         shift = [(r, (r + k) % rep_count) for r in range(rep_count)]
         parts.append(lax.ppermute(mine, "rep", shift))
         sources.append((rep_index - k) % rep_count)
-    far_pair = jnp.stack(parts, 2).reshape(2, slot_count * far_count * MASK_BLOCK_SIZE, columns)
     far_pick = jnp.stack(pick_list, 1)
     far_valid = jnp.stack(valid_list, 1)
     share_ids = jnp.arange(far_share, dtype=jnp.int32)
-    candidates = (jnp.stack(sources)[:, None] * far_share + share_ids[None, :]).reshape(far_count)
-    far_mask = far_valid[:, :, None] & (far_pick[:, :, None] == candidates[None, None, :])
-    far_mask = jnp.repeat(far_mask.reshape(query_blocks, 1, slot_count * far_count), MASK_BLOCK_SIZE, axis=2)
+    far_keys = []
+    far_masks = []
+    for part, source in zip(parts, sources):
+        far_keys.append(part.reshape(2, slot_count * far_share * MASK_BLOCK_SIZE, columns))
+        named = source * far_share + share_ids
+        mask = far_valid[:, :, None] & (far_pick[:, :, None] == named[None, None, :])
+        mask = mask.reshape(query_blocks, 1, slot_count * far_share)
+        far_masks.append(jnp.repeat(mask, MASK_BLOCK_SIZE, axis=2))
 
     outputs = []
     for head in range(head_count):
         cols = slice(head * HEAD_WIDTH, (head + 1) * HEAD_WIDTH)
         near_top, own_exp, halo_exp, near_total = near[head]
-        far_scores = (
-            jnp.dot(query[:, cols], far_pair[0, :, cols].T, preferred_element_type=jnp.float32)
-            * score_scale
-        )
-        far_scores = jnp.where(
-            far_mask, far_scores.reshape(query_blocks, MASK_BLOCK_SIZE, -1), -jnp.inf
-        ).reshape(query_count, -1)
-        row_top = jnp.maximum(near_top, jnp.max(far_scores, axis=1, keepdims=True))
+        row_top = near_top
+        far_scores = []
+        for keys, mask in zip(far_keys, far_masks):
+            scores = (
+                jnp.dot(query[:, cols], keys[0, :, cols].T, preferred_element_type=jnp.float32)
+                * score_scale
+            )
+            scores = jnp.where(
+                mask, scores.reshape(query_blocks, MASK_BLOCK_SIZE, -1), -jnp.inf
+            ).reshape(query_count, -1)
+            far_scores.append(scores)
+            row_top = jnp.maximum(row_top, jnp.max(scores, axis=1, keepdims=True))
         near_factor = jnp.exp(near_top - row_top)
-        far_exp = jnp.exp(far_scores - row_top)
-        row_total = near_total * near_factor + jnp.sum(far_exp, axis=1, keepdims=True)
+        far_exp = [jnp.exp(scores - row_top) for scores in far_scores]
+        row_total = near_total * near_factor
+        for part_exp in far_exp:
+            row_total = row_total + jnp.sum(part_exp, axis=1, keepdims=True)
         near_scale = near_factor / row_total
         own_prob = (own_exp * near_scale).astype(jnp.bfloat16)
         halo_prob = (halo_exp * near_scale).astype(jnp.bfloat16)
-        far_prob = (far_exp / row_total).astype(jnp.bfloat16)
         mixed = jnp.dot(own_prob, key_value[1, :, cols], preferred_element_type=jnp.float32)
         mixed = mixed + jnp.dot(halo_prob, halo[1, :, cols], preferred_element_type=jnp.float32)
-        mixed = mixed + jnp.dot(far_prob, far_pair[1, :, cols], preferred_element_type=jnp.float32)
+        for part_exp, keys in zip(far_exp, far_keys):
+            part_prob = (part_exp / row_total).astype(jnp.bfloat16)
+            mixed = mixed + jnp.dot(part_prob, keys[1, :, cols], preferred_element_type=jnp.float32)
         outputs.append(mixed.astype(jnp.bfloat16))
-    return jnp.concatenate(outputs, axis=1)
+    return jnp.stack(outputs, axis=1).reshape(query_count, columns)
 
 
 def solution(mesh):

time: 52.7 us -> 53.6 us (1.017)
  matrix products: 10.9 us -> 12.7 us
  waiting for transfers between devices: 20.8 us -> 20.2 us
    dot_general x10 -> x20, matrix products: 2.51 us -> 4.33 us  [the longest x10 2.24 us: per_device(): jnp.dot(part_prob, keys[1, :, cols], preferred_element_type=jnp.float32)]
    reshape x0 -> x1, local copies, waits for them, and re-layouts: none -> 1.08 us  [per_device(): return jnp.stack(outputs, axis=1).reshape(query_count, columns)]
    concatenate x1 -> x0, local copies, waits for them, and re-layouts: 1.08 us -> none  [per_device(): return jnp.concatenate(outputs, axis=1)]
where the time goes in v9:
time: 53.6 us; the launch traced here: 53 us
  waiting for transfers between devices  20.2 us (38%)
  matrix products  12.7 us (24%)
  starting transfers between devices  8.34 us (16%)
  other arithmetic  4.95 us (9%)
  local copies, waits for them, and re-layouts  4.52 us (8%)
  between operations  2.25 us (4%)
    ppermute x1, waiting for transfers between devices, per_device(): lax.ppermute(chosen, 'seq', back)  19 us
    ppermute x1, starting transfers between devices, per_device(): wanted = lax.ppermute(phase[None], 'seq', pairs)[0]  4.05 us
    dot_general x5, matrix products, per_device(): jnp.dot(own_prob, key_value[1, :, cols], preferred_element_type=jnp.float32)  2.86 us
    dynamic_slice x1, local copies, waits for them, and re-layouts, halo_frame(): payload = lax.dynamic_slice_in_dim(key_value, start, frame_rows, 1)  2.65 us
    dot_general x5, matrix products, per_device(): jnp.dot(query_head, key_value[0, :, cols].T, preferred_element_type=jnp.f...  2.6 us
    ppermute x1, starting transfers between devices, per_device(): lax.ppermute(chosen, 'seq', back)  2.48 us
    reduce_sum x3, other arithmetic, per_device(): jnp.sum(own_exp, axis=1, keepdims=True)  2.32 us
    dot_general x10, matrix products, per_device(): jnp.dot(part_prob, keys[1, :, cols], preferred_element_type=jnp.float32)  2.24 us
  transfers between devices with their start and end apart: 4, of which 2 were waited for; matrix products, arithmetic and copies ran while one was open for 17% of the time, Pallas kernels for 0%

profile of v9, /device:TPU:0, one launch (start us, length us, event | category | flops | bytes accessed | tf_op | source)
XLA Modules:
  0.0 53.0 jit_solution(15698059987007894007)
XLA Ops:
  0.0 2.7 %constant_dynamic-slice_fusion = bf16[2,512,640]{2,1,0:T(8,128)(2,1)} fusion(bf16[2,1024,640]{2,1,0:T(8,128)(2,1)} %param.4, s32[]{:T(128)S(6)} %select_n.119), kind=kLoop, calls=%fused_computation.258 | loop fusion | bytes 2621444 | tf_op jit(solution)/shard_map/dynamic_slice | solution.py:24
  2.7 0.6 %dynamic_slice.18 = s32[1]{0:T(128)} dynamic-slice(s32[8]{0:T(128)S(1)} %and_select_fusion.1, s32[]{:T(128)S(6)} %select_n.121), dynamic_slice_sizes={1} | dynamic-slice | bytes 12 | tf_op jit(solution)/shard_map/jit(dynamic_index_in_dim)/dynamic_slice | solution.py:78
  3.3 4.0 %collective-permute-start = (s32[1]{0:T(128)}, s32[1]{0:T(128)}, u32[]{:S(2)}, u32[]{:S(2)}) collective-permute-start(s32[1]{0:T(128)} %dynamic_slice.18), channel_id=1, source_target_pairs={{0,8},{4,12},{8,0},{12,4},{1,9},{5,13},{9,1},{13,5},{2,10},{6,14},... | collective-permute-start | bytes 20 | tf_op jit(solution)/shard_map/ppermute | solution.py:79
  7.3 1.7 %collective-permute-start.2 = (bf16[2,512,640]{2,1,0:T(8,128)(2,1)}, bf16[2,512,640]{2,1,0:T(8,128)(2,1)}, u32[]{:S(2)}, u32[]{:S(2)}) collective-permute-start(bf16[2,512,640]{2,1,0:T(8,128)(2,1)} %constant_dynamic-slice_fusion), channel_id=1, source_target_pairs={{1,4},{5,8},{9,12},{4,1},{8,5},{12,9},{3,6},{7,10},{11,14},{6,3},{... | collective-permute-start | bytes 3932168 | tf_op jit(solution)/shard_map/ppermute | solution.py:28
  9.0 0.2 and_reduce_fusion
  9.2 0.8 %subtract_reduce_fusion = s32[4]{0:T(128)S(1)} fusion(s32[4,8]{1,0:T(4,128)S(1)} %copy-done.2, s32[]{:T(128)S(6)} %select_n.121, s32[]{:T(128)} %bitcast.24, s32[]{:T(128)S(6)} %mul.186), kind=kLoop, calls=%fused_computation.247 | loop fusion | flops 8 | bytes 44 | tf_op jit(solution)/shard_map/sub | solution.py:85
  10.1 0.1 broadcast_bitcast_fusion.1
  10.2 0.1 broadcast_bitcast_fusion
  12.2 2.5 %collective-permute-start.1 = (bf16[2,1,128,640]{3,2,0,1:T(8,128)(2,1)S(1)}, bf16[2,1,128,640]{3,2,0,1:T(8,128)(2,1)S(1)}, u32[]{:S(2)}, u32[]{:S(2)}) collective-permute-start(bf16[2,1,128,640]{3,2,0,1:T(8,128)(2,1)S(1)} %dynamic-slice_bitcast_fusion), channel_id=1, source_target_pairs={{8,0},{12,4},{0,8},{4,12},{9,1},{13,5},{1,9},{5,13},{10,2},{14,6},... | collective-permute-start | bytes 983048 | tf_op jit(solution)/shard_map/ppermute | solution.py:89
  14.7 0.5 multiply_reduce_fusion.1
  15.2 0.5 multiply_reduce_fusion
  15.7 0.5 multiply_reduce_fusion.3
  16.2 0.5 multiply_reduce_fusion.2
  16.7 0.5 multiply_reduce_fusion.4
  17.3 0.1 broadcast_select_fusion
  17.4 0.3 fusion.148
  17.7 0.3 fusion.149
  18.0 0.3 fusion.146
  18.3 0.3 fusion.147
  18.7 0.3 fusion.145
  19.0 0.3 fusion.135
  19.3 0.9 %fusion.136 = (f32[512]{0:T(512)S(1)}, f32[512,1024]{1,0:T(8,128)S(1)}, f32[512]{0:T(512)S(1)}, f32[512,1024]{1,0:T(8,128)S(1)}) fusion(f32[512]{0:T(512)S(1)} %max.118, f32[512,1024]{1,0:T(8,128)S(1)} %get-tuple-element.114, f32[512]{0:T(512)S(1)} %max.116, f32[512,1024]{1,0:T(8,128)S(1)} %get-tuple-element.110), kind=kLoop, calls=%fused_computation.265 | loop fusion | flops 3144704 | bytes 8396800 | tf_op jit(solution)/shard_map/reduce_sum | solution.py:110
  20.3 0.3 fusion.139
  20.6 0.9 %fusion.140 = (f32[512]{0:T(512)S(1)}, f32[512,1024]{1,0:T(8,128)S(1)}, f32[512]{0:T(512)S(1)}, f32[512,1024]{1,0:T(8,128)S(1)}) fusion(f32[512]{0:T(512)S(1)} %max.114, f32[512,1024]{1,0:T(8,128)S(1)} %get-tuple-element.106, f32[512]{0:T(512)S(1)} %max.112, f32[512,1024]{1,0:T(8,128)S(1)} %get-tuple-element.102), kind=kLoop, calls=%fused_computation.269 | loop fusion | flops 3144704 | bytes 8396800 | tf_op jit(solution)/shard_map/reduce_sum | solution.py:110
  21.5 0.2 fusion.143
  21.7 0.5 fusion.144
  22.2 19.0 %collective-permute-done.1 = bf16[2,1,128,640]{3,2,0,1:T(8,128)(2,1)S(1)} collective-permute-done((bf16[2,1,128,640]{3,2,0,1:T(8,128)(2,1)S(1)}, bf16[2,1,128,640]{3,2,0,1:T(8,128)(2,1)S(1)}, u32[]{:S(2)}, u32[]{:S(2)}) %collective-permute-start.1) | collective-permute-done | bytes 327712 | tf_op jit(solution)/shard_map/ppermute | solution.py:89
  41.2 0.2 fusion.159
  41.4 0.2 fusion.157
  41.6 0.2 fusion.155
  41.9 0.2 fusion.153
  42.2 0.2 fusion.151
  42.4 1.2 %collective-permute-done.3 = bf16[2,1,1,128,640]{4,3,0,2,1:T(8,128)(2,1)S(1)} collective-permute-done((bf16[2,1,1,128,640]{4,3,0,2,1:T(8,128)(2,1)S(1)}, bf16[2,1,1,128,640]{4,3,0,2,1:T(8,128)(2,1)S(1)}, u32[]{:S(2)}, u32[]{:S(2)}) %collective-permute-start.3) | collective-permute-done | bytes 327712 | tf_op jit(solution)/shard_map/ppermute | solution.py:121
  43.6 0.2 fusion.158
  43.8 0.2 fusion.156
  44.0 0.2 fusion.154
  44.2 0.2 fusion.152
  44.4 0.2 fusion.150
  44.6 0.1 fusion.80
  44.8 0.3 fusion.45
  45.0 0.6 %fusion.31 = f32[512,128]{0,1:T(8,128)S(1)} fusion(f32[512,128]{0,1:T(8,128)S(1)} %fusion.45, f32[512,1024]{1,0:T(8,128)S(1)} %get-tuple-element.34, f32[512]{0:T(512)S(1)} %bitcast.255, bf16[2,1024,640]{2,1,0:T(8,128)(2,1)S(1)} %copy-done), kind=kOutput, calls=%fused_computation.72 | convolution fusion | flops 135331840 | bytes 2885632 | tf_op jit(solution)/shard_map/dot_general | solution.py:159
  45.6 0.2 convolution_add_fusion.9
  45.9 0.2 fusion.29
  46.1 0.1 fusion.88
  46.2 0.3 fusion.49
  46.5 0.6 %fusion.39 = f32[512,128]{0,1:T(8,128)S(1)} fusion(f32[512,128]{0,1:T(8,128)S(1)} %fusion.49, f32[512,1024]{1,0:T(8,128)S(1)} %get-tuple-element.51, f32[512]{0:T(512)S(1)} %bitcast.257, bf16[2,1024,640]{2,1,0:T(8,128)(2,1)S(1)} %copy-done), kind=kOutput, calls=%fused_computation.80 | convolution fusion | flops 135331840 | bytes 2885632 | tf_op jit(solution)/shard_map/dot_general | solution.py:159
  47.1 0.2 convolution_add_fusion.1
  47.3 0.1 fusion.86
  47.5 0.3 fusion.48
  47.7 0.6 %fusion.37 = f32[512,128]{0,1:T(8,128)S(1)} fusion(f32[512,128]{0,1:T(8,128)S(1)} %fusion.48, f32[512,1024]{1,0:T(8,128)S(1)} %get-tuple-element.47, f32[512]{0:T(512)S(1)} %bitcast.259, bf16[2,1024,640]{2,1,0:T(8,128)(2,1)S(1)} %copy-done), kind=kOutput, calls=%fused_computation.78 | convolution fusion | flops 135331840 | bytes 2885632 | tf_op jit(solution)/shard_map/dot_general | solution.py:159
  48.3 0.2 convolution_add_fusion.3
  48.6 0.1 fusion.84
  48.7 0.3 fusion.47
  49.0 0.6 %fusion.35 = f32[512,128]{0,1:T(8,128)S(1)} fusion(f32[512,128]{0,1:T(8,128)S(1)} %fusion.47, f32[512,1024]{1,0:T(8,128)S(1)} %get-tuple-element.43, f32[512]{0:T(512)S(1)} %bitcast.261, bf16[2,1024,640]{2,1,0:T(8,128)(2,1)S(1)} %copy-done), kind=kOutput, calls=%fused_computation.76 | convolution fusion | flops 135331840 | bytes 2885632 | tf_op jit(solution)/shard_map/dot_general | solution.py:159
  49.5 0.2 convolution_add_fusion.5
  49.8 0.1 fusion.82
  49.9 0.3 fusion.46
  50.2 0.6 %fusion.33 = f32[512,128]{0,1:T(8,128)S(1)} fusion(f32[512,128]{0,1:T(8,128)S(1)} %fusion.46, f32[512,1024]{1,0:T(8,128)S(1)} %get-tuple-element.39, f32[512]{0:T(512)S(1)} %bitcast.253, bf16[2,1024,640]{2,1,0:T(8,128)(2,1)S(1)} %copy-done), kind=kOutput, calls=%fused_computation.74 | convolution fusion | flops 135331840 | bytes 2885632 | tf_op jit(solution)/shard_map/dot_general | solution.py:159
  50.8 0.2 convolution_add_fusion.7
  51.0 0.2 fusion.27
  51.2 0.2 fusion.25
  51.5 0.2 fusion.23
  51.7 0.2 fusion.21
  51.9 1.1 %copy.5 = bf16[512,640]{1,0:T(8,128)(2,1)} copy(bf16[512,640]{0,1:T(8,128)(2,1)S(1)} %bitcast.241) | data formatting | bytes 1310720 | tf_op jit(solution)/shard_map/reshape | solution.py:165
  (33 shorter events, 0.3 us)
Async XLA Ops:
  0.0 12.1 %copy-start = (bf16[2,1024,640]{2,1,0:T(8,128)(2,1)S(1)}, bf16[2,1024,640]{2,1,0:T(8,128)(2,1)}, u32[]{:S(2)}) copy-start(bf16[2,1024,640]{2,1,0:T(8,128)(2,1)} %param.4) | copy-start | bytes 7864324
  0.0 2.7 %copy-start.2 = (s32[4,8]{1,0:T(4,128)S(1)}, s32[4,8]{1,0:T(4,128)}, u32[]{:S(2)}) copy-start(s32[4,8]{1,0:T(4,128)} %param.5) | copy-start | bytes 388
  0.0 14.6 %copy-start.1 = (bf16[512,640]{1,0:T(8,128)(2,1)S(1)}, bf16[512,640]{1,0:T(8,128)(2,1)}, u32[]{:S(2)}) copy-start(bf16[512,640]{1,0:T(8,128)(2,1)} %param.3) | copy-start | bytes 1966084
  3.3 7.0 %collective-permute-start = (s32[1]{0:T(128)}, s32[1]{0:T(128)}, u32[]{:S(2)}, u32[]{:S(2)}) collective-permute-start(s32[1]{0:T(128)} %dynamic_slice.18), channel_id=1, source_target_pairs={{0,8},{4,12},{8,0},{12,4},{1,9},{5,13},{9,1},{13,5},{2,10},{6,14},... | collective-permute-start | bytes 20 | tf_op jit(solution)/shard_map/ppermute | solution.py:79
  7.3 9.9 %collective-permute-start.2 = (bf16[2,512,640]{2,1,0:T(8,128)(2,1)}, bf16[2,512,640]{2,1,0:T(8,128)(2,1)}, u32[]{:S(2)}, u32[]{:S(2)}) collective-permute-start(bf16[2,512,640]{2,1,0:T(8,128)(2,1)} %constant_dynamic-slice_fusion), channel_id=1, source_target_pairs={{1,4},{5,8},{9,12},{4,1},{8,5},{12,9},{3,6},{7,10},{11,14},{6,3},{... | collective-permute-start | bytes 3932168 | tf_op jit(solution)/shard_map/ppermute | solution.py:28
  12.2 29.1 %collective-permute-start.1 = (bf16[2,1,128,640]{3,2,0,1:T(8,128)(2,1)S(1)}, bf16[2,1,128,640]{3,2,0,1:T(8,128)(2,1)S(1)}, u32[]{:S(2)}, u32[]{:S(2)}) collective-permute-start(bf16[2,1,128,640]{3,2,0,1:T(8,128)(2,1)S(1)} %dynamic-slice_bitcast_fusion), channel_id=1, source_target_pairs={{8,0},{12,4},{0,8},{4,12},{9,1},{13,5},{1,9},{5,13},{10,2},{14,6},... | collective-permute-start | bytes 983048 | tf_op jit(solution)/shard_map/ppermute | solution.py:89
  41.9 1.7 %collective-permute-start.3 = (bf16[2,1,1,128,640]{4,3,0,2,1:T(8,128)(2,1)S(1)}, bf16[2,1,1,128,640]{4,3,0,2,1:T(8,128)(2,1)S(1)}, u32[]{:S(2)}, u32[]{:S(2)}) collective-permute-start(bf16[2,1,1,128,640]{4,3,0,2,1:T(8,128)(2,1)S(1)} %bitcast.315), channel_id=1, source_target_pairs={{0,1},{1,0},{2,3},{3,2},{4,5},{5,4},{6,7},{7,6},{8,9},{9,8},{10,11... | collective-permute-start | bytes 983048 | tf_op jit(solution)/shard_map/ppermute | solution.py:121

commit v10 on v8

--- a/solution.py
+++ b/solution.py
@@ -86,7 +86,10 @@
             pick_list.append(pick)
             valid_list.append((named >= 0) & inside)
     query, payloads = lax.optimization_barrier((query, [chosen for chosen, _ in received]))
-    received = [lax.ppermute(chosen, "seq", back) for chosen, (_, back) in zip(payloads, received)]
+    received = [
+        jnp.stack([lax.ppermute(chosen[i], "seq", back) for i in range(2)])
+        for chosen, (_, back) in zip(payloads, received)
+    ]
     slot_count = len(received)
 
     near = []

time: 52.7 us -> 57.2 us (1.085)
  waiting for transfers between devices: 20.8 us -> 25.2 us
  starting transfers between devices: 8.27 us -> 8.85 us
    ppermute x1 -> x2, waiting for transfers between devices: 19.3 us -> 23.8 us  [per_device(): lax.ppermute(chosen[i], 'seq', back)]
    ppermute x1 -> x2, starting transfers between devices: 2.48 us -> 2.99 us  [per_device(): lax.ppermute(chosen[i], 'seq', back)]
  transfers between devices with their start and end apart: 4 -> 5, of which waited for: 2 -> 3; matrix products, arithmetic and copies ran while one was open for 17% -> 7% of each run, Pallas kernels for 0% -> 0%
where the time goes in v10:
time: 57.2 us; the launch traced here: 57 us
  waiting for transfers between devices  25.2 us (44%)
  matrix products  10.9 us (19%)
  starting transfers between devices  8.85 us (15%)
  other arithmetic  5.23 us (9%)
  local copies, waits for them, and re-layouts  4.82 us (8%)
  between operations  2.05 us (4%)
    ppermute x2, waiting for transfers between devices, per_device(): lax.ppermute(chosen[i], 'seq', back)  23.8 us
    ppermute x1, starting transfers between devices, per_device(): wanted = lax.ppermute(phase[None], 'seq', pairs)[0]  4.05 us
    ppermute x2, starting transfers between devices, per_device(): lax.ppermute(chosen[i], 'seq', back)  2.99 us
    dot_general x5, matrix products, per_device(): jnp.dot(own_prob, key_value[1, :, cols], preferred_element_type=jnp.float32)  2.82 us
    dynamic_slice x1, local copies, waits for them, and re-layouts, halo_frame(): payload = lax.dynamic_slice_in_dim(key_value, start, frame_rows, 1)  2.65 us
    dot_general x5, matrix products, per_device(): jnp.dot(query_head, key_value[0, :, cols].T, preferred_element_type=jnp.f...  2.6 us
    reduce_sum x3, other arithmetic, per_device(): jnp.sum(own_exp, axis=1, keepdims=True)  2.3 us
    ppermute x1, starting transfers between devices, halo_frame(): return (lax.ppermute(payload, ('seq', 'rep'), pairs), key_blocks)  1.74 us
  transfers between devices with their start and end apart: 5, of which 3 were waited for; matrix products, arithmetic and copies ran while one was open for 7% of the time, Pallas kernels for 0%

profile of v10, /device:TPU:0, one launch (start us, length us, event | category | flops | bytes accessed | tf_op | source)
XLA Modules:
  0.0 57.0 jit_solution(7442989432542135019)
XLA Ops:
  0.0 2.7 %constant_dynamic-slice_fusion = bf16[2,512,640]{2,1,0:T(8,128)(2,1)} fusion(bf16[2,1024,640]{2,1,0:T(8,128)(2,1)} %param.4, s32[]{:T(128)S(6)} %select_n.99), kind=kLoop, calls=%fused_computation.189 | loop fusion | bytes 2621444 | tf_op jit(solution)/shard_map/dynamic_slice | solution.py:24
  2.7 0.0 copy-done.2
  2.7 0.7 %dynamic_slice.18 = s32[1]{0:T(128)} dynamic-slice(s32[8]{0:T(128)S(1)} %and_select_fusion.1, s32[]{:T(128)S(6)} %select_n.101), dynamic_slice_sizes={1} | dynamic-slice | bytes 12 | tf_op jit(solution)/shard_map/jit(dynamic_index_in_dim)/dynamic_slice | solution.py:78
  3.3 4.0 %collective-permute-start = (s32[1]{0:T(128)}, s32[1]{0:T(128)}, u32[]{:S(2)}, u32[]{:S(2)}) collective-permute-start(s32[1]{0:T(128)} %dynamic_slice.18), channel_id=1, source_target_pairs={{0,8},{4,12},{8,0},{12,4},{1,9},{5,13},{9,1},{13,5},{2,10},{6,14},... | collective-permute-start | bytes 20 | tf_op jit(solution)/shard_map/ppermute | solution.py:79
  7.4 1.7 %collective-permute-start.3 = (bf16[2,512,640]{2,1,0:T(8,128)(2,1)}, bf16[2,512,640]{2,1,0:T(8,128)(2,1)}, u32[]{:S(2)}, u32[]{:S(2)}) collective-permute-start(bf16[2,512,640]{2,1,0:T(8,128)(2,1)} %constant_dynamic-slice_fusion), channel_id=1, source_target_pairs={{1,4},{5,8},{9,12},{4,1},{8,5},{12,9},{3,6},{7,10},{11,14},{6,3},{... | collective-permute-start | bytes 3932168 | tf_op jit(solution)/shard_map/ppermute | solution.py:28
  9.1 0.8 %subtract_reduce_fusion = s32[4]{0:T(128)S(1)} fusion(s32[4,8]{1,0:T(4,128)S(1)} %copy-done.2, s32[]{:T(128)S(6)} %select_n.101, s32[]{:T(128)} %bitcast.29, s32[]{:T(128)S(6)} %mul.171), kind=kLoop, calls=%fused_computation.181 | loop fusion | flops 8 | bytes 44 | tf_op jit(solution)/shard_map/sub | solution.py:85
  9.9 0.2 and_reduce_fusion
  10.2 0.0 collective-permute-done
  11.8 0.0 copy-done
  11.9 0.0 copy-done.1
  11.9 0.5 multiply_reduce_fusion.1
  12.5 2.5 %collective-permute-start.1 = (bf16[1,128,640]{2,1,0:T(8,128)(2,1)S(1)}, bf16[1,128,640]{2,1,0:T(8,128)(2,1)S(1)}, u32[]{:S(2)}, u32[]{:S(2)}) collective-permute-start(bf16[1,128,640]{2,1,0:T(8,128)(2,1)S(1)} %get-tuple-element.85), channel_id=1, source_target_pairs={{8,0},{12,4},{0,8},{4,12},{9,1},{13,5},{1,9},{5,13},{10,2},{14,6},... | collective-permute-start | bytes 491528 | tf_op jit(solution)/shard_map/ppermute | solution.py:90
  14.9 0.5 collective-permute-start.2
  15.5 0.5 multiply_reduce_fusion
  16.0 0.5 multiply_reduce_fusion.3
  16.5 0.5 multiply_reduce_fusion.2
  17.0 0.5 multiply_reduce_fusion.4
  17.5 22.0 %collective-permute-done.1 = bf16[1,128,640]{2,1,0:T(8,128)(2,1)S(1)} collective-permute-done((bf16[1,128,640]{2,1,0:T(8,128)(2,1)S(1)}, bf16[1,128,640]{2,1,0:T(8,128)(2,1)S(1)}, u32[]{:S(2)}, u32[]{:S(2)}) %collective-permute-start.1) | collective-permute-done | bytes 163872 | tf_op jit(solution)/shard_map/ppermute | solution.py:90
  39.5 1.8 %collective-permute-done.2 = bf16[1,128,640]{2,1,0:T(8,128)(2,1)S(1)} collective-permute-done((bf16[1,128,640]{2,1,0:T(8,128)(2,1)S(1)}, bf16[1,128,640]{2,1,0:T(8,128)(2,1)S(1)}, u32[]{:S(2)}, u32[]{:S(2)}) %collective-permute-start.2) | collective-permute-done | bytes 163872 | tf_op jit(solution)/shard_map/ppermute | solution.py:90
  41.3 0.0 collective-permute-done.3
  41.3 0.1 broadcast_select_fusion
  41.5 0.3 fusion.108
  41.8 0.3 fusion.109
  42.1 0.3 fusion.106
  42.4 0.3 fusion.107
  42.7 0.3 fusion.105
  43.1 0.2 fusion.103
  43.3 0.5 fusion.104
  43.8 0.3 fusion.95
  44.1 0.9 %fusion.96 = (f32[512]{0:T(512)S(1)}, f32[512,1024]{1,0:T(8,128)S(1)}, f32[512]{0:T(512)S(1)}, f32[512,1024]{1,0:T(8,128)S(1)}) fusion(f32[512]{0:T(512)S(1)} %max.103, f32[512,1024]{1,0:T(8,128)S(1)} %get-tuple-element.104, f32[512]{0:T(512)S(1)} %max.101, f32[512,1024]{1,0:T(8,128)S(1)} %get-tuple-element.100), kind=kLoop, calls=%fused_computation.197 | loop fusion | flops 3144704 | bytes 8396800 | tf_op jit(solution)/shard_map/reduce_sum | solution.py:113
  45.1 0.3 fusion.99
  45.4 0.9 %fusion.100 = (f32[512]{0:T(512)S(1)}, f32[512,1024]{1,0:T(8,128)S(1)}, f32[512]{0:T(512)S(1)}, f32[512,1024]{1,0:T(8,128)S(1)}) fusion(f32[512]{0:T(512)S(1)} %max.99, f32[512,1024]{1,0:T(8,128)S(1)} %get-tuple-element.96, f32[512]{0:T(512)S(1)} %max.97, f32[512,1024]{1,0:T(8,128)S(1)} %get-tuple-element.92), kind=kLoop, calls=%fused_computation.201 | loop fusion | flops 3144704 | bytes 8396800 | tf_op jit(solution)/shard_map/reduce_sum | solution.py:113
  46.3 0.1 collective-permute-start.4
  46.4 0.1 pad_add_fusion
  46.4 0.1 compare_and_fusion
  46.5 1.5 %collective-permute-done.4 = bf16[2,1,1,128,640]{4,3,0,2,1:T(8,128)(2,1)S(1)} collective-permute-done((bf16[2,1,1,128,640]{4,3,0,2,1:T(8,128)(2,1)S(1)}, bf16[2,1,1,128,640]{4,3,0,2,1:T(8,128)(2,1)S(1)}, u32[]{:S(2)}, u32[]{:S(2)}) %collective-permute-start.4) | collective-permute-done | bytes 327712 | tf_op jit(solution)/shard_map/ppermute | solution.py:124
  48.0 0.1 pad_maximum_fusion
  48.1 0.3 broadcast_in_dim.101
  48.4 0.3 fusion.114
  48.7 0.3 fusion.113
  48.9 0.3 fusion.112
  49.2 0.3 fusion.111
  49.4 0.3 fusion.110
  49.7 0.1 fusion.39
  49.8 0.6 fusion.24
  50.4 0.3 convolution_add_fusion.1
  50.7 0.1 fusion.38
  50.8 0.6 fusion.23
  51.4 0.3 convolution_add_fusion.3
  51.7 0.1 fusion.37
  51.8 0.6 fusion.22
  52.4 0.3 convolution_add_fusion.5
  52.7 0.1 fusion.36
  52.8 0.6 fusion.21
  53.4 0.3 convolution_add_fusion.7
  53.7 0.1 fusion.35
  53.8 0.6 fusion.20
  54.4 0.3 convolution_add_fusion.9
  54.7 0.3 fusion.11
  54.9 0.3 fusion.13
  55.2 0.3 fusion.15
  55.5 0.2 fusion.17
  55.7 0.2 fusion.19
  56.0 1.1 %copy.9 = bf16[512,640]{1,0:T(8,128)(2,1)} copy(bf16[512,640]{0,1:T(8,128)(2,1)S(1)} %fusion.19) | data formatting | bytes 1310720 | tf_op jit(solution)/shard_map/concatenate | solution.py:157
  (29 shorter events, 0.3 us)
Async XLA Ops:
  0.0 11.8 %copy-start = (bf16[2,1024,640]{2,1,0:T(8,128)(2,1)S(1)}, bf16[2,1024,640]{2,1,0:T(8,128)(2,1)}, u32[]{:S(2)}) copy-start(bf16[2,1024,640]{2,1,0:T(8,128)(2,1)} %param.4) | copy-start | bytes 7864324
  0.0 2.7 %copy-start.2 = (s32[4,8]{1,0:T(4,128)S(1)}, s32[4,8]{1,0:T(4,128)}, u32[]{:S(2)}) copy-start(s32[4,8]{1,0:T(4,128)} %param.5) | copy-start | bytes 388
  0.0 11.9 %copy-start.1 = (bf16[512,640]{1,0:T(8,128)(2,1)S(1)}, bf16[512,640]{1,0:T(8,128)(2,1)}, u32[]{:S(2)}) copy-start(bf16[512,640]{1,0:T(8,128)(2,1)} %param.3) | copy-start | bytes 1966084
  3.3 6.8 %collective-permute-start = (s32[1]{0:T(128)}, s32[1]{0:T(128)}, u32[]{:S(2)}, u32[]{:S(2)}) collective-permute-start(s32[1]{0:T(128)} %dynamic_slice.18), channel_id=1, source_target_pairs={{0,8},{4,12},{8,0},{12,4},{1,9},{5,13},{9,1},{13,5},{2,10},{6,14},... | collective-permute-start | bytes 20 | tf_op jit(solution)/shard_map/ppermute | solution.py:79
  7.4 34.0 %collective-permute-start.3 = (bf16[2,512,640]{2,1,0:T(8,128)(2,1)}, bf16[2,512,640]{2,1,0:T(8,128)(2,1)}, u32[]{:S(2)}, u32[]{:S(2)}) collective-permute-start(bf16[2,512,640]{2,1,0:T(8,128)(2,1)} %constant_dynamic-slice_fusion), channel_id=1, source_target_pairs={{1,4},{5,8},{9,12},{4,1},{8,5},{12,9},{3,6},{7,10},{11,14},{6,3},{... | collective-permute-start | bytes 3932168 | tf_op jit(solution)/shard_map/ppermute | solution.py:28
  12.5 27.1 %collective-permute-start.1 = (bf16[1,128,640]{2,1,0:T(8,128)(2,1)S(1)}, bf16[1,128,640]{2,1,0:T(8,128)(2,1)S(1)}, u32[]{:S(2)}, u32[]{:S(2)}) collective-permute-start(bf16[1,128,640]{2,1,0:T(8,128)(2,1)S(1)} %get-tuple-element.85), channel_id=1, source_target_pairs={{8,0},{12,4},{0,8},{4,12},{9,1},{13,5},{1,9},{5,13},{10,2},{14,6},... | collective-permute-start | bytes 491528 | tf_op jit(solution)/shard_map/ppermute | solution.py:90
  14.9 26.4 %collective-permute-start.2 = (bf16[1,128,640]{2,1,0:T(8,128)(2,1)S(1)}, bf16[1,128,640]{2,1,0:T(8,128)(2,1)S(1)}, u32[]{:S(2)}, u32[]{:S(2)}) collective-permute-start(bf16[1,128,640]{2,1,0:T(8,128)(2,1)S(1)} %get-tuple-element.86), channel_id=1, source_target_pairs={{8,0},{12,4},{0,8},{4,12},{9,1},{13,5},{1,9},{5,13},{10,2},{14,6},... | collective-permute-start | bytes 491528 | tf_op jit(solution)/shard_map/ppermute | solution.py:90
  46.3 1.7 %collective-permute-start.4 = (bf16[2,1,1,128,640]{4,3,0,2,1:T(8,128)(2,1)S(1)}, bf16[2,1,1,128,640]{4,3,0,2,1:T(8,128)(2,1)S(1)}, u32[]{:S(2)}, u32[]{:S(2)}) collective-permute-start(bf16[2,1,1,128,640]{4,3,0,2,1:T(8,128)(2,1)S(1)} %bitcast.191), channel_id=1, source_target_pairs={{0,1},{1,0},{2,3},{3,2},{4,5},{5,4},{6,7},{7,6},{8,9},{9,8},{10,11... | collective-permute-start | bytes 983048 | tf_op jit(solution)/shard_map/ppermute | solution.py:124

commit v11 on v8

--- a/solution.py
+++ b/solution.py
@@ -86,7 +86,9 @@
             pick_list.append(pick)
             valid_list.append((named >= 0) & inside)
     query, payloads = lax.optimization_barrier((query, [chosen for chosen, _ in received]))
-    received = [lax.ppermute(chosen, "seq", back) for chosen, (_, back) in zip(payloads, received)]
+    backs = [back for _, back in received]
+    received = [lax.ppermute(chosen[0][None], "seq", back) for chosen, back in zip(payloads, backs)]
+    later_values = [chosen[1][None] for chosen in payloads]
     slot_count = len(received)
 
     near = []
@@ -111,16 +113,19 @@
             halo_exp, axis=1, keepdims=True
         )
         near.append((near_top, own_exp, halo_exp, near_total))
-    received, near = lax.optimization_barrier((received, near))
+    received, near, later_values = lax.optimization_barrier((received, near, later_values))
+    values = [lax.ppermute(chosen, "seq", back) for chosen, back in zip(later_values, backs)]
 
-    mine = jnp.stack(received, 1)
-    parts = [mine]
-    sources = [rep_index]
-    for k in range(1, rep_count):
-        shift = [(r, (r + k) % rep_count) for r in range(rep_count)]
-        parts.append(lax.ppermute(mine, "rep", shift))
-        sources.append((rep_index - k) % rep_count)
-    far_pair = jnp.stack(parts, 2).reshape(2, slot_count * far_count * MASK_BLOCK_SIZE, columns)
+    def gather_reps(pieces):
+        mine = jnp.stack(pieces, 1)
+        parts = [mine]
+        for k in range(1, rep_count):
+            shift = [(r, (r + k) % rep_count) for r in range(rep_count)]
+            parts.append(lax.ppermute(mine, "rep", shift))
+        return jnp.stack(parts, 2).reshape(slot_count * far_count * MASK_BLOCK_SIZE, columns)
+
+    sources = [(rep_index - k) % rep_count for k in range(rep_count)]
+    far_keys = gather_reps(received)
     far_pick = jnp.stack(pick_list, 1)
     far_valid = jnp.stack(valid_list, 1)
     share_ids = jnp.arange(far_share, dtype=jnp.int32)
@@ -133,7 +138,7 @@
         cols = slice(head * HEAD_WIDTH, (head + 1) * HEAD_WIDTH)
         near_top, own_exp, halo_exp, near_total = near[head]
         far_scores = (
-            jnp.dot(query[:, cols], far_pair[0, :, cols].T, preferred_element_type=jnp.float32)
+            jnp.dot(query[:, cols], far_keys[:, cols].T, preferred_element_type=jnp.float32)
             * score_scale
         )
         far_scores = jnp.where(
@@ -149,9 +154,15 @@
         far_prob = (far_exp / row_total).astype(jnp.bfloat16)
         mixed = jnp.dot(own_prob, key_value[1, :, cols], preferred_element_type=jnp.float32)
         mixed = mixed + jnp.dot(halo_prob, halo[1, :, cols], preferred_element_type=jnp.float32)
-        mixed = mixed + jnp.dot(far_prob, far_pair[1, :, cols], preferred_element_type=jnp.float32)
-        outputs.append(mixed.astype(jnp.bfloat16))
-    return jnp.concatenate(outputs, axis=1)
+        outputs.append((mixed, far_prob))
+    values, outputs = lax.optimization_barrier((values, outputs))
+    far_values = gather_reps(values)
+    finished = []
+    for head, (mixed, far_prob) in enumerate(outputs):
+        cols = slice(head * HEAD_WIDTH, (head + 1) * HEAD_WIDTH)
+        mixed = mixed + jnp.dot(far_prob, far_values[:, cols], preferred_element_type=jnp.float32)
+        finished.append(mixed.astype(jnp.bfloat16))
+    return jnp.concatenate(finished, axis=1)
 
 
 def solution(mesh):

time: 52.7 us -> 51.6 us (0.979)
  waiting for transfers between devices: 20.8 us -> 14.8 us
  starting transfers between devices: 8.27 us -> 12.5 us
  other arithmetic: 5.21 us -> 6.55 us
    ppermute x1, waiting for transfers between devices: 19.3 us -> 1.36 us  [per_device(): lax.ppermute(chosen, 'seq', back)]
    ppermute x1 -> x3, waiting for transfers between devices: 1.47 us -> 13.4 us  [the longest x1 12 us: per_device(): lax.ppermute(chosen[0][None], 'seq', back)]
    ppermute x1 -> x3, starting transfers between devices: 0.01 us -> 2.84 us  [the longest x1 2.48 us: per_device(): lax.ppermute(chosen[0][None], 'seq', back)]
    ppermute x1, starting transfers between devices: 2.48 us -> 3.89 us  [per_device(): lax.ppermute(chosen, 'seq', back)]
    concatenate x1 -> x0, local copies, waits for them, and re-layouts: 1.08 us -> none  [per_device(): return jnp.concatenate(outputs, axis=1)]
    unnamed x6 -> x8, local copies, waits for them, and re-layouts: 0.01 us -> 0.84 us
    concatenate x0 -> x1, other arithmetic: none -> 0.68 us  [per_device(): return jnp.concatenate(finished, axis=1)]
  transfers between devices with their start and end apart: 4 -> 6, of which waited for: 2 -> 3; matrix products, arithmetic and copies ran while one was open for 17% -> 30% of each run, Pallas kernels for 0% -> 0%
where the time goes in v11:
time: 51.6 us; the launch traced here: 51.4 us
  waiting for transfers between devices  14.8 us (29%)
  starting transfers between devices  12.5 us (24%)
  matrix products  10.8 us (21%)
  other arithmetic  6.55 us (13%)
  local copies, waits for them, and re-layouts  4.5 us (9%)
  between operations  2.27 us (4%)
    ppermute x1, waiting for transfers between devices, per_device(): lax.ppermute(chosen[0][None], 'seq', back)  12 us
    ppermute x1, starting transfers between devices, per_device(): wanted = lax.ppermute(phase[None], 'seq', pairs)[0]  4.05 us
    ppermute x1, starting transfers between devices, per_device(): lax.ppermute(chosen, 'seq', back)  3.89 us
    dynamic_slice x1, local copies, waits for them, and re-layouts, halo_frame(): payload = lax.dynamic_slice_in_dim(key_value, start, frame_rows, 1)  2.65 us
    dot_general x5, matrix products, per_device(): jnp.dot(query_head, key_value[0, :, cols].T, preferred_element_type=jnp.f...  2.6 us
    ppermute x1, starting transfers between devices, per_device(): lax.ppermute(chosen[0][None], 'seq', back)  2.48 us
    dot_general x5, matrix products, per_device(): jnp.dot(own_prob, key_value[1, :, cols], preferred_element_type=jnp.float32)  2.42 us
    reduce_sum x3, other arithmetic, per_device(): jnp.sum(own_exp, axis=1, keepdims=True)  2.32 us
  transfers between devices with their start and end apart: 6, of which 3 were waited for; matrix products, arithmetic and copies ran while one was open for 30% of the time, Pallas kernels for 0%

profile of v11, /device:TPU:0, one launch (start us, length us, event | category | flops | bytes accessed | tf_op | source)
XLA Modules:
  0.0 51.4 jit_solution(6688660356084218938)
XLA Ops:
  0.0 2.7 %constant_dynamic-slice_fusion = bf16[2,512,640]{2,1,0:T(8,128)(2,1)} fusion(bf16[2,1024,640]{2,1,0:T(8,128)(2,1)} %param.4, s32[]{:T(128)S(6)} %select_n.103), kind=kLoop, calls=%fused_computation.182 | loop fusion | bytes 2621444 | tf_op jit(solution)/shard_map/dynamic_slice | solution.py:24
  2.7 0.6 %dynamic_slice.18 = s32[1]{0:T(128)} dynamic-slice(s32[8]{0:T(128)S(1)} %and_select_fusion.1, s32[]{:T(128)S(6)} %select_n.105), dynamic_slice_sizes={1} | dynamic-slice | bytes 12 | tf_op jit(solution)/shard_map/jit(dynamic_index_in_dim)/dynamic_slice | solution.py:78
  3.3 4.0 %collective-permute-start = (s32[1]{0:T(128)}, s32[1]{0:T(128)}, u32[]{:S(2)}, u32[]{:S(2)}) collective-permute-start(s32[1]{0:T(128)} %dynamic_slice.18), channel_id=1, source_target_pairs={{0,8},{4,12},{8,0},{12,4},{1,9},{5,13},{9,1},{13,5},{2,10},{6,14},... | collective-permute-start | bytes 20 | tf_op jit(solution)/shard_map/ppermute | solution.py:79
  7.3 1.7 %collective-permute-start.2 = (bf16[2,512,640]{2,1,0:T(8,128)(2,1)}, bf16[2,512,640]{2,1,0:T(8,128)(2,1)}, u32[]{:S(2)}, u32[]{:S(2)}) collective-permute-start(bf16[2,512,640]{2,1,0:T(8,128)(2,1)} %constant_dynamic-slice_fusion), channel_id=1, source_target_pairs={{1,4},{5,8},{9,12},{4,1},{8,5},{12,9},{3,6},{7,10},{11,14},{6,3},{... | collective-permute-start | bytes 3932168 | tf_op jit(solution)/shard_map/ppermute | solution.py:28
  9.0 0.8 %subtract_reduce_fusion = s32[4]{0:T(128)S(1)} fusion(s32[4,8]{1,0:T(4,128)S(1)} %copy-done.3, s32[]{:T(128)S(6)} %select_n.105, s32[]{:T(128)} %bitcast.24, s32[]{:T(128)S(6)} %mul.171), kind=kLoop, calls=%fused_computation.174 | loop fusion | flops 8 | bytes 44 | tf_op jit(solution)/shard_map/sub | solution.py:85
  9.9 0.2 and_reduce_fusion
  10.1 0.1 pad_add_fusion
  12.1 2.5 %collective-permute-start.1 = (bf16[1,1,128,640]{3,2,0,1:T(8,128)(2,1)S(1)}, bf16[1,1,128,640]{3,2,0,1:T(8,128)(2,1)S(1)}, u32[]{:S(2)}, u32[]{:S(2)}) collective-permute-start(bf16[1,1,128,640]{3,2,0,1:T(8,128)(2,1)S(1)} %get-tuple-element.110), channel_id=1, source_target_pairs={{8,0},{12,4},{0,8},{4,12},{9,1},{13,5},{1,9},{5,13},{10,2},{14,6},... | collective-permute-start | bytes 491528 | tf_op jit(solution)/shard_map/ppermute | solution.py:90
  14.6 0.5 multiply_reduce_fusion.1
  15.1 0.5 %multiply_reduce_fusion = (f32[512]{0:T(512)S(1)}, f32[512,1024]{1,0:T(8,128)S(1)}) fusion(bf16[2,1024,640]{2,1,0:T(8,128)(2,1)S(1)} %copy-done, bf16[512,640]{1,0:T(8,128)(2,1)S(1)} %copy-done.1), kind=kOutput, calls=%fused_computation.10 | convolution fusion | flops 135265792 | bytes 2492416 | tf_op jit(solution)/shard_map/dot_general | solution.py:99
  15.7 0.5 %multiply_reduce_fusion.3 = (f32[512]{0:T(512)S(1)}, f32[512,1024]{1,0:T(8,128)S(1)}) fusion(bf16[2,1024,640]{2,1,0:T(8,128)(2,1)S(1)} %copy-done, bf16[512,640]{1,0:T(8,128)(2,1)S(1)} %copy-done.1), kind=kOutput, calls=%fused_computation.13 | convolution fusion | flops 135265792 | bytes 2492416 | tf_op jit(solution)/shard_map/dot_general | solution.py:99
  16.2 0.5 %multiply_reduce_fusion.2 = (f32[512]{0:T(512)S(1)}, f32[512,1024]{1,0:T(8,128)S(1)}) fusion(bf16[2,1024,640]{2,1,0:T(8,128)(2,1)S(1)} %copy-done, bf16[512,640]{1,0:T(8,128)(2,1)S(1)} %copy-done.1), kind=kOutput, calls=%fused_computation.12 | convolution fusion | flops 135265792 | bytes 2492416 | tf_op jit(solution)/shard_map/dot_general | solution.py:99
  16.7 0.5 %multiply_reduce_fusion.4 = (f32[512]{0:T(512)S(1)}, f32[512,1024]{1,0:T(8,128)S(1)}) fusion(bf16[2,1024,640]{2,1,0:T(8,128)(2,1)S(1)} %copy-done, bf16[512,640]{1,0:T(8,128)(2,1)S(1)} %copy-done.1), kind=kOutput, calls=%fused_computation.14 | convolution fusion | flops 135265792 | bytes 2492416 | tf_op jit(solution)/shard_map/dot_general | solution.py:99
  17.2 0.1 broadcast_select_fusion
  17.4 0.3 fusion.119
  17.7 0.3 fusion.120
  18.0 0.3 fusion.117
  18.3 0.3 fusion.118
  18.6 0.3 fusion.116
  19.0 0.3 fusion.105
  19.3 0.9 %fusion.106 = (f32[512]{0:T(512)S(1)}, f32[512,1024]{1,0:T(8,128)S(1)}, f32[512]{0:T(512)S(1)}, f32[512,1024]{1,0:T(8,128)S(1)}) fusion(f32[512]{0:T(512)S(1)} %max.103, f32[512,1024]{1,0:T(8,128)S(1)} %get-tuple-element.128, f32[512]{0:T(512)S(1)} %max.101, f32[512,1024]{1,0:T(8,128)S(1)} %get-tuple-element.124), kind=kLoop, calls=%fused_computation.190 | loop fusion | flops 3144704 | bytes 8396800 | tf_op jit(solution)/shard_map/reduce_sum | solution.py:112
  20.2 0.3 fusion.109
  20.5 0.9 %fusion.110 = (f32[512]{0:T(512)S(1)}, f32[512,1024]{1,0:T(8,128)S(1)}, f32[512]{0:T(512)S(1)}, f32[512,1024]{1,0:T(8,128)S(1)}) fusion(f32[512]{0:T(512)S(1)} %max.99, f32[512,1024]{1,0:T(8,128)S(1)} %get-tuple-element.120, f32[512]{0:T(512)S(1)} %max.97, f32[512,1024]{1,0:T(8,128)S(1)} %get-tuple-element.116), kind=kLoop, calls=%fused_computation.194 | loop fusion | flops 3144704 | bytes 8396800 | tf_op jit(solution)/shard_map/reduce_sum | solution.py:112
  21.5 0.5 %fusion.114 = (f32[512]{0:T(512)S(1)}, f32[512,1024]{1,0:T(8,128)S(1)}) fusion(f32[512]{0:T(512)S(1)} %max.95, f32[512,1024]{1,0:T(8,128)S(1)} %get-tuple-element.112), kind=kLoop, calls=%fused_computation.198 | loop fusion | flops 1572352 | bytes 4198400 | tf_op jit(solution)/shard_map/reduce_sum | solution.py:112
  22.0 0.2 fusion.113
  22.2 12.0 %collective-permute-done.1 = bf16[1,1,128,640]{3,2,0,1:T(8,128)(2,1)S(1)} collective-permute-done((bf16[1,1,128,640]{3,2,0,1:T(8,128)(2,1)S(1)}, bf16[1,1,128,640]{3,2,0,1:T(8,128)(2,1)S(1)}, u32[]{:S(2)}, u32[]{:S(2)}) %collective-permute-start.1) | collective-permute-done | bytes 163872 | tf_op jit(solution)/shard_map/ppermute | solution.py:90
  34.2 0.4 collective-permute-start.4
  34.6 0.1 compare_and_fusion
  34.6 3.9 %collective-permute-start.3 = (bf16[1,1,128,640]{3,2,0,1:T(8,128)(2,1)S(1)}, bf16[1,1,128,640]{3,2,0,1:T(8,128)(2,1)S(1)}, u32[]{:S(2)}, u32[]{:S(2)}) collective-permute-start(bf16[1,1,128,640]{3,2,0,1:T(8,128)(2,1)S(1)} %get-tuple-element.46), channel_id=1, source_target_pairs={{8,0},{12,4},{0,8},{4,12},{9,1},{13,5},{1,9},{5,13},{10,2},{14,6},... | collective-permute-start | bytes 491528 | tf_op jit(solution)/shard_map/ppermute | solution.py:117
  38.6 0.3 broadcast_in_dim.101
  38.9 0.3 fusion.125
  39.2 0.3 fusion.124
  39.4 0.3 fusion.123
  39.7 0.3 fusion.122
  40.0 0.3 fusion.121
  40.2 0.1 fusion.39
  40.4 0.1 divide_convert_fusion
  40.5 0.1 fusion.38
  40.6 0.1 divide_convert_fusion.1
  40.7 0.1 fusion.37
  40.8 0.1 divide_convert_fusion.2
  41.0 0.1 fusion.36
  41.1 0.1 divide_convert_fusion.3
  41.2 0.3 fusion.29
  41.5 0.5 fusion.19
  42.0 0.3 fusion.28
  42.3 0.5 fusion.17
  42.8 0.3 fusion.27
  43.2 0.5 fusion.15
  43.6 0.3 fusion.26
  44.0 0.5 fusion.13
  44.5 0.1 fusion.35
  44.6 0.3 fusion.25
  44.9 0.5 fusion.11
  45.4 0.1 divide_convert_fusion.4
  45.5 1.4 %collective-permute-done.3 = bf16[1,1,128,640]{3,2,0,1:T(8,128)(2,1)S(1)} collective-permute-done((bf16[1,1,128,640]{3,2,0,1:T(8,128)(2,1)S(1)}, bf16[1,1,128,640]{3,2,0,1:T(8,128)(2,1)S(1)}, u32[]{:S(2)}, u32[]{:S(2)}) %collective-permute-start.3) | collective-permute-done | bytes 163872 | tf_op jit(solution)/shard_map/ppermute | solution.py:117
  46.9 1.4 %collective-permute-done.5 = bf16[1,1,1,128,640]{4,3,2,1,0:T(8,128)(2,1)S(1)} collective-permute-done((bf16[1,1,1,128,640]{4,3,2,1,0:T(8,128)(2,1)S(1)}, bf16[1,1,1,128,640]{4,3,2,1,0:T(8,128)(2,1)S(1)}, u32[]{:S(2)}, u32[]{:S(2)}) %collective-permute-start.5) | collective-permute-done | bytes 163872 | tf_op jit(solution)/shard_map/ppermute | solution.py:124
  48.3 0.3 fusion.85
  48.6 0.3 fusion.87
  48.9 0.3 fusion.89
  49.1 0.3 fusion.91
  49.4 0.3 fusion.93
  49.9 0.8 %copy-done.2 = bf16[512,640]{1,0:T(8,128)(2,1)} copy-done((bf16[512,640]{1,0:T(8,128)(2,1)}, bf16[512,640]{1,0:T(8,128)(2,1)S(1)}, u32[]{:S(2)}) %copy-start.2) | copy-done | bytes 655384
  50.8 0.7 %fusion.69 = bf16[512,640]{1,0:T(8,128)(2,1)} fusion(bf16[512,640]{1,0:T(8,128)(2,1)} %copy-done.2, f32[512,128]{1,0:T(8,128)S(1)} %fusion.19, f32[512,128]{1,0:T(8,128)S(1)} %fusion.85), kind=kLoop, calls=%fused_computation.123 | loop fusion | flops 131072 | bytes 655360 | tf_op jit(solution)/shard_map/concatenate | solution.py:165
  (42 shorter events, 0.6 us)
Async XLA Ops:
  0.0 12.0 %copy-start = (bf16[2,1024,640]{2,1,0:T(8,128)(2,1)S(1)}, bf16[2,1024,640]{2,1,0:T(8,128)(2,1)}, u32[]{:S(2)}) copy-start(bf16[2,1024,640]{2,1,0:T(8,128)(2,1)} %param.4) | copy-start | bytes 7864324
  0.0 2.7 %copy-start.3 = (s32[4,8]{1,0:T(4,128)S(1)}, s32[4,8]{1,0:T(4,128)}, u32[]{:S(2)}) copy-start(s32[4,8]{1,0:T(4,128)} %param.5) | copy-start | bytes 388
  0.0 14.6 %copy-start.1 = (bf16[512,640]{1,0:T(8,128)(2,1)S(1)}, bf16[512,640]{1,0:T(8,128)(2,1)}, u32[]{:S(2)}) copy-start(bf16[512,640]{1,0:T(8,128)(2,1)} %param.3) | copy-start | bytes 1966084
  3.3 6.9 %collective-permute-start = (s32[1]{0:T(128)}, s32[1]{0:T(128)}, u32[]{:S(2)}, u32[]{:S(2)}) collective-permute-start(s32[1]{0:T(128)} %dynamic_slice.18), channel_id=1, source_target_pairs={{0,8},{4,12},{8,0},{12,4},{1,9},{5,13},{9,1},{13,5},{2,10},{6,14},... | collective-permute-start | bytes 20 | tf_op jit(solution)/shard_map/ppermute | solution.py:79
  7.3 9.9 %collective-permute-start.2 = (bf16[2,512,640]{2,1,0:T(8,128)(2,1)}, bf16[2,512,640]{2,1,0:T(8,128)(2,1)}, u32[]{:S(2)}, u32[]{:S(2)}) collective-permute-start(bf16[2,512,640]{2,1,0:T(8,128)(2,1)} %constant_dynamic-slice_fusion), channel_id=1, source_target_pairs={{1,4},{5,8},{9,12},{4,1},{8,5},{12,9},{3,6},{7,10},{11,14},{6,3},{... | collective-permute-start | bytes 3932168 | tf_op jit(solution)/shard_map/ppermute | solution.py:28
  12.1 22.1 %collective-permute-start.1 = (bf16[1,1,128,640]{3,2,0,1:T(8,128)(2,1)S(1)}, bf16[1,1,128,640]{3,2,0,1:T(8,128)(2,1)S(1)}, u32[]{:S(2)}, u32[]{:S(2)}) collective-permute-start(bf16[1,1,128,640]{3,2,0,1:T(8,128)(2,1)S(1)} %get-tuple-element.110), channel_id=1, source_target_pairs={{8,0},{12,4},{0,8},{4,12},{9,1},{13,5},{1,9},{5,13},{10,2},{14,6},... | collective-permute-start | bytes 491528 | tf_op jit(solution)/shard_map/ppermute | solution.py:90
  34.2 4.3 %collective-permute-start.4 = (bf16[1,1,1,128,640]{4,3,2,1,0:T(8,128)(2,1)S(1)}, bf16[1,1,1,128,640]{4,3,2,1,0:T(8,128)(2,1)S(1)}, u32[]{:S(2)}, u32[]{:S(2)}) collective-permute-start(bf16[1,1,1,128,640]{4,3,2,1,0:T(8,128)(2,1)S(1)} %bitcast.160), channel_id=1, source_target_pairs={{0,1},{1,0},{2,3},{3,2},{4,5},{5,4},{6,7},{7,6},{8,9},{9,8},{10,11... | collective-permute-start | bytes 491528 | tf_op jit(solution)/shard_map/ppermute | solution.py:124
  34.6 12.3 %collective-permute-start.3 = (bf16[1,1,128,640]{3,2,0,1:T(8,128)(2,1)S(1)}, bf16[1,1,128,640]{3,2,0,1:T(8,128)(2,1)S(1)}, u32[]{:S(2)}, u32[]{:S(2)}) collective-permute-start(bf16[1,1,128,640]{3,2,0,1:T(8,128)(2,1)S(1)} %get-tuple-element.46), channel_id=1, source_target_pairs={{8,0},{12,4},{0,8},{4,12},{9,1},{13,5},{1,9},{5,13},{10,2},{14,6},... | collective-permute-start | bytes 491528 | tf_op jit(solution)/shard_map/ppermute | solution.py:117
  46.9 1.4 %collective-permute-start.5 = (bf16[1,1,1,128,640]{4,3,2,1,0:T(8,128)(2,1)S(1)}, bf16[1,1,1,128,640]{4,3,2,1,0:T(8,128)(2,1)S(1)}, u32[]{:S(2)}, u32[]{:S(2)}) collective-permute-start(bf16[1,1,1,128,640]{4,3,2,1,0:T(8,128)(2,1)S(1)} %bitcast.158), channel_id=1, source_target_pairs={{0,1},{1,0},{2,3},{3,2},{4,5},{5,4},{6,7},{7,6},{8,9},{9,8},{10,11... | collective-permute-start | bytes 491528 | tf_op jit(solution)/shard_map/ppermute | solution.py:124
  49.9 0.8 %copy-start.2 = (bf16[512,640]{1,0:T(8,128)(2,1)}, bf16[512,640]{1,0:T(8,128)(2,1)S(1)}, u32[]{:S(2)}) copy-start(bf16[512,640]{1,0:T(8,128)(2,1)S(1)} %fusion.68) | copy-start | bytes 1966084

commit v12 on v11

--- a/solution.py
+++ b/solution.py
@@ -157,12 +157,15 @@
         outputs.append((mixed, far_prob))
     values, outputs = lax.optimization_barrier((values, outputs))
     far_values = gather_reps(values)
-    finished = []
-    for head, (mixed, far_prob) in enumerate(outputs):
-        cols = slice(head * HEAD_WIDTH, (head + 1) * HEAD_WIDTH)
-        mixed = mixed + jnp.dot(far_prob, far_values[:, cols], preferred_element_type=jnp.float32)
-        finished.append(mixed.astype(jnp.bfloat16))
-    return jnp.concatenate(finished, axis=1)
+    near_part = jnp.stack([mixed for mixed, _ in outputs], axis=1)
+    far_probs = jnp.stack([far_prob for _, far_prob in outputs], axis=0)
+    far_part = jnp.einsum(
+        "hqk,khd->qhd",
+        far_probs,
+        far_values.reshape(-1, head_count, HEAD_WIDTH),
+        preferred_element_type=jnp.float32,
+    )
+    return (near_part + far_part).astype(jnp.bfloat16).reshape(query_count, columns)
 
 
 def solution(mesh):

time: 51.6 us -> 53.4 us (1.035)
  local copies, waits for them, and re-layouts: 4.5 us -> 7.06 us
  other arithmetic: 6.55 us -> 5.85 us
    another operation x0 -> x4, local copies, waits for them, and re-layouts: none -> 1.91 us  [the longest x1 0.93 us: gather_reps(): jnp.stack(parts, 2)]
    reshape x0 -> x1, local copies, waits for them, and re-layouts: none -> 1.08 us  [per_device(): (near_part + far_part).astype(jnp.bfloat16).reshape(query_count, columns)]
    concatenate x1 -> x0, other arithmetic: 0.68 us -> none  [per_device(): return jnp.concatenate(finished, axis=1)]
    unnamed x8 -> x14, local copies, waits for them, and re-layouts: 0.84 us -> 0.17 us
    dot_general x5 -> x1, matrix products: 1.32 us -> 1.59 us  [per_device(): jnp.einsum('hqk,khd->qhd', far_probs, far_values.reshape(-1, head_count,...]
where the time goes in v12:
time: 53.4 us; the launch traced here: 53.2 us
  waiting for transfers between devices  14.3 us (27%)
  starting transfers between devices  12.6 us (24%)
  matrix products  11.1 us (21%)
  local copies, waits for them, and re-layouts  7.06 us (13%)
  other arithmetic  5.85 us (11%)
  between operations  2.29 us (4%)
    ppermute x1, waiting for transfers between devices, per_device(): lax.ppermute(chosen[0][None], 'seq', back)  12 us
    ppermute x1, starting transfers between devices, per_device(): wanted = lax.ppermute(phase[None], 'seq', pairs)[0]  4.05 us
    ppermute x1, starting transfers between devices, per_device(): lax.ppermute(chosen, 'seq', back)  3.86 us
    dynamic_slice x1, local copies, waits for them, and re-layouts, halo_frame(): payload = lax.dynamic_slice_in_dim(key_value, start, frame_rows, 1)  2.65 us
    dot_general x5, matrix products, per_device(): jnp.dot(query_head, key_value[0, :, cols].T, preferred_element_type=jnp.f...  2.6 us
    ppermute x1, starting transfers between devices, per_device(): lax.ppermute(chosen[0][None], 'seq', back)  2.48 us
    dot_general x5, matrix products, per_device(): jnp.dot(own_prob, key_value[1, :, cols], preferred_element_type=jnp.float32)  2.45 us
    reduce_sum x3, other arithmetic, per_device(): jnp.sum(own_exp, axis=1, keepdims=True)  2.32 us
  transfers between devices with their start and end apart: 6, of which 3 were waited for; matrix products, arithmetic and copies ran while one was open for 30% of the time, Pallas kernels for 0%

profile of v12, /device:TPU:0, one launch (start us, length us, event | category | flops | bytes accessed | tf_op | source)
XLA Modules:
  0.0 53.2 jit_solution(8738831671376620045)
XLA Ops:
  0.0 2.7 %constant_dynamic-slice_fusion = bf16[2,512,640]{2,1,0:T(8,128)(2,1)} fusion(bf16[2,1024,640]{2,1,0:T(8,128)(2,1)} %param.4, s32[]{:T(128)S(6)} %select_n.103), kind=kLoop, calls=%fused_computation.175 | loop fusion | bytes 2621444 | tf_op jit(solution)/shard_map/dynamic_slice | solution.py:24
  2.7 0.6 %dynamic_slice.18 = s32[1]{0:T(128)} dynamic-slice(s32[8]{0:T(128)S(1)} %and_select_fusion.1, s32[]{:T(128)S(6)} %select_n.105), dynamic_slice_sizes={1} | dynamic-slice | bytes 12 | tf_op jit(solution)/shard_map/jit(dynamic_index_in_dim)/dynamic_slice | solution.py:78
  3.3 4.0 %collective-permute-start = (s32[1]{0:T(128)}, s32[1]{0:T(128)}, u32[]{:S(2)}, u32[]{:S(2)}) collective-permute-start(s32[1]{0:T(128)} %dynamic_slice.18), channel_id=1, source_target_pairs={{0,8},{4,12},{8,0},{12,4},{1,9},{5,13},{9,1},{13,5},{2,10},{6,14},... | collective-permute-start | bytes 20 | tf_op jit(solution)/shard_map/ppermute | solution.py:79
  7.3 1.7 %collective-permute-start.2 = (bf16[2,512,640]{2,1,0:T(8,128)(2,1)}, bf16[2,512,640]{2,1,0:T(8,128)(2,1)}, u32[]{:S(2)}, u32[]{:S(2)}) collective-permute-start(bf16[2,512,640]{2,1,0:T(8,128)(2,1)} %constant_dynamic-slice_fusion), channel_id=1, source_target_pairs={{1,4},{5,8},{9,12},{4,1},{8,5},{12,9},{3,6},{7,10},{11,14},{6,3},{... | collective-permute-start | bytes 3932168 | tf_op jit(solution)/shard_map/ppermute | solution.py:28
  9.0 0.8 %subtract_reduce_fusion = s32[4]{0:T(128)S(1)} fusion(s32[4,8]{1,0:T(4,128)S(1)} %copy-done.2, s32[]{:T(128)S(6)} %select_n.105, s32[]{:T(128)} %bitcast.24, s32[]{:T(128)S(6)} %mul.171), kind=kLoop, calls=%fused_computation.167 | loop fusion | flops 8 | bytes 44 | tf_op jit(solution)/shard_map/sub | solution.py:85
  9.9 0.2 and_reduce_fusion
  10.1 0.1 pad_add_fusion
  12.1 2.5 %collective-permute-start.1 = (bf16[1,1,128,640]{3,2,1,0:T(8,128)(2,1)S(1)}, bf16[1,1,128,640]{3,2,1,0:T(8,128)(2,1)S(1)}, u32[]{:S(2)}, u32[]{:S(2)}) collective-permute-start(bf16[1,1,128,640]{3,2,1,0:T(8,128)(2,1)S(1)} %get-tuple-element.110), channel_id=1, source_target_pairs={{8,0},{12,4},{0,8},{4,12},{9,1},{13,5},{1,9},{5,13},{10,2},{14,6},... | collective-permute-start | bytes 491528 | tf_op jit(solution)/shard_map/ppermute | solution.py:90
  14.6 0.5 multiply_reduce_fusion.1
  15.1 0.5 multiply_reduce_fusion
  15.7 0.5 multiply_reduce_fusion.3
  16.2 0.5 multiply_reduce_fusion.2
  16.7 0.5 multiply_reduce_fusion.4
  17.2 0.1 broadcast_select_fusion
  17.4 0.3 fusion.106
  17.7 0.3 fusion.107
  18.0 0.3 fusion.104
  18.3 0.3 fusion.105
  18.6 0.3 fusion.103
  19.0 0.3 fusion.92
  19.3 0.9 %fusion.93 = (f32[512]{0:T(512)S(1)}, f32[512,1024]{1,0:T(8,128)S(1)}, f32[512]{0:T(512)S(1)}, f32[512,1024]{1,0:T(8,128)S(1)}) fusion(f32[512]{0:T(512)S(1)} %max.103, f32[512,1024]{1,0:T(8,128)S(1)} %get-tuple-element.128, f32[512]{0:T(512)S(1)} %max.101, f32[512,1024]{1,0:T(8,128)S(1)} %get-tuple-element.124), kind=kLoop, calls=%fused_computation.183 | loop fusion | flops 3144704 | bytes 8396800 | tf_op jit(solution)/shard_map/reduce_sum | solution.py:112
  20.2 0.3 fusion.96
  20.5 0.9 %fusion.97 = (f32[512]{0:T(512)S(1)}, f32[512,1024]{1,0:T(8,128)S(1)}, f32[512]{0:T(512)S(1)}, f32[512,1024]{1,0:T(8,128)S(1)}) fusion(f32[512]{0:T(512)S(1)} %max.99, f32[512,1024]{1,0:T(8,128)S(1)} %get-tuple-element.120, f32[512]{0:T(512)S(1)} %max.97, f32[512,1024]{1,0:T(8,128)S(1)} %get-tuple-element.116), kind=kLoop, calls=%fused_computation.187 | loop fusion | flops 3144704 | bytes 8396800 | tf_op jit(solution)/shard_map/reduce_sum | solution.py:112
  21.5 0.5 fusion.101
  22.0 0.2 fusion.100
  22.2 12.0 %collective-permute-done.1 = bf16[1,1,128,640]{3,2,1,0:T(8,128)(2,1)S(1)} collective-permute-done((bf16[1,1,128,640]{3,2,1,0:T(8,128)(2,1)S(1)}, bf16[1,1,128,640]{3,2,1,0:T(8,128)(2,1)S(1)}, u32[]{:S(2)}, u32[]{:S(2)}) %collective-permute-start.1) | collective-permute-done | bytes 163872 | tf_op jit(solution)/shard_map/ppermute | solution.py:90
  34.2 0.4 collective-permute-start.4
  34.6 0.1 compare_and_fusion
  34.7 3.9 %collective-permute-start.3 = (bf16[1,1,128,640]{3,2,1,0:T(8,128)(2,1)S(1)}, bf16[1,1,128,640]{3,2,1,0:T(8,128)(2,1)S(1)}, u32[]{:S(2)}, u32[]{:S(2)}) collective-permute-start(bf16[1,1,128,640]{3,2,1,0:T(8,128)(2,1)S(1)} %get-tuple-element.46), channel_id=1, source_target_pairs={{8,0},{12,4},{0,8},{4,12},{9,1},{13,5},{1,9},{5,13},{10,2},{14,6},... | collective-permute-start | bytes 491528 | tf_op jit(solution)/shard_map/ppermute | solution.py:117
  38.6 0.3 broadcast_in_dim.101
  38.9 0.3 fusion.112
  39.2 0.3 fusion.111
  39.4 0.3 fusion.110
  39.7 0.3 fusion.109
  40.0 0.3 fusion.108
  40.2 0.1 fusion.41
  40.4 0.1 divide_convert_fusion
  40.5 0.1 fusion.40
  40.6 0.1 divide_convert_fusion.1
  40.7 0.1 fusion.39
  40.8 0.1 divide_convert_fusion.2
  41.0 0.1 fusion.38
  41.1 0.1 divide_convert_fusion.3
  41.2 0.3 fusion.31
  41.5 0.5 fusion.21
  42.0 0.3 fusion.30
  42.3 0.5 fusion.19
  42.8 0.3 fusion.29
  43.2 0.5 fusion.17
  43.7 0.3 fusion.28
  44.0 0.5 fusion.15
  44.5 0.1 fusion.37
  44.6 0.2 fusion.87
  44.8 0.3 fusion.27
  45.2 0.5 fusion.13
  45.6 0.1 divide_convert_fusion.4
  45.7 1.2 %collective-permute-done.3 = bf16[1,1,128,640]{3,2,1,0:T(8,128)(2,1)S(1)} collective-permute-done((bf16[1,1,128,640]{3,2,1,0:T(8,128)(2,1)S(1)}, bf16[1,1,128,640]{3,2,1,0:T(8,128)(2,1)S(1)}, u32[]{:S(2)}, u32[]{:S(2)}) %collective-permute-start.3) | collective-permute-done | bytes 163872 | tf_op jit(solution)/shard_map/ppermute | solution.py:117
  46.9 0.1 collective-permute-start.5
  47.2 1.1 %collective-permute-done.5 = bf16[1,1,1,128,640]{4,3,2,1,0:T(8,128)(2,1)S(1)} collective-permute-done((bf16[1,1,1,128,640]{4,3,2,1,0:T(8,128)(2,1)S(1)}, bf16[1,1,1,128,640]{4,3,2,1,0:T(8,128)(2,1)S(1)}, u32[]{:S(2)}, u32[]{:S(2)}) %collective-permute-start.5) | collective-permute-done | bytes 163872 | tf_op jit(solution)/shard_map/ppermute | solution.py:124
  48.4 0.9 %copy.10 = bf16[1,1,2,1,128,640]{4,2,5,3,1,0:T(2,128)(2,1)S(1)} copy(bf16[1,1,2,1,128,640]{5,4,3,2,1,0:T(8,128)(2,1)S(1)} %pad_maximum_fusion.1) | data formatting | bytes 655360 | tf_op jit(solution)/shard_map/stack | solution.py:125
  49.4 0.9 %reshape_reshape.3 = bf16[256,5,128]{0,2,1:T(8,128)(2,1)} reshape(bf16[1,1,2,1,128,640]{4,2,5,3,1,0:T(2,128)(2,1)S(1)} %copy.10) | data formatting | bytes 655360 | tf_op jit(solution)/shard_map/reshape;reshape | solution.py:165
  50.3 1.6 %fusion.6 = bf16[512,5,128]{2,0,1:T(8,128)(2,1)S(1)} fusion(f32[512,5,128]{2,0,1:T(8,128)S(1)} %bitcast_dynamic-update-slice_fusion.5, bf16[256,5,128]{0,2,1:T(8,128)(2,1)} %reshape_reshape.3, bf16[5,512,256]{1,2,0:T(8,128)(2,1)S(1)} %bitcast_dynamic-update-slice_fusion), kind=kOutput, calls=%fused_computation.27 | convolution fusion | flops 168427520 | bytes 3604480 | tf_op jit(solution)/shard_map/hqk,khd->qhd/dot_general | solution.py:162
  51.9 0.2 copy.13
  52.1 1.1 %copy.14 = bf16[512,640]{1,0:T(8,128)(2,1)} copy(bf16[512,640]{0,1:T(8,128)(2,1)S(1)} %bitcast.177) | data formatting | bytes 1310720 | tf_op jit(solution)/shard_map/reshape | solution.py:168
  (45 shorter events, 0.5 us)
Async XLA Ops:
  0.0 12.0 %copy-start = (bf16[2,1024,640]{2,1,0:T(8,128)(2,1)S(1)}, bf16[2,1024,640]{2,1,0:T(8,128)(2,1)}, u32[]{:S(2)}) copy-start(bf16[2,1024,640]{2,1,0:T(8,128)(2,1)} %param.4) | copy-start | bytes 7864324
  0.0 2.7 %copy-start.2 = (s32[4,8]{1,0:T(4,128)S(1)}, s32[4,8]{1,0:T(4,128)}, u32[]{:S(2)}) copy-start(s32[4,8]{1,0:T(4,128)} %param.5) | copy-start | bytes 388
  0.0 14.6 %copy-start.1 = (bf16[512,640]{1,0:T(8,128)(2,1)S(1)}, bf16[512,640]{1,0:T(8,128)(2,1)}, u32[]{:S(2)}) copy-start(bf16[512,640]{1,0:T(8,128)(2,1)} %param.3) | copy-start | bytes 1966084
  3.3 6.9 %collective-permute-start = (s32[1]{0:T(128)}, s32[1]{0:T(128)}, u32[]{:S(2)}, u32[]{:S(2)}) collective-permute-start(s32[1]{0:T(128)} %dynamic_slice.18), channel_id=1, source_target_pairs={{0,8},{4,12},{8,0},{12,4},{1,9},{5,13},{9,1},{13,5},{2,10},{6,14},... | collective-permute-start | bytes 20 | tf_op jit(solution)/shard_map/ppermute | solution.py:79
  7.3 9.9 %collective-permute-start.2 = (bf16[2,512,640]{2,1,0:T(8,128)(2,1)}, bf16[2,512,640]{2,1,0:T(8,128)(2,1)}, u32[]{:S(2)}, u32[]{:S(2)}) collective-permute-start(bf16[2,512,640]{2,1,0:T(8,128)(2,1)} %constant_dynamic-slice_fusion), channel_id=1, source_target_pairs={{1,4},{5,8},{9,12},{4,1},{8,5},{12,9},{3,6},{7,10},{11,14},{6,3},{... | collective-permute-start | bytes 3932168 | tf_op jit(solution)/shard_map/ppermute | solution.py:28
  12.1 22.1 %collective-permute-start.1 = (bf16[1,1,128,640]{3,2,1,0:T(8,128)(2,1)S(1)}, bf16[1,1,128,640]{3,2,1,0:T(8,128)(2,1)S(1)}, u32[]{:S(2)}, u32[]{:S(2)}) collective-permute-start(bf16[1,1,128,640]{3,2,1,0:T(8,128)(2,1)S(1)} %get-tuple-element.110), channel_id=1, source_target_pairs={{8,0},{12,4},{0,8},{4,12},{9,1},{13,5},{1,9},{5,13},{10,2},{14,6},... | collective-permute-start | bytes 491528 | tf_op jit(solution)/shard_map/ppermute | solution.py:90
  34.2 4.3 %collective-permute-start.4 = (bf16[1,1,1,128,640]{4,3,2,1,0:T(8,128)(2,1)S(1)}, bf16[1,1,1,128,640]{4,3,2,1,0:T(8,128)(2,1)S(1)}, u32[]{:S(2)}, u32[]{:S(2)}) collective-permute-start(bf16[1,1,1,128,640]{4,3,2,1,0:T(8,128)(2,1)S(1)} %bitcast.185), channel_id=1, source_target_pairs={{0,1},{1,0},{2,3},{3,2},{4,5},{5,4},{6,7},{7,6},{8,9},{9,8},{10,11... | collective-permute-start | bytes 491528 | tf_op jit(solution)/shard_map/ppermute | solution.py:124
  34.7 12.2 %collective-permute-start.3 = (bf16[1,1,128,640]{3,2,1,0:T(8,128)(2,1)S(1)}, bf16[1,1,128,640]{3,2,1,0:T(8,128)(2,1)S(1)}, u32[]{:S(2)}, u32[]{:S(2)}) collective-permute-start(bf16[1,1,128,640]{3,2,1,0:T(8,128)(2,1)S(1)} %get-tuple-element.46), channel_id=1, source_target_pairs={{8,0},{12,4},{0,8},{4,12},{9,1},{13,5},{1,9},{5,13},{10,2},{14,6},... | collective-permute-start | bytes 491528 | tf_op jit(solution)/shard_map/ppermute | solution.py:117
  46.9 1.5 %collective-permute-start.5 = (bf16[1,1,1,128,640]{4,3,2,1,0:T(8,128)(2,1)S(1)}, bf16[1,1,1,128,640]{4,3,2,1,0:T(8,128)(2,1)S(1)}, u32[]{:S(2)}, u32[]{:S(2)}) collective-permute-start(bf16[1,1,1,128,640]{4,3,2,1,0:T(8,128)(2,1)S(1)} %bitcast.183), channel_id=1, source_target_pairs={{0,1},{1,0},{2,3},{3,2},{4,5},{5,4},{6,7},{7,6},{8,9},{9,8},{10,11... | collective-permute-start | bytes 491528 | tf_op jit(solution)/shard_map/ppermute | solution.py:124

commit v13 on v11

--- a/solution.py
+++ b/solution.py
@@ -156,11 +156,20 @@
         mixed = mixed + jnp.dot(halo_prob, halo[1, :, cols], preferred_element_type=jnp.float32)
         outputs.append((mixed, far_prob))
     values, outputs = lax.optimization_barrier((values, outputs))
-    far_values = gather_reps(values)
+    mine = jnp.stack(values, 1)
+    value_parts = [mine]
+    for k in range(1, rep_count):
+        shift = [(r, (r + k) % rep_count) for r in range(rep_count)]
+        value_parts.append(lax.ppermute(mine, "rep", shift))
+    part_rows = slot_count * far_share * MASK_BLOCK_SIZE
+    value_parts = [part.reshape(part_rows, columns) for part in value_parts]
     finished = []
     for head, (mixed, far_prob) in enumerate(outputs):
         cols = slice(head * HEAD_WIDTH, (head + 1) * HEAD_WIDTH)
-        mixed = mixed + jnp.dot(far_prob, far_values[:, cols], preferred_element_type=jnp.float32)
+        far_prob = far_prob.reshape(query_count, slot_count, rep_count, far_share * MASK_BLOCK_SIZE)
+        for k, part in enumerate(value_parts):
+            part_prob = far_prob[:, :, k].reshape(query_count, part_rows)
+            mixed = mixed + jnp.dot(part_prob, part[:, cols], preferred_element_type=jnp.float32)
         finished.append(mixed.astype(jnp.bfloat16))
     return jnp.concatenate(finished, axis=1)
 

time: 51.6 us -> 52 us (level)
  matrix products: 10.8 us -> 12.3 us
  other arithmetic: 6.55 us -> 5.63 us
    dot_general x5 -> x10, matrix products: 1.32 us -> 2.8 us  [per_device(): jnp.dot(part_prob, part[:, cols], preferred_element_type=jnp.float32)]
    ppermute x2 -> x1, waiting for transfers between devices: 1.39 us -> 0.01 us  [gather_reps(): parts.append(lax.ppermute(mine, 'rep', shift))]
    ppermute x0 -> x1, waiting for transfers between devices: none -> 1.17 us  [per_device(): value_parts.append(lax.ppermute(mine, 'rep', shift))]
    concatenate x1 -> x0, other arithmetic: 0.68 us -> none  [per_device(): return jnp.concatenate(finished, axis=1)]
where the time goes in v13:
time: 52 us; the launch traced here: 51.8 us
  waiting for transfers between devices  14.5 us (28%)
  starting transfers between devices  12.6 us (24%)
  matrix products  12.3 us (24%)
  other arithmetic  5.63 us (11%)
  local copies, waits for them, and re-layouts  4.5 us (9%)
  between operations  2.26 us (4%)
    ppermute x1, waiting for transfers between devices, per_device(): lax.ppermute(chosen[0][None], 'seq', back)  12 us
    ppermute x1, starting transfers between devices, per_device(): wanted = lax.ppermute(phase[None], 'seq', pairs)[0]  4.05 us
    ppermute x1, starting transfers between devices, per_device(): lax.ppermute(chosen, 'seq', back)  3.89 us
    dot_general x10, matrix products, per_device(): jnp.dot(part_prob, part[:, cols], preferred_element_type=jnp.float32)  2.8 us
    dynamic_slice x1, local copies, waits for them, and re-layouts, halo_frame(): payload = lax.dynamic_slice_in_dim(key_value, start, frame_rows, 1)  2.65 us
    dot_general x5, matrix products, per_device(): jnp.dot(query_head, key_value[0, :, cols].T, preferred_element_type=jnp.f...  2.6 us
    ppermute x1, starting transfers between devices, per_device(): lax.ppermute(chosen[0][None], 'seq', back)  2.48 us
    dot_general x5, matrix products, per_device(): jnp.dot(own_prob, key_value[1, :, cols], preferred_element_type=jnp.float32)  2.44 us
  transfers between devices with their start and end apart: 6, of which 3 were waited for; matrix products, arithmetic and copies ran while one was open for 30% of the time, Pallas kernels for 0%

profile of v13, /device:TPU:0, one launch (start us, length us, event | category | flops | bytes accessed | tf_op | source)
XLA Modules:
  0.0 51.8 jit_solution(17481112787392034322)
XLA Ops:
  0.0 2.7 %constant_dynamic-slice_fusion = bf16[2,512,640]{2,1,0:T(8,128)(2,1)} fusion(bf16[2,1024,640]{2,1,0:T(8,128)(2,1)} %param.4, s32[]{:T(128)S(6)} %select_n.103), kind=kLoop, calls=%fused_computation.201 | loop fusion | bytes 2621444 | tf_op jit(solution)/shard_map/dynamic_slice | solution.py:24
  2.7 0.6 %dynamic_slice.18 = s32[1]{0:T(128)} dynamic-slice(s32[8]{0:T(128)S(1)} %and_select_fusion.1, s32[]{:T(128)S(6)} %select_n.105), dynamic_slice_sizes={1} | dynamic-slice | bytes 12 | tf_op jit(solution)/shard_map/jit(dynamic_index_in_dim)/dynamic_slice | solution.py:78
  3.3 4.0 %collective-permute-start = (s32[1]{0:T(128)}, s32[1]{0:T(128)}, u32[]{:S(2)}, u32[]{:S(2)}) collective-permute-start(s32[1]{0:T(128)} %dynamic_slice.18), channel_id=1, source_target_pairs={{0,8},{4,12},{8,0},{12,4},{1,9},{5,13},{9,1},{13,5},{2,10},{6,14},... | collective-permute-start | bytes 20 | tf_op jit(solution)/shard_map/ppermute | solution.py:79
  7.3 1.7 %collective-permute-start.2 = (bf16[2,512,640]{2,1,0:T(8,128)(2,1)}, bf16[2,512,640]{2,1,0:T(8,128)(2,1)}, u32[]{:S(2)}, u32[]{:S(2)}) collective-permute-start(bf16[2,512,640]{2,1,0:T(8,128)(2,1)} %constant_dynamic-slice_fusion), channel_id=1, source_target_pairs={{1,4},{5,8},{9,12},{4,1},{8,5},{12,9},{3,6},{7,10},{11,14},{6,3},{... | collective-permute-start | bytes 3932168 | tf_op jit(solution)/shard_map/ppermute | solution.py:28
  9.0 0.8 %subtract_reduce_fusion = s32[4]{0:T(128)S(1)} fusion(s32[4,8]{1,0:T(4,128)S(1)} %copy-done.3, s32[]{:T(128)S(6)} %select_n.105, s32[]{:T(128)} %bitcast.24, s32[]{:T(128)S(6)} %mul.171), kind=kLoop, calls=%fused_computation.193 | loop fusion | flops 8 | bytes 44 | tf_op jit(solution)/shard_map/sub | solution.py:85
  9.9 0.2 and_reduce_fusion
  12.1 2.5 %collective-permute-start.1 = (bf16[1,1,128,640]{3,2,0,1:T(8,128)(2,1)S(1)}, bf16[1,1,128,640]{3,2,0,1:T(8,128)(2,1)S(1)}, u32[]{:S(2)}, u32[]{:S(2)}) collective-permute-start(bf16[1,1,128,640]{3,2,0,1:T(8,128)(2,1)S(1)} %get-tuple-element.110), channel_id=1, source_target_pairs={{8,0},{12,4},{0,8},{4,12},{9,1},{13,5},{1,9},{5,13},{10,2},{14,6},... | collective-permute-start | bytes 491528 | tf_op jit(solution)/shard_map/ppermute | solution.py:90
  14.6 0.5 multiply_reduce_fusion.1
  15.1 0.5 %multiply_reduce_fusion = (f32[512]{0:T(512)S(1)}, f32[512,1024]{1,0:T(8,128)S(1)}) fusion(bf16[2,1024,640]{2,1,0:T(8,128)(2,1)S(1)} %copy-done, bf16[512,640]{1,0:T(8,128)(2,1)S(1)} %copy-done.1), kind=kOutput, calls=%fused_computation.10 | convolution fusion | flops 135265792 | bytes 2492416 | tf_op jit(solution)/shard_map/dot_general | solution.py:99
  15.7 0.5 %multiply_reduce_fusion.3 = (f32[512]{0:T(512)S(1)}, f32[512,1024]{1,0:T(8,128)S(1)}) fusion(bf16[2,1024,640]{2,1,0:T(8,128)(2,1)S(1)} %copy-done, bf16[512,640]{1,0:T(8,128)(2,1)S(1)} %copy-done.1), kind=kOutput, calls=%fused_computation.13 | convolution fusion | flops 135265792 | bytes 2492416 | tf_op jit(solution)/shard_map/dot_general | solution.py:99
  16.2 0.5 %multiply_reduce_fusion.2 = (f32[512]{0:T(512)S(1)}, f32[512,1024]{1,0:T(8,128)S(1)}) fusion(bf16[2,1024,640]{2,1,0:T(8,128)(2,1)S(1)} %copy-done, bf16[512,640]{1,0:T(8,128)(2,1)S(1)} %copy-done.1), kind=kOutput, calls=%fused_computation.12 | convolution fusion | flops 135265792 | bytes 2492416 | tf_op jit(solution)/shard_map/dot_general | solution.py:99
  16.7 0.5 %multiply_reduce_fusion.4 = (f32[512]{0:T(512)S(1)}, f32[512,1024]{1,0:T(8,128)S(1)}) fusion(bf16[2,1024,640]{2,1,0:T(8,128)(2,1)S(1)} %copy-done, bf16[512,640]{1,0:T(8,128)(2,1)S(1)} %copy-done.1), kind=kOutput, calls=%fused_computation.14 | convolution fusion | flops 135265792 | bytes 2492416 | tf_op jit(solution)/shard_map/dot_general | solution.py:99
  17.2 0.1 broadcast_select_fusion
  17.4 0.3 fusion.129
  17.7 0.3 fusion.130
  18.0 0.3 fusion.127
  18.3 0.3 fusion.128
  18.6 0.3 fusion.126
  19.0 0.3 fusion.115
  19.3 0.9 %fusion.116 = (f32[512]{0:T(512)S(1)}, f32[512,1024]{1,0:T(8,128)S(1)}, f32[512]{0:T(512)S(1)}, f32[512,1024]{1,0:T(8,128)S(1)}) fusion(f32[512]{0:T(512)S(1)} %max.103, f32[512,1024]{1,0:T(8,128)S(1)} %get-tuple-element.128, f32[512]{0:T(512)S(1)} %max.101, f32[512,1024]{1,0:T(8,128)S(1)} %get-tuple-element.124), kind=kLoop, calls=%fused_computation.209 | loop fusion | flops 3144704 | bytes 8396800 | tf_op jit(solution)/shard_map/reduce_sum | solution.py:112
  20.2 0.3 fusion.119
  20.5 0.9 %fusion.120 = (f32[512]{0:T(512)S(1)}, f32[512,1024]{1,0:T(8,128)S(1)}, f32[512]{0:T(512)S(1)}, f32[512,1024]{1,0:T(8,128)S(1)}) fusion(f32[512]{0:T(512)S(1)} %max.99, f32[512,1024]{1,0:T(8,128)S(1)} %get-tuple-element.120, f32[512]{0:T(512)S(1)} %max.97, f32[512,1024]{1,0:T(8,128)S(1)} %get-tuple-element.116), kind=kLoop, calls=%fused_computation.213 | loop fusion | flops 3144704 | bytes 8396800 | tf_op jit(solution)/shard_map/reduce_sum | solution.py:112
  21.5 0.5 %fusion.124 = (f32[512]{0:T(512)S(1)}, f32[512,1024]{1,0:T(8,128)S(1)}) fusion(f32[512]{0:T(512)S(1)} %max.95, f32[512,1024]{1,0:T(8,128)S(1)} %get-tuple-element.112), kind=kLoop, calls=%fused_computation.217 | loop fusion | flops 1572352 | bytes 4198400 | tf_op jit(solution)/shard_map/reduce_sum | solution.py:112
  22.0 0.2 fusion.123
  22.2 12.0 %collective-permute-done.1 = bf16[1,1,128,640]{3,2,0,1:T(8,128)(2,1)S(1)} collective-permute-done((bf16[1,1,128,640]{3,2,0,1:T(8,128)(2,1)S(1)}, bf16[1,1,128,640]{3,2,0,1:T(8,128)(2,1)S(1)}, u32[]{:S(2)}, u32[]{:S(2)}) %collective-permute-start.1) | collective-permute-done | bytes 163872 | tf_op jit(solution)/shard_map/ppermute | solution.py:90
  34.2 0.4 collective-permute-start.4
  34.6 3.9 %collective-permute-start.3 = (bf16[1,1,128,640]{3,2,0,1:T(8,128)(2,1)S(1)}, bf16[1,1,128,640]{3,2,0,1:T(8,128)(2,1)S(1)}, u32[]{:S(2)}, u32[]{:S(2)}) collective-permute-start(bf16[1,1,128,640]{3,2,0,1:T(8,128)(2,1)S(1)} %get-tuple-element.46), channel_id=1, source_target_pairs={{8,0},{12,4},{0,8},{4,12},{9,1},{13,5},{1,9},{5,13},{10,2},{14,6},... | collective-permute-start | bytes 491528 | tf_op jit(solution)/shard_map/ppermute | solution.py:117
  38.6 0.3 broadcast_in_dim.101
  38.9 0.3 fusion.135
  39.2 0.3 fusion.134
  39.4 0.3 fusion.133
  39.7 0.3 fusion.132
  40.0 0.3 fusion.131
  40.2 0.1 fusion.39
  40.4 0.1 divide_convert_fusion
  40.5 0.1 fusion.38
  40.6 0.1 divide_convert_fusion.1
  40.7 0.1 fusion.37
  41.0 0.1 fusion.36
  41.2 0.3 fusion.29
  41.5 0.5 fusion.19
  42.0 0.3 fusion.28
  42.3 0.5 fusion.17
  42.8 0.3 fusion.27
  43.2 0.5 fusion.15
  43.7 0.3 fusion.26
  44.0 0.5 fusion.13
  44.5 0.1 fusion.35
  44.6 0.3 fusion.25
  45.0 0.5 fusion.11
  45.5 0.1 divide_convert_fusion.4
  45.6 1.3 %collective-permute-done.3 = bf16[1,1,128,640]{3,2,0,1:T(8,128)(2,1)S(1)} collective-permute-done((bf16[1,1,128,640]{3,2,0,1:T(8,128)(2,1)S(1)}, bf16[1,1,128,640]{3,2,0,1:T(8,128)(2,1)S(1)}, u32[]{:S(2)}, u32[]{:S(2)}) %collective-permute-start.3) | collective-permute-done | bytes 163872 | tf_op jit(solution)/shard_map/ppermute | solution.py:117
  46.9 0.2 fusion.71
  47.1 0.2 fusion.73
  47.3 0.2 fusion.75
  47.5 0.2 fusion.77
  47.8 0.2 fusion.79
  48.0 1.2 %collective-permute-done.5 = bf16[1,1,1,128,640]{4,3,2,1,0:T(8,128)(2,1)S(1)} collective-permute-done((bf16[1,1,1,128,640]{4,3,2,1,0:T(8,128)(2,1)S(1)}, bf16[1,1,1,128,640]{4,3,2,1,0:T(8,128)(2,1)S(1)}, u32[]{:S(2)}, u32[]{:S(2)}) %collective-permute-start.5) | collective-permute-done | bytes 163872 | tf_op jit(solution)/shard_map/ppermute | solution.py:163
  49.2 0.2 fusion.65
  49.4 0.2 fusion.66
  49.7 0.2 fusion.67
  49.9 0.2 fusion.68
  50.2 0.8 %copy-done.2 = bf16[512,640]{1,0:T(8,128)(2,1)} copy-done((bf16[512,640]{1,0:T(8,128)(2,1)}, bf16[512,640]{1,0:T(8,128)(2,1)S(1)}, u32[]{:S(2)}) %copy-start.2) | copy-done | bytes 655384
  51.0 0.9 %fusion.69 = bf16[512,640]{1,0:T(8,128)(2,1)} fusion(bf16[512,640]{1,0:T(8,128)(2,1)} %copy-done.2, f32[512,128]{1,0:T(8,128)S(1)} %fusion.19, f32[512,128]{1,0:T(8,128)S(1)} %fusion.71, bf16[512,1,2,128]{0,3,2,1:T(8,128)(2,1)S(1)} %bitcast.188, bf16[128,640]{1,0:T(8,128)(2,1)S(1)} %bitcast.208), kind=kOutput, calls=%fused_computation.122 | convolution fusion | flops 16973824 | bytes 819200 | tf_op jit(solution)/shard_map/dot_general | solution.py:172
  (41 shorter events, 0.7 us)
Async XLA Ops:
  0.0 12.0 %copy-start = (bf16[2,1024,640]{2,1,0:T(8,128)(2,1)S(1)}, bf16[2,1024,640]{2,1,0:T(8,128)(2,1)}, u32[]{:S(2)}) copy-start(bf16[2,1024,640]{2,1,0:T(8,128)(2,1)} %param.4) | copy-start | bytes 7864324
  0.0 2.7 %copy-start.3 = (s32[4,8]{1,0:T(4,128)S(1)}, s32[4,8]{1,0:T(4,128)}, u32[]{:S(2)}) copy-start(s32[4,8]{1,0:T(4,128)} %param.5) | copy-start | bytes 388
  0.0 14.6 %copy-start.1 = (bf16[512,640]{1,0:T(8,128)(2,1)S(1)}, bf16[512,640]{1,0:T(8,128)(2,1)}, u32[]{:S(2)}) copy-start(bf16[512,640]{1,0:T(8,128)(2,1)} %param.3) | copy-start | bytes 1966084
  3.3 6.9 %collective-permute-start = (s32[1]{0:T(128)}, s32[1]{0:T(128)}, u32[]{:S(2)}, u32[]{:S(2)}) collective-permute-start(s32[1]{0:T(128)} %dynamic_slice.18), channel_id=1, source_target_pairs={{0,8},{4,12},{8,0},{12,4},{1,9},{5,13},{9,1},{13,5},{2,10},{6,14},... | collective-permute-start | bytes 20 | tf_op jit(solution)/shard_map/ppermute | solution.py:79
  7.3 9.9 %collective-permute-start.2 = (bf16[2,512,640]{2,1,0:T(8,128)(2,1)}, bf16[2,512,640]{2,1,0:T(8,128)(2,1)}, u32[]{:S(2)}, u32[]{:S(2)}) collective-permute-start(bf16[2,512,640]{2,1,0:T(8,128)(2,1)} %constant_dynamic-slice_fusion), channel_id=1, source_target_pairs={{1,4},{5,8},{9,12},{4,1},{8,5},{12,9},{3,6},{7,10},{11,14},{6,3},{... | collective-permute-start | bytes 3932168 | tf_op jit(solution)/shard_map/ppermute | solution.py:28
  12.1 22.1 %collective-permute-start.1 = (bf16[1,1,128,640]{3,2,0,1:T(8,128)(2,1)S(1)}, bf16[1,1,128,640]{3,2,0,1:T(8,128)(2,1)S(1)}, u32[]{:S(2)}, u32[]{:S(2)}) collective-permute-start(bf16[1,1,128,640]{3,2,0,1:T(8,128)(2,1)S(1)} %get-tuple-element.110), channel_id=1, source_target_pairs={{8,0},{12,4},{0,8},{4,12},{9,1},{13,5},{1,9},{5,13},{10,2},{14,6},... | collective-permute-start | bytes 491528 | tf_op jit(solution)/shard_map/ppermute | solution.py:90
  34.2 4.3 %collective-permute-start.4 = (bf16[1,1,1,128,640]{4,3,2,1,0:T(8,128)(2,1)S(1)}, bf16[1,1,1,128,640]{4,3,2,1,0:T(8,128)(2,1)S(1)}, u32[]{:S(2)}, u32[]{:S(2)}) collective-permute-start(bf16[1,1,1,128,640]{4,3,2,1,0:T(8,128)(2,1)S(1)} %bitcast.202), channel_id=1, source_target_pairs={{0,1},{1,0},{2,3},{3,2},{4,5},{5,4},{6,7},{7,6},{8,9},{9,8},{10,11... | collective-permute-start | bytes 491528 | tf_op jit(solution)/shard_map/ppermute | solution.py:124
  34.6 12.3 %collective-permute-start.3 = (bf16[1,1,128,640]{3,2,0,1:T(8,128)(2,1)S(1)}, bf16[1,1,128,640]{3,2,0,1:T(8,128)(2,1)S(1)}, u32[]{:S(2)}, u32[]{:S(2)}) collective-permute-start(bf16[1,1,128,640]{3,2,0,1:T(8,128)(2,1)S(1)} %get-tuple-element.46), channel_id=1, source_target_pairs={{8,0},{12,4},{0,8},{4,12},{9,1},{13,5},{1,9},{5,13},{10,2},{14,6},... | collective-permute-start | bytes 491528 | tf_op jit(solution)/shard_map/ppermute | solution.py:117
  47.7 1.5 %collective-permute-start.5 = (bf16[1,1,1,128,640]{4,3,2,1,0:T(8,128)(2,1)S(1)}, bf16[1,1,1,128,640]{4,3,2,1,0:T(8,128)(2,1)S(1)}, u32[]{:S(2)}, u32[]{:S(2)}) collective-permute-start(bf16[1,1,1,128,640]{4,3,2,1,0:T(8,128)(2,1)S(1)} %bitcast.214), channel_id=1, source_target_pairs={{0,1},{1,0},{2,3},{3,2},{4,5},{5,4},{6,7},{7,6},{8,9},{9,8},{10,11... | collective-permute-start | bytes 491528 | tf_op jit(solution)/shard_map/ppermute | solution.py:163
  50.1 0.8 %copy-start.2 = (bf16[512,640]{1,0:T(8,128)(2,1)}, bf16[512,640]{1,0:T(8,128)(2,1)S(1)}, u32[]{:S(2)}) copy-start(bf16[512,640]{1,0:T(8,128)(2,1)S(1)} %fusion.68) | copy-start | bytes 1966084

commit v14 on v11

--- a/solution.py
+++ b/solution.py
@@ -157,12 +157,12 @@
         outputs.append((mixed, far_prob))
     values, outputs = lax.optimization_barrier((values, outputs))
     far_values = gather_reps(values)
-    finished = []
-    for head, (mixed, far_prob) in enumerate(outputs):
+    near_part = jnp.concatenate([mixed for mixed, _ in outputs], axis=1)
+    far_part = []
+    for head, (_, far_prob) in enumerate(outputs):
         cols = slice(head * HEAD_WIDTH, (head + 1) * HEAD_WIDTH)
-        mixed = mixed + jnp.dot(far_prob, far_values[:, cols], preferred_element_type=jnp.float32)
-        finished.append(mixed.astype(jnp.bfloat16))
-    return jnp.concatenate(finished, axis=1)
+        far_part.append(jnp.dot(far_prob, far_values[:, cols], preferred_element_type=jnp.float32))
+    return (near_part + jnp.concatenate(far_part, axis=1)).astype(jnp.bfloat16)
 
 
 def solution(mesh):

time: 51.6 us -> 50.8 us (0.984)
  local copies, waits for them, and re-layouts: 4.5 us -> 3.77 us
    convert_element_type x0 -> x1, other arithmetic: none -> 0.96 us  [per_device(): return (near_part + jnp.concatenate(far_part, axis=1)).astype(jnp.bfloat16)]
    unnamed x8 -> x10, local copies, waits for them, and re-layouts: 0.84 us -> 0.09 us
    concatenate x1 -> x0, other arithmetic: 0.68 us -> none  [per_device(): return jnp.concatenate(finished, axis=1)]
  transfers between devices with their start and end apart: 6 -> 6, of which waited for: 3 -> 3; matrix products, arithmetic and copies ran while one was open for 30% -> 31% of each run, Pallas kernels for 0% -> 0%
where the time goes in v14:
time: 50.8 us; the launch traced here: 50.7 us
  waiting for transfers between devices  14.6 us (29%)
  starting transfers between devices  12.5 us (25%)
  matrix products  10.8 us (21%)
  other arithmetic  6.64 us (13%)
  local copies, waits for them, and re-layouts  3.77 us (7%)
  between operations  2.26 us (4%)
    ppermute x1, waiting for transfers between devices, per_device(): lax.ppermute(chosen[0][None], 'seq', back)  12 us
    ppermute x1, starting transfers between devices, per_device(): wanted = lax.ppermute(phase[None], 'seq', pairs)[0]  4.05 us
    ppermute x1, starting transfers between devices, per_device(): lax.ppermute(chosen, 'seq', back)  3.89 us
    dynamic_slice x1, local copies, waits for them, and re-layouts, halo_frame(): payload = lax.dynamic_slice_in_dim(key_value, start, frame_rows, 1)  2.65 us
    dot_general x5, matrix products, per_device(): jnp.dot(query_head, key_value[0, :, cols].T, preferred_element_type=jnp.f...  2.6 us
    ppermute x1, starting transfers between devices, per_device(): lax.ppermute(chosen[0][None], 'seq', back)  2.48 us
    dot_general x5, matrix products, per_device(): jnp.dot(own_prob, key_value[1, :, cols], preferred_element_type=jnp.float32)  2.44 us
    reduce_sum x3, other arithmetic, per_device(): jnp.sum(own_exp, axis=1, keepdims=True)  2.32 us
  transfers between devices with their start and end apart: 6, of which 3 were waited for; matrix products, arithmetic and copies ran while one was open for 31% of the time, Pallas kernels for 0%

profile of v14, /device:TPU:0, one launch (start us, length us, event | category | flops | bytes accessed | tf_op | source)
XLA Modules:
  0.0 50.7 jit_solution(3362663214665477465)
XLA Ops:
  0.0 2.7 %constant_dynamic-slice_fusion = bf16[2,512,640]{2,1,0:T(8,128)(2,1)} fusion(bf16[2,1024,640]{2,1,0:T(8,128)(2,1)} %param.4, s32[]{:T(128)S(6)} %select_n.103), kind=kLoop, calls=%fused_computation.178 | loop fusion | bytes 2621444 | tf_op jit(solution)/shard_map/dynamic_slice | solution.py:24
  2.7 0.6 %dynamic_slice.18 = s32[1]{0:T(128)} dynamic-slice(s32[8]{0:T(128)S(1)} %and_select_fusion.1, s32[]{:T(128)S(6)} %select_n.105), dynamic_slice_sizes={1} | dynamic-slice | bytes 12 | tf_op jit(solution)/shard_map/jit(dynamic_index_in_dim)/dynamic_slice | solution.py:78
  3.3 4.0 %collective-permute-start = (s32[1]{0:T(128)}, s32[1]{0:T(128)}, u32[]{:S(2)}, u32[]{:S(2)}) collective-permute-start(s32[1]{0:T(128)} %dynamic_slice.18), channel_id=1, source_target_pairs={{0,8},{4,12},{8,0},{12,4},{1,9},{5,13},{9,1},{13,5},{2,10},{6,14},... | collective-permute-start | bytes 20 | tf_op jit(solution)/shard_map/ppermute | solution.py:79
  7.3 1.7 %collective-permute-start.2 = (bf16[2,512,640]{2,1,0:T(8,128)(2,1)}, bf16[2,512,640]{2,1,0:T(8,128)(2,1)}, u32[]{:S(2)}, u32[]{:S(2)}) collective-permute-start(bf16[2,512,640]{2,1,0:T(8,128)(2,1)} %constant_dynamic-slice_fusion), channel_id=1, source_target_pairs={{1,4},{5,8},{9,12},{4,1},{8,5},{12,9},{3,6},{7,10},{11,14},{6,3},{... | collective-permute-start | bytes 3932168 | tf_op jit(solution)/shard_map/ppermute | solution.py:28
  9.0 0.8 %subtract_reduce_fusion = s32[4]{0:T(128)S(1)} fusion(s32[4,8]{1,0:T(4,128)S(1)} %copy-done.2, s32[]{:T(128)S(6)} %select_n.105, s32[]{:T(128)} %bitcast.24, s32[]{:T(128)S(6)} %mul.171), kind=kLoop, calls=%fused_computation.170 | loop fusion | flops 8 | bytes 44 | tf_op jit(solution)/shard_map/sub | solution.py:85
  9.9 0.2 and_reduce_fusion
  10.1 0.1 pad_add_fusion
  12.1 2.5 %collective-permute-start.1 = (bf16[1,1,128,640]{3,2,0,1:T(8,128)(2,1)S(1)}, bf16[1,1,128,640]{3,2,0,1:T(8,128)(2,1)S(1)}, u32[]{:S(2)}, u32[]{:S(2)}) collective-permute-start(bf16[1,1,128,640]{3,2,0,1:T(8,128)(2,1)S(1)} %get-tuple-element.110), channel_id=1, source_target_pairs={{8,0},{12,4},{0,8},{4,12},{9,1},{13,5},{1,9},{5,13},{10,2},{14,6},... | collective-permute-start | bytes 491528 | tf_op jit(solution)/shard_map/ppermute | solution.py:90
  14.6 0.5 %multiply_reduce_fusion.1 = (f32[512]{0:T(512)S(1)}, f32[512,1024]{1,0:T(8,128)S(1)}) fusion(bf16[2,1024,640]{2,1,0:T(8,128)(2,1)S(1)} %copy-done, bf16[512,640]{1,0:T(8,128)(2,1)S(1)} %copy-done.1), kind=kOutput, calls=%fused_computation.11 | convolution fusion | flops 135265792 | bytes 2492416 | tf_op jit(solution)/shard_map/dot_general | solution.py:99
  15.1 0.5 %multiply_reduce_fusion = (f32[512]{0:T(512)S(1)}, f32[512,1024]{1,0:T(8,128)S(1)}) fusion(bf16[2,1024,640]{2,1,0:T(8,128)(2,1)S(1)} %copy-done, bf16[512,640]{1,0:T(8,128)(2,1)S(1)} %copy-done.1), kind=kOutput, calls=%fused_computation.10 | convolution fusion | flops 135265792 | bytes 2492416 | tf_op jit(solution)/shard_map/dot_general | solution.py:99
  15.7 0.5 %multiply_reduce_fusion.3 = (f32[512]{0:T(512)S(1)}, f32[512,1024]{1,0:T(8,128)S(1)}) fusion(bf16[2,1024,640]{2,1,0:T(8,128)(2,1)S(1)} %copy-done, bf16[512,640]{1,0:T(8,128)(2,1)S(1)} %copy-done.1), kind=kOutput, calls=%fused_computation.13 | convolution fusion | flops 135265792 | bytes 2492416 | tf_op jit(solution)/shard_map/dot_general | solution.py:99
  16.2 0.5 %multiply_reduce_fusion.2 = (f32[512]{0:T(512)S(1)}, f32[512,1024]{1,0:T(8,128)S(1)}) fusion(bf16[2,1024,640]{2,1,0:T(8,128)(2,1)S(1)} %copy-done, bf16[512,640]{1,0:T(8,128)(2,1)S(1)} %copy-done.1), kind=kOutput, calls=%fused_computation.12 | convolution fusion | flops 135265792 | bytes 2492416 | tf_op jit(solution)/shard_map/dot_general | solution.py:99
  16.7 0.5 %multiply_reduce_fusion.4 = (f32[512]{0:T(512)S(1)}, f32[512,1024]{1,0:T(8,128)S(1)}) fusion(bf16[2,1024,640]{2,1,0:T(8,128)(2,1)S(1)} %copy-done, bf16[512,640]{1,0:T(8,128)(2,1)S(1)} %copy-done.1), kind=kOutput, calls=%fused_computation.14 | convolution fusion | flops 135265792 | bytes 2492416 | tf_op jit(solution)/shard_map/dot_general | solution.py:99
  17.2 0.0 collective-permute-done.2
  17.2 0.1 broadcast_select_fusion
  17.4 0.3 fusion.109
  17.7 0.3 fusion.110
  18.0 0.3 fusion.107
  18.3 0.3 fusion.108
  18.6 0.3 fusion.106
  19.0 0.3 fusion.95
  19.3 0.9 %fusion.96 = (f32[512]{0:T(512)S(1)}, f32[512,1024]{1,0:T(8,128)S(1)}, f32[512]{0:T(512)S(1)}, f32[512,1024]{1,0:T(8,128)S(1)}) fusion(f32[512]{0:T(512)S(1)} %max.103, f32[512,1024]{1,0:T(8,128)S(1)} %get-tuple-element.128, f32[512]{0:T(512)S(1)} %max.101, f32[512,1024]{1,0:T(8,128)S(1)} %get-tuple-element.124), kind=kLoop, calls=%fused_computation.186 | loop fusion | flops 3144704 | bytes 8396800 | tf_op jit(solution)/shard_map/reduce_sum | solution.py:112
  20.2 0.3 fusion.99
  20.5 0.9 %fusion.100 = (f32[512]{0:T(512)S(1)}, f32[512,1024]{1,0:T(8,128)S(1)}, f32[512]{0:T(512)S(1)}, f32[512,1024]{1,0:T(8,128)S(1)}) fusion(f32[512]{0:T(512)S(1)} %max.99, f32[512,1024]{1,0:T(8,128)S(1)} %get-tuple-element.120, f32[512]{0:T(512)S(1)} %max.97, f32[512,1024]{1,0:T(8,128)S(1)} %get-tuple-element.116), kind=kLoop, calls=%fused_computation.190 | loop fusion | flops 3144704 | bytes 8396800 | tf_op jit(solution)/shard_map/reduce_sum | solution.py:112
  21.5 0.5 %fusion.104 = (f32[512]{0:T(512)S(1)}, f32[512,1024]{1,0:T(8,128)S(1)}) fusion(f32[512]{0:T(512)S(1)} %max.95, f32[512,1024]{1,0:T(8,128)S(1)} %get-tuple-element.112), kind=kLoop, calls=%fused_computation.194 | loop fusion | flops 1572352 | bytes 4198400 | tf_op jit(solution)/shard_map/reduce_sum | solution.py:112
  22.0 0.2 fusion.103
  22.2 12.0 %collective-permute-done.1 = bf16[1,1,128,640]{3,2,0,1:T(8,128)(2,1)S(1)} collective-permute-done((bf16[1,1,128,640]{3,2,0,1:T(8,128)(2,1)S(1)}, bf16[1,1,128,640]{3,2,0,1:T(8,128)(2,1)S(1)}, u32[]{:S(2)}, u32[]{:S(2)}) %collective-permute-start.1) | collective-permute-done | bytes 163872 | tf_op jit(solution)/shard_map/ppermute | solution.py:90
  34.2 0.4 collective-permute-start.4
  34.6 0.1 compare_and_fusion
  34.6 3.9 %collective-permute-start.3 = (bf16[1,1,128,640]{3,2,0,1:T(8,128)(2,1)S(1)}, bf16[1,1,128,640]{3,2,0,1:T(8,128)(2,1)S(1)}, u32[]{:S(2)}, u32[]{:S(2)}) collective-permute-start(bf16[1,1,128,640]{3,2,0,1:T(8,128)(2,1)S(1)} %get-tuple-element.46), channel_id=1, source_target_pairs={{8,0},{12,4},{0,8},{4,12},{9,1},{13,5},{1,9},{5,13},{10,2},{14,6},... | collective-permute-start | bytes 491528 | tf_op jit(solution)/shard_map/ppermute | solution.py:117
  38.6 0.3 broadcast_in_dim.101
  38.9 0.3 fusion.115
  39.2 0.3 fusion.114
  39.4 0.3 fusion.113
  39.7 0.3 fusion.112
  40.0 0.3 fusion.111
  40.2 0.1 fusion.39
  40.4 0.1 divide_convert_fusion
  40.5 0.1 fusion.38
  40.6 0.1 divide_convert_fusion.1
  40.7 0.1 fusion.37
  40.8 0.1 divide_convert_fusion.2
  41.0 0.1 fusion.36
  41.1 0.1 divide_convert_fusion.3
  41.2 0.3 fusion.29
  41.5 0.5 fusion.19
  42.0 0.3 fusion.28
  42.4 0.5 fusion.17
  42.8 0.3 fusion.27
  43.2 0.5 fusion.15
  43.7 0.3 fusion.26
  44.0 0.5 fusion.13
  44.5 0.1 fusion.35
  44.6 0.3 fusion.25
  45.0 0.5 fusion.11
  45.5 0.1 divide_convert_fusion.4
  45.6 1.3 %collective-permute-done.3 = bf16[1,1,128,640]{3,2,0,1:T(8,128)(2,1)S(1)} collective-permute-done((bf16[1,1,128,640]{3,2,0,1:T(8,128)(2,1)S(1)}, bf16[1,1,128,640]{3,2,0,1:T(8,128)(2,1)S(1)}, u32[]{:S(2)}, u32[]{:S(2)}) %collective-permute-start.3) | collective-permute-done | bytes 163872 | tf_op jit(solution)/shard_map/ppermute | solution.py:117
  47.0 1.3 %collective-permute-done.5 = bf16[1,1,1,128,640]{4,3,2,1,0:T(8,128)(2,1)S(1)} collective-permute-done((bf16[1,1,1,128,640]{4,3,2,1,0:T(8,128)(2,1)S(1)}, bf16[1,1,1,128,640]{4,3,2,1,0:T(8,128)(2,1)S(1)}, u32[]{:S(2)}, u32[]{:S(2)}) %collective-permute-start.5) | collective-permute-done | bytes 163872 | tf_op jit(solution)/shard_map/ppermute | solution.py:124
  48.3 0.3 convolution_dynamic-update-slice_fusion.4
  48.6 0.3 convolution_dynamic-update-slice_fusion.3
  48.9 0.3 convolution_dynamic-update-slice_fusion.2
  49.1 0.3 convolution_dynamic-update-slice_fusion.1
  49.4 0.3 convolution_dynamic-update-slice_fusion
  49.7 1.0 %add_convert_fusion = bf16[512,640]{1,0:T(8,128)(2,1)} fusion(f32[512,640]{1,0:T(8,128)S(1)} %constant_dynamic-update-slice_fusion, f32[512,640]{1,0:T(8,128)S(1)} %convolution_dynamic-update-slice_fusion), kind=kLoop, calls=%fused_computation.25 | loop fusion | flops 655360 | bytes 3276800 | tf_op jit(solution)/shard_map/convert_element_type | solution.py:165
  (41 shorter events, 0.5 us)
Async XLA Ops:
  0.0 12.0 %copy-start = (bf16[2,1024,640]{2,1,0:T(8,128)(2,1)S(1)}, bf16[2,1024,640]{2,1,0:T(8,128)(2,1)}, u32[]{:S(2)}) copy-start(bf16[2,1024,640]{2,1,0:T(8,128)(2,1)} %param.4) | copy-start | bytes 7864324
  0.0 2.7 %copy-start.2 = (s32[4,8]{1,0:T(4,128)S(1)}, s32[4,8]{1,0:T(4,128)}, u32[]{:S(2)}) copy-start(s32[4,8]{1,0:T(4,128)} %param.5) | copy-start | bytes 388
  0.0 14.6 %copy-start.1 = (bf16[512,640]{1,0:T(8,128)(2,1)S(1)}, bf16[512,640]{1,0:T(8,128)(2,1)}, u32[]{:S(2)}) copy-start(bf16[512,640]{1,0:T(8,128)(2,1)} %param.3) | copy-start | bytes 1966084
  3.3 6.9 %collective-permute-start = (s32[1]{0:T(128)}, s32[1]{0:T(128)}, u32[]{:S(2)}, u32[]{:S(2)}) collective-permute-start(s32[1]{0:T(128)} %dynamic_slice.18), channel_id=1, source_target_pairs={{0,8},{4,12},{8,0},{12,4},{1,9},{5,13},{9,1},{13,5},{2,10},{6,14},... | collective-permute-start | bytes 20 | tf_op jit(solution)/shard_map/ppermute | solution.py:79
  7.3 9.9 %collective-permute-start.2 = (bf16[2,512,640]{2,1,0:T(8,128)(2,1)}, bf16[2,512,640]{2,1,0:T(8,128)(2,1)}, u32[]{:S(2)}, u32[]{:S(2)}) collective-permute-start(bf16[2,512,640]{2,1,0:T(8,128)(2,1)} %constant_dynamic-slice_fusion), channel_id=1, source_target_pairs={{1,4},{5,8},{9,12},{4,1},{8,5},{12,9},{3,6},{7,10},{11,14},{6,3},{... | collective-permute-start | bytes 3932168 | tf_op jit(solution)/shard_map/ppermute | solution.py:28
  12.1 22.1 %collective-permute-start.1 = (bf16[1,1,128,640]{3,2,0,1:T(8,128)(2,1)S(1)}, bf16[1,1,128,640]{3,2,0,1:T(8,128)(2,1)S(1)}, u32[]{:S(2)}, u32[]{:S(2)}) collective-permute-start(bf16[1,1,128,640]{3,2,0,1:T(8,128)(2,1)S(1)} %get-tuple-element.110), channel_id=1, source_target_pairs={{8,0},{12,4},{0,8},{4,12},{9,1},{13,5},{1,9},{5,13},{10,2},{14,6},... | collective-permute-start | bytes 491528 | tf_op jit(solution)/shard_map/ppermute | solution.py:90
  34.2 4.3 %collective-permute-start.4 = (bf16[1,1,1,128,640]{4,3,2,1,0:T(8,128)(2,1)S(1)}, bf16[1,1,1,128,640]{4,3,2,1,0:T(8,128)(2,1)S(1)}, u32[]{:S(2)}, u32[]{:S(2)}) collective-permute-start(bf16[1,1,1,128,640]{4,3,2,1,0:T(8,128)(2,1)S(1)} %bitcast.160), channel_id=1, source_target_pairs={{0,1},{1,0},{2,3},{3,2},{4,5},{5,4},{6,7},{7,6},{8,9},{9,8},{10,11... | collective-permute-start | bytes 491528 | tf_op jit(solution)/shard_map/ppermute | solution.py:124
  34.6 12.3 %collective-permute-start.3 = (bf16[1,1,128,640]{3,2,0,1:T(8,128)(2,1)S(1)}, bf16[1,1,128,640]{3,2,0,1:T(8,128)(2,1)S(1)}, u32[]{:S(2)}, u32[]{:S(2)}) collective-permute-start(bf16[1,1,128,640]{3,2,0,1:T(8,128)(2,1)S(1)} %get-tuple-element.46), channel_id=1, source_target_pairs={{8,0},{12,4},{0,8},{4,12},{9,1},{13,5},{1,9},{5,13},{10,2},{14,6},... | collective-permute-start | bytes 491528 | tf_op jit(solution)/shard_map/ppermute | solution.py:117
  46.9 1.4 %collective-permute-start.5 = (bf16[1,1,1,128,640]{4,3,2,1,0:T(8,128)(2,1)S(1)}, bf16[1,1,1,128,640]{4,3,2,1,0:T(8,128)(2,1)S(1)}, u32[]{:S(2)}, u32[]{:S(2)}) collective-permute-start(bf16[1,1,1,128,640]{4,3,2,1,0:T(8,128)(2,1)S(1)} %bitcast.158), channel_id=1, source_target_pairs={{0,1},{1,0},{2,3},{3,2},{4,5},{5,4},{6,7},{7,6},{8,9},{9,8},{10,11... | collective-permute-start | bytes 491528 | tf_op jit(solution)/shard_map/ppermute | solution.py:124

commit v15 on v14

--- a/solution.py
+++ b/solution.py
@@ -157,12 +157,12 @@
         outputs.append((mixed, far_prob))
     values, outputs = lax.optimization_barrier((values, outputs))
     far_values = gather_reps(values)
-    near_part = jnp.concatenate([mixed for mixed, _ in outputs], axis=1)
-    far_part = []
+    total = jnp.concatenate([mixed for mixed, _ in outputs], axis=1)
     for head, (_, far_prob) in enumerate(outputs):
         cols = slice(head * HEAD_WIDTH, (head + 1) * HEAD_WIDTH)
-        far_part.append(jnp.dot(far_prob, far_values[:, cols], preferred_element_type=jnp.float32))
-    return (near_part + jnp.concatenate(far_part, axis=1)).astype(jnp.bfloat16)
+        far_part = jnp.dot(far_prob, far_values[:, cols], preferred_element_type=jnp.float32)
+        total = total.at[:, cols].add(far_part)
+    return total.astype(jnp.bfloat16)
 
 
 def solution(mesh):

time: 50.8 us -> 53.4 us (1.051)
  waiting for transfers between devices: 14.6 us -> 11.7 us
  other arithmetic: 6.64 us -> 9.27 us
  matrix products: 10.8 us -> 13.4 us
    ppermute x1, waiting for transfers between devices: 12 us -> 9.11 us  [per_device(): lax.ppermute(chosen[0][None], 'seq', back)]
    another operation x0 -> x4, other arithmetic: none -> 2.68 us
    dot_general x5, matrix products: 1.32 us -> 3.89 us  [per_device(): jnp.dot(far_prob, far_values[:, cols], preferred_element_type=jnp.float32)]
  transfers between devices with their start and end apart: 6 -> 6, of which waited for: 3 -> 3; matrix products, arithmetic and copies ran while one was open for 31% -> 35% of each run, Pallas kernels for 0% -> 0%
where the time goes in v15:
time: 53.4 us; the launch traced here: 53.2 us
  matrix products  13.4 us (25%)
  starting transfers between devices  12.5 us (23%)
  waiting for transfers between devices  11.7 us (22%)
  other arithmetic  9.27 us (17%)
  local copies, waits for them, and re-layouts  3.77 us (7%)
  between operations  2.49 us (5%)
    ppermute x1, waiting for transfers between devices, per_device(): lax.ppermute(chosen[0][None], 'seq', back)  9.11 us
    ppermute x1, starting transfers between devices, per_device(): wanted = lax.ppermute(phase[None], 'seq', pairs)[0]  4.05 us
    ppermute x1, starting transfers between devices, per_device(): lax.ppermute(chosen, 'seq', back)  3.89 us
    dot_general x5, matrix products, per_device(): jnp.dot(far_prob, far_values[:, cols], preferred_element_type=jnp.float32)  3.89 us
    another operation x4, other arithmetic  2.68 us
    dynamic_slice x1, local copies, waits for them, and re-layouts, halo_frame(): payload = lax.dynamic_slice_in_dim(key_value, start, frame_rows, 1)  2.65 us
    dot_general x5, matrix products, per_device(): jnp.dot(query_head, key_value[0, :, cols].T, preferred_element_type=jnp.f...  2.6 us
    ppermute x1, starting transfers between devices, per_device(): lax.ppermute(chosen[0][None], 'seq', back)  2.47 us
  transfers between devices with their start and end apart: 6, of which 3 were waited for; matrix products, arithmetic and copies ran while one was open for 35% of the time, Pallas kernels for 0%

profile of v15, /device:TPU:0, one launch (start us, length us, event | category | flops | bytes accessed | tf_op | source)
XLA Modules:
  0.0 53.2 jit_solution(553935790090330756)
XLA Ops:
  0.0 2.7 %constant_dynamic-slice_fusion.1 = bf16[2,512,640]{2,1,0:T(8,128)(2,1)} fusion(bf16[2,1024,640]{2,1,0:T(8,128)(2,1)} %param.14, s32[]{:T(128)S(6)} %select_n.103), kind=kLoop, calls=%fused_computation.180 | loop fusion | bytes 2621444 | tf_op jit(solution)/shard_map/dynamic_slice | solution.py:24
  2.7 0.6 %dynamic_slice.18 = s32[1]{0:T(128)} dynamic-slice(s32[8]{0:T(128)S(1)} %and_select_fusion.1, s32[]{:T(128)S(6)} %select_n.105), dynamic_slice_sizes={1} | dynamic-slice | bytes 12 | tf_op jit(solution)/shard_map/jit(dynamic_index_in_dim)/dynamic_slice | solution.py:78
  3.3 4.0 %collective-permute-start = (s32[1]{0:T(128)}, s32[1]{0:T(128)}, u32[]{:S(2)}, u32[]{:S(2)}) collective-permute-start(s32[1]{0:T(128)} %dynamic_slice.18), channel_id=1, source_target_pairs={{0,8},{4,12},{8,0},{12,4},{1,9},{5,13},{9,1},{13,5},{2,10},{6,14},... | collective-permute-start | bytes 20 | tf_op jit(solution)/shard_map/ppermute | solution.py:79
  7.3 1.7 %collective-permute-start.2 = (bf16[2,512,640]{2,1,0:T(8,128)(2,1)}, bf16[2,512,640]{2,1,0:T(8,128)(2,1)}, u32[]{:S(2)}, u32[]{:S(2)}) collective-permute-start(bf16[2,512,640]{2,1,0:T(8,128)(2,1)} %constant_dynamic-slice_fusion.1), channel_id=1, source_target_pairs={{1,4},{5,8},{9,12},{4,1},{8,5},{12,9},{3,6},{7,10},{11,14},{6,3},{... | collective-permute-start | bytes 3932168 | tf_op jit(solution)/shard_map/ppermute | solution.py:28
  9.0 0.6 %compare_reduce_fusion.3 = pred[]{:T(512)} fusion(), kind=kLoop, calls=%fused_computation.184 | loop fusion | flops 5 | bytes 1 | tf_op jit(solution)/shard_map/reduce.5
  9.7 0.7 %compare_reduce_fusion.2 = pred[]{:T(512)} fusion(), kind=kLoop, calls=%fused_computation.183 | loop fusion | flops 7 | bytes 1 | tf_op jit(solution)/shard_map/reduce.6
  10.4 0.6 %compare_reduce_fusion.1 = pred[]{:T(512)} fusion(), kind=kLoop, calls=%fused_computation.182 | loop fusion | flops 7 | bytes 1 | tf_op jit(solution)/shard_map/reduce.7
  11.0 0.7 %compare_reduce_fusion = pred[]{:T(512)} fusion(), kind=kLoop, calls=%fused_computation.181 | loop fusion | flops 7 | bytes 1 | tf_op jit(solution)/shard_map/reduce.8
  11.7 0.8 %subtract_reduce_fusion = s32[4]{0:T(128)S(1)} fusion(s32[4,8]{1,0:T(4,128)S(1)} %copy-done.2, s32[]{:T(128)S(6)} %select_n.105, s32[]{:T(128)} %bitcast.24, s32[]{:T(128)S(6)} %mul.171), kind=kLoop, calls=%fused_computation.178 | loop fusion | flops 8 | bytes 44 | tf_op jit(solution)/shard_map/sub | solution.py:85
  12.6 0.2 and_reduce_fusion
  15.0 2.5 %collective-permute-start.1 = (bf16[1,1,128,640]{3,2,0,1:T(8,128)(2,1)S(1)}, bf16[1,1,128,640]{3,2,0,1:T(8,128)(2,1)S(1)}, u32[]{:S(2)}, u32[]{:S(2)}) collective-permute-start(bf16[1,1,128,640]{3,2,0,1:T(8,128)(2,1)S(1)} %get-tuple-element.170), channel_id=1, source_target_pairs={{8,0},{12,4},{0,8},{4,12},{9,1},{13,5},{1,9},{5,13},{10,2},{14,6},... | collective-permute-start | bytes 491528 | tf_op jit(solution)/shard_map/ppermute | solution.py:90
  17.5 0.5 multiply_reduce_fusion.1
  18.0 0.5 multiply_reduce_fusion
  18.6 0.5 multiply_reduce_fusion.3
  19.1 0.5 multiply_reduce_fusion.2
  19.6 0.5 multiply_reduce_fusion.4
  20.1 0.1 broadcast_select_fusion
  20.3 0.3 fusion.118
  20.6 0.3 fusion.119
  20.9 0.3 fusion.116
  21.2 0.3 fusion.117
  21.5 0.3 fusion.115
  21.9 0.3 fusion.104
  22.2 0.9 %fusion.105 = (f32[512]{0:T(512)S(1)}, f32[512,1024]{1,0:T(8,128)S(1)}, f32[512]{0:T(512)S(1)}, f32[512,1024]{1,0:T(8,128)S(1)}) fusion(f32[512]{0:T(512)S(1)} %max.103, f32[512,1024]{1,0:T(8,128)S(1)} %get-tuple-element.188, f32[512]{0:T(512)S(1)} %max.101, f32[512,1024]{1,0:T(8,128)S(1)} %get-tuple-element.184), kind=kLoop, calls=%fused_computation.200 | loop fusion | flops 3144704 | bytes 8396800 | tf_op jit(solution)/shard_map/reduce_sum | solution.py:112
  23.1 0.3 fusion.108
  23.4 0.9 %fusion.109 = (f32[512]{0:T(512)S(1)}, f32[512,1024]{1,0:T(8,128)S(1)}, f32[512]{0:T(512)S(1)}, f32[512,1024]{1,0:T(8,128)S(1)}) fusion(f32[512]{0:T(512)S(1)} %max.99, f32[512,1024]{1,0:T(8,128)S(1)} %get-tuple-element.180, f32[512]{0:T(512)S(1)} %max.97, f32[512,1024]{1,0:T(8,128)S(1)} %get-tuple-element.176), kind=kLoop, calls=%fused_computation.204 | loop fusion | flops 3144704 | bytes 8396800 | tf_op jit(solution)/shard_map/reduce_sum | solution.py:112
  24.4 0.5 fusion.113
  24.9 0.2 fusion.112
  25.1 9.1 %collective-permute-done.1 = bf16[1,1,128,640]{3,2,0,1:T(8,128)(2,1)S(1)} collective-permute-done((bf16[1,1,128,640]{3,2,0,1:T(8,128)(2,1)S(1)}, bf16[1,1,128,640]{3,2,0,1:T(8,128)(2,1)S(1)}, u32[]{:S(2)}, u32[]{:S(2)}) %collective-permute-start.1) | collective-permute-done | bytes 163872 | tf_op jit(solution)/shard_map/ppermute | solution.py:90
  34.2 0.4 collective-permute-start.4
  34.6 3.9 %collective-permute-start.3 = (bf16[1,1,128,640]{3,2,0,1:T(8,128)(2,1)S(1)}, bf16[1,1,128,640]{3,2,0,1:T(8,128)(2,1)S(1)}, u32[]{:S(2)}, u32[]{:S(2)}) collective-permute-start(bf16[1,1,128,640]{3,2,0,1:T(8,128)(2,1)S(1)} %get-tuple-element.106), channel_id=1, source_target_pairs={{8,0},{12,4},{0,8},{4,12},{9,1},{13,5},{1,9},{5,13},{10,2},{14,6},... | collective-permute-start | bytes 491528 | tf_op jit(solution)/shard_map/ppermute | solution.py:117
  38.6 0.3 broadcast_in_dim.101
  38.9 0.3 fusion.124
  39.2 0.3 fusion.123
  39.4 0.3 fusion.122
  39.7 0.3 fusion.121
  40.0 0.3 fusion.120
  40.2 0.1 fusion.48
  40.4 0.1 divide_convert_fusion
  40.5 0.1 fusion.47
  40.7 0.1 fusion.46
  40.8 0.1 divide_convert_fusion.2
  41.0 0.1 fusion.45
  41.1 0.1 divide_convert_fusion.3
  41.2 0.3 fusion.38
  41.5 0.5 fusion.28
  42.0 0.3 fusion.37
  42.3 0.5 fusion.26
  42.8 0.3 fusion.36
  43.2 0.5 fusion.24
  43.7 0.3 fusion.35
  44.0 0.5 fusion.22
  44.5 0.1 fusion.44
  44.6 0.3 fusion.34
  45.0 0.5 fusion.20
  45.5 0.1 divide_convert_fusion.4
  45.6 1.3 %collective-permute-done.3 = bf16[1,1,128,640]{3,2,0,1:T(8,128)(2,1)S(1)} collective-permute-done((bf16[1,1,128,640]{3,2,0,1:T(8,128)(2,1)S(1)}, bf16[1,1,128,640]{3,2,0,1:T(8,128)(2,1)S(1)}, u32[]{:S(2)}, u32[]{:S(2)}) %collective-permute-start.3) | collective-permute-done | bytes 163872 | tf_op jit(solution)/shard_map/ppermute | solution.py:117
  47.0 1.3 %collective-permute-done.5 = bf16[1,1,1,128,640]{4,3,2,1,0:T(8,128)(2,1)S(1)} collective-permute-done((bf16[1,1,1,128,640]{4,3,2,1,0:T(8,128)(2,1)S(1)}, bf16[1,1,1,128,640]{4,3,2,1,0:T(8,128)(2,1)S(1)}, u32[]{:S(2)}, u32[]{:S(2)}) %collective-permute-start.5) | collective-permute-done | bytes 163872 | tf_op jit(solution)/shard_map/ppermute | solution.py:124
  48.3 0.9 %fusion.18 = f32[512,640]{1,0:T(8,128)S(1)} fusion(f32[512,640]{1,0:T(8,128)S(1)} %constant_dynamic-update-slice_fusion, f32[512,128]{1,0:T(8,128)S(1)} %fusion.20, bf16[512,256]{0,1:T(8,128)(2,1)S(1)} %divide_convert_fusion.4, pred[]{:T(512)} %compare_reduce_fusion.3, bf16[256,640]{1,0:T(8,128)(2,1)S(1)} %bitcast.148), kind=kOutput, calls=%fused_computation.49 | convolution fusion | flops 33685504 | bytes 851969 | tf_op jit(solution)/shard_map/dot_general | solution.py:163
  49.2 0.9 %fusion.16 = f32[512,640]{1,0:T(8,128)S(1)} fusion(f32[512,640]{1,0:T(8,128)S(1)} %fusion.18, bf16[512,256]{0,1:T(8,128)(2,1)S(1)} %divide_convert_fusion.3, pred[]{:T(512)} %compare_reduce_fusion.2, bf16[256,640]{1,0:T(8,128)(2,1)S(1)} %bitcast.149), kind=kOutput, calls=%fused_computation.46 | convolution fusion | flops 33685504 | bytes 851969 | tf_op jit(solution)/shard_map/dot_general | solution.py:163
  50.1 0.8 %fusion.14 = f32[512,640]{1,0:T(8,128)S(1)} fusion(f32[512,640]{1,0:T(8,128)S(1)} %fusion.16, bf16[512,256]{0,1:T(8,128)(2,1)S(1)} %divide_convert_fusion.2, pred[]{:T(512)} %compare_reduce_fusion.1, bf16[256,640]{1,0:T(8,128)(2,1)S(1)} %bitcast.150), kind=kOutput, calls=%fused_computation.43 | convolution fusion | flops 33685504 | bytes 851969 | tf_op jit(solution)/shard_map/dot_general | solution.py:163
  51.0 1.0 %fusion.12 = f32[512,640]{1,0:T(8,128)S(1)} fusion(f32[512,640]{1,0:T(8,128)S(1)} %fusion.14, bf16[512,256]{0,1:T(8,128)(2,1)S(1)} %divide_convert_fusion.1, pred[]{:T(512)} %compare_reduce_fusion, bf16[256,640]{1,0:T(8,128)(2,1)S(1)} %bitcast.151), kind=kOutput, calls=%fused_computation.40 | convolution fusion | flops 33685504 | bytes 851969 | tf_op jit(solution)/shard_map/dot_general | solution.py:163
  52.0 0.3 fusion.10
  52.3 0.9 %convert_element_type.67 = bf16[512,640]{1,0:T(8,128)(2,1)} convert(f32[512,640]{1,0:T(8,128)S(1)} %fusion.10) | non-fusion elementwise | flops 327680 | bytes 1966080 | tf_op jit(solution)/shard_map/convert_element_type | solution.py:165
  (45 shorter events, 0.7 us)
Async XLA Ops:
  0.0 15.0 %copy-start = (bf16[2,1024,640]{2,1,0:T(8,128)(2,1)S(1)}, bf16[2,1024,640]{2,1,0:T(8,128)(2,1)}, u32[]{:S(2)}) copy-start(bf16[2,1024,640]{2,1,0:T(8,128)(2,1)} %param.14) | copy-start | bytes 7864324
  0.0 2.7 %copy-start.2 = (s32[4,8]{1,0:T(4,128)S(1)}, s32[4,8]{1,0:T(4,128)}, u32[]{:S(2)}) copy-start(s32[4,8]{1,0:T(4,128)} %param.15) | copy-start | bytes 388
  0.0 17.5 %copy-start.1 = (bf16[512,640]{1,0:T(8,128)(2,1)S(1)}, bf16[512,640]{1,0:T(8,128)(2,1)}, u32[]{:S(2)}) copy-start(bf16[512,640]{1,0:T(8,128)(2,1)} %param.13) | copy-start | bytes 1966084
  3.3 9.6 %collective-permute-start = (s32[1]{0:T(128)}, s32[1]{0:T(128)}, u32[]{:S(2)}, u32[]{:S(2)}) collective-permute-start(s32[1]{0:T(128)} %dynamic_slice.18), channel_id=1, source_target_pairs={{0,8},{4,12},{8,0},{12,4},{1,9},{5,13},{9,1},{13,5},{2,10},{6,14},... | collective-permute-start | bytes 20 | tf_op jit(solution)/shard_map/ppermute | solution.py:79
  7.3 12.8 %collective-permute-start.2 = (bf16[2,512,640]{2,1,0:T(8,128)(2,1)}, bf16[2,512,640]{2,1,0:T(8,128)(2,1)}, u32[]{:S(2)}, u32[]{:S(2)}) collective-permute-start(bf16[2,512,640]{2,1,0:T(8,128)(2,1)} %constant_dynamic-slice_fusion.1), channel_id=1, source_target_pairs={{1,4},{5,8},{9,12},{4,1},{8,5},{12,9},{3,6},{7,10},{11,14},{6,3},{... | collective-permute-start | bytes 3932168 | tf_op jit(solution)/shard_map/ppermute | solution.py:28
  15.0 19.2 %collective-permute-start.1 = (bf16[1,1,128,640]{3,2,0,1:T(8,128)(2,1)S(1)}, bf16[1,1,128,640]{3,2,0,1:T(8,128)(2,1)S(1)}, u32[]{:S(2)}, u32[]{:S(2)}) collective-permute-start(bf16[1,1,128,640]{3,2,0,1:T(8,128)(2,1)S(1)} %get-tuple-element.170), channel_id=1, source_target_pairs={{8,0},{12,4},{0,8},{4,12},{9,1},{13,5},{1,9},{5,13},{10,2},{14,6},... | collective-permute-start | bytes 491528 | tf_op jit(solution)/shard_map/ppermute | solution.py:90
  34.2 4.3 %collective-permute-start.4 = (bf16[1,1,1,128,640]{4,3,2,1,0:T(8,128)(2,1)S(1)}, bf16[1,1,1,128,640]{4,3,2,1,0:T(8,128)(2,1)S(1)}, u32[]{:S(2)}, u32[]{:S(2)}) collective-permute-start(bf16[1,1,1,128,640]{4,3,2,1,0:T(8,128)(2,1)S(1)} %bitcast.160), channel_id=1, source_target_pairs={{0,1},{1,0},{2,3},{3,2},{4,5},{5,4},{6,7},{7,6},{8,9},{9,8},{10,11... | collective-permute-start | bytes 491528 | tf_op jit(solution)/shard_map/ppermute | solution.py:124
  34.6 12.3 %collective-permute-start.3 = (bf16[1,1,128,640]{3,2,0,1:T(8,128)(2,1)S(1)}, bf16[1,1,128,640]{3,2,0,1:T(8,128)(2,1)S(1)}, u32[]{:S(2)}, u32[]{:S(2)}) collective-permute-start(bf16[1,1,128,640]{3,2,0,1:T(8,128)(2,1)S(1)} %get-tuple-element.106), channel_id=1, source_target_pairs={{8,0},{12,4},{0,8},{4,12},{9,1},{13,5},{1,9},{5,13},{10,2},{14,6},... | collective-permute-start | bytes 491528 | tf_op jit(solution)/shard_map/ppermute | solution.py:117
  46.9 1.4 %collective-permute-start.5 = (bf16[1,1,1,128,640]{4,3,2,1,0:T(8,128)(2,1)S(1)}, bf16[1,1,1,128,640]{4,3,2,1,0:T(8,128)(2,1)S(1)}, u32[]{:S(2)}, u32[]{:S(2)}) collective-permute-start(bf16[1,1,1,128,640]{4,3,2,1,0:T(8,128)(2,1)S(1)} %bitcast.158), channel_id=1, source_target_pairs={{0,1},{1,0},{2,3},{3,2},{4,5},{5,4},{6,7},{7,6},{8,9},{9,8},{10,11... | collective-permute-start | bytes 491528 | tf_op jit(solution)/shard_map/ppermute | solution.py:124

commit v16 on v14

--- a/solution.py
+++ b/solution.py
@@ -25,7 +25,7 @@
     key_blocks, payload = lax.optimization_barrier((key_blocks, payload))
     pairs = [(s * rep_count + rep_count - 1, (s + 1) * rep_count) for s in range(seq_count - 1)]
     pairs += [(s * rep_count, (s - 1) * rep_count + rep_count - 1) for s in range(1, seq_count)]
-    return lax.ppermute(payload, ("seq", "rep"), pairs), key_blocks
+    return lax.ppermute(payload[0], ("seq", "rep"), pairs), payload[1], pairs, key_blocks
 
 
 def per_device(query, key_value, key_blocks):
@@ -48,11 +48,13 @@
     assert far_count % rep_count == 0
     far_share = far_count // rep_count
 
-    halo, key_blocks = halo_frame(key_value, key_blocks, frame_rows, seq_count, rep_count, rep_index)
+    halo_keys, halo_value_payload, halo_pairs, key_blocks = halo_frame(
+        key_value, key_blocks, frame_rows, seq_count, rep_count, rep_index
+    )
     halo_valid = ((rep_index == 0) & (slab_index > 0)) | (
         (rep_index == rep_count - 1) & (slab_index < seq_count - 1)
     )
-    halo = jnp.where(halo_valid, halo, jnp.zeros_like(halo))
+    halo_keys = jnp.where(halo_valid, halo_keys, jnp.zeros_like(halo_keys))
 
     phases = jnp.maximum(key_blocks[0], 0) % FAR_STRIDE
     stride_grid = key_value.reshape(2, far_count, FAR_STRIDE, MASK_BLOCK_SIZE, columns)
@@ -100,7 +102,7 @@
             * score_scale
         )
         halo_scores = (
-            jnp.dot(query_head, halo[0, :, cols].T, preferred_element_type=jnp.float32)
+            jnp.dot(query_head, halo_keys[:, cols].T, preferred_element_type=jnp.float32)
             * score_scale
         )
         halo_scores = jnp.where(halo_valid, halo_scores, -jnp.inf)
@@ -113,8 +115,11 @@
             halo_exp, axis=1, keepdims=True
         )
         near.append((near_top, own_exp, halo_exp, near_total))
-    received, near, later_values = lax.optimization_barrier((received, near, later_values))
+    received, near, later_values, halo_value_payload = lax.optimization_barrier(
+        (received, near, later_values, halo_value_payload)
+    )
     values = [lax.ppermute(chosen, "seq", back) for chosen, back in zip(later_values, backs)]
+    halo_values = lax.ppermute(halo_value_payload, ("seq", "rep"), halo_pairs)
 
     def gather_reps(pieces):
         mine = jnp.stack(pieces, 1)
@@ -153,9 +158,14 @@
         halo_prob = (halo_exp * near_scale).astype(jnp.bfloat16)
         far_prob = (far_exp / row_total).astype(jnp.bfloat16)
         mixed = jnp.dot(own_prob, key_value[1, :, cols], preferred_element_type=jnp.float32)
-        mixed = mixed + jnp.dot(halo_prob, halo[1, :, cols], preferred_element_type=jnp.float32)
-        outputs.append((mixed, far_prob))
-    values, outputs = lax.optimization_barrier((values, outputs))
+        outputs.append((mixed, far_prob, halo_prob))
+    values, halo_values, outputs = lax.optimization_barrier((values, halo_values, outputs))
+    halo_values = jnp.where(halo_valid, halo_values, jnp.zeros_like(halo_values))
+    outputs = [
+        (mixed + jnp.dot(halo_prob, halo_values[:, head * HEAD_WIDTH : (head + 1) * HEAD_WIDTH],
+                         preferred_element_type=jnp.float32), far_prob)
+        for head, (mixed, far_prob, halo_prob) in enumerate(outputs)
+    ]
     far_values = gather_reps(values)
     near_part = jnp.concatenate([mixed for mixed, _ in outputs], axis=1)
     far_part = []

time: 50.8 us -> 58.1 us (1.14)
  starting transfers between devices: 12.5 us -> 16.6 us
  local copies, waits for them, and re-layouts: 3.77 us -> 6.17 us
  other arithmetic: 6.64 us -> 7.38 us
    ppermute x1, waiting for transfers between devices: 1.34 us -> 9.35 us  [per_device(): lax.ppermute(chosen, 'seq', back)]
    ppermute x1, waiting for transfers between devices: 12 us -> 5.04 us  [per_device(): lax.ppermute(chosen[0][None], 'seq', back)]
    ppermute x1, starting transfers between devices: 3.89 us -> 7.51 us  [per_device(): lax.ppermute(chosen, 'seq', back)]
    squeeze x0 -> x1, local copies, waits for them, and re-layouts: none -> 2.48 us  [halo_frame(): payload[1]]
    ppermute x2, waiting for transfers between devices: 1.26 us -> 0.01 us  [gather_reps(): parts.append(lax.ppermute(mine, 'rep', shift))]
    ppermute x1 -> x2, starting transfers between devices: 1.74 us -> 2.36 us  [the longest x1 1.49 us: halo_frame(): lax.ppermute(payload[0], ('seq', 'rep'), pairs)]
    convert_element_type x0 -> x5, other arithmetic: none -> 0.6 us  [per_device(): halo_prob = (halo_exp * near_scale).astype(jnp.bfloat16)]
  transfers between devices with their start and end apart: 6 -> 7, of which waited for: 3 -> 2; matrix products, arithmetic and copies ran while one was open for 31% -> 33% of each run, Pallas kernels for 0% -> 0%
where the time goes in v16:
time: 58.1 us; the launch traced here: 57.8 us
  starting transfers between devices  16.6 us (29%)
  waiting for transfers between devices  14.4 us (25%)
  matrix products  10.8 us (19%)
  other arithmetic  7.38 us (13%)
  local copies, waits for them, and re-layouts  6.17 us (11%)
  between operations  2.36 us (4%)
    ppermute x1, waiting for transfers between devices, per_device(): lax.ppermute(chosen, 'seq', back)  9.35 us
    ppermute x1, starting transfers between devices, per_device(): lax.ppermute(chosen, 'seq', back)  7.51 us
    ppermute x1, waiting for transfers between devices, per_device(): lax.ppermute(chosen[0][None], 'seq', back)  5.04 us
    ppermute x1, starting transfers between devices, per_device(): wanted = lax.ppermute(phase[None], 'seq', pairs)[0]  4.04 us
    ppermute x1, starting transfers between devices, per_device(): lax.ppermute(chosen[0][None], 'seq', back)  2.72 us
    dynamic_slice x1, local copies, waits for them, and re-layouts, halo_frame(): payload = lax.dynamic_slice_in_dim(key_value, start, frame_rows, 1)  2.64 us
    dot_general x5, matrix products, per_device(): jnp.dot(query_head, key_value[0, :, cols].T, preferred_element_type=jnp.f...  2.59 us
    squeeze x1, local copies, waits for them, and re-layouts, halo_frame(): payload[1]  2.48 us
  transfers between devices with their start and end apart: 7, of which 2 were waited for; matrix products, arithmetic and copies ran while one was open for 33% of the time, Pallas kernels for 0%

profile of v16, /device:TPU:0, one launch (start us, length us, event | category | flops | bytes accessed | tf_op | source)
XLA Modules:
  0.0 57.8 jit_solution(11362395359220221461)
XLA Ops:
  0.0 2.6 %constant_dynamic-slice_fusion = bf16[2,512,640]{2,1,0:T(8,128)(2,1)} fusion(bf16[2,1024,640]{2,1,0:T(8,128)(2,1)} %param.4, s32[]{:T(128)S(6)} %select_n.107), kind=kLoop, calls=%fused_computation.171 | loop fusion | bytes 2621444 | tf_op jit(solution)/shard_map/dynamic_slice | solution.py:24
  2.7 0.6 %dynamic_slice.18 = s32[1]{0:T(128)} dynamic-slice(s32[8]{0:T(128)S(1)} %and_select_fusion.1, s32[]{:T(128)S(6)} %select_n.109), dynamic_slice_sizes={1} | dynamic-slice | bytes 12 | tf_op jit(solution)/shard_map/jit(dynamic_index_in_dim)/dynamic_slice | solution.py:80
  3.3 4.0 %collective-permute-start = (s32[1]{0:T(128)}, s32[1]{0:T(128)}, u32[]{:S(2)}, u32[]{:S(2)}) collective-permute-start(s32[1]{0:T(128)} %dynamic_slice.18), channel_id=1, source_target_pairs={{0,8},{4,12},{8,0},{12,4},{1,9},{5,13},{9,1},{13,5},{2,10},{6,14},... | collective-permute-start | bytes 20 | tf_op jit(solution)/shard_map/ppermute | solution.py:81
  7.3 2.5 %slice_bitcast_fusion = (bf16[512,640]{1,0:T(8,128)(2,1)}, bf16[512,640]{1,0:T(8,128)(2,1)}) fusion(bf16[2,512,640]{2,1,0:T(8,128)(2,1)} %constant_dynamic-slice_fusion), kind=kLoop, calls=%fused_computation.61 | loop fusion | bytes 2621440 | tf_op jit(solution)/shard_map/squeeze | solution.py:28
  9.8 1.5 %collective-permute-start.2 = (bf16[512,640]{1,0:T(8,128)(2,1)}, bf16[512,640]{1,0:T(8,128)(2,1)}, u32[]{:S(2)}, u32[]{:S(2)}) collective-permute-start(bf16[512,640]{1,0:T(8,128)(2,1)} %get-tuple-element.124), channel_id=1, source_target_pairs={{1,4},{5,8},{9,12},{4,1},{8,5},{12,9},{3,6},{7,10},{11,14},{6,3},{... | collective-permute-start | bytes 1966088 | tf_op jit(solution)/shard_map/ppermute | solution.py:28
  11.3 0.8 %subtract_reduce_fusion = s32[4]{0:T(128)S(1)} fusion(s32[4,8]{1,0:T(4,128)S(1)} %copy-done.3, s32[]{:T(128)S(6)} %select_n.109, s32[]{:T(128)} %bitcast.21, s32[]{:T(128)S(6)} %mul.171), kind=kLoop, calls=%fused_computation.163 | loop fusion | flops 8 | bytes 44 | tf_op jit(solution)/shard_map/sub | solution.py:87
  12.1 0.2 and_reduce_fusion
  14.3 0.5 multiply_reduce_fusion.1
  14.9 0.5 multiply_reduce_fusion
  15.4 0.5 multiply_reduce_fusion.3
  15.9 2.7 %collective-permute-start.1 = (bf16[1,1,128,640]{3,2,0,1:T(8,128)(2,1)S(1)}, bf16[1,1,128,640]{3,2,0,1:T(8,128)(2,1)S(1)}, u32[]{:S(2)}, u32[]{:S(2)}) collective-permute-start(bf16[1,1,128,640]{3,2,0,1:T(8,128)(2,1)S(1)} %get-tuple-element.126), channel_id=1, source_target_pairs={{8,0},{12,4},{0,8},{4,12},{9,1},{13,5},{1,9},{5,13},{10,2},{14,6},... | collective-permute-start | bytes 491528 | tf_op jit(solution)/shard_map/ppermute | solution.py:92
  18.7 0.5 multiply_reduce_fusion.2
  19.2 0.5 multiply_reduce_fusion.4
  19.8 0.3 fusion.109
  20.1 0.3 fusion.110
  20.4 0.3 fusion.107
  20.7 0.3 fusion.108
  21.1 0.3 fusion.106
  21.4 0.3 fusion.95
  21.7 0.9 %fusion.96 = (f32[512]{0:T(512)S(1)}, f32[512,1024]{1,0:T(8,128)S(1)}, f32[512]{0:T(512)S(1)}, f32[512,1024]{1,0:T(8,128)S(1)}) fusion(f32[512]{0:T(512)S(1)} %max.103, f32[512,1024]{1,0:T(8,128)S(1)} %get-tuple-element.144, f32[512]{0:T(512)S(1)} %max.101, f32[512,1024]{1,0:T(8,128)S(1)} %get-tuple-element.140), kind=kLoop, calls=%fused_computation.179 | loop fusion | flops 3144704 | bytes 8396800 | tf_op jit(solution)/shard_map/reduce_sum | solution.py:114
  22.6 0.3 fusion.99
  23.0 0.9 %fusion.100 = (f32[512]{0:T(512)S(1)}, f32[512,1024]{1,0:T(8,128)S(1)}, f32[512]{0:T(512)S(1)}, f32[512,1024]{1,0:T(8,128)S(1)}) fusion(f32[512]{0:T(512)S(1)} %max.99, f32[512,1024]{1,0:T(8,128)S(1)} %get-tuple-element.136, f32[512]{0:T(512)S(1)} %max.97, f32[512,1024]{1,0:T(8,128)S(1)} %get-tuple-element.132), kind=kLoop, calls=%fused_computation.183 | loop fusion | flops 3144704 | bytes 8396800 | tf_op jit(solution)/shard_map/reduce_sum | solution.py:114
  23.9 0.5 fusion.104
  24.4 0.2 fusion.103
  24.6 5.0 %collective-permute-done.1 = bf16[1,1,128,640]{3,2,0,1:T(8,128)(2,1)S(1)} collective-permute-done((bf16[1,1,128,640]{3,2,0,1:T(8,128)(2,1)S(1)}, bf16[1,1,128,640]{3,2,0,1:T(8,128)(2,1)S(1)}, u32[]{:S(2)}, u32[]{:S(2)}) %collective-permute-start.1) | collective-permute-done | bytes 163872 | tf_op jit(solution)/shard_map/ppermute | solution.py:92
  29.7 0.9 %collective-permute-start.4 = (bf16[512,640]{1,0:T(8,128)(2,1)S(1)}, bf16[512,640]{1,0:T(8,128)(2,1)S(1)}, u32[]{:S(2)}, u32[]{:S(2)}) collective-permute-start(bf16[512,640]{1,0:T(8,128)(2,1)S(1)} %copy-done.2), channel_id=1, source_target_pairs={{1,4},{5,8},{9,12},{4,1},{8,5},{12,9},{3,6},{7,10},{11,14},{6,3},{... | collective-permute-start | bytes 1966088 | tf_op jit(solution)/shard_map/ppermute | solution.py:122
  30.6 7.5 %collective-permute-start.3 = (bf16[1,1,128,640]{3,2,0,1:T(8,128)(2,1)S(1)}, bf16[1,1,128,640]{3,2,0,1:T(8,128)(2,1)S(1)}, u32[]{:S(2)}, u32[]{:S(2)}) collective-permute-start(bf16[1,1,128,640]{3,2,0,1:T(8,128)(2,1)S(1)} %get-tuple-element.53), channel_id=1, source_target_pairs={{8,0},{12,4},{0,8},{4,12},{9,1},{13,5},{1,9},{5,13},{10,2},{14,6},... | collective-permute-start | bytes 491528 | tf_op jit(solution)/shard_map/ppermute | solution.py:121
  38.2 0.3 broadcast_in_dim.97
  38.5 0.3 fusion.115
  38.8 0.3 fusion.114
  39.0 0.3 fusion.113
  39.3 0.3 fusion.112
  39.6 0.3 fusion.111
  39.8 0.1 fusion.24
  40.1 0.1 multiply_convert_fusion.10
  40.2 0.5 fusion.14
  40.7 0.1 fusion.23
  40.8 0.1 divide_convert_fusion.1
  40.9 0.1 multiply_convert_fusion.11
  41.0 0.5 fusion.13
  41.5 0.1 fusion.22
  41.7 0.1 divide_convert_fusion.2
  41.8 0.1 multiply_convert_fusion.12
  41.9 0.5 fusion.12
  42.4 0.1 fusion.21
  42.5 0.1 multiply_convert_fusion.13
  42.7 0.5 fusion.11
  43.2 0.1 fusion.20
  43.3 0.1 multiply_convert_fusion.14
  43.4 0.1 divide_convert_fusion.3
  43.5 0.5 fusion.10
  44.0 0.1 divide_convert_fusion.4
  44.1 9.3 %collective-permute-done.3 = bf16[1,1,128,640]{3,2,0,1:T(8,128)(2,1)S(1)} collective-permute-done((bf16[1,1,128,640]{3,2,0,1:T(8,128)(2,1)S(1)}, bf16[1,1,128,640]{3,2,0,1:T(8,128)(2,1)S(1)}, u32[]{:S(2)}, u32[]{:S(2)}) %collective-permute-start.3) | collective-permute-done | bytes 163872 | tf_op jit(solution)/shard_map/ppermute | solution.py:121
  53.5 0.3 fusion.50
  53.9 0.3 fusion.52
  54.2 0.3 fusion.54
  54.5 0.3 fusion.56
  54.9 0.3 fusion.58
  55.5 0.3 convolution_dynamic-update-slice_fusion.4
  55.7 0.3 convolution_dynamic-update-slice_fusion.3
  56.0 0.3 convolution_dynamic-update-slice_fusion.2
  56.3 0.3 convolution_dynamic-update-slice_fusion.1
  56.5 0.3 convolution_dynamic-update-slice_fusion
  56.8 1.0 %add_convert_fusion = bf16[512,640]{1,0:T(8,128)(2,1)} fusion(f32[512,640]{1,0:T(8,128)S(1)} %add_dynamic-update-slice_fusion, f32[512,640]{1,0:T(8,128)S(1)} %convolution_dynamic-update-slice_fusion), kind=kLoop, calls=%fused_computation.25 | loop fusion | flops 655360 | bytes 3276800 | tf_op jit(solution)/shard_map/convert_element_type | solution.py:175
  (52 shorter events, 0.9 us)
Async XLA Ops:
  0.0 2.6 %copy-start.3 = (s32[4,8]{1,0:T(4,128)S(1)}, s32[4,8]{1,0:T(4,128)}, u32[]{:S(2)}) copy-start(s32[4,8]{1,0:T(4,128)} %param.5) | copy-start | bytes 388
  0.0 14.3 %copy-start = (bf16[2,1024,640]{2,1,0:T(8,128)(2,1)S(1)}, bf16[2,1024,640]{2,1,0:T(8,128)(2,1)}, u32[]{:S(2)}) copy-start(bf16[2,1024,640]{2,1,0:T(8,128)(2,1)} %param.4) | copy-start | bytes 7864324
  2.6 11.7 %copy-start.1 = (bf16[512,640]{1,0:T(8,128)(2,1)S(1)}, bf16[512,640]{1,0:T(8,128)(2,1)}, u32[]{:S(2)}) copy-start(bf16[512,640]{1,0:T(8,128)(2,1)} %param.3) | copy-start | bytes 1966084
  3.3 9.1 %collective-permute-start = (s32[1]{0:T(128)}, s32[1]{0:T(128)}, u32[]{:S(2)}, u32[]{:S(2)}) collective-permute-start(s32[1]{0:T(128)} %dynamic_slice.18), channel_id=1, source_target_pairs={{0,8},{4,12},{8,0},{12,4},{1,9},{5,13},{9,1},{13,5},{2,10},{6,14},... | collective-permute-start | bytes 20 | tf_op jit(solution)/shard_map/ppermute | solution.py:81
  9.8 9.9 %collective-permute-start.2 = (bf16[512,640]{1,0:T(8,128)(2,1)}, bf16[512,640]{1,0:T(8,128)(2,1)}, u32[]{:S(2)}, u32[]{:S(2)}) collective-permute-start(bf16[512,640]{1,0:T(8,128)(2,1)} %get-tuple-element.124), channel_id=1, source_target_pairs={{1,4},{5,8},{9,12},{4,1},{8,5},{12,9},{3,6},{7,10},{11,14},{6,3},{... | collective-permute-start | bytes 1966088 | tf_op jit(solution)/shard_map/ppermute | solution.py:28
  15.9 13.7 %collective-permute-start.1 = (bf16[1,1,128,640]{3,2,0,1:T(8,128)(2,1)S(1)}, bf16[1,1,128,640]{3,2,0,1:T(8,128)(2,1)S(1)}, u32[]{:S(2)}, u32[]{:S(2)}) collective-permute-start(bf16[1,1,128,640]{3,2,0,1:T(8,128)(2,1)S(1)} %get-tuple-element.126), channel_id=1, source_target_pairs={{8,0},{12,4},{0,8},{4,12},{9,1},{13,5},{1,9},{5,13},{10,2},{14,6},... | collective-permute-start | bytes 491528 | tf_op jit(solution)/shard_map/ppermute | solution.py:92
  24.4 5.3 %copy-start.2 = (bf16[512,640]{1,0:T(8,128)(2,1)S(1)}, bf16[512,640]{1,0:T(8,128)(2,1)}, u32[]{:S(2)}) copy-start(bf16[512,640]{1,0:T(8,128)(2,1)} %get-tuple-element.54) | copy-start | bytes 1966084
  29.7 8.5 %collective-permute-start.5 = (bf16[1,1,1,128,640]{4,3,2,1,0:T(8,128)(2,1)S(1)}, bf16[1,1,1,128,640]{4,3,2,1,0:T(8,128)(2,1)S(1)}, u32[]{:S(2)}, u32[]{:S(2)}) collective-permute-start(bf16[1,1,1,128,640]{4,3,2,1,0:T(8,128)(2,1)S(1)} %bitcast.129), channel_id=1, source_target_pairs={{0,1},{1,0},{2,3},{3,2},{4,5},{5,4},{6,7},{7,6},{8,9},{9,8},{10,11... | collective-permute-start | bytes 491528 | tf_op jit(solution)/shard_map/ppermute | solution.py:129
  29.7 23.7 %collective-permute-start.4 = (bf16[512,640]{1,0:T(8,128)(2,1)S(1)}, bf16[512,640]{1,0:T(8,128)(2,1)S(1)}, u32[]{:S(2)}, u32[]{:S(2)}) collective-permute-start(bf16[512,640]{1,0:T(8,128)(2,1)S(1)} %copy-done.2), channel_id=1, source_target_pairs={{1,4},{5,8},{9,12},{4,1},{8,5},{12,9},{3,6},{7,10},{11,14},{6,3},{... | collective-permute-start | bytes 1966088 | tf_op jit(solution)/shard_map/ppermute | solution.py:122
  30.6 22.8 %collective-permute-start.3 = (bf16[1,1,128,640]{3,2,0,1:T(8,128)(2,1)S(1)}, bf16[1,1,128,640]{3,2,0,1:T(8,128)(2,1)S(1)}, u32[]{:S(2)}, u32[]{:S(2)}) collective-permute-start(bf16[1,1,128,640]{3,2,0,1:T(8,128)(2,1)S(1)} %get-tuple-element.53), channel_id=1, source_target_pairs={{8,0},{12,4},{0,8},{4,12},{9,1},{13,5},{1,9},{5,13},{10,2},{14,6},... | collective-permute-start | bytes 491528 | tf_op jit(solution)/shard_map/ppermute | solution.py:121
  53.4 2.0 %collective-permute-start.6 = (bf16[1,1,1,128,640]{4,3,2,1,0:T(8,128)(2,1)S(1)}, bf16[1,1,1,128,640]{4,3,2,1,0:T(8,128)(2,1)S(1)}, u32[]{:S(2)}, u32[]{:S(2)}) collective-permute-start(bf16[1,1,1,128,640]{4,3,2,1,0:T(8,128)(2,1)S(1)} %bitcast.127), channel_id=1, source_target_pairs={{0,1},{1,0},{2,3},{3,2},{4,5},{5,4},{6,7},{7,6},{8,9},{9,8},{10,11... | collective-permute-start | bytes 491528 | tf_op jit(solution)/shard_map/ppermute | solution.py:129

commit v17 on v14

--- a/solution.py
+++ b/solution.py
@@ -20,8 +20,9 @@
 
 def halo_frame(key_value, key_blocks, frame_rows, seq_count, rep_count, rep_index):
     slab_rows = key_value.shape[1]
-    start = jnp.where(rep_index == rep_count - 1, slab_rows - frame_rows, 0)
-    payload = lax.dynamic_slice_in_dim(key_value, start, frame_rows, 1)
+    last = lax.slice_in_dim(key_value, slab_rows - frame_rows, slab_rows, axis=1)
+    first = lax.slice_in_dim(key_value, 0, frame_rows, axis=1)
+    payload = jnp.where(rep_index == rep_count - 1, last, first)
     key_blocks, payload = lax.optimization_barrier((key_blocks, payload))
     pairs = [(s * rep_count + rep_count - 1, (s + 1) * rep_count) for s in range(seq_count - 1)]
     pairs += [(s * rep_count, (s - 1) * rep_count + rep_count - 1) for s in range(1, seq_count)]

time: 50.8 us -> 51.2 us (level)
  other arithmetic: 6.64 us -> 9.71 us
  local copies, waits for them, and re-layouts: 3.77 us -> 1.12 us
    select_n x0 -> x1, other arithmetic: none -> 3.07 us  [halo_frame(): payload = jnp.where(rep_index == rep_count - 1, last, first)]
    dynamic_slice x1 -> x0, local copies, waits for them, and re-layouts: 2.65 us -> none  [halo_frame(): payload = lax.dynamic_slice_in_dim(key_value, start, frame_rows, 1)]
where the time goes in v17:
time: 51.2 us; the launch traced here: 51.1 us
  waiting for transfers between devices  14.6 us (29%)
  starting transfers between devices  12.5 us (24%)
  matrix products  10.8 us (21%)
  other arithmetic  9.71 us (19%)
  between operations  2.26 us (4%)
  local copies, waits for them, and re-layouts  1.12 us (2%)
    ppermute x1, waiting for transfers between devices, per_device(): lax.ppermute(chosen[0][None], 'seq', back)  12 us
    ppermute x1, starting transfers between devices, per_device(): wanted = lax.ppermute(phase[None], 'seq', pairs)[0]  4.04 us
    ppermute x1, starting transfers between devices, per_device(): lax.ppermute(chosen, 'seq', back)  3.86 us
    select_n x1, other arithmetic, halo_frame(): payload = jnp.where(rep_index == rep_count - 1, last, first)  3.07 us
    dot_general x5, matrix products, per_device(): jnp.dot(query_head, key_value[0, :, cols].T, preferred_element_type=jnp.f...  2.6 us
    ppermute x1, starting transfers between devices, per_device(): lax.ppermute(chosen[0][None], 'seq', back)  2.48 us
    dot_general x5, matrix products, per_device(): jnp.dot(own_prob, key_value[1, :, cols], preferred_element_type=jnp.float32)  2.42 us
    reduce_sum x3, other arithmetic, per_device(): jnp.sum(own_exp, axis=1, keepdims=True)  2.32 us
  transfers between devices with their start and end apart: 6, of which 3 were waited for; matrix products, arithmetic and copies ran while one was open for 31% of the time, Pallas kernels for 0%

profile of v17, /device:TPU:0, one launch (start us, length us, event | category | flops | bytes accessed | tf_op | source)
XLA Modules:
  0.0 51.1 jit_solution(3817206373766903806)
XLA Ops:
  0.0 3.1 %slice_select_fusion = bf16[2,512,640]{2,1,0:T(8,128)(2,1)} fusion(bf16[2,1024,640]{2,1,0:T(8,128)(2,1)} %param.4, pred[]{:T(512)S(6)} %eq.28), kind=kLoop, calls=%fused_computation.26 | loop fusion | flops 655360 | bytes 3932161 | tf_op jit(solution)/shard_map/jit(_where)/select_n | solution.py:25
  3.1 0.6 %dynamic_slice.14 = s32[1]{0:T(128)} dynamic-slice(s32[8]{0:T(128)S(1)} %and_select_fusion.1, s32[]{:T(128)S(6)} %select_n.107), dynamic_slice_sizes={1} | dynamic-slice | bytes 12 | tf_op jit(solution)/shard_map/jit(dynamic_index_in_dim)/dynamic_slice | solution.py:79
  3.7 4.0 %collective-permute-start = (s32[1]{0:T(128)}, s32[1]{0:T(128)}, u32[]{:S(2)}, u32[]{:S(2)}) collective-permute-start(s32[1]{0:T(128)} %dynamic_slice.14), channel_id=1, source_target_pairs={{0,8},{4,12},{8,0},{12,4},{1,9},{5,13},{9,1},{13,5},{2,10},{6,14},... | collective-permute-start | bytes 20 | tf_op jit(solution)/shard_map/ppermute | solution.py:80
  7.7 1.7 %collective-permute-start.2 = (bf16[2,512,640]{2,1,0:T(8,128)(2,1)}, bf16[2,512,640]{2,1,0:T(8,128)(2,1)}, u32[]{:S(2)}, u32[]{:S(2)}) collective-permute-start(bf16[2,512,640]{2,1,0:T(8,128)(2,1)} %slice_select_fusion), channel_id=1, source_target_pairs={{1,4},{5,8},{9,12},{4,1},{8,5},{12,9},{3,6},{7,10},{11,14},{6,3},{... | collective-permute-start | bytes 3932168 | tf_op jit(solution)/shard_map/ppermute | solution.py:29
  9.5 0.8 %subtract_reduce_fusion = s32[4]{0:T(128)S(1)} fusion(s32[4,8]{1,0:T(4,128)S(1)} %copy-done.2, s32[]{:T(128)S(6)} %select_n.107, s32[]{:T(128)} %bitcast.24, s32[]{:T(128)S(6)} %mul.171), kind=kLoop, calls=%fused_computation.171 | loop fusion | flops 8 | bytes 44 | tf_op jit(solution)/shard_map/sub | solution.py:86
  10.3 0.2 and_reduce_fusion
  10.5 0.1 pad_add_fusion
  10.6 0.0 collective-permute-done
  12.5 2.5 %collective-permute-start.1 = (bf16[1,1,128,640]{3,2,0,1:T(8,128)(2,1)S(1)}, bf16[1,1,128,640]{3,2,0,1:T(8,128)(2,1)S(1)}, u32[]{:S(2)}, u32[]{:S(2)}) collective-permute-start(bf16[1,1,128,640]{3,2,0,1:T(8,128)(2,1)S(1)} %get-tuple-element.110), channel_id=1, source_target_pairs={{8,0},{12,4},{0,8},{4,12},{9,1},{13,5},{1,9},{5,13},{10,2},{14,6},... | collective-permute-start | bytes 491528 | tf_op jit(solution)/shard_map/ppermute | solution.py:91
  15.0 0.5 %multiply_reduce_fusion.1 = (f32[512]{0:T(512)S(1)}, f32[512,1024]{1,0:T(8,128)S(1)}) fusion(bf16[2,1024,640]{2,1,0:T(8,128)(2,1)S(1)} %copy-done, bf16[512,640]{1,0:T(8,128)(2,1)S(1)} %copy-done.1), kind=kOutput, calls=%fused_computation.11 | convolution fusion | flops 135265792 | bytes 2492416 | tf_op jit(solution)/shard_map/dot_general | solution.py:100
  15.5 0.5 %multiply_reduce_fusion = (f32[512]{0:T(512)S(1)}, f32[512,1024]{1,0:T(8,128)S(1)}) fusion(bf16[2,1024,640]{2,1,0:T(8,128)(2,1)S(1)} %copy-done, bf16[512,640]{1,0:T(8,128)(2,1)S(1)} %copy-done.1), kind=kOutput, calls=%fused_computation.10 | convolution fusion | flops 135265792 | bytes 2492416 | tf_op jit(solution)/shard_map/dot_general | solution.py:100
  16.1 0.5 %multiply_reduce_fusion.3 = (f32[512]{0:T(512)S(1)}, f32[512,1024]{1,0:T(8,128)S(1)}) fusion(bf16[2,1024,640]{2,1,0:T(8,128)(2,1)S(1)} %copy-done, bf16[512,640]{1,0:T(8,128)(2,1)S(1)} %copy-done.1), kind=kOutput, calls=%fused_computation.13 | convolution fusion | flops 135265792 | bytes 2492416 | tf_op jit(solution)/shard_map/dot_general | solution.py:100
  16.6 0.5 %multiply_reduce_fusion.2 = (f32[512]{0:T(512)S(1)}, f32[512,1024]{1,0:T(8,128)S(1)}) fusion(bf16[2,1024,640]{2,1,0:T(8,128)(2,1)S(1)} %copy-done, bf16[512,640]{1,0:T(8,128)(2,1)S(1)} %copy-done.1), kind=kOutput, calls=%fused_computation.12 | convolution fusion | flops 135265792 | bytes 2492416 | tf_op jit(solution)/shard_map/dot_general | solution.py:100
  17.1 0.5 %multiply_reduce_fusion.4 = (f32[512]{0:T(512)S(1)}, f32[512,1024]{1,0:T(8,128)S(1)}) fusion(bf16[2,1024,640]{2,1,0:T(8,128)(2,1)S(1)} %copy-done, bf16[512,640]{1,0:T(8,128)(2,1)S(1)} %copy-done.1), kind=kOutput, calls=%fused_computation.14 | convolution fusion | flops 135265792 | bytes 2492416 | tf_op jit(solution)/shard_map/dot_general | solution.py:100
  17.6 0.1 broadcast_select_fusion
  17.8 0.3 fusion.109
  18.1 0.3 fusion.110
  18.4 0.3 fusion.107
  18.7 0.3 fusion.108
  19.0 0.3 fusion.106
  19.4 0.3 fusion.95
  19.7 0.9 %fusion.96 = (f32[512]{0:T(512)S(1)}, f32[512,1024]{1,0:T(8,128)S(1)}, f32[512]{0:T(512)S(1)}, f32[512,1024]{1,0:T(8,128)S(1)}) fusion(f32[512]{0:T(512)S(1)} %max.103, f32[512,1024]{1,0:T(8,128)S(1)} %get-tuple-element.128, f32[512]{0:T(512)S(1)} %max.101, f32[512,1024]{1,0:T(8,128)S(1)} %get-tuple-element.124), kind=kLoop, calls=%fused_computation.186 | loop fusion | flops 3144704 | bytes 8396800 | tf_op jit(solution)/shard_map/reduce_sum | solution.py:113
  20.6 0.3 fusion.99
  20.9 0.9 %fusion.100 = (f32[512]{0:T(512)S(1)}, f32[512,1024]{1,0:T(8,128)S(1)}, f32[512]{0:T(512)S(1)}, f32[512,1024]{1,0:T(8,128)S(1)}) fusion(f32[512]{0:T(512)S(1)} %max.99, f32[512,1024]{1,0:T(8,128)S(1)} %get-tuple-element.120, f32[512]{0:T(512)S(1)} %max.97, f32[512,1024]{1,0:T(8,128)S(1)} %get-tuple-element.116), kind=kLoop, calls=%fused_computation.190 | loop fusion | flops 3144704 | bytes 8396800 | tf_op jit(solution)/shard_map/reduce_sum | solution.py:113
  21.9 0.5 %fusion.104 = (f32[512]{0:T(512)S(1)}, f32[512,1024]{1,0:T(8,128)S(1)}) fusion(f32[512]{0:T(512)S(1)} %max.95, f32[512,1024]{1,0:T(8,128)S(1)} %get-tuple-element.112), kind=kLoop, calls=%fused_computation.194 | loop fusion | flops 1572352 | bytes 4198400 | tf_op jit(solution)/shard_map/reduce_sum | solution.py:113
  22.4 0.2 fusion.103
  22.6 12.0 %collective-permute-done.1 = bf16[1,1,128,640]{3,2,0,1:T(8,128)(2,1)S(1)} collective-permute-done((bf16[1,1,128,640]{3,2,0,1:T(8,128)(2,1)S(1)}, bf16[1,1,128,640]{3,2,0,1:T(8,128)(2,1)S(1)}, u32[]{:S(2)}, u32[]{:S(2)}) %collective-permute-start.1) | collective-permute-done | bytes 163872 | tf_op jit(solution)/shard_map/ppermute | solution.py:91
  34.6 0.4 collective-permute-start.4
  35.0 0.1 compare_and_fusion
  35.1 3.9 %collective-permute-start.3 = (bf16[1,1,128,640]{3,2,0,1:T(8,128)(2,1)S(1)}, bf16[1,1,128,640]{3,2,0,1:T(8,128)(2,1)S(1)}, u32[]{:S(2)}, u32[]{:S(2)}) collective-permute-start(bf16[1,1,128,640]{3,2,0,1:T(8,128)(2,1)S(1)} %get-tuple-element.46), channel_id=1, source_target_pairs={{8,0},{12,4},{0,8},{4,12},{9,1},{13,5},{1,9},{5,13},{10,2},{14,6},... | collective-permute-start | bytes 491528 | tf_op jit(solution)/shard_map/ppermute | solution.py:118
  39.0 0.3 broadcast_in_dim.101
  39.3 0.3 fusion.115
  39.6 0.3 fusion.114
  39.9 0.3 fusion.113
  40.1 0.3 fusion.112
  40.4 0.3 fusion.111
  40.6 0.1 fusion.39
  40.8 0.1 divide_convert_fusion
  40.9 0.1 fusion.38
  41.0 0.1 divide_convert_fusion.1
  41.1 0.1 fusion.37
  41.3 0.1 divide_convert_fusion.2
  41.4 0.1 fusion.36
  41.5 0.1 divide_convert_fusion.3
  41.6 0.3 fusion.29
  41.9 0.5 fusion.19
  42.4 0.3 fusion.28
  42.7 0.5 fusion.17
  43.2 0.3 fusion.27
  43.6 0.5 fusion.15
  44.1 0.3 fusion.26
  44.4 0.5 fusion.13
  44.9 0.1 fusion.35
  45.0 0.3 fusion.25
  45.4 0.5 fusion.11
  45.8 0.1 divide_convert_fusion.4
  45.9 1.4 %collective-permute-done.3 = bf16[1,1,128,640]{3,2,0,1:T(8,128)(2,1)S(1)} collective-permute-done((bf16[1,1,128,640]{3,2,0,1:T(8,128)(2,1)S(1)}, bf16[1,1,128,640]{3,2,0,1:T(8,128)(2,1)S(1)}, u32[]{:S(2)}, u32[]{:S(2)}) %collective-permute-start.3) | collective-permute-done | bytes 163872 | tf_op jit(solution)/shard_map/ppermute | solution.py:118
  47.4 1.3 %collective-permute-done.5 = bf16[1,1,1,128,640]{4,3,2,1,0:T(8,128)(2,1)S(1)} collective-permute-done((bf16[1,1,1,128,640]{4,3,2,1,0:T(8,128)(2,1)S(1)}, bf16[1,1,1,128,640]{4,3,2,1,0:T(8,128)(2,1)S(1)}, u32[]{:S(2)}, u32[]{:S(2)}) %collective-permute-start.5) | collective-permute-done | bytes 163872 | tf_op jit(solution)/shard_map/ppermute | solution.py:125
  48.7 0.3 convolution_dynamic-update-slice_fusion.4
  49.0 0.3 convolution_dynamic-update-slice_fusion.3
  49.3 0.3 convolution_dynamic-update-slice_fusion.2
  49.5 0.3 convolution_dynamic-update-slice_fusion.1
  49.8 0.3 convolution_dynamic-update-slice_fusion
  50.1 1.0 %add_convert_fusion = bf16[512,640]{1,0:T(8,128)(2,1)} fusion(f32[512,640]{1,0:T(8,128)S(1)} %constant_dynamic-update-slice_fusion, f32[512,640]{1,0:T(8,128)S(1)} %convolution_dynamic-update-slice_fusion), kind=kLoop, calls=%fused_computation.25 | loop fusion | flops 655360 | bytes 3276800 | tf_op jit(solution)/shard_map/convert_element_type | solution.py:166
  (41 shorter events, 0.5 us)
Async XLA Ops:
  0.0 12.5 %copy-start = (bf16[2,1024,640]{2,1,0:T(8,128)(2,1)S(1)}, bf16[2,1024,640]{2,1,0:T(8,128)(2,1)}, u32[]{:S(2)}) copy-start(bf16[2,1024,640]{2,1,0:T(8,128)(2,1)} %param.4) | copy-start | bytes 7864324
  0.0 3.1 %copy-start.2 = (s32[4,8]{1,0:T(4,128)S(1)}, s32[4,8]{1,0:T(4,128)}, u32[]{:S(2)}) copy-start(s32[4,8]{1,0:T(4,128)} %param.5) | copy-start | bytes 388
  0.0 15.0 %copy-start.1 = (bf16[512,640]{1,0:T(8,128)(2,1)S(1)}, bf16[512,640]{1,0:T(8,128)(2,1)}, u32[]{:S(2)}) copy-start(bf16[512,640]{1,0:T(8,128)(2,1)} %param.3) | copy-start | bytes 1966084
  3.7 6.9 %collective-permute-start = (s32[1]{0:T(128)}, s32[1]{0:T(128)}, u32[]{:S(2)}, u32[]{:S(2)}) collective-permute-start(s32[1]{0:T(128)} %dynamic_slice.14), channel_id=1, source_target_pairs={{0,8},{4,12},{8,0},{12,4},{1,9},{5,13},{9,1},{13,5},{2,10},{6,14},... | collective-permute-start | bytes 20 | tf_op jit(solution)/shard_map/ppermute | solution.py:80
  7.7 9.9 %collective-permute-start.2 = (bf16[2,512,640]{2,1,0:T(8,128)(2,1)}, bf16[2,512,640]{2,1,0:T(8,128)(2,1)}, u32[]{:S(2)}, u32[]{:S(2)}) collective-permute-start(bf16[2,512,640]{2,1,0:T(8,128)(2,1)} %slice_select_fusion), channel_id=1, source_target_pairs={{1,4},{5,8},{9,12},{4,1},{8,5},{12,9},{3,6},{7,10},{11,14},{6,3},{... | collective-permute-start | bytes 3932168 | tf_op jit(solution)/shard_map/ppermute | solution.py:29
  12.5 22.1 %collective-permute-start.1 = (bf16[1,1,128,640]{3,2,0,1:T(8,128)(2,1)S(1)}, bf16[1,1,128,640]{3,2,0,1:T(8,128)(2,1)S(1)}, u32[]{:S(2)}, u32[]{:S(2)}) collective-permute-start(bf16[1,1,128,640]{3,2,0,1:T(8,128)(2,1)S(1)} %get-tuple-element.110), channel_id=1, source_target_pairs={{8,0},{12,4},{0,8},{4,12},{9,1},{13,5},{1,9},{5,13},{10,2},{14,6},... | collective-permute-start | bytes 491528 | tf_op jit(solution)/shard_map/ppermute | solution.py:91
  34.6 4.3 %collective-permute-start.4 = (bf16[1,1,1,128,640]{4,3,2,1,0:T(8,128)(2,1)S(1)}, bf16[1,1,1,128,640]{4,3,2,1,0:T(8,128)(2,1)S(1)}, u32[]{:S(2)}, u32[]{:S(2)}) collective-permute-start(bf16[1,1,1,128,640]{4,3,2,1,0:T(8,128)(2,1)S(1)} %bitcast.160), channel_id=1, source_target_pairs={{0,1},{1,0},{2,3},{3,2},{4,5},{5,4},{6,7},{7,6},{8,9},{9,8},{10,11... | collective-permute-start | bytes 491528 | tf_op jit(solution)/shard_map/ppermute | solution.py:125
  35.1 12.2 %collective-permute-start.3 = (bf16[1,1,128,640]{3,2,0,1:T(8,128)(2,1)S(1)}, bf16[1,1,128,640]{3,2,0,1:T(8,128)(2,1)S(1)}, u32[]{:S(2)}, u32[]{:S(2)}) collective-permute-start(bf16[1,1,128,640]{3,2,0,1:T(8,128)(2,1)S(1)} %get-tuple-element.46), channel_id=1, source_target_pairs={{8,0},{12,4},{0,8},{4,12},{9,1},{13,5},{1,9},{5,13},{10,2},{14,6},... | collective-permute-start | bytes 491528 | tf_op jit(solution)/shard_map/ppermute | solution.py:118
  47.3 1.4 %collective-permute-start.5 = (bf16[1,1,1,128,640]{4,3,2,1,0:T(8,128)(2,1)S(1)}, bf16[1,1,1,128,640]{4,3,2,1,0:T(8,128)(2,1)S(1)}, u32[]{:S(2)}, u32[]{:S(2)}) collective-permute-start(bf16[1,1,1,128,640]{4,3,2,1,0:T(8,128)(2,1)S(1)} %bitcast.158), channel_id=1, source_target_pairs={{0,1},{1,0},{2,3},{3,2},{4,5},{5,4},{6,7},{7,6},{8,9},{9,8},{10,11... | collective-permute-start | bytes 491528 | tf_op jit(solution)/shard_map/ppermute | solution.py:125

commit v18 on v17

--- a/solution.py
+++ b/solution.py
@@ -23,7 +23,8 @@
     last = lax.slice_in_dim(key_value, slab_rows - frame_rows, slab_rows, axis=1)
     first = lax.slice_in_dim(key_value, 0, frame_rows, axis=1)
     payload = jnp.where(rep_index == rep_count - 1, last, first)
-    key_blocks, payload = lax.optimization_barrier((key_blocks, payload))
+    payload = lax.optimization_barrier(payload)
+    key_blocks = key_blocks + jnp.sum(jnp.isnan(payload), dtype=jnp.int32)
     pairs = [(s * rep_count + rep_count - 1, (s + 1) * rep_count) for s in range(seq_count - 1)]
     pairs += [(s * rep_count, (s - 1) * rep_count + rep_count - 1) for s in range(1, seq_count)]
     return lax.ppermute(payload, ("seq", "rep"), pairs), key_blocks

time: 51.2 us -> 51.3 us (level)
  starting transfers between devices: 12.5 us -> 9.18 us
  other arithmetic: 9.71 us -> 13 us
    ppermute x1, waiting for transfers between devices: 0.01 us -> 10.8 us  [per_device(): wanted = lax.ppermute(phase[None], 'seq', pairs)[0]]
    ppermute x1, waiting for transfers between devices: 12 us -> 1.3 us  [per_device(): lax.ppermute(chosen[0][None], 'seq', back)]
    reduce_sum x0 -> x1, other arithmetic: none -> 2.63 us  [halo_frame(): key_blocks = key_blocks + jnp.sum(jnp.isnan(payload), dtype=jnp.int32)]
    ppermute x1, starting transfers between devices: 2.48 us -> 0.07 us  [per_device(): lax.ppermute(chosen[0][None], 'seq', back)]
    ppermute x1, starting transfers between devices: 3.86 us -> 2.21 us  [per_device(): lax.ppermute(chosen, 'seq', back)]
    add x0 -> x1, other arithmetic: none -> 0.65 us  [halo_frame(): key_blocks = key_blocks + jnp.sum(jnp.isnan(payload), dtype=jnp.int32)]
  transfers between devices with their start and end apart: 6 -> 6, of which waited for: 3 -> 4; matrix products, arithmetic and copies ran while one was open for 31% -> 39% of each run, Pallas kernels for 0% -> 0%
where the time goes in v18:
time: 51.3 us; the launch traced here: 51.1 us
  waiting for transfers between devices  14.5 us (28%)
  other arithmetic  13 us (25%)
  matrix products  11 us (21%)
  starting transfers between devices  9.18 us (18%)
  between operations  2.29 us (4%)
  local copies, waits for them, and re-layouts  1.12 us (2%)
    ppermute x1, waiting for transfers between devices, per_device(): wanted = lax.ppermute(phase[None], 'seq', pairs)[0]  10.8 us
    ppermute x1, starting transfers between devices, per_device(): wanted = lax.ppermute(phase[None], 'seq', pairs)[0]  4.23 us
    select_n x1, other arithmetic, halo_frame(): payload = jnp.where(rep_index == rep_count - 1, last, first)  3.06 us
    reduce_sum x1, other arithmetic, halo_frame(): key_blocks = key_blocks + jnp.sum(jnp.isnan(payload), dtype=jnp.int32)  2.63 us
    dot_general x5, matrix products, per_device(): jnp.dot(query_head, key_value[0, :, cols].T, preferred_element_type=jnp.f...  2.6 us
    dot_general x5, matrix products, per_device(): jnp.dot(own_prob, key_value[1, :, cols], preferred_element_type=jnp.float32)  2.43 us
    reduce_sum x3, other arithmetic, per_device(): jnp.sum(own_exp, axis=1, keepdims=True)  2.32 us
    ppermute x1, starting transfers between devices, per_device(): lax.ppermute(chosen, 'seq', back)  2.21 us
  transfers between devices with their start and end apart: 6, of which 4 were waited for; matrix products, arithmetic and copies ran while one was open for 39% of the time, Pallas kernels for 0%

profile of v18, /device:TPU:0, one launch (start us, length us, event | category | flops | bytes accessed | tf_op | source)
XLA Modules:
  0.0 51.1 jit_solution(16960879510180164939)
XLA Ops:
  0.0 3.1 %slice_select_fusion = bf16[2,512,640]{2,1,0:T(8,128)(2,1)} fusion(bf16[2,1024,640]{2,1,0:T(8,128)(2,1)} %param.4, pred[]{:T(512)S(6)} %eq.28), kind=kLoop, calls=%fused_computation.27 | loop fusion | flops 655360 | bytes 3932161 | tf_op jit(solution)/shard_map/jit(_where)/select_n | solution.py:25
  3.1 1.9 %collective-permute-start.2 = (bf16[2,512,640]{2,1,0:T(8,128)(2,1)}, bf16[2,512,640]{2,1,0:T(8,128)(2,1)}, u32[]{:S(2)}, u32[]{:S(2)}) collective-permute-start(bf16[2,512,640]{2,1,0:T(8,128)(2,1)} %slice_select_fusion), channel_id=1, source_target_pairs={{1,4},{5,8},{9,12},{4,1},{8,5},{12,9},{3,6},{7,10},{11,14},{6,3},{... | collective-permute-start | bytes 3932168 | tf_op jit(solution)/shard_map/ppermute | solution.py:30
  4.9 2.6 %convert_reduce_fusion = s32[]{:T(128)} fusion(bf16[2,512,640]{2,1,0:T(8,128)(2,1)} %slice_select_fusion), kind=kLoop, calls=%fused_computation | loop fusion | flops 1966079 | bytes 1310724 | tf_op jit(solution)/shard_map/reduce_sum | solution.py:27
  7.6 0.6 %broadcast_add_fusion = s32[4,8]{1,0:T(4,128)S(1)} fusion(s32[4,8]{1,0:T(4,128)S(1)} %copy-done.2, s32[]{:T(128)} %convert_reduce_fusion), kind=kLoop, calls=%fused_computation.180 | loop fusion | flops 32 | bytes 260 | tf_op jit(solution)/shard_map/add | solution.py:27
  8.2 0.6 %dynamic_slice.14 = s32[1]{0:T(128)} dynamic-slice(s32[8]{0:T(128)S(1)} %and_select_fusion.1, s32[]{:T(128)S(6)} %select_n.107), dynamic_slice_sizes={1} | dynamic-slice | bytes 12 | tf_op jit(solution)/shard_map/jit(dynamic_index_in_dim)/dynamic_slice | solution.py:80
  8.8 4.2 %collective-permute-start = (s32[1]{0:T(128)}, s32[1]{0:T(128)}, u32[]{:S(2)}, u32[]{:S(2)}) collective-permute-start(s32[1]{0:T(128)} %dynamic_slice.14), channel_id=1, source_target_pairs={{0,8},{4,12},{8,0},{12,4},{1,9},{5,13},{9,1},{13,5},{2,10},{6,14},... | collective-permute-start | bytes 20 | tf_op jit(solution)/shard_map/ppermute | solution.py:81
  13.1 0.9 %subtract_reduce_fusion = s32[4]{0:T(128)S(1)} fusion(s32[4,8]{1,0:T(4,128)S(1)} %broadcast_add_fusion, s32[]{:T(128)S(6)} %select_n.107, s32[]{:T(128)} %bitcast.24, s32[]{:T(128)S(6)} %mul.171), kind=kLoop, calls=%fused_computation.172 | loop fusion | flops 8 | bytes 44 | tf_op jit(solution)/shard_map/sub | solution.py:87
  13.9 0.2 and_reduce_fusion
  14.1 0.1 pad_add_fusion
  14.2 10.8 %collective-permute-done = s32[1]{0:T(128)} collective-permute-done((s32[1]{0:T(128)}, s32[1]{0:T(128)}, u32[]{:S(2)}, u32[]{:S(2)}) %collective-permute-start) | collective-permute-done | bytes 36 | tf_op jit(solution)/shard_map/ppermute | solution.py:81
  27.1 0.5 %multiply_reduce_fusion.1 = (f32[512]{0:T(512)S(1)}, f32[512,1024]{1,0:T(8,128)S(1)}) fusion(bf16[2,1024,640]{2,1,0:T(8,128)(2,1)S(1)} %copy-done, bf16[512,640]{1,0:T(8,128)(2,1)S(1)} %copy-done.1), kind=kOutput, calls=%fused_computation.12 | convolution fusion | flops 135265792 | bytes 2492416 | tf_op jit(solution)/shard_map/dot_general | solution.py:101
  27.6 0.5 %multiply_reduce_fusion = (f32[512]{0:T(512)S(1)}, f32[512,1024]{1,0:T(8,128)S(1)}) fusion(bf16[2,1024,640]{2,1,0:T(8,128)(2,1)S(1)} %copy-done, bf16[512,640]{1,0:T(8,128)(2,1)S(1)} %copy-done.1), kind=kOutput, calls=%fused_computation.11 | convolution fusion | flops 135265792 | bytes 2492416 | tf_op jit(solution)/shard_map/dot_general | solution.py:101
  28.1 0.5 %multiply_reduce_fusion.3 = (f32[512]{0:T(512)S(1)}, f32[512,1024]{1,0:T(8,128)S(1)}) fusion(bf16[2,1024,640]{2,1,0:T(8,128)(2,1)S(1)} %copy-done, bf16[512,640]{1,0:T(8,128)(2,1)S(1)} %copy-done.1), kind=kOutput, calls=%fused_computation.14 | convolution fusion | flops 135265792 | bytes 2492416 | tf_op jit(solution)/shard_map/dot_general | solution.py:101
  28.6 0.5 %multiply_reduce_fusion.2 = (f32[512]{0:T(512)S(1)}, f32[512,1024]{1,0:T(8,128)S(1)}) fusion(bf16[2,1024,640]{2,1,0:T(8,128)(2,1)S(1)} %copy-done, bf16[512,640]{1,0:T(8,128)(2,1)S(1)} %copy-done.1), kind=kOutput, calls=%fused_computation.13 | convolution fusion | flops 135265792 | bytes 2492416 | tf_op jit(solution)/shard_map/dot_general | solution.py:101
  29.1 0.5 %multiply_reduce_fusion.4 = (f32[512]{0:T(512)S(1)}, f32[512,1024]{1,0:T(8,128)S(1)}) fusion(bf16[2,1024,640]{2,1,0:T(8,128)(2,1)S(1)} %copy-done, bf16[512,640]{1,0:T(8,128)(2,1)S(1)} %copy-done.1), kind=kOutput, calls=%fused_computation.15 | convolution fusion | flops 135265792 | bytes 2492416 | tf_op jit(solution)/shard_map/dot_general | solution.py:101
  29.7 0.1 broadcast_select_fusion
  29.8 0.3 fusion.109
  30.1 0.3 fusion.110
  30.4 0.3 fusion.107
  30.8 0.3 fusion.108
  31.1 0.3 fusion.106
  31.4 0.3 fusion.95
  31.7 0.9 %fusion.96 = (f32[512]{0:T(512)S(1)}, f32[512,1024]{1,0:T(8,128)S(1)}, f32[512]{0:T(512)S(1)}, f32[512,1024]{1,0:T(8,128)S(1)}) fusion(f32[512]{0:T(512)S(1)} %max.103, f32[512,1024]{1,0:T(8,128)S(1)} %get-tuple-element.124, f32[512]{0:T(512)S(1)} %max.101, f32[512,1024]{1,0:T(8,128)S(1)} %get-tuple-element.120), kind=kLoop, calls=%fused_computation.188 | loop fusion | flops 3144704 | bytes 8396800 | tf_op jit(solution)/shard_map/reduce_sum | solution.py:114
  32.7 0.3 fusion.99
  33.0 0.9 %fusion.100 = (f32[512]{0:T(512)S(1)}, f32[512,1024]{1,0:T(8,128)S(1)}, f32[512]{0:T(512)S(1)}, f32[512,1024]{1,0:T(8,128)S(1)}) fusion(f32[512]{0:T(512)S(1)} %max.99, f32[512,1024]{1,0:T(8,128)S(1)} %get-tuple-element.116, f32[512]{0:T(512)S(1)} %max.97, f32[512,1024]{1,0:T(8,128)S(1)} %get-tuple-element.112), kind=kLoop, calls=%fused_computation.192 | loop fusion | flops 3144704 | bytes 8396800 | tf_op jit(solution)/shard_map/reduce_sum | solution.py:114
  33.9 0.5 %fusion.104 = (f32[512]{0:T(512)S(1)}, f32[512,1024]{1,0:T(8,128)S(1)}) fusion(f32[512]{0:T(512)S(1)} %max.95, f32[512,1024]{1,0:T(8,128)S(1)} %get-tuple-element.108), kind=kLoop, calls=%fused_computation.196 | loop fusion | flops 1572352 | bytes 4198400 | tf_op jit(solution)/shard_map/reduce_sum | solution.py:114
  34.4 0.2 fusion.103
  34.6 1.3 %collective-permute-done.1 = bf16[1,1,128,640]{3,2,0,1:T(8,128)(2,1)S(1)} collective-permute-done((bf16[1,1,128,640]{3,2,0,1:T(8,128)(2,1)S(1)}, bf16[1,1,128,640]{3,2,0,1:T(8,128)(2,1)S(1)}, u32[]{:S(2)}, u32[]{:S(2)}) %collective-permute-start.1) | collective-permute-done | bytes 163872 | tf_op jit(solution)/shard_map/ppermute | solution.py:92
  35.9 0.8 %collective-permute-start.4 = (bf16[1,1,1,128,640]{4,3,2,1,0:T(8,128)(2,1)S(1)}, bf16[1,1,1,128,640]{4,3,2,1,0:T(8,128)(2,1)S(1)}, u32[]{:S(2)}, u32[]{:S(2)}) collective-permute-start(bf16[1,1,1,128,640]{4,3,2,1,0:T(8,128)(2,1)S(1)} %bitcast.160), channel_id=1, source_target_pairs={{0,1},{1,0},{2,3},{3,2},{4,5},{5,4},{6,7},{7,6},{8,9},{9,8},{10,11... | collective-permute-start | bytes 491528 | tf_op jit(solution)/shard_map/ppermute | solution.py:126
  36.8 2.2 %collective-permute-start.3 = (bf16[1,1,128,640]{3,2,0,1:T(8,128)(2,1)S(1)}, bf16[1,1,128,640]{3,2,0,1:T(8,128)(2,1)S(1)}, u32[]{:S(2)}, u32[]{:S(2)}) collective-permute-start(bf16[1,1,128,640]{3,2,0,1:T(8,128)(2,1)S(1)} %get-tuple-element.42), channel_id=1, source_target_pairs={{8,0},{12,4},{0,8},{4,12},{9,1},{13,5},{1,9},{5,13},{10,2},{14,6},... | collective-permute-start | bytes 491528 | tf_op jit(solution)/shard_map/ppermute | solution.py:119
  39.1 0.3 broadcast_in_dim.101
  39.4 0.3 fusion.115
  39.7 0.3 fusion.114
  39.9 0.3 fusion.113
  40.2 0.3 fusion.112
  40.4 0.3 fusion.111
  40.7 0.1 fusion.39
  40.8 0.1 divide_convert_fusion
  41.0 0.1 fusion.38
  41.1 0.1 divide_convert_fusion.1
  41.2 0.1 fusion.37
  41.3 0.1 divide_convert_fusion.2
  41.4 0.1 fusion.36
  41.6 0.1 divide_convert_fusion.3
  41.7 0.3 fusion.29
  42.0 0.5 fusion.19
  42.5 0.3 fusion.28
  42.8 0.5 fusion.17
  43.3 0.3 fusion.27
  43.7 0.5 fusion.15
  44.1 0.5 fusion.26
  44.7 0.5 fusion.13
  45.2 0.1 fusion.35
  45.3 0.3 fusion.25
  45.6 0.5 fusion.11
  46.1 0.1 divide_convert_fusion.4
  46.2 1.2 %collective-permute-done.3 = bf16[1,1,128,640]{3,2,0,1:T(8,128)(2,1)S(1)} collective-permute-done((bf16[1,1,128,640]{3,2,0,1:T(8,128)(2,1)S(1)}, bf16[1,1,128,640]{3,2,0,1:T(8,128)(2,1)S(1)}, u32[]{:S(2)}, u32[]{:S(2)}) %collective-permute-start.3) | collective-permute-done | bytes 163872 | tf_op jit(solution)/shard_map/ppermute | solution.py:119
  47.5 1.3 %collective-permute-done.5 = bf16[1,1,1,128,640]{4,3,2,1,0:T(8,128)(2,1)S(1)} collective-permute-done((bf16[1,1,1,128,640]{4,3,2,1,0:T(8,128)(2,1)S(1)}, bf16[1,1,1,128,640]{4,3,2,1,0:T(8,128)(2,1)S(1)}, u32[]{:S(2)}, u32[]{:S(2)}) %collective-permute-start.5) | collective-permute-done | bytes 163872 | tf_op jit(solution)/shard_map/ppermute | solution.py:126
  48.8 0.3 convolution_dynamic-update-slice_fusion.4
  49.1 0.3 convolution_dynamic-update-slice_fusion.3
  49.4 0.3 convolution_dynamic-update-slice_fusion.2
  49.6 0.3 convolution_dynamic-update-slice_fusion.1
  49.9 0.3 convolution_dynamic-update-slice_fusion
  50.2 1.0 %add_convert_fusion = bf16[512,640]{1,0:T(8,128)(2,1)} fusion(f32[512,640]{1,0:T(8,128)S(1)} %constant_dynamic-update-slice_fusion, f32[512,640]{1,0:T(8,128)S(1)} %convolution_dynamic-update-slice_fusion), kind=kLoop, calls=%fused_computation.26 | loop fusion | flops 655360 | bytes 3276800 | tf_op jit(solution)/shard_map/convert_element_type | solution.py:167
  (43 shorter events, 0.6 us)
Async XLA Ops:
  0.0 7.6 %copy-start.2 = (s32[4,8]{1,0:T(4,128)S(1)}, s32[4,8]{1,0:T(4,128)}, u32[]{:S(2)}) copy-start(s32[4,8]{1,0:T(4,128)} %param.5) | copy-start | bytes 388
  0.0 26.9 %copy-start = (bf16[2,1024,640]{2,1,0:T(8,128)(2,1)S(1)}, bf16[2,1024,640]{2,1,0:T(8,128)(2,1)}, u32[]{:S(2)}) copy-start(bf16[2,1024,640]{2,1,0:T(8,128)(2,1)} %param.4) | copy-start | bytes 7864324
  3.1 24.0 %copy-start.1 = (bf16[512,640]{1,0:T(8,128)(2,1)S(1)}, bf16[512,640]{1,0:T(8,128)(2,1)}, u32[]{:S(2)}) copy-start(bf16[512,640]{1,0:T(8,128)(2,1)} %param.3) | copy-start | bytes 1966084
  3.1 26.6 %collective-permute-start.2 = (bf16[2,512,640]{2,1,0:T(8,128)(2,1)}, bf16[2,512,640]{2,1,0:T(8,128)(2,1)}, u32[]{:S(2)}, u32[]{:S(2)}) collective-permute-start(bf16[2,512,640]{2,1,0:T(8,128)(2,1)} %slice_select_fusion), channel_id=1, source_target_pairs={{1,4},{5,8},{9,12},{4,1},{8,5},{12,9},{3,6},{7,10},{11,14},{6,3},{... | collective-permute-start | bytes 3932168 | tf_op jit(solution)/shard_map/ppermute | solution.py:30
  8.8 16.2 %collective-permute-start = (s32[1]{0:T(128)}, s32[1]{0:T(128)}, u32[]{:S(2)}, u32[]{:S(2)}) collective-permute-start(s32[1]{0:T(128)} %dynamic_slice.14), channel_id=1, source_target_pairs={{0,8},{4,12},{8,0},{12,4},{1,9},{5,13},{9,1},{13,5},{2,10},{6,14},... | collective-permute-start | bytes 20 | tf_op jit(solution)/shard_map/ppermute | solution.py:81
  27.0 9.0 %collective-permute-start.1 = (bf16[1,1,128,640]{3,2,0,1:T(8,128)(2,1)S(1)}, bf16[1,1,128,640]{3,2,0,1:T(8,128)(2,1)S(1)}, u32[]{:S(2)}, u32[]{:S(2)}) collective-permute-start(bf16[1,1,128,640]{3,2,0,1:T(8,128)(2,1)S(1)} %get-tuple-element.106), channel_id=1, source_target_pairs={{8,0},{12,4},{0,8},{4,12},{9,1},{13,5},{1,9},{5,13},{10,2},{14,6},... | collective-permute-start | bytes 491528 | tf_op jit(solution)/shard_map/ppermute | solution.py:92
  35.9 3.1 %collective-permute-start.4 = (bf16[1,1,1,128,640]{4,3,2,1,0:T(8,128)(2,1)S(1)}, bf16[1,1,1,128,640]{4,3,2,1,0:T(8,128)(2,1)S(1)}, u32[]{:S(2)}, u32[]{:S(2)}) collective-permute-start(bf16[1,1,1,128,640]{4,3,2,1,0:T(8,128)(2,1)S(1)} %bitcast.160), channel_id=1, source_target_pairs={{0,1},{1,0},{2,3},{3,2},{4,5},{5,4},{6,7},{7,6},{8,9},{9,8},{10,11... | collective-permute-start | bytes 491528 | tf_op jit(solution)/shard_map/ppermute | solution.py:126
  36.8 10.6 %collective-permute-start.3 = (bf16[1,1,128,640]{3,2,0,1:T(8,128)(2,1)S(1)}, bf16[1,1,128,640]{3,2,0,1:T(8,128)(2,1)S(1)}, u32[]{:S(2)}, u32[]{:S(2)}) collective-permute-start(bf16[1,1,128,640]{3,2,0,1:T(8,128)(2,1)S(1)} %get-tuple-element.42), channel_id=1, source_target_pairs={{8,0},{12,4},{0,8},{4,12},{9,1},{13,5},{1,9},{5,13},{10,2},{14,6},... | collective-permute-start | bytes 491528 | tf_op jit(solution)/shard_map/ppermute | solution.py:119
  47.4 1.4 %collective-permute-start.5 = (bf16[1,1,1,128,640]{4,3,2,1,0:T(8,128)(2,1)S(1)}, bf16[1,1,1,128,640]{4,3,2,1,0:T(8,128)(2,1)S(1)}, u32[]{:S(2)}, u32[]{:S(2)}) collective-permute-start(bf16[1,1,1,128,640]{4,3,2,1,0:T(8,128)(2,1)S(1)} %bitcast.158), channel_id=1, source_target_pairs={{0,1},{1,0},{2,3},{3,2},{4,5},{5,4},{6,7},{7,6},{8,9},{9,8},{10,11... | collective-permute-start | bytes 491528 | tf_op jit(solution)/shard_map/ppermute | solution.py:126

commit v19 on v17

--- a/solution.py
+++ b/solution.py
@@ -23,7 +23,6 @@
     last = lax.slice_in_dim(key_value, slab_rows - frame_rows, slab_rows, axis=1)
     first = lax.slice_in_dim(key_value, 0, frame_rows, axis=1)
     payload = jnp.where(rep_index == rep_count - 1, last, first)
-    key_blocks, payload = lax.optimization_barrier((key_blocks, payload))
     pairs = [(s * rep_count + rep_count - 1, (s + 1) * rep_count) for s in range(seq_count - 1)]
     pairs += [(s * rep_count, (s - 1) * rep_count + rep_count - 1) for s in range(1, seq_count)]
     return lax.ppermute(payload, ("seq", "rep"), pairs), key_blocks

time: 51.2 us -> 52 us (1.016)
  other arithmetic: 9.71 us -> 10.4 us
    select_n x1, other arithmetic: 0.01 us -> 0.84 us  [per_device(): phases = jnp.maximum(key_blocks[0], 0) % FAR_STRIDE]
  transfers between devices with their start and end apart: 6 -> 6, of which waited for: 3 -> 3; matrix products, arithmetic and copies ran while one was open for 31% -> 36% of each run, Pallas kernels for 0% -> 0%
where the time goes in v19:
time: 52 us; the launch traced here: 51.8 us
  waiting for transfers between devices  14.6 us (28%)
  starting transfers between devices  12.5 us (24%)
  matrix products  10.8 us (21%)
  other arithmetic  10.4 us (20%)
  between operations  2.26 us (4%)
  local copies, waits for them, and re-layouts  1.11 us (2%)
    ppermute x1, waiting for transfers between devices, per_device(): lax.ppermute(chosen[0][None], 'seq', back)  12 us
    ppermute x1, starting transfers between devices, per_device(): wanted = lax.ppermute(phase[None], 'seq', pairs)[0]  4.04 us
    ppermute x1, starting transfers between devices, per_device(): lax.ppermute(chosen, 'seq', back)  3.86 us
    select_n x1, other arithmetic, halo_frame(): payload = jnp.where(rep_index == rep_count - 1, last, first)  2.98 us
    dot_general x5, matrix products, per_device(): jnp.dot(query_head, key_value[0, :, cols].T, preferred_element_type=jnp.f...  2.6 us
    ppermute x1, starting transfers between devices, per_device(): lax.ppermute(chosen[0][None], 'seq', back)  2.49 us
    dot_general x5, matrix products, per_device(): jnp.dot(own_prob, key_value[1, :, cols], preferred_element_type=jnp.float32)  2.44 us
    reduce_sum x3, other arithmetic, per_device(): jnp.sum(own_exp, axis=1, keepdims=True)  2.32 us
  transfers between devices with their start and end apart: 6, of which 3 were waited for; matrix products, arithmetic and copies ran while one was open for 36% of the time, Pallas kernels for 0%

profile of v19, /device:TPU:0, one launch (start us, length us, event | category | flops | bytes accessed | tf_op | source)
XLA Modules:
  0.0 51.8 jit_solution(14100350029540988243)
XLA Ops:
  0.0 0.8 %and_select_fusion.1 = s32[8]{0:T(128)S(1)} fusion(s32[4,8]{1,0:T(4,128)} %param.5), kind=kLoop, calls=%fused_computation.175 | loop fusion | flops 56 | bytes 64 | tf_op jit(solution)/shard_map/jit(remainder)/select_n | solution.py:57
  0.8 0.6 %dynamic_slice.14 = s32[1]{0:T(128)} dynamic-slice(s32[8]{0:T(128)S(1)} %and_select_fusion.1, s32[]{:T(128)S(6)} %select_n.105), dynamic_slice_sizes={1} | dynamic-slice | bytes 12 | tf_op jit(solution)/shard_map/jit(dynamic_index_in_dim)/dynamic_slice | solution.py:78
  1.4 4.0 %collective-permute-start = (s32[1]{0:T(128)}, s32[1]{0:T(128)}, u32[]{:S(2)}, u32[]{:S(2)}) collective-permute-start(s32[1]{0:T(128)} %dynamic_slice.14), channel_id=1, source_target_pairs={{0,8},{4,12},{8,0},{12,4},{1,9},{5,13},{9,1},{13,5},{2,10},{6,14},... | collective-permute-start | bytes 20 | tf_op jit(solution)/shard_map/ppermute | solution.py:79
  5.5 3.0 %slice_select_fusion = bf16[2,512,640]{2,1,0:T(8,128)(2,1)} fusion(bf16[2,1024,640]{2,1,0:T(8,128)(2,1)} %param.4, pred[]{:T(512)S(6)} %eq.29), kind=kLoop, calls=%fused_computation.26 | loop fusion | flops 655360 | bytes 3932161 | tf_op jit(solution)/shard_map/jit(_where)/select_n | solution.py:25
  8.4 1.7 %collective-permute-start.2 = (bf16[2,512,640]{2,1,0:T(8,128)(2,1)}, bf16[2,512,640]{2,1,0:T(8,128)(2,1)}, u32[]{:S(2)}, u32[]{:S(2)}) collective-permute-start(bf16[2,512,640]{2,1,0:T(8,128)(2,1)} %slice_select_fusion), channel_id=1, source_target_pairs={{1,4},{5,8},{9,12},{4,1},{8,5},{12,9},{3,6},{7,10},{11,14},{6,3},{... | collective-permute-start | bytes 3932168 | tf_op jit(solution)/shard_map/ppermute | solution.py:28
  10.2 0.8 %subtract_reduce_fusion = s32[4]{0:T(128)S(1)} fusion(s32[4,8]{1,0:T(4,128)S(1)} %copy-done.2, s32[]{:T(128)S(6)} %select_n.105, s32[]{:T(128)} %bitcast.24, s32[]{:T(128)S(6)} %mul.171), kind=kLoop, calls=%fused_computation.171 | loop fusion | flops 8 | bytes 44 | tf_op jit(solution)/shard_map/sub | solution.py:85
  11.0 0.2 and_reduce_fusion
  11.2 0.1 pad_add_fusion
  13.3 2.5 %collective-permute-start.1 = (bf16[1,1,128,640]{3,2,0,1:T(8,128)(2,1)S(1)}, bf16[1,1,128,640]{3,2,0,1:T(8,128)(2,1)S(1)}, u32[]{:S(2)}, u32[]{:S(2)}) collective-permute-start(bf16[1,1,128,640]{3,2,0,1:T(8,128)(2,1)S(1)} %get-tuple-element.106), channel_id=1, source_target_pairs={{8,0},{12,4},{0,8},{4,12},{9,1},{13,5},{1,9},{5,13},{10,2},{14,6},... | collective-permute-start | bytes 491528 | tf_op jit(solution)/shard_map/ppermute | solution.py:90
  15.8 0.5 multiply_reduce_fusion.1
  16.3 0.5 %multiply_reduce_fusion = (f32[512]{0:T(512)S(1)}, f32[512,1024]{1,0:T(8,128)S(1)}) fusion(bf16[2,1024,640]{2,1,0:T(8,128)(2,1)S(1)} %copy-done, bf16[512,640]{1,0:T(8,128)(2,1)S(1)} %copy-done.1), kind=kOutput, calls=%fused_computation.10 | convolution fusion | flops 135265792 | bytes 2492416 | tf_op jit(solution)/shard_map/dot_general | solution.py:99
  16.8 0.5 %multiply_reduce_fusion.3 = (f32[512]{0:T(512)S(1)}, f32[512,1024]{1,0:T(8,128)S(1)}) fusion(bf16[2,1024,640]{2,1,0:T(8,128)(2,1)S(1)} %copy-done, bf16[512,640]{1,0:T(8,128)(2,1)S(1)} %copy-done.1), kind=kOutput, calls=%fused_computation.13 | convolution fusion | flops 135265792 | bytes 2492416 | tf_op jit(solution)/shard_map/dot_general | solution.py:99
  17.3 0.5 %multiply_reduce_fusion.2 = (f32[512]{0:T(512)S(1)}, f32[512,1024]{1,0:T(8,128)S(1)}) fusion(bf16[2,1024,640]{2,1,0:T(8,128)(2,1)S(1)} %copy-done, bf16[512,640]{1,0:T(8,128)(2,1)S(1)} %copy-done.1), kind=kOutput, calls=%fused_computation.12 | convolution fusion | flops 135265792 | bytes 2492416 | tf_op jit(solution)/shard_map/dot_general | solution.py:99
  17.8 0.5 %multiply_reduce_fusion.4 = (f32[512]{0:T(512)S(1)}, f32[512,1024]{1,0:T(8,128)S(1)}) fusion(bf16[2,1024,640]{2,1,0:T(8,128)(2,1)S(1)} %copy-done, bf16[512,640]{1,0:T(8,128)(2,1)S(1)} %copy-done.1), kind=kOutput, calls=%fused_computation.14 | convolution fusion | flops 135265792 | bytes 2492416 | tf_op jit(solution)/shard_map/dot_general | solution.py:99
  18.4 0.1 broadcast_select_fusion
  18.5 0.3 fusion.109
  18.8 0.3 fusion.110
  19.1 0.3 fusion.107
  19.5 0.3 fusion.108
  19.8 0.3 fusion.106
  20.1 0.3 fusion.95
  20.4 0.9 %fusion.96 = (f32[512]{0:T(512)S(1)}, f32[512,1024]{1,0:T(8,128)S(1)}, f32[512]{0:T(512)S(1)}, f32[512,1024]{1,0:T(8,128)S(1)}) fusion(f32[512]{0:T(512)S(1)} %max.103, f32[512,1024]{1,0:T(8,128)S(1)} %get-tuple-element.124, f32[512]{0:T(512)S(1)} %max.101, f32[512,1024]{1,0:T(8,128)S(1)} %get-tuple-element.120), kind=kLoop, calls=%fused_computation.186 | loop fusion | flops 3144704 | bytes 8396800 | tf_op jit(solution)/shard_map/reduce_sum | solution.py:112
  21.4 0.3 fusion.99
  21.7 0.9 %fusion.100 = (f32[512]{0:T(512)S(1)}, f32[512,1024]{1,0:T(8,128)S(1)}, f32[512]{0:T(512)S(1)}, f32[512,1024]{1,0:T(8,128)S(1)}) fusion(f32[512]{0:T(512)S(1)} %max.99, f32[512,1024]{1,0:T(8,128)S(1)} %get-tuple-element.116, f32[512]{0:T(512)S(1)} %max.97, f32[512,1024]{1,0:T(8,128)S(1)} %get-tuple-element.112), kind=kLoop, calls=%fused_computation.190 | loop fusion | flops 3144704 | bytes 8396800 | tf_op jit(solution)/shard_map/reduce_sum | solution.py:112
  22.6 0.5 %fusion.104 = (f32[512]{0:T(512)S(1)}, f32[512,1024]{1,0:T(8,128)S(1)}) fusion(f32[512]{0:T(512)S(1)} %max.95, f32[512,1024]{1,0:T(8,128)S(1)} %get-tuple-element.108), kind=kLoop, calls=%fused_computation.194 | loop fusion | flops 1572352 | bytes 4198400 | tf_op jit(solution)/shard_map/reduce_sum | solution.py:112
  23.1 0.2 fusion.103
  23.3 12.0 %collective-permute-done.1 = bf16[1,1,128,640]{3,2,0,1:T(8,128)(2,1)S(1)} collective-permute-done((bf16[1,1,128,640]{3,2,0,1:T(8,128)(2,1)S(1)}, bf16[1,1,128,640]{3,2,0,1:T(8,128)(2,1)S(1)}, u32[]{:S(2)}, u32[]{:S(2)}) %collective-permute-start.1) | collective-permute-done | bytes 163872 | tf_op jit(solution)/shard_map/ppermute | solution.py:90
  35.3 0.4 collective-permute-start.4
  35.7 0.1 compare_and_fusion
  35.8 3.9 %collective-permute-start.3 = (bf16[1,1,128,640]{3,2,0,1:T(8,128)(2,1)S(1)}, bf16[1,1,128,640]{3,2,0,1:T(8,128)(2,1)S(1)}, u32[]{:S(2)}, u32[]{:S(2)}) collective-permute-start(bf16[1,1,128,640]{3,2,0,1:T(8,128)(2,1)S(1)} %get-tuple-element.42), channel_id=1, source_target_pairs={{8,0},{12,4},{0,8},{4,12},{9,1},{13,5},{1,9},{5,13},{10,2},{14,6},... | collective-permute-start | bytes 491528 | tf_op jit(solution)/shard_map/ppermute | solution.py:117
  39.7 0.3 broadcast_in_dim.101
  40.1 0.3 fusion.115
  40.3 0.3 fusion.114
  40.6 0.3 fusion.113
  40.8 0.3 fusion.112
  41.1 0.3 fusion.111
  41.4 0.1 fusion.39
  41.5 0.1 divide_convert_fusion
  41.6 0.1 fusion.38
  41.7 0.1 divide_convert_fusion.1
  41.8 0.1 fusion.37
  42.0 0.1 divide_convert_fusion.2
  42.1 0.1 fusion.36
  42.2 0.1 divide_convert_fusion.3
  42.3 0.3 fusion.29
  42.6 0.5 fusion.19
  43.2 0.3 fusion.28
  43.5 0.5 fusion.17
  44.0 0.3 fusion.27
  44.3 0.5 fusion.15
  44.8 0.3 fusion.26
  45.1 0.5 fusion.13
  45.6 0.1 fusion.35
  45.8 0.3 fusion.25
  46.1 0.5 fusion.11
  46.6 0.1 divide_convert_fusion.4
  46.7 1.3 %collective-permute-done.3 = bf16[1,1,128,640]{3,2,0,1:T(8,128)(2,1)S(1)} collective-permute-done((bf16[1,1,128,640]{3,2,0,1:T(8,128)(2,1)S(1)}, bf16[1,1,128,640]{3,2,0,1:T(8,128)(2,1)S(1)}, u32[]{:S(2)}, u32[]{:S(2)}) %collective-permute-start.3) | collective-permute-done | bytes 163872 | tf_op jit(solution)/shard_map/ppermute | solution.py:117
  48.2 1.3 %collective-permute-done.5 = bf16[1,1,1,128,640]{4,3,2,1,0:T(8,128)(2,1)S(1)} collective-permute-done((bf16[1,1,1,128,640]{4,3,2,1,0:T(8,128)(2,1)S(1)}, bf16[1,1,1,128,640]{4,3,2,1,0:T(8,128)(2,1)S(1)}, u32[]{:S(2)}, u32[]{:S(2)}) %collective-permute-start.5) | collective-permute-done | bytes 163872 | tf_op jit(solution)/shard_map/ppermute | solution.py:124
  49.5 0.3 convolution_dynamic-update-slice_fusion.4
  49.7 0.3 convolution_dynamic-update-slice_fusion.3
  50.0 0.3 convolution_dynamic-update-slice_fusion.2
  50.3 0.3 convolution_dynamic-update-slice_fusion.1
  50.6 0.3 convolution_dynamic-update-slice_fusion
  50.8 1.0 %add_convert_fusion = bf16[512,640]{1,0:T(8,128)(2,1)} fusion(f32[512,640]{1,0:T(8,128)S(1)} %constant_dynamic-update-slice_fusion, f32[512,640]{1,0:T(8,128)S(1)} %convolution_dynamic-update-slice_fusion), kind=kLoop, calls=%fused_computation.25 | loop fusion | flops 655360 | bytes 3276800 | tf_op jit(solution)/shard_map/convert_element_type | solution.py:165
  (41 shorter events, 0.4 us)
Async XLA Ops:
  0.0 10.2 %copy-start.2 = (s32[4,8]{1,0:T(4,128)S(1)}, s32[4,8]{1,0:T(4,128)}, u32[]{:S(2)}) copy-start(s32[4,8]{1,0:T(4,128)} %param.5) | copy-start | bytes 388
  0.0 13.2 %copy-start = (bf16[2,1024,640]{2,1,0:T(8,128)(2,1)S(1)}, bf16[2,1024,640]{2,1,0:T(8,128)(2,1)}, u32[]{:S(2)}) copy-start(bf16[2,1024,640]{2,1,0:T(8,128)(2,1)} %param.4) | copy-start | bytes 7864324
  1.4 9.9 %collective-permute-start = (s32[1]{0:T(128)}, s32[1]{0:T(128)}, u32[]{:S(2)}, u32[]{:S(2)}) collective-permute-start(s32[1]{0:T(128)} %dynamic_slice.14), channel_id=1, source_target_pairs={{0,8},{4,12},{8,0},{12,4},{1,9},{5,13},{9,1},{13,5},{2,10},{6,14},... | collective-permute-start | bytes 20 | tf_op jit(solution)/shard_map/ppermute | solution.py:79
  5.5 10.3 %copy-start.1 = (bf16[512,640]{1,0:T(8,128)(2,1)S(1)}, bf16[512,640]{1,0:T(8,128)(2,1)}, u32[]{:S(2)}) copy-start(bf16[512,640]{1,0:T(8,128)(2,1)} %param.3) | copy-start | bytes 1966084
  8.4 9.9 %collective-permute-start.2 = (bf16[2,512,640]{2,1,0:T(8,128)(2,1)}, bf16[2,512,640]{2,1,0:T(8,128)(2,1)}, u32[]{:S(2)}, u32[]{:S(2)}) collective-permute-start(bf16[2,512,640]{2,1,0:T(8,128)(2,1)} %slice_select_fusion), channel_id=1, source_target_pairs={{1,4},{5,8},{9,12},{4,1},{8,5},{12,9},{3,6},{7,10},{11,14},{6,3},{... | collective-permute-start | bytes 3932168 | tf_op jit(solution)/shard_map/ppermute | solution.py:28
  13.3 22.1 %collective-permute-start.1 = (bf16[1,1,128,640]{3,2,0,1:T(8,128)(2,1)S(1)}, bf16[1,1,128,640]{3,2,0,1:T(8,128)(2,1)S(1)}, u32[]{:S(2)}, u32[]{:S(2)}) collective-permute-start(bf16[1,1,128,640]{3,2,0,1:T(8,128)(2,1)S(1)} %get-tuple-element.106), channel_id=1, source_target_pairs={{8,0},{12,4},{0,8},{4,12},{9,1},{13,5},{1,9},{5,13},{10,2},{14,6},... | collective-permute-start | bytes 491528 | tf_op jit(solution)/shard_map/ppermute | solution.py:90
  35.3 4.3 %collective-permute-start.4 = (bf16[1,1,1,128,640]{4,3,2,1,0:T(8,128)(2,1)S(1)}, bf16[1,1,1,128,640]{4,3,2,1,0:T(8,128)(2,1)S(1)}, u32[]{:S(2)}, u32[]{:S(2)}) collective-permute-start(bf16[1,1,1,128,640]{4,3,2,1,0:T(8,128)(2,1)S(1)} %bitcast.160), channel_id=1, source_target_pairs={{0,1},{1,0},{2,3},{3,2},{4,5},{5,4},{6,7},{7,6},{8,9},{9,8},{10,11... | collective-permute-start | bytes 491528 | tf_op jit(solution)/shard_map/ppermute | solution.py:124
  35.8 12.2 %collective-permute-start.3 = (bf16[1,1,128,640]{3,2,0,1:T(8,128)(2,1)S(1)}, bf16[1,1,128,640]{3,2,0,1:T(8,128)(2,1)S(1)}, u32[]{:S(2)}, u32[]{:S(2)}) collective-permute-start(bf16[1,1,128,640]{3,2,0,1:T(8,128)(2,1)S(1)} %get-tuple-element.42), channel_id=1, source_target_pairs={{8,0},{12,4},{0,8},{4,12},{9,1},{13,5},{1,9},{5,13},{10,2},{14,6},... | collective-permute-start | bytes 491528 | tf_op jit(solution)/shard_map/ppermute | solution.py:117
  48.0 1.4 %collective-permute-start.5 = (bf16[1,1,1,128,640]{4,3,2,1,0:T(8,128)(2,1)S(1)}, bf16[1,1,1,128,640]{4,3,2,1,0:T(8,128)(2,1)S(1)}, u32[]{:S(2)}, u32[]{:S(2)}) collective-permute-start(bf16[1,1,1,128,640]{4,3,2,1,0:T(8,128)(2,1)S(1)} %bitcast.158), channel_id=1, source_target_pairs={{0,1},{1,0},{2,3},{3,2},{4,5},{5,4},{6,7},{7,6},{8,9},{9,8},{10,11... | collective-permute-start | bytes 491528 | tf_op jit(solution)/shard_map/ppermute | solution.py:124
